TPU v7x, 32 devices: a whole 2x2x4 slice. The times are simulated.
32 devices in a mesh: groups: 2 (over x), dp: 4 (over y, core), tensor: 4 (over z).
Axes of the slice: x: 2, y: 2, z: 4, core: 2. Of those that a mesh axis runs over, the one named last changes fastest.
Arguments:
- queries: bfloat16 [64, 64, 8192], P(('groups', 'dp'), None, 'tensor'), parts along dimension 0, may hold values from -5 to 5
- suffix_kv: bfloat16 [64, 2, 64, 1024], P(('groups', 'dp'), None, None, 'tensor'), parts along dimension 0, may hold values from -5 to 5
- out_grad: bfloat16 [64, 64, 8192], P(('groups', 'dp'), None, 'tensor'), parts along dimension 0, may hold values from -12 to 12
- prefix_kv: bfloat16 [8, 2, 448, 1024], P(('groups', 'dp'), None, None, 'tensor'), parts along dimension 0, may hold values from -5 to 5
- logratio: float32 [64], P(('groups', 'dp')), parts along dimension 0, may hold values from -8 to 8
- pair_slots: int32 [32, 2], P(('groups', 'dp')), parts along dimension 0, may hold values from 0 to 7, as said below
- pair_goal: int32 [32, 1], P(('groups', 'dp')), parts along dimension 0, may hold values from 0 to 3, as said below
- prefix_len: int32 [8], P('groups'), parts along dimension 0, may hold values from 1 to 448, 896 in all
Outputs:
- query_grad: bfloat16 [64, 64, 8192], P(('groups', 'dp'), None, 'tensor'), parts along dimension 0
- suffix_kv_grad: bfloat16 [64, 2, 64, 1024], P(('groups', 'dp'), None, None, 'tensor'), parts along dimension 0
- prefix_kv_grad: bfloat16 [8, 2, 448, 1024], P(('groups', 'dp'), None, None, 'tensor'), parts along dimension 0
There are 2 independent parts, one for each index of `groups`. A program takes and returns all parts, laid end to end along the dimension named above; each array names one. Nothing has to cross between parts.
Inputs may be any that keep to these rules, and one draw needn't show every extreme that they name: `pair_slots`: within the 4 rows of one owner, the two columns together name each of that owner's 8 suffixes exactly once. `pair_goal`: within the 4 rows of one owner no goal appears twice; in every draw one goal receives exactly one pair from every owner. `prefix_len`: the lengths sum to 896.
All inputs are finite; a program needn't handle non-finite values.
Results may differ from a plain program's by a relative error of at most 0.007.
Values may be sent and summed in bfloat16 or wider, within the bound.
No kernel may reach another device: no remote copies, remote signals or barrier semaphores. Data moves between devices by JAX's collectives and lax.ppermute only.
A program may use at most 128 MiB of HBM per device.

v0:
```python
import jax
import jax.numpy as jnp
from jax import lax
from jax.sharding import PartitionSpec as P

HD = 128


dpo_beta = 0.5


def attend(query, keys_own, values_own, cotangent, keys_pre, values_pre, length, score_scale):
    all_keys = jnp.concatenate([keys_pre, keys_own], 0)
    all_values = jnp.concatenate([values_pre, values_own], 0)
    scores = (
        jnp.einsum("tkgd,skd->kgts", query, all_keys, preferred_element_type=jnp.float32)
        * score_scale
    )
    prefix_rows = keys_pre.shape[0]
    key_index = jnp.arange(all_keys.shape[0])[None, :]
    query_index = jnp.arange(query.shape[0])[:, None]
    allowed = jnp.where(
        key_index < prefix_rows, key_index < length, key_index - prefix_rows <= query_index
    )
    scores = jnp.where(allowed, scores, -1e30)
    row_max = jnp.max(scores, -1, keepdims=True)
    raised = jnp.exp(scores - row_max)
    probability = raised / jnp.sum(raised, -1, keepdims=True)
    probability_low = probability.astype(jnp.bfloat16)
    output = jnp.einsum(
        "kgts,skd->tkgd", probability_low, all_values, preferred_element_type=jnp.float32
    )
    row_dot = jnp.einsum("tkgd,tkgd->kgt", cotangent.astype(jnp.float32), output)
    grad_prob = jnp.einsum(
        "tkgd,skd->kgts", cotangent, all_values, preferred_element_type=jnp.float32
    )
    grad_score = (probability * (grad_prob - row_dot[..., None])).astype(jnp.bfloat16)
    grad_query = (
        score_scale
        * jnp.einsum("kgts,skd->tkgd", grad_score, all_keys, preferred_element_type=jnp.float32)
    ).astype(jnp.bfloat16)
    grad_keys = score_scale * jnp.einsum(
        "kgts,tkgd->skd", grad_score, query, preferred_element_type=jnp.float32
    )
    grad_values = jnp.einsum(
        "kgts,tkgd->skd", probability_low, cotangent, preferred_element_type=jnp.float32
    )
    return (grad_query, grad_keys, grad_values)


def shards(queries, suffix_kv, out_grad, prefix_kv, logratio, pair_slots, pair_goal, prefix_len):
    suffix_count = queries.shape[0]
    seq_rows = queries.shape[1]
    head_size = HD
    kv_width = suffix_kv.shape[-1]
    kv_local = kv_width // head_size
    group_size = queries.shape[2] // kv_width
    prefix_rows = prefix_kv.shape[2]
    score_scale = head_size ** (-0.5)
    chosen = pair_slots[:, 0]
    rejected = pair_slots[:, 1]
    pair_goals = pair_goal[:, 0]
    positions = jnp.arange(suffix_count)
    pick_chosen = chosen[:, None] == positions[None, :]
    pick_rejected = rejected[:, None] == positions[None, :]
    ratio_chosen = jnp.sum(jnp.where(pick_chosen, logratio[None, :], 0.0), 1)
    ratio_rejected = jnp.sum(jnp.where(pick_rejected, logratio[None, :], 0.0), 1)
    weight = dpo_beta * jax.nn.sigmoid(-dpo_beta * (ratio_chosen - ratio_rejected))
    coefficient = jnp.sum(
        jnp.where(pick_rejected, weight[:, None], 0.0)
        - jnp.where(pick_chosen, weight[:, None], 0.0),
        0,
    )
    cotangent = (coefficient[:, None, None] * out_grad.astype(jnp.float32)).astype(jnp.bfloat16)

    def one_suffix(one_query, one_kv, one_cot, keys_pre, values_pre, length):
        grad_query, grad_keys, grad_values = attend(
            one_query.reshape(seq_rows, kv_local, group_size, head_size),
            one_kv[0].reshape(seq_rows, kv_local, head_size),
            one_kv[1].reshape(seq_rows, kv_local, head_size),
            one_cot.reshape(seq_rows, kv_local, group_size, head_size),
            keys_pre,
            values_pre,
            length,
            score_scale,
        )
        prefix_part = jnp.stack([grad_keys[:prefix_rows], grad_values[:prefix_rows]], 0).reshape(
            2, prefix_rows, kv_width
        )
        own_part = (
            jnp.stack([grad_keys[prefix_rows:], grad_values[prefix_rows:]], 0)
            .astype(jnp.bfloat16)
            .reshape(2, seq_rows, kv_width)
        )
        return (grad_query.reshape(seq_rows, -1), own_part, prefix_part)

    dp_size = lax.axis_size("dp")
    pair_count = pair_goals.shape[0]
    cap_pairs = max(1, -(-pair_count // dp_size))
    capacity = 2 * cap_pairs
    slot_total = dp_size * capacity
    pair_order = jnp.arange(pair_count)
    earlier = (pair_goals[None, :] == pair_goals[:, None]) & (
        pair_order[None, :] < pair_order[:, None]
    )
    pair_rank = jnp.sum(earlier.astype(jnp.int32), 1)
    base_slot = pair_goals * capacity + 2 * pair_rank
    slot_of = jnp.sum(
        jnp.where(pick_chosen, base_slot[:, None], 0)
        + jnp.where(pick_rejected, base_slot[:, None] + 1, 0),
        0,
    )
    slot_hits = slot_of[None, :] == jnp.arange(slot_total)[:, None]
    source_row = jnp.sum(jnp.where(slot_hits, positions[None, :], 0), 1)
    filled = jnp.any(slot_hits, 1)

    def pack(values_in):
        picked = jnp.take(values_in, source_row, axis=0)
        keep_rows = filled.reshape((slot_total,) + (1,) * (values_in.ndim - 1))
        packed = jnp.where(keep_rows, picked, jnp.zeros((), values_in.dtype))
        return packed.reshape((dp_size, capacity) + values_in.shape[1:])

    own_goal = lax.axis_index("dp")
    own_length = prefix_len[own_goal]
    keys_pre = prefix_kv[0, 0].reshape(prefix_rows, kv_local, head_size)
    values_pre = prefix_kv[0, 1].reshape(prefix_rows, kv_local, head_size)
    recv_query = lax.all_to_all(pack(queries), "dp", split_axis=0, concat_axis=0, tiled=True)
    recv_kv = lax.all_to_all(pack(suffix_kv), "dp", split_axis=0, concat_axis=0, tiled=True)
    recv_cot = lax.all_to_all(pack(cotangent), "dp", split_axis=0, concat_axis=0, tiled=True)
    item_count = recv_query.shape[1]

    def per_source(carry, source):
        src_query, src_kv, src_cot = source
        grad_query, own_part, prefix_part = jax.vmap(
            lambda one_query, one_kv, one_cot: one_suffix(
                one_query, one_kv, one_cot, keys_pre, values_pre, own_length
            )
        )(src_query, src_kv, src_cot)
        return (carry + prefix_part, (grad_query, own_part))

    initial = jnp.zeros((item_count, 2, prefix_rows, kv_width), jnp.float32)
    prefix_sum, (grad_queries, grad_kvs) = lax.scan(
        per_source, initial, (recv_query, recv_kv, recv_cot)
    )
    back_query = lax.all_to_all(grad_queries, "dp", split_axis=0, concat_axis=0, tiled=True)
    back_kv = lax.all_to_all(grad_kvs, "dp", split_axis=0, concat_axis=0, tiled=True)
    back_query, back_kv, prefix_terms = (back_query, back_kv, prefix_sum[None])
    query_grad = jnp.take(back_query.reshape((slot_total,) + back_query.shape[2:]), slot_of, axis=0)
    kv_grad = jnp.take(back_kv.reshape((slot_total,) + back_kv.shape[2:]), slot_of, axis=0)
    prefix_grad = jnp.sum(prefix_terms, (0, 1)).astype(jnp.bfloat16)[None]
    return (query_grad, kv_grad, prefix_grad)


def solution(mesh):
    return jax.shard_map(
        shards,
        mesh=mesh,
        in_specs=(
            P(("groups", "dp"), None, "tensor"),
            P(("groups", "dp"), None, None, "tensor"),
            P(("groups", "dp"), None, "tensor"),
            P(("groups", "dp"), None, None, "tensor"),
            P(("groups", "dp")),
            P(("groups", "dp"), None),
            P(("groups", "dp"), None),
            P("groups"),
        ),
        out_specs=(
            P(("groups", "dp"), None, "tensor"),
            P(("groups", "dp"), None, None, "tensor"),
            P(("groups", "dp"), None, None, "tensor"),
        ),
        check_vma=False,
    )
```

profile of v0, /device:TPU:0, one launch (start us, length us, event | category | flops | bytes accessed | tf_op | source)
XLA Modules:
  0.0 253.8 jit_solution(4109455296973152637)
XLA Ops:
  5.3 4.3 %all-to-all-start.1 = ((bf16[4,2,2,64,256]{4,3,2,1,0:T(8,128)(2,1)}), bf16[4,2,2,64,256]{4,3,2,1,0:T(8,128)(2,1)}, u32[]{:S(2)}, u32[]{:S(2)}) async-start(bf16[4,2,2,64,256]{4,3,2,1,0:T(8,128)(2,1)} %bitcast.10), calls=%async_computation.1 | async-start | bytes 1048576 | tf_op jit(solution)/shard_map/all_to_all | solution.py:128
  9.9 3.6 %multiply_convert_fusion = bf16[8,64,2048]{2,1,0:T(8,128)(2,1)} fusion(bf16[8,64,2048]{2,1,0:T(8,128)(2,1)} %param.16, f32[8]{0:T(128)S(1)} %subtract_reduce_fusion), kind=kLoop, calls=%fused_computation.65 | loop fusion | flops 3145728 | bytes 4194336 | tf_op jit(solution)/shard_map/convert_element_type | solution.py:74
  13.5 3.6 %gather_fusion.2 = bf16[8,64,2048]{2,1,0:T(8,128)(2,1)} fusion(bf16[8,64,2048]{2,1,0:T(8,128)(2,1)} %multiply_convert_fusion, s32[1024]{0:T(1024)S(1)} %pad_clamp_fusion.1), kind=kCustom, calls=%fused_computation.2.clone | custom fusion | bytes 4194336 | tf_op jit(solution)/shard_map/jit(_take)/gather | solution.py:118
  17.1 2.0 gather_fusion
  19.1 4.8 %select_select_fusion = (bf16[8,64,2048]{2,1,0:T(8,128)(2,1)}, bf16[8,64,2048]{2,1,0:T(8,128)(2,1)}) fusion(bf16[8,64,2048]{2,1,0:T(8,128)(2,1)} %gather_fusion.2, pred[8]{0:T(512)(128)(4,1)S(1)} %compare_and_fusion.1, pred[8]{0:T(512)(128)(4,1)S(1)} %fusion.42, bf16[8,64,2048]{2,1,0:T(8,128)(2,1)} %gather_fusion), kind=kLoop, calls=%fused_computation.66 | loop fusion | flops 4194304 | bytes 8388624 | tf_op jit(solution)/shard_map/jit(_where)/select_n | solution.py:120
  23.9 30.7 %all_to_all.25 = bf16[4,2,64,2048]{3,2,1,0:T(8,128)(2,1)} all-to-all(bf16[4,2,64,2048]{3,2,1,0:T(8,128)(2,1)} %bitcast.183), channel_id=1, replica_groups=mesh['groups'=2,'dp'=4,'tensor'=4] {'dp'}, dimensions={0} | all-to-all | bytes 4194304 | tf_op jit(solution)/shard_map/all_to_all | solution.py:127
  54.6 4.6 %all-to-all-start.2 = ((bf16[4,2,64,2048]{3,2,1,0:T(8,128)(2,1)}), bf16[4,2,64,2048]{3,2,1,0:T(8,128)(2,1)}, u32[]{:S(2)}, u32[]{:S(2)}) async-start(bf16[4,2,64,2048]{3,2,1,0:T(8,128)(2,1)} %bitcast.182), calls=%async_computation.2 | async-start | bytes 4194304 | tf_op jit(solution)/shard_map/all_to_all | solution.py:129
  60.9 24.1 %all-to-all-done.2 = bf16[4,2,64,2048]{3,2,1,0:T(8,128)(2,1)} async-done(((bf16[4,2,64,2048]{3,2,1,0:T(8,128)(2,1)}), bf16[4,2,64,2048]{3,2,1,0:T(8,128)(2,1)}, u32[]{:S(2)}, u32[]{:S(2)}) %all-to-all-start.2) | async-done | bytes 2097184 | tf_op jit(solution)/shard_map/all_to_all | solution.py:129
  84.9 119.7 %while.17 = (s32[]{:T(128)}, f32[2,2,448,256]{2,3,0,1:T(8,128)}, bf16[4,2,64,2048]{3,2,1,0:T(8,128)(2,1)}, bf16[4,2,2,64,256]{4,3,2,1,0:T(8,128)(2,1)}, bf16[4,2...) while((s32[]{:T(128)}, f32[2,2,448,256]{2,3,0,1:T(8,128)}, ...), condition=%wide.region_10.13_spmd.clone, body=%wide.region_7.12_spmd.clone.sunk | while | flops 1630470144 | bytes 148947088 | solution.py:142
  89.8 1.7 fusion.82
  91.5 2.0 fusion.83
  95.5 2.9 %fusion.85 = f32[2,2,8,64]{3,2,1,0:T(8,128)S(1)} fusion(bf16[2,2,8,64,512]{4,3,2,1,0:T(8,128)(2,1)} %fusion.83, f32[2,2,8,64,128]{4,2,1,3,0:T(8,128)} %bitcast_convert_fusion.2, bf16[2,64,2,128]{3,1,2,0:T(8,128)(2,1)S(1)} %copy.124, bf16[2,448,2,128]{3,1,2,0:T(8,128)(2,1)S(1)} %broadcast_in_dim.303), kind=kOutput, calls=%fused_computation.31.clone.1 | convolution fusion | flops 270006272 | bytes 3678208 | tf_op jit(solution)/shard_map/while/body/eval_jaxpr/vmap(kgts,skd->tkgd)/dot_general | solution.py:30
  108.7 3.6 %bitcast_add_fusion.3 = f32[2,2,448,256]{2,3,0,1:T(8,128)} fusion(f32[2,2,448,2,128]{2,4,3,1,0:T(8,128)} %pad_maximum_fusion.4, f32[2,2,448,256]{2,3,0,1:T(8,128)} %get-tuple-element.344, pred[]{:T(512)S(6)} %compare.3), kind=kLoop, calls=%fused_computation.13.clone.1 | loop fusion | flops 917504 | bytes 5505025 | tf_op jit(solution)/shard_map/while/body/eval_jaxpr/add | solution.py:139
  119.2 1.7 fusion.82
  120.9 2.0 fusion.83
  125.0 2.9 %fusion.85 = f32[2,2,8,64]{3,2,1,0:T(8,128)S(1)} fusion(bf16[2,2,8,64,512]{4,3,2,1,0:T(8,128)(2,1)} %fusion.83, f32[2,2,8,64,128]{4,2,1,3,0:T(8,128)} %bitcast_convert_fusion.2, bf16[2,64,2,128]{3,1,2,0:T(8,128)(2,1)S(1)} %copy.124, bf16[2,448,2,128]{3,1,2,0:T(8,128)(2,1)S(1)} %broadcast_in_dim.303), kind=kOutput, calls=%fused_computation.31.clone.1 | convolution fusion | flops 270006272 | bytes 3678208 | tf_op jit(solution)/shard_map/while/body/eval_jaxpr/vmap(kgts,skd->tkgd)/dot_general | solution.py:30
  138.1 4.2 %bitcast_add_fusion.3 = f32[2,2,448,256]{2,3,0,1:T(8,128)} fusion(f32[2,2,448,2,128]{2,4,3,1,0:T(8,128)} %pad_maximum_fusion.4, f32[2,2,448,256]{2,3,0,1:T(8,128)} %get-tuple-element.344, pred[]{:T(512)S(6)} %compare.3), kind=kLoop, calls=%fused_computation.13.clone.1 | loop fusion | flops 917504 | bytes 5505025 | tf_op jit(solution)/shard_map/while/body/eval_jaxpr/add | solution.py:139
  149.3 1.7 fusion.82
  151.0 2.0 fusion.83
  155.1 2.9 %fusion.85 = f32[2,2,8,64]{3,2,1,0:T(8,128)S(1)} fusion(bf16[2,2,8,64,512]{4,3,2,1,0:T(8,128)(2,1)} %fusion.83, f32[2,2,8,64,128]{4,2,1,3,0:T(8,128)} %bitcast_convert_fusion.2, bf16[2,64,2,128]{3,1,2,0:T(8,128)(2,1)S(1)} %copy.124, bf16[2,448,2,128]{3,1,2,0:T(8,128)(2,1)S(1)} %broadcast_in_dim.303), kind=kOutput, calls=%fused_computation.31.clone.1 | convolution fusion | flops 270006272 | bytes 3678208 | tf_op jit(solution)/shard_map/while/body/eval_jaxpr/vmap(kgts,skd->tkgd)/dot_general | solution.py:30
  164.8 1.7 constant_dynamic-update-slice_fusion.5
  168.2 4.2 %bitcast_add_fusion.3 = f32[2,2,448,256]{2,3,0,1:T(8,128)} fusion(f32[2,2,448,2,128]{2,4,3,1,0:T(8,128)} %pad_maximum_fusion.4, f32[2,2,448,256]{2,3,0,1:T(8,128)} %get-tuple-element.344, pred[]{:T(512)S(6)} %compare.3), kind=kLoop, calls=%fused_computation.13.clone.1 | loop fusion | flops 917504 | bytes 5505025 | tf_op jit(solution)/shard_map/while/body/eval_jaxpr/add | solution.py:139
  179.4 1.7 fusion.82
  181.1 2.0 fusion.83
  185.1 2.9 %fusion.85 = f32[2,2,8,64]{3,2,1,0:T(8,128)S(1)} fusion(bf16[2,2,8,64,512]{4,3,2,1,0:T(8,128)(2,1)} %fusion.83, f32[2,2,8,64,128]{4,2,1,3,0:T(8,128)} %bitcast_convert_fusion.2, bf16[2,64,2,128]{3,1,2,0:T(8,128)(2,1)S(1)} %copy.124, bf16[2,448,2,128]{3,1,2,0:T(8,128)(2,1)S(1)} %broadcast_in_dim.303), kind=kOutput, calls=%fused_computation.31.clone.1 | convolution fusion | flops 270006272 | bytes 3678208 | tf_op jit(solution)/shard_map/while/body/eval_jaxpr/vmap(kgts,skd->tkgd)/dot_general | solution.py:30
  198.3 4.2 %bitcast_add_fusion.3 = f32[2,2,448,256]{2,3,0,1:T(8,128)} fusion(f32[2,2,448,2,128]{2,4,3,1,0:T(8,128)} %pad_maximum_fusion.4, f32[2,2,448,256]{2,3,0,1:T(8,128)} %get-tuple-element.344, pred[]{:T(512)S(6)} %compare.3), kind=kLoop, calls=%fused_computation.13.clone.1 | loop fusion | flops 917504 | bytes 5505025 | tf_op jit(solution)/shard_map/while/body/eval_jaxpr/add | solution.py:139
  204.6 12.3 %all_to_all.26 = bf16[4,2,2,64,256]{4,3,2,1,0:T(8,128)(2,1)S(1)} all-to-all(bf16[4,2,2,64,256]{4,3,2,1,0:T(8,128)(2,1)} %get-tuple-element.133), channel_id=1, replica_groups=mesh['groups'=2,'dp'=4,'tensor'=4] {'dp'}, dimensions={0} | all-to-all | bytes 1048576 | tf_op jit(solution)/shard_map/all_to_all | solution.py:146
  216.9 4.4 %all-to-all-start.3 = ((bf16[4,2,64,2048]{3,2,1,0:T(8,128)(2,1)}), bf16[4,2,64,2048]{3,2,1,0:T(8,128)(2,1)}, u32[]{:S(2)}, u32[]{:S(2)}) async-start(bf16[4,2,64,2048]{3,2,1,0:T(8,128)(2,1)} %get-tuple-element.132), calls=%async_computation.3 | async-start | bytes 4194304 | tf_op jit(solution)/shard_map/all_to_all | solution.py:145
  221.4 1.8 reduce_sum.84
  225.7 21.4 %all-to-all-done.3 = bf16[4,2,64,2048]{3,2,1,0:T(8,128)(2,1)} async-done(((bf16[4,2,64,2048]{3,2,1,0:T(8,128)(2,1)}), bf16[4,2,64,2048]{3,2,1,0:T(8,128)(2,1)}, u32[]{:S(2)}, u32[]{:S(2)}) %all-to-all-start.3) | async-done | bytes 2097184 | tf_op jit(solution)/shard_map/all_to_all | solution.py:145
  247.1 3.6 %gather_fusion.3 = bf16[8,64,2048]{2,1,0:T(8,128)(2,1)} fusion(bf16[8,64,2048]{2,1,0:T(8,128)(2,1)} %bitcast.12, s32[1024]{0:T(1024)S(1)} %pad_clamp_fusion), kind=kCustom, calls=%fused_computation.3.clone | custom fusion | bytes 4194336 | tf_op jit(solution)/shard_map/jit(_take)/gather | solution.py:148
  250.7 3.2 %broadcast_select_fusion = bf16[8,64,2048]{2,1,0:T(8,128)(2,1)} fusion(bf16[8,64,2048]{2,1,0:T(8,128)(2,1)} %gather_fusion.3, pred[8]{0:T(512)(128)(4,1)S(1)} %compare_and_fusion), kind=kLoop, calls=%fused_computation.68 | loop fusion | flops 1048576 | bytes 4194312 | tf_op jit(solution)/shard_map/jit(_take)/select_n | solution.py:148
  (296 shorter events, 83.9 us)
Async XLA Ops:
  0.6 16.5 %copy-start = (bf16[8,64,2048]{2,1,0:T(8,128)(2,1)S(1)}, bf16[8,64,2048]{2,1,0:T(8,128)(2,1)}, u32[]{:S(2)}) copy-start(bf16[8,64,2048]{2,1,0:T(8,128)(2,1)} %param.14) | copy-start | bytes 6291460
  0.6 9.0 %copy-start.19 = (f32[8]{0:T(128)S(1)}, f32[8]{0:T(128)}, u32[]{:S(2)}) copy-start(f32[8]{0:T(128)} %param.18) | copy-start | bytes 100
  5.3 18.5 %all-to-all-start.1 = ((bf16[4,2,2,64,256]{4,3,2,1,0:T(8,128)(2,1)}), bf16[4,2,2,64,256]{4,3,2,1,0:T(8,128)(2,1)}, u32[]{:S(2)}, u32[]{:S(2)}) async-start(bf16[4,2,2,64,256]{4,3,2,1,0:T(8,128)(2,1)} %bitcast.10), calls=%async_computation.1 | async-start | bytes 1048576 | tf_op jit(solution)/shard_map/all_to_all | solution.py:128
  54.6 4.6 %copy-start.18 = (bf16[1,2,448,256]{3,2,1,0:T(8,128)(2,1)S(1)}, bf16[1,2,448,256]{3,2,1,0:T(8,128)(2,1)}, u32[]{:S(2)}) copy-start(bf16[1,2,448,256]{3,2,1,0:T(8,128)(2,1)} %param.17) | copy-start | bytes 1376260
  54.6 30.3 %all-to-all-start.2 = ((bf16[4,2,64,2048]{3,2,1,0:T(8,128)(2,1)}), bf16[4,2,64,2048]{3,2,1,0:T(8,128)(2,1)}, u32[]{:S(2)}, u32[]{:S(2)}) async-start(bf16[4,2,64,2048]{3,2,1,0:T(8,128)(2,1)} %bitcast.182), calls=%async_computation.2 | async-start | bytes 4194304 | tf_op jit(solution)/shard_map/all_to_all | solution.py:129
  84.9 3.3 %copy-start.14 = (bf16[448,2,128]{2,0,1:T(8,128)(2,1)}, bf16[448,2,128]{2,0,1:T(8,128)(2,1)S(1)}, u32[]{:S(2)}) copy-start(bf16[448,2,128]{2,0,1:T(8,128)(2,1)S(1)} %get-tuple-element.361) | copy-start | bytes 688132 | tf_op jit(solution)/shard_map/while
  91.5 2.7 %copy-start.10 = (f32[2,2,8,64,512]{4,3,2,1,0:T(8,128)}, f32[2,2,8,64,512]{4,3,2,1,0:T(8,128)S(1)}, u32[]{:S(2)}) copy-start(f32[2,2,8,64,512]{4,3,2,1,0:T(8,128)S(1)} %get-tuple-element.327) | copy-start | bytes 12582916 | tf_op jit(solution)/shard_map/while
  94.3 4.1 %copy-start.8 = (bf16[16,8,16,128]{3,2,1,0:T(8,128)(2,1)}, bf16[16,8,16,128]{3,2,1,0:T(8,128)(2,1)S(1)}, u32[]{:S(2)}) copy-start(bf16[16,8,16,128]{3,2,1,0:T(8,128)(2,1)S(1)} %copy.123) | copy-start | bytes 1572868 | tf_op jit(solution)/shard_map/while
  95.4 3.1 %copy-start.11 = (f32[2,2,8,64,512]{4,3,2,1,0:T(8,128)S(1)}, f32[2,2,8,64,512]{4,3,2,1,0:T(8,128)}, u32[]{:S(2)}) copy-start(f32[2,2,8,64,512]{4,3,2,1,0:T(8,128)} %copy-done.10) | copy-start | bytes 12582916 | tf_op jit(solution)/shard_map/while
  99.6 3.8 %copy-start.2 = (bf16[2,2,8,64,512]{4,3,2,1,0:T(8,128)(2,1)}, bf16[2,2,8,64,512]{4,3,2,1,0:T(8,128)(2,1)S(1)}, u32[]{:S(2)}) copy-start(bf16[2,2,8,64,512]{4,3,2,1,0:T(8,128)(2,1)S(1)} %fusion.86) | copy-start | bytes 6291460 | tf_op jit(solution)/shard_map/while
  108.7 3.6 %copy-start.3 = (bf16[2,2,8,64,512]{4,3,2,1,0:T(8,128)(2,1)S(1)}, bf16[2,2,8,64,512]{4,3,2,1,0:T(8,128)(2,1)}, u32[]{:S(2)}) copy-start(bf16[2,2,8,64,512]{4,3,2,1,0:T(8,128)(2,1)} %copy-done.2) | copy-start | bytes 6291460 | tf_op jit(solution)/shard_map/while
  108.7 3.6 %copy-start.13 = (bf16[2,448,2,128]{3,1,2,0:T(8,128)(2,1)S(1)}, bf16[2,448,2,128]{3,1,2,0:T(8,128)(2,1)}, u32[]{:S(2)}) copy-start(bf16[2,448,2,128]{3,1,2,0:T(8,128)(2,1)} %copy-done.12) | copy-start | bytes 1376260 | tf_op jit(solution)/shard_map/while
  114.4 3.3 %copy-start.14 = (bf16[448,2,128]{2,0,1:T(8,128)(2,1)}, bf16[448,2,128]{2,0,1:T(8,128)(2,1)S(1)}, u32[]{:S(2)}) copy-start(bf16[448,2,128]{2,0,1:T(8,128)(2,1)S(1)} %get-tuple-element.361) | copy-start | bytes 688132 | tf_op jit(solution)/shard_map/while
  120.9 2.7 %copy-start.10 = (f32[2,2,8,64,512]{4,3,2,1,0:T(8,128)}, f32[2,2,8,64,512]{4,3,2,1,0:T(8,128)S(1)}, u32[]{:S(2)}) copy-start(f32[2,2,8,64,512]{4,3,2,1,0:T(8,128)S(1)} %get-tuple-element.327) | copy-start | bytes 12582916 | tf_op jit(solution)/shard_map/while
  123.7 4.1 %copy-start.8 = (bf16[16,8,16,128]{3,2,1,0:T(8,128)(2,1)}, bf16[16,8,16,128]{3,2,1,0:T(8,128)(2,1)S(1)}, u32[]{:S(2)}) copy-start(bf16[16,8,16,128]{3,2,1,0:T(8,128)(2,1)S(1)} %copy.123) | copy-start | bytes 1572868 | tf_op jit(solution)/shard_map/while
  124.9 3.1 %copy-start.11 = (f32[2,2,8,64,512]{4,3,2,1,0:T(8,128)S(1)}, f32[2,2,8,64,512]{4,3,2,1,0:T(8,128)}, u32[]{:S(2)}) copy-start(f32[2,2,8,64,512]{4,3,2,1,0:T(8,128)} %copy-done.10) | copy-start | bytes 12582916 | tf_op jit(solution)/shard_map/while
  129.1 3.8 %copy-start.2 = (bf16[2,2,8,64,512]{4,3,2,1,0:T(8,128)(2,1)}, bf16[2,2,8,64,512]{4,3,2,1,0:T(8,128)(2,1)S(1)}, u32[]{:S(2)}) copy-start(bf16[2,2,8,64,512]{4,3,2,1,0:T(8,128)(2,1)S(1)} %fusion.86) | copy-start | bytes 6291460 | tf_op jit(solution)/shard_map/while
  138.1 4.2 %copy-start.3 = (bf16[2,2,8,64,512]{4,3,2,1,0:T(8,128)(2,1)S(1)}, bf16[2,2,8,64,512]{4,3,2,1,0:T(8,128)(2,1)}, u32[]{:S(2)}) copy-start(bf16[2,2,8,64,512]{4,3,2,1,0:T(8,128)(2,1)} %copy-done.2) | copy-start | bytes 6291460 | tf_op jit(solution)/shard_map/while
  138.1 4.2 %copy-start.13 = (bf16[2,448,2,128]{3,1,2,0:T(8,128)(2,1)S(1)}, bf16[2,448,2,128]{3,1,2,0:T(8,128)(2,1)}, u32[]{:S(2)}) copy-start(bf16[2,448,2,128]{3,1,2,0:T(8,128)(2,1)} %copy-done.12) | copy-start | bytes 1376260 | tf_op jit(solution)/shard_map/while
  144.5 3.3 %copy-start.14 = (bf16[448,2,128]{2,0,1:T(8,128)(2,1)}, bf16[448,2,128]{2,0,1:T(8,128)(2,1)S(1)}, u32[]{:S(2)}) copy-start(bf16[448,2,128]{2,0,1:T(8,128)(2,1)S(1)} %get-tuple-element.361) | copy-start | bytes 688132 | tf_op jit(solution)/shard_map/while
  153.8 4.1 %copy-start.8 = (bf16[16,8,16,128]{3,2,1,0:T(8,128)(2,1)}, bf16[16,8,16,128]{3,2,1,0:T(8,128)(2,1)S(1)}, u32[]{:S(2)}) copy-start(bf16[16,8,16,128]{3,2,1,0:T(8,128)(2,1)S(1)} %copy.123) | copy-start | bytes 1572868 | tf_op jit(solution)/shard_map/while
  155.0 3.1 %copy-start.11 = (f32[2,2,8,64,512]{4,3,2,1,0:T(8,128)S(1)}, f32[2,2,8,64,512]{4,3,2,1,0:T(8,128)}, u32[]{:S(2)}) copy-start(f32[2,2,8,64,512]{4,3,2,1,0:T(8,128)} %copy-done.10) | copy-start | bytes 12582916 | tf_op jit(solution)/shard_map/while
  159.2 3.8 %copy-start.2 = (bf16[2,2,8,64,512]{4,3,2,1,0:T(8,128)(2,1)}, bf16[2,2,8,64,512]{4,3,2,1,0:T(8,128)(2,1)S(1)}, u32[]{:S(2)}) copy-start(bf16[2,2,8,64,512]{4,3,2,1,0:T(8,128)(2,1)S(1)} %fusion.86) | copy-start | bytes 6291460 | tf_op jit(solution)/shard_map/while
  168.2 4.2 %copy-start.3 = (bf16[2,2,8,64,512]{4,3,2,1,0:T(8,128)(2,1)S(1)}, bf16[2,2,8,64,512]{4,3,2,1,0:T(8,128)(2,1)}, u32[]{:S(2)}) copy-start(bf16[2,2,8,64,512]{4,3,2,1,0:T(8,128)(2,1)} %copy-done.2) | copy-start | bytes 6291460 | tf_op jit(solution)/shard_map/while
  168.2 4.2 %copy-start.13 = (bf16[2,448,2,128]{3,1,2,0:T(8,128)(2,1)S(1)}, bf16[2,448,2,128]{3,1,2,0:T(8,128)(2,1)}, u32[]{:S(2)}) copy-start(bf16[2,448,2,128]{3,1,2,0:T(8,128)(2,1)} %copy-done.12) | copy-start | bytes 1376260 | tf_op jit(solution)/shard_map/while
  174.6 3.3 %copy-start.14 = (bf16[448,2,128]{2,0,1:T(8,128)(2,1)}, bf16[448,2,128]{2,0,1:T(8,128)(2,1)S(1)}, u32[]{:S(2)}) copy-start(bf16[448,2,128]{2,0,1:T(8,128)(2,1)S(1)} %get-tuple-element.361) | copy-start | bytes 688132 | tf_op jit(solution)/shard_map/while
  183.9 4.1 %copy-start.8 = (bf16[16,8,16,128]{3,2,1,0:T(8,128)(2,1)}, bf16[16,8,16,128]{3,2,1,0:T(8,128)(2,1)S(1)}, u32[]{:S(2)}) copy-start(bf16[16,8,16,128]{3,2,1,0:T(8,128)(2,1)S(1)} %copy.123) | copy-start | bytes 1572868 | tf_op jit(solution)/shard_map/while
  185.1 3.1 %copy-start.11 = (f32[2,2,8,64,512]{4,3,2,1,0:T(8,128)S(1)}, f32[2,2,8,64,512]{4,3,2,1,0:T(8,128)}, u32[]{:S(2)}) copy-start(f32[2,2,8,64,512]{4,3,2,1,0:T(8,128)} %copy-done.10) | copy-start | bytes 12582916 | tf_op jit(solution)/shard_map/while
  189.2 3.8 %copy-start.2 = (bf16[2,2,8,64,512]{4,3,2,1,0:T(8,128)(2,1)}, bf16[2,2,8,64,512]{4,3,2,1,0:T(8,128)(2,1)S(1)}, u32[]{:S(2)}) copy-start(bf16[2,2,8,64,512]{4,3,2,1,0:T(8,128)(2,1)S(1)} %fusion.86) | copy-start | bytes 6291460 | tf_op jit(solution)/shard_map/while
  198.3 4.2 %copy-start.3 = (bf16[2,2,8,64,512]{4,3,2,1,0:T(8,128)(2,1)S(1)}, bf16[2,2,8,64,512]{4,3,2,1,0:T(8,128)(2,1)}, u32[]{:S(2)}) copy-start(bf16[2,2,8,64,512]{4,3,2,1,0:T(8,128)(2,1)} %copy-done.2) | copy-start | bytes 6291460 | tf_op jit(solution)/shard_map/while
  198.3 4.2 %copy-start.13 = (bf16[2,448,2,128]{3,1,2,0:T(8,128)(2,1)S(1)}, bf16[2,448,2,128]{3,1,2,0:T(8,128)(2,1)}, u32[]{:S(2)}) copy-start(bf16[2,448,2,128]{3,1,2,0:T(8,128)(2,1)} %copy-done.12) | copy-start | bytes 1376260 | tf_op jit(solution)/shard_map/while
  216.9 30.2 %all-to-all-start.3 = ((bf16[4,2,64,2048]{3,2,1,0:T(8,128)(2,1)}), bf16[4,2,64,2048]{3,2,1,0:T(8,128)(2,1)}, u32[]{:S(2)}, u32[]{:S(2)}) async-start(bf16[4,2,64,2048]{3,2,1,0:T(8,128)(2,1)} %get-tuple-element.132), calls=%async_computation.3 | async-start | bytes 4194304 | tf_op jit(solution)/shard_map/all_to_all | solution.py:145
  (43 other events, 69.7 us)
where the time goes:
time: 255 us; the launch traced here: 254 us
  other arithmetic  62.1 us (24%)
  local copies, waits for them, and re-layouts  56.2 us (22%)
  waiting for transfers between devices  45.4 us (18%)
  blocking collectives  43 us (17%)
  matrix products  31.9 us (13%)
  starting transfers between devices  13.3 us (5%)
    all_to_all x1, blocking collectives, shards(): lax.all_to_all(pack(queries), 'dp', split_axis=0, concat_axis=0, tiled=True)  30.7 us
    all_to_all x1, waiting for transfers between devices, shards(): lax.all_to_all(pack(cotangent), 'dp', split_axis=0, concat_axis=0, tiled=...  24.1 us
    all_to_all x1, waiting for transfers between devices, shards(): lax.all_to_all(grad_queries, 'dp', split_axis=0, concat_axis=0, tiled=True)  21.4 us
    add x4, other arithmetic, per_source(): return (carry + prefix_part, (grad_query, own_part))  16.1 us
    dynamic_update_slice x12, local copies, waits for them, and re-layouts, shards(): lax.scan(per_source, initial, (recv_query, recv_kv, recv_cot))  13.1 us
    while x144, local copies, waits for them, and re-layouts  12.4 us
    all_to_all x1, blocking collectives, shards(): lax.all_to_all(grad_kvs, 'dp', split_axis=0, concat_axis=0, tiled=True)  12.3 us
    dot_general x4, matrix products, attend(): jnp.einsum('kgts,skd->tkgd', probability_low, all_values, preferred_eleme...  11.4 us
  transfers between devices with their start and end apart: 3, of which 2 were waited for; matrix products, arithmetic and copies ran while one was open for 8% of the time, Pallas kernels for 0%

commit v1 on v0

v1 whole, which is shorter than its diff:
```python
import functools

import jax
import jax.numpy as jnp
from jax import lax
from jax.experimental import pallas as pl
from jax.experimental.pallas import tpu as pltpu
from jax.sharding import PartitionSpec as P

HD = 128

dpo_beta = 0.5


def attend_kernel(slots_ref, goal_ref, len_ref, coef_ref,
                  q_ref, og_ref, skv_ref, pkv_ref,
                  dq_ref, dkv_ref, dpre_ref, *, group, seq, prefix_rows):
    p = pl.program_id(0)
    member = pl.program_id(2)
    s = slots_ref[2 * p + member]
    goal = goal_ref[p]
    length = len_ref[goal]
    coef = coef_ref[s]
    scale = HD ** (-0.5)
    keys_all = prefix_rows + seq
    rows = group * seq

    q_blk = q_ref[0]
    og_blk = og_ref[0]
    cot_blk = (coef * og_blk.astype(jnp.float32)).astype(jnp.bfloat16)
    q_rows = jnp.concatenate([q_blk[:, g * HD:(g + 1) * HD] for g in range(group)], 0)
    c_rows = jnp.concatenate([cot_blk[:, g * HD:(g + 1) * HD] for g in range(group)], 0)
    keys = jnp.concatenate([pkv_ref[0, 0], skv_ref[0, 0]], 0)
    values = jnp.concatenate([pkv_ref[0, 1], skv_ref[0, 1]], 0)

    nt = (((1,), (1,)), ((), ()))
    tn = (((0,), (0,)), ((), ()))
    scores = lax.dot_general(q_rows, keys, nt, preferred_element_type=jnp.float32) * scale
    key_index = lax.broadcasted_iota(jnp.int32, (rows, keys_all), 1)
    tok_index = lax.broadcasted_iota(jnp.int32, (rows, keys_all), 0) % seq
    in_prefix = key_index < prefix_rows
    allowed = (in_prefix & (key_index < length)) | (
        jnp.logical_not(in_prefix) & (key_index - prefix_rows <= tok_index))
    scores = jnp.where(allowed, scores, -1e30)
    row_max = jnp.max(scores, -1, keepdims=True)
    raised = jnp.exp(scores - row_max)
    prob = raised / jnp.sum(raised, -1, keepdims=True)
    prob_low = prob.astype(jnp.bfloat16)
    output = jnp.dot(prob_low, values, preferred_element_type=jnp.float32)
    row_dot = jnp.sum(c_rows.astype(jnp.float32) * output, -1, keepdims=True)
    grad_prob = lax.dot_general(c_rows, values, nt, preferred_element_type=jnp.float32)
    grad_score = (prob * (grad_prob - row_dot)).astype(jnp.bfloat16)
    grad_q = (scale * jnp.dot(grad_score, keys, preferred_element_type=jnp.float32)).astype(jnp.bfloat16)
    grad_k = scale * lax.dot_general(grad_score, q_rows, tn, preferred_element_type=jnp.float32)
    grad_v = lax.dot_general(prob_low, c_rows, tn, preferred_element_type=jnp.float32)

    for g in range(group):
        dq_ref[0, :, g * HD:(g + 1) * HD] = grad_q[g * seq:(g + 1) * seq]
    dkv_ref[0, 0] = grad_k[prefix_rows:].astype(jnp.bfloat16)
    dkv_ref[0, 1] = grad_v[prefix_rows:].astype(jnp.bfloat16)

    @pl.when(member == 0)
    def _():
        dpre_ref[0, 0] = grad_k[:prefix_rows]
        dpre_ref[0, 1] = grad_v[:prefix_rows]

    @pl.when(member != 0)
    def _():
        dpre_ref[0, 0] += grad_k[:prefix_rows]
        dpre_ref[0, 1] += grad_v[:prefix_rows]


def attend_all(slots, goals, lengths, coef, queries, out_grad, suffix_kv, prefix_all):
    suffix_count, seq, qwidth = queries.shape
    kv_width = suffix_kv.shape[-1]
    kv_local = kv_width // HD
    group = qwidth // kv_width
    goal_count, _, prefix_rows, _ = prefix_all.shape
    pair_count = goals.shape[0]
    qb = group * HD

    def q_map(p, k, m, slots_ref, goal_ref, len_ref):
        return (slots_ref[2 * p + m], 0, k)

    def skv_map(p, k, m, slots_ref, goal_ref, len_ref):
        return (slots_ref[2 * p + m], 0, 0, k)

    def pkv_map(p, k, m, slots_ref, goal_ref, len_ref):
        return (goal_ref[p], 0, 0, k)

    kernel = functools.partial(attend_kernel, group=group, seq=seq, prefix_rows=prefix_rows)
    out_shape = (
        jax.ShapeDtypeStruct((suffix_count, seq, qwidth), jnp.bfloat16),
        jax.ShapeDtypeStruct((suffix_count, 2, seq, kv_width), jnp.bfloat16),
        jax.ShapeDtypeStruct((goal_count, 2, prefix_rows, kv_width), jnp.float32),
    )
    in_specs = [
        pl.BlockSpec(memory_space=pltpu.SMEM),
        pl.BlockSpec((1, seq, qb), q_map),
        pl.BlockSpec((1, seq, qb), q_map),
        pl.BlockSpec((1, 2, seq, HD), skv_map),
        pl.BlockSpec((1, 2, prefix_rows, HD), pkv_map),
    ]
    operands = [coef, queries, out_grad, suffix_kv, prefix_all]
    aliases = {}
    if pair_count < goal_count:
        in_specs.append(pl.BlockSpec(memory_space=pl.ANY))
        operands.append(jnp.zeros(out_shape[2].shape, jnp.float32))
        aliases = {3 + len(operands) - 1: 2}

        def kernel_with_zero(*refs):
            return kernel(*refs[:8], *refs[9:])
        body = kernel_with_zero
    else:
        body = kernel
    grid_spec = pltpu.PrefetchScalarGridSpec(
        num_scalar_prefetch=3,
        grid=(pair_count, kv_local, 2),
        in_specs=in_specs,
        out_specs=[
            pl.BlockSpec((1, seq, qb), q_map),
            pl.BlockSpec((1, 2, seq, HD), skv_map),
            pl.BlockSpec((1, 2, prefix_rows, HD), pkv_map),
        ],
    )
    return pl.pallas_call(
        body,
        grid_spec=grid_spec,
        out_shape=out_shape,
        input_output_aliases=aliases,
        compiler_params=pltpu.CompilerParams(
            dimension_semantics=("arbitrary", "arbitrary", "arbitrary")),
    )(slots, goals, lengths, *operands)


def shards(queries, suffix_kv, out_grad, prefix_kv, logratio, pair_slots, pair_goal, prefix_len):
    suffix_count = queries.shape[0]
    chosen = pair_slots[:, 0]
    rejected = pair_slots[:, 1]
    positions = jnp.arange(suffix_count)
    pick_chosen = chosen[:, None] == positions[None, :]
    pick_rejected = rejected[:, None] == positions[None, :]
    ratio_chosen = jnp.sum(jnp.where(pick_chosen, logratio[None, :], 0.0), 1)
    ratio_rejected = jnp.sum(jnp.where(pick_rejected, logratio[None, :], 0.0), 1)
    weight = dpo_beta * jax.nn.sigmoid(-dpo_beta * (ratio_chosen - ratio_rejected))
    coefficient = jnp.sum(
        jnp.where(pick_rejected, weight[:, None], 0.0)
        - jnp.where(pick_chosen, weight[:, None], 0.0),
        0,
    )
    slots = pair_slots.reshape(-1).astype(jnp.int32)
    goals = pair_goal[:, 0].astype(jnp.int32)
    prefix_all = lax.all_gather(prefix_kv, "dp", axis=0, tiled=True)
    grad_q, grad_kv, partial = attend_all(
        slots, goals, prefix_len.astype(jnp.int32), coefficient,
        queries, out_grad, suffix_kv, prefix_all)
    prefix_grad = lax.psum_scatter(partial, "dp", scatter_dimension=0, tiled=True)
    return grad_q, grad_kv, prefix_grad.astype(jnp.bfloat16)


def solution(mesh):
    return jax.shard_map(
        shards,
        mesh=mesh,
        in_specs=(
            P(("groups", "dp"), None, "tensor"),
            P(("groups", "dp"), None, None, "tensor"),
            P(("groups", "dp"), None, "tensor"),
            P(("groups", "dp"), None, None, "tensor"),
            P(("groups", "dp")),
            P(("groups", "dp"), None),
            P(("groups", "dp"), None),
            P("groups"),
        ),
        out_specs=(
            P(("groups", "dp"), None, "tensor"),
            P(("groups", "dp"), None, None, "tensor"),
            P(("groups", "dp"), None, None, "tensor"),
        ),
        check_vma=False,
    )
```

time: 255 us -> 115 us (0.45)
  other arithmetic: 62.1 us -> 3.45 us
  local copies, waits for them, and re-layouts: 56.2 us -> 2.12 us
  blocking collectives: 43 us -> 0 us
  matrix products: 31.9 us -> 0 us
  Pallas kernels: 0 us -> 30.9 us
  waiting for transfers between devices: 45.4 us -> 63.9 us
  starting transfers between devices: 13.3 us -> 0.08 us
  between operations: 0.8 us -> 14 us
    all_to_all x3 -> x0, waiting for transfers between devices: 45.4 us -> none  [the longest x1 24.1 us: shards(): lax.all_to_all(pack(cotangent), 'dp', split_axis=0, concat_axis=0, tiled=...]
    all_to_all x2 -> x0, blocking collectives: 43 us -> none  [the longest x1 30.7 us: shards(): lax.all_to_all(pack(queries), 'dp', split_axis=0, concat_axis=0, tiled=True)]
    reduce_scatter x0 -> x1, waiting for transfers between devices: none -> 41.4 us  [shards(): lax.psum_scatter(partial, 'dp', scatter_dimension=0, tiled=True)]
    dot_general x24 -> x0, matrix products: 31.9 us -> none  [the longest x4 11.4 us: attend(): jnp.einsum('kgts,skd->tkgd', probability_low, all_values, preferred_eleme...]
    pallas_call x0 -> x1, Pallas kernels: none -> 30.9 us  [attend_all(): pl.pallas_call(body, grid_spec=grid_spec, out_shape=out_shape, input_outp...]
    all_gather x0 -> x1, waiting for transfers between devices: none -> 21.9 us  [shards(): prefix_all = lax.all_gather(prefix_kv, 'dp', axis=0, tiled=True)]
    add x4 -> x0, other arithmetic: 16.1 us -> none  [per_source(): return (carry + prefix_part, (grad_query, own_part))]
    all_to_all x3 -> x0, starting transfers between devices: 13.3 us -> none  [the longest x1 4.59 us: shards(): lax.all_to_all(pack(cotangent), 'dp', split_axis=0, concat_axis=0, tiled=...]
  transfers between devices with their start and end apart: 3 -> 2, of which waited for: 2 -> 2; matrix products, arithmetic and copies ran while one was open for 8% -> 3% of each run, Pallas kernels for 0% -> 0%
where the time goes in v1:
time: 115 us
  waiting for transfers between devices  63.9 us (56%)
  Pallas kernels  30.9 us (27%)
  between operations  14 us (12%)
  other arithmetic  3.45 us (3%)
  local copies, waits for them, and re-layouts  2.12 us (2%)
    reduce_scatter x1, waiting for transfers between devices, shards(): lax.psum_scatter(partial, 'dp', scatter_dimension=0, tiled=True)  41.4 us
    pallas_call x1, Pallas kernels, attend_all(): pl.pallas_call(body, grid_spec=grid_spec, out_shape=out_shape, input_outp...  30.9 us
    all_gather x1, waiting for transfers between devices, shards(): prefix_all = lax.all_gather(prefix_kv, 'dp', axis=0, tiled=True)  21.9 us
  transfers between devices with their start and end apart: 2, of which 2 were waited for; matrix products, arithmetic and copies ran while one was open for 3% of the time, Pallas kernels for 0%

profile of v1, /device:TPU:0, one launch (start us, length us, event | category | flops | bytes accessed | tf_op | source)
XLA Modules:
  0.0 114.5 jit_solution(12513356137126122516)
XLA Ops:
  7.2 0.0 all-gather.2.cloned.1.call-start
  7.2 0.7 all-gather.2.cloned.1.call-update
  7.9 0.0 reduce-scatter.2.cloned.1.call-start
  7.9 0.8 copy.14
  8.7 0.6 reshape.21.slots_ref
  9.3 0.8 slice_bitcast_fusion
  10.1 0.9 select_reduce_fusion
  10.9 0.6 subtract_reduce_fusion.coef_ref
  11.5 21.9 %all-gather.2.cloned.1.call-done.pkv_ref = bf16[4,2,448,256]{3,2,1,0:T(8,128)(2,1)} async-done(((bf16[1,2,448,256]{3,2,1,0:T(8,128)(2,1)}), bf16[4,2,448,256]{3,2,1,0:T(8,128)(2,1)}) %all-gather.2.cloned.1.call-update) | async-done | bytes 1835024 | tf_op jit(solution)/shard_map/all_gather | solution.py:153
  33.4 30.9 %shard_map.103 = (bf16[8,64,2048]{2,1,0:T(8,128)(2,1)}, bf16[8,2,64,256]{3,2,1,0:T(8,128)(2,1)}, f32[4,2,448,256]{3,2,1,0:T(8,128)}) custom-call(s32[8]{0:T(128)} %reshape.21.slots_ref, s32[4]{0:T(128)} %bitcast.5, s32[4]{0:T(128)} %len_ref.1, f32[8]{0:T(128)} %subtract_reduce_fusion.coef_ref, bf16[8,64,2048]{2,1,0:T(8,128)(2,1)} %q_ref.1, ...), custom_call_target="tpu_custom_call" | custom-call | tf_op jit(solution)/shard_map/pallas_call | solution.py:126
  64.3 0.0 reduce-scatter.2.cloned.1.call-update
  64.3 41.4 %reduce-scatter.2.cloned.1.call-done = f32[1,2,448,256]{3,2,1,0:T(8,128)} async-done(((f32[4,2,448,256]{3,2,1,0:T(8,128)}), f32[1,2,448,256]{3,2,1,0:T(8,128)}) %reduce-scatter.2.cloned.1.call-update) | async-done | bytes 917520 | tf_op jit(solution)/shard_map/reduce_scatter | solution.py:157
  105.7 2.0 %convert_element_type.3 = bf16[1,2,448,256]{3,2,1,0:T(8,128)(2,1)} convert(f32[1,2,448,256]{3,2,1,0:T(8,128)} %reduce-scatter.2.cloned.1.call-done) | non-fusion elementwise | flops 229376 | bytes 1376256 | tf_op jit(solution)/shard_map/convert_element_type | solution.py:158
  (1 shorter events, 0.0 us)
Async XLA Ops:
  7.2 26.2 %all-gather.2.cloned.1.call-start = ((), (), s32[]{:S(2)}) async-start(), calls=%async_computation.1 | async-start | bytes 2293760 | tf_op jit(solution)/shard_map/all_gather | solution.py:153
  7.9 97.8 %reduce-scatter.2.cloned.1.call-start = ((), (), s32[]{:S(2)}) async-start(), calls=%async_computation.2 | async-start | bytes 4587520 | tf_op jit(solution)/shard_map/reduce_scatter | solution.py:157
Sparse Core Ops, SparseCore 0:
  9.5 23.8 all-gather.1
  64.4 41.2 reduce-scatter.1

commit v2 on v1

--- a/solution.py
+++ b/solution.py
@@ -12,26 +12,16 @@
 dpo_beta = 0.5
 
 
-def attend_kernel(slots_ref, goal_ref, len_ref, coef_ref,
-                  q_ref, og_ref, skv_ref, pkv_ref,
-                  dq_ref, dkv_ref, dpre_ref, *, group, seq, prefix_rows):
-    p = pl.program_id(0)
-    member = pl.program_id(2)
-    s = slots_ref[2 * p + member]
-    goal = goal_ref[p]
-    length = len_ref[goal]
-    coef = coef_ref[s]
+def attend_math(q_blk, og_blk, keys_pre, values_pre, keys_own, values_own, length, coef,
+                *, group, seq, prefix_rows):
     scale = HD ** (-0.5)
     keys_all = prefix_rows + seq
     rows = group * seq
-
-    q_blk = q_ref[0]
-    og_blk = og_ref[0]
     cot_blk = (coef * og_blk.astype(jnp.float32)).astype(jnp.bfloat16)
     q_rows = jnp.concatenate([q_blk[:, g * HD:(g + 1) * HD] for g in range(group)], 0)
     c_rows = jnp.concatenate([cot_blk[:, g * HD:(g + 1) * HD] for g in range(group)], 0)
-    keys = jnp.concatenate([pkv_ref[0, 0], skv_ref[0, 0]], 0)
-    values = jnp.concatenate([pkv_ref[0, 1], skv_ref[0, 1]], 0)
+    keys = jnp.concatenate([keys_pre, keys_own], 0)
+    values = jnp.concatenate([values_pre, values_own], 0)
 
     nt = (((1,), (1,)), ((), ()))
     tn = (((0,), (0,)), ((), ()))
@@ -53,7 +43,10 @@
     grad_q = (scale * jnp.dot(grad_score, keys, preferred_element_type=jnp.float32)).astype(jnp.bfloat16)
     grad_k = scale * lax.dot_general(grad_score, q_rows, tn, preferred_element_type=jnp.float32)
     grad_v = lax.dot_general(prob_low, c_rows, tn, preferred_element_type=jnp.float32)
-
+    return grad_q, grad_k, grad_v
+
+
+def store_grads(grad_q, grad_k, grad_v, member, dq_ref, dkv_ref, dpre_ref, *, group, seq, prefix_rows):
     for g in range(group):
         dq_ref[0, :, g * HD:(g + 1) * HD] = grad_q[g * seq:(g + 1) * seq]
     dkv_ref[0, 0] = grad_k[prefix_rows:].astype(jnp.bfloat16)
@@ -68,6 +61,95 @@
     def _():
         dpre_ref[0, 0] += grad_k[:prefix_rows]
         dpre_ref[0, 1] += grad_v[:prefix_rows]
+
+
+def attend_kernel(slots_ref, goal_ref, len_ref, coef_ref,
+                  q_ref, og_ref, skv_ref, pkv_ref,
+                  dq_ref, dkv_ref, dpre_ref, *, group, seq, prefix_rows):
+    p = pl.program_id(0)
+    member = pl.program_id(2)
+    s = slots_ref[2 * p + member]
+    length = len_ref[goal_ref[p]]
+    dims = dict(group=group, seq=seq, prefix_rows=prefix_rows)
+    grads = attend_math(q_ref[0], og_ref[0], pkv_ref[0, 0], pkv_ref[0, 1], skv_ref[0, 0], skv_ref[0, 1],
+                        length, coef_ref[s], **dims)
+    store_grads(*grads, member, dq_ref, dkv_ref, dpre_ref, **dims)
+
+
+def slot_kernel(sidx_ref, len_ref, coef_ref, q_ref, og_ref, skv_ref, pkv_ref, *rest,
+                group, seq, prefix_rows, chained):
+    if chained:
+        rest = rest[2:]
+    dq_ref, dkv_ref, dpre_ref = rest
+    member = pl.program_id(1)
+    dims = dict(group=group, seq=seq, prefix_rows=prefix_rows)
+    grads = attend_math(q_ref[0], og_ref[0], pkv_ref[0, 0], pkv_ref[0, 1], skv_ref[0, 0], skv_ref[0, 1],
+                        len_ref[0], coef_ref[member], **dims)
+    store_grads(*grads, member, dq_ref, dkv_ref, dpre_ref, **dims)
+
+
+def attend_slot(sidx, length, coef, queries, out_grad, suffix_kv, prefix_one, chain):
+    suffix_count, seq, qwidth = queries.shape
+    kv_width = suffix_kv.shape[-1]
+    kv_local = kv_width // HD
+    group = qwidth // kv_width
+    prefix_rows = prefix_one.shape[2]
+    qb = group * HD
+
+    def q_map(k, m, sidx_ref):
+        return (sidx_ref[m], 0, k)
+
+    def skv_map(k, m, sidx_ref):
+        return (sidx_ref[m], 0, 0, k)
+
+    def pkv_map(k, m, sidx_ref):
+        return (0, 0, 0, k)
+
+    out_shape = (
+        jax.ShapeDtypeStruct((suffix_count, seq, qwidth), jnp.bfloat16),
+        jax.ShapeDtypeStruct((suffix_count, 2, seq, kv_width), jnp.bfloat16),
+        jax.ShapeDtypeStruct((1, 2, prefix_rows, kv_width), jnp.float32),
+    )
+    in_specs = [
+        pl.BlockSpec(memory_space=pltpu.SMEM),
+        pl.BlockSpec(memory_space=pltpu.SMEM),
+        pl.BlockSpec((1, seq, qb), q_map),
+        pl.BlockSpec((1, seq, qb), q_map),
+        pl.BlockSpec((1, 2, seq, HD), skv_map),
+        pl.BlockSpec((1, 2, prefix_rows, HD), pkv_map),
+    ]
+    operands = [length, coef, queries, out_grad, suffix_kv, prefix_one]
+    aliases = {}
+    if chain is not None:
+        in_specs += [pl.BlockSpec(memory_space=pl.ANY)] * 2
+        operands += list(chain)
+        aliases = {7: 0, 8: 1}
+    kernel = functools.partial(slot_kernel, group=group, seq=seq, prefix_rows=prefix_rows,
+                               chained=chain is not None)
+    grid_spec = pltpu.PrefetchScalarGridSpec(
+        num_scalar_prefetch=1,
+        grid=(kv_local, 2),
+        in_specs=in_specs,
+        out_specs=[
+            pl.BlockSpec((1, seq, qb), q_map),
+            pl.BlockSpec((1, 2, seq, HD), skv_map),
+            pl.BlockSpec((1, 2, prefix_rows, HD), pkv_map),
+        ],
+    )
+    steps = 2 * kv_local
+    cost = pl.CostEstimate(
+        flops=steps * 2_200_000_000,
+        transcendentals=steps * group * seq * (prefix_rows + seq),
+        bytes_accessed=steps * (4 * seq * qb + 4 * seq * HD + 6 * prefix_rows * HD) * 2,
+    )
+    return pl.pallas_call(
+        kernel,
+        grid_spec=grid_spec,
+        out_shape=out_shape,
+        input_output_aliases=aliases,
+        cost_estimate=cost,
+        compiler_params=pltpu.CompilerParams(dimension_semantics=("arbitrary", "arbitrary")),
+    )(sidx, *operands)
 
 
 def attend_all(slots, goals, lengths, coef, queries, out_grad, suffix_kv, prefix_all):
@@ -148,6 +230,11 @@
         - jnp.where(pick_chosen, weight[:, None], 0.0),
         0,
     )
+    dp_size = lax.axis_size("dp")
+    pair_count = pair_slots.shape[0]
+    if dp_size == 4 and pair_count == dp_size:
+        return pipelined(queries, suffix_kv, out_grad, prefix_kv, coefficient,
+                         pair_slots, pair_goal, prefix_len)
     slots = pair_slots.reshape(-1).astype(jnp.int32)
     goals = pair_goal[:, 0].astype(jnp.int32)
     prefix_all = lax.all_gather(prefix_kv, "dp", axis=0, tiled=True)
@@ -158,6 +245,37 @@
     return grad_q, grad_kv, prefix_grad.astype(jnp.bfloat16)
 
 
+def pipelined(queries, suffix_kv, out_grad, prefix_kv, coefficient, pair_slots, pair_goal, prefix_len):
+    me = lax.axis_index("dp")
+    partner = [(i, i ^ 1) for i in range(4)]
+    across = [(i, i ^ 2) for i in range(4)]
+    pre_partner = lax.ppermute(prefix_kv, "dp", partner)
+    pre_across = lax.ppermute(prefix_kv, "dp", across)
+    pre_relay = lax.ppermute(pre_across, "dp", partner)
+    pair_ids = jnp.arange(pair_slots.shape[0], dtype=jnp.int32)
+    goals = pair_goal[:, 0].astype(jnp.int32)
+
+    def slot_args(goal):
+        pair = jnp.sum(jnp.where(goals == goal, pair_ids, 0))
+        sidx = lax.dynamic_index_in_dim(pair_slots, pair, 0, keepdims=False).astype(jnp.int32)
+        length = lax.dynamic_slice_in_dim(prefix_len, goal, 1).astype(jnp.int32)
+        return sidx, length, coefficient[sidx]
+
+    chain = None
+    partials = []
+    for goal, prefix_one in ((me, prefix_kv), (me ^ 2, pre_across), (me ^ 3, pre_relay),
+                             (me ^ 1, pre_partner)):
+        sidx, length, coef = slot_args(goal)
+        grad_q, grad_kv, partial = attend_slot(sidx, length, coef, queries, out_grad, suffix_kv,
+                                               prefix_one, chain)
+        chain = (grad_q, grad_kv)
+        partials.append(partial)
+    own, cross, relay, near = partials
+    forward = (cross + lax.ppermute(relay, "dp", partner)).astype(jnp.bfloat16)
+    total = own + lax.ppermute(near, "dp", partner) + lax.ppermute(forward, "dp", across).astype(jnp.float32)
+    return chain[0], chain[1], total.astype(jnp.bfloat16)
+
+
 def solution(mesh):
     return jax.shard_map(
         shards,

time: 115 us -> 79.2 us (0.69)
  waiting for transfers between devices: 63.9 us -> 12.8 us
  Pallas kernels: 30.9 us -> 40.5 us
  local copies, waits for them, and re-layouts: 2.12 us -> 8.87 us
  between operations: 14 us -> 8.71 us
  starting transfers between devices: 0.08 us -> 4.32 us
    reduce_scatter x1 -> x0, waiting for transfers between devices: 41.4 us -> none  [shards(): lax.psum_scatter(partial, 'dp', scatter_dimension=0, tiled=True)]
    all_gather x1 -> x0, waiting for transfers between devices: 21.9 us -> none  [shards(): prefix_all = lax.all_gather(prefix_kv, 'dp', axis=0, tiled=True)]
    ppermute x0 -> x6, waiting for transfers between devices: none -> 12.8 us  [the longest x1 10.5 us: pipelined(): lax.ppermute(forward, 'dp', across).astype(jnp.float32)]
    pallas_call x1 -> x4, Pallas kernels: 30.9 us -> 40.5 us  [attend_slot(): pl.pallas_call(kernel, grid_spec=grid_spec, out_shape=out_shape, input_ou...]
    gather x0 -> x4, local copies, waits for them, and re-layouts: none -> 4.66 us  [slot_args(): return (sidx, length, coefficient[sidx])]
    ppermute x0 -> x6, starting transfers between devices: none -> 4.32 us  [the longest x1 3.06 us: pipelined(): pre_across = lax.ppermute(prefix_kv, 'dp', across)]
    dynamic_slice x0 -> x2, local copies, waits for them, and re-layouts: none -> 1.71 us  [the longest x1 1.05 us: slot_args(): lax.dynamic_index_in_dim(pair_slots, pair, 0, keepdims=False)]
    reduce_sum x0 -> x1, other arithmetic: none -> 1.41 us  [slot_args(): pair = jnp.sum(jnp.where(goals == goal, pair_ids, 0))]
  transfers between devices with their start and end apart: 2 -> 6, of which waited for: 2 -> 2; matrix products, arithmetic and copies ran while one was open for 3% -> 12% of each run, Pallas kernels for 0% -> 51%
where the time goes in v2:
time: 79.2 us; the launch traced here: 78.8 us
  Pallas kernels  40.5 us (51%)
  waiting for transfers between devices  12.8 us (16%)
  local copies, waits for them, and re-layouts  8.87 us (11%)
  between operations  8.71 us (11%)
  starting transfers between devices  4.32 us (5%)
  other arithmetic  3.51 us (4%)
    pallas_call x4, Pallas kernels, attend_slot(): pl.pallas_call(kernel, grid_spec=grid_spec, out_shape=out_shape, input_ou...  40.5 us
    ppermute x1, waiting for transfers between devices, pipelined(): lax.ppermute(forward, 'dp', across).astype(jnp.float32)  10.5 us
    gather x4, local copies, waits for them, and re-layouts, slot_args(): return (sidx, length, coefficient[sidx])  4.66 us
    ppermute x1, starting transfers between devices, pipelined(): pre_across = lax.ppermute(prefix_kv, 'dp', across)  3.06 us
    ppermute x1, waiting for transfers between devices, pipelined(): lax.ppermute(near, 'dp', partner)  2.35 us
    unnamed x20, local copies, waits for them, and re-layouts  1.75 us
  transfers between devices with their start and end apart: 6, of which 2 were waited for; matrix products, arithmetic and copies ran while one was open for 12% of the time, Pallas kernels for 51%

profile of v2, /device:TPU:0, one launch (start us, length us, event | category | flops | bytes accessed | tf_op | source)
XLA Modules:
  0.0 78.8 jit_solution(3270052939615768338)
XLA Ops:
  0.6 3.1 %collective-permute-start.1 = (bf16[1,2,448,256]{3,2,1,0:T(8,128)(2,1)}, bf16[1,2,448,256]{3,2,1,0:T(8,128)(2,1)S(1)}, u32[]{:S(2)}, u32[]{:S(2)}) collective-permute-start(bf16[1,2,448,256]{3,2,1,0:T(8,128)(2,1)} %pkv_ref.1), channel_id=1, source_target_pairs={{0,8},{4,12},{8,0},{12,4},{1,9},{5,13},{9,1},{13,5},{2,10},{6,14},... | collective-permute-start | bytes 1376264 | tf_op jit(solution)/shard_map/ppermute | solution.py:253
  3.7 0.0 collective-permute-start
  3.7 1.4 %fusion.3 = (s32[]{:T(128)}, s32[]{:T(128)}, s32[]{:T(128)}, s32[]{:T(128)}) fusion(s32[4,1]{0,1:T(1,128)} %param.14, s32[]{:T(128)S(6)} %axis_index.15, s32[]{:T(128)S(6)} %xor.10, s32[]{:T(128)S(6)} %xor.9, s32[]{:T(128)S(6)} %xor.11), kind=kLoop, calls=%fused_computation.30 | loop fusion | flops 44 | bytes 48 | tf_op jit(solution)/shard_map/reduce_sum | solution.py:259
  10.4 0.8 slice_bitcast_fusion
  13.8 1.0 %dynamic-slice_reduce_fusion = (s32[2]{0:T(128)S(1)}, s32[2]{0:T(128)S(1)}, s32[2]{0:T(128)S(1)}, s32[2]{0:T(128)S(1)}) fusion(s32[4,2]{0,1:T(2,128)} %param.13, s32[]{:T(128)S(6)} %select_n.109, s32[]{:T(128)S(6)} %select_n.101, s32[]{:T(128)S(6)} %select_n.93, s32[]{:T(128)S(6)} %select_n.105), kind=kLoop, calls=%fused_computation.23 | loop fusion | bytes 80 | tf_op jit(solution)/shard_map/jit(dynamic_index_in_dim)/dynamic_slice | solution.py:260
  14.9 0.9 %select_reduce_fusion = (f32[4]{0:T(128)S(1)}, f32[4]{0:T(128)S(1)}) fusion(f32[8]{0:T(128)} %param.12, s32[4]{0:T(128)S(1)} %get-tuple-element.38, s32[4]{0:T(128)S(1)} %get-tuple-element.37), kind=kLoop, calls=%fused_computation.15 | loop fusion | flops 184 | bytes 96 | tf_op jit(solution)/shard_map/reduce_sum | solution.py:226
  15.8 0.1 subtract_reduce_fusion
  15.9 1.2 %gather_fusion.3 = f32[2]{0:T(128)} fusion(f32[8]{0:T(128)S(1)} %subtract_reduce_fusion, s32[1024]{0:T(1024)S(1)} %pad_clamp_fusion), kind=kCustom, calls=%fused_computation.3 | custom fusion | bytes 24 | tf_op jit(solution)/shard_map/gather | solution.py:262
  17.1 1.1 %gather_fusion.2 = f32[2]{0:T(128)} fusion(f32[8]{0:T(128)S(1)} %subtract_reduce_fusion, s32[1024]{0:T(1024)S(1)} %pad_clamp_fusion.1), kind=kCustom, calls=%fused_computation.2 | custom fusion | bytes 24 | tf_op jit(solution)/shard_map/gather | solution.py:262
  18.2 1.1 %gather_fusion.1 = f32[2]{0:T(128)} fusion(f32[8]{0:T(128)S(1)} %subtract_reduce_fusion, s32[1024]{0:T(1024)S(1)} %pad_clamp_fusion.2), kind=kCustom, calls=%fused_computation.1 | custom fusion | bytes 24 | tf_op jit(solution)/shard_map/gather | solution.py:262
  19.4 1.2 %gather_fusion = f32[2]{0:T(128)} fusion(f32[8]{0:T(128)S(1)} %subtract_reduce_fusion, s32[1024]{0:T(1024)S(1)} %pad_clamp_fusion.3), kind=kCustom, calls=%fused_computation | custom fusion | bytes 24 | tf_op jit(solution)/shard_map/gather | solution.py:262
  20.6 0.7 fusion.8
  21.3 10.1 %shard_map.103 = (bf16[8,64,2048]{2,1,0:T(8,128)(2,1)}, bf16[8,2,64,256]{3,2,1,0:T(8,128)(2,1)}, f32[1,2,448,256]{3,2,1,0:T(8,128)}) custom-call(s32[2]{0:T(128)} %copy-done.6, s32[1]{0:T(128)} %get-tuple-element.39.len_ref, f32[2]{0:T(128)} %gather_fusion.3, bf16[8,64,2048]{2,1,0:T(8,128)(2,1)} %q_ref.7, bf16[8,64,2048]{2,1,0:T(8,128)(2,1)} %og_ref.7, ...), custom_call_target="tpu_custom_call" | custom-call | flops 8800000000 | bytes 5111808 | tf_op jit(solution)/shard_map/pallas_call | solution.py:145
  31.4 0.0 collective-permute-done.1.pkv_ref
  31.4 0.0 copy-start.8
  31.5 0.6 collective-permute-start.2
  32.0 0.2 copy-done.8
  32.2 10.0 %shard_map.104 = (bf16[8,64,2048]{2,1,0:T(8,128)(2,1)}, bf16[8,2,64,256]{3,2,1,0:T(8,128)(2,1)}, f32[1,2,448,256]{3,2,1,0:T(8,128)}) custom-call(s32[2]{0:T(128)} %copy-done.4, s32[1]{0:T(128)} %get-tuple-element.42.len_ref, f32[2]{0:T(128)} %gather_fusion.2, bf16[8,64,2048]{2,1,0:T(8,128)(2,1)} %q_ref.7, ...), custom_call_target="tpu_custom_call", output_to_operand_aliasing={{0}: (7, {}), {1}: (8, {})} | custom-call | flops 8800000000 | bytes 5111808 | tf_op jit(solution)/shard_map/pallas_call | solution.py:145
  42.3 0.0 collective-permute-done.2.pkv_ref
  42.3 0.0 copy-start.9
  42.3 0.8 copy-done.9
  43.0 10.1 %shard_map.105 = (bf16[8,64,2048]{2,1,0:T(8,128)(2,1)}, bf16[8,2,64,256]{3,2,1,0:T(8,128)(2,1)}, f32[1,2,448,256]{3,2,1,0:T(8,128)}) custom-call(s32[2]{0:T(128)} %copy-done.3, s32[1]{0:T(128)} %get-tuple-element.40.len_ref, f32[2]{0:T(128)} %gather_fusion.1, bf16[8,64,2048]{2,1,0:T(8,128)(2,1)} %q_ref.7, ...), custom_call_target="tpu_custom_call", output_to_operand_aliasing={{0}: (7, {}), {1}: (8, {})} | custom-call | flops 8800000000 | bytes 5111808 | tf_op jit(solution)/shard_map/pallas_call | solution.py:145
  53.2 0.5 collective-permute-start.4
  53.7 0.0 collective-permute-done.pkv_ref
  53.7 0.8 copy-done.7
  54.4 10.2 %shard_map.106 = (bf16[8,64,2048]{2,1,0:T(8,128)(2,1)}, bf16[8,2,64,256]{3,2,1,0:T(8,128)(2,1)}, f32[1,2,448,256]{3,2,1,0:T(8,128)}) custom-call(s32[2]{0:T(128)} %copy-done.5, s32[1]{0:T(128)} %get-tuple-element.41.len_ref, f32[2]{0:T(128)} %gather_fusion, bf16[8,64,2048]{2,1,0:T(8,128)(2,1)} %q_ref.7, ...), custom_call_target="tpu_custom_call", output_to_operand_aliasing={{0}: (7, {}), {1}: (8, {})} | custom-call | flops 8800000000 | bytes 5111808 | tf_op jit(solution)/shard_map/pallas_call | solution.py:145
  64.7 0.0 collective-permute-start.3
  64.7 0.1 add_convert_fusion.1
  64.9 0.1 collective-permute-start.5
  65.0 2.4 %collective-permute-done.3 = f32[1,2,448,256]{3,2,1,0:T(8,128)S(1)} collective-permute-done((f32[1,2,448,256]{3,2,1,0:T(8,128)}, f32[1,2,448,256]{3,2,1,0:T(8,128)S(1)}, u32[]{:S(2)}, u32[]{:S(2)}) %collective-permute-start.3) | collective-permute-done | bytes 917536 | tf_op jit(solution)/shard_map/ppermute | solution.py:275
  67.4 10.5 %collective-permute-done.5 = bf16[1,2,448,256]{3,2,1,0:T(8,128)(2,1)S(1)} collective-permute-done((bf16[1,2,448,256]{3,2,1,0:T(8,128)(2,1)S(1)}, bf16[1,2,448,256]{3,2,1,0:T(8,128)(2,1)S(1)}, u32[]{:S(2)}, u32[]{:S(2)}) %collective-permute-start.5) | collective-permute-done | bytes 458784 | tf_op jit(solution)/shard_map/ppermute | solution.py:275
  77.8 0.9 %add_convert_fusion = bf16[1,2,448,256]{3,2,1,0:T(8,128)(2,1)} fusion(bf16[1,2,448,256]{3,2,1,0:T(8,128)(2,1)S(1)} %collective-permute-done.5, f32[1,2,448,256]{3,2,1,0:T(8,128)S(1)} %copy-done.1, f32[1,2,448,256]{3,2,1,0:T(8,128)S(1)} %collective-permute-done.3), kind=kLoop, calls=%fused_computation.4 | loop fusion | flops 917504 | bytes 2752512 | tf_op jit(solution)/shard_map/convert_element_type | solution.py:276
  (24 shorter events, 0.1 us)
Async XLA Ops:
  0.6 20.0 %copy-start.2 = (s32[4]{0:T(128)S(1)}, s32[4]{0:T(128)}, u32[]{:S(2)}) copy-start(s32[4]{0:T(128)} %param.15) | copy-start | bytes 52
  0.6 30.8 %collective-permute-start.1 = (bf16[1,2,448,256]{3,2,1,0:T(8,128)(2,1)}, bf16[1,2,448,256]{3,2,1,0:T(8,128)(2,1)S(1)}, u32[]{:S(2)}, u32[]{:S(2)}) collective-permute-start(bf16[1,2,448,256]{3,2,1,0:T(8,128)(2,1)} %pkv_ref.1), channel_id=1, source_target_pairs={{0,8},{4,12},{8,0},{12,4},{1,9},{5,13},{9,1},{13,5},{2,10},{6,14},... | collective-permute-start | bytes 1376264 | tf_op jit(solution)/shard_map/ppermute | solution.py:253
  3.7 50.0 %collective-permute-start = (bf16[1,2,448,256]{3,2,1,0:T(8,128)(2,1)}, bf16[1,2,448,256]{3,2,1,0:T(8,128)(2,1)S(1)}, u32[]{:S(2)}, u32[]{:S(2)}) collective-permute-start(bf16[1,2,448,256]{3,2,1,0:T(8,128)(2,1)} %pkv_ref.1), channel_id=1, source_target_pairs={{0,4},{4,0},{8,12},{12,8},{1,5},{5,1},{9,13},{13,9},{2,6},{6,2},{1... | collective-permute-start | bytes 1376264 | tf_op jit(solution)/shard_map/ppermute | solution.py:252
  14.8 6.4 %copy-start.6 = (s32[2]{0:T(128)}, s32[2]{0:T(128)S(1)}, u32[]{:S(2)}) copy-start(s32[2]{0:T(128)S(1)} %get-tuple-element.27.sidx_ref) | copy-start | bytes 28
  14.9 16.6 %copy-start.3 = (s32[2]{0:T(128)}, s32[2]{0:T(128)S(1)}, u32[]{:S(2)}) copy-start(s32[2]{0:T(128)S(1)} %get-tuple-element.28.sidx_ref) | copy-start | bytes 28
  14.9 16.6 %copy-start.4 = (s32[2]{0:T(128)}, s32[2]{0:T(128)S(1)}, u32[]{:S(2)}) copy-start(s32[2]{0:T(128)S(1)} %get-tuple-element.30.sidx_ref) | copy-start | bytes 28
  14.9 16.5 %copy-start.5 = (s32[2]{0:T(128)}, s32[2]{0:T(128)S(1)}, u32[]{:S(2)}) copy-start(s32[2]{0:T(128)S(1)} %get-tuple-element.29.sidx_ref) | copy-start | bytes 28
  31.4 0.8 copy-start.8
  31.5 10.8 %collective-permute-start.2 = (bf16[1,2,448,256]{3,2,1,0:T(8,128)(2,1)S(1)}, bf16[1,2,448,256]{3,2,1,0:T(8,128)(2,1)S(1)}, u32[]{:S(2)}, u32[]{:S(2)}) collective-permute-start(bf16[1,2,448,256]{3,2,1,0:T(8,128)(2,1)S(1)} %collective-permute-done.1.pkv_ref), channel_id=1, source_target_pairs={{0,4},{4,0},{8,12},{12,8},{1,5},{5,1},{9,13},{13,9},{2,6},{6,2},{1... | collective-permute-start | bytes 1376264 | tf_op jit(solution)/shard_map/ppermute | solution.py:254
  42.3 0.8 copy-start.9
  53.2 11.5 %collective-permute-start.4 = (f32[1,2,448,256]{3,2,1,0:T(8,128)}, f32[1,2,448,256]{3,2,1,0:T(8,128)S(1)}, u32[]{:S(2)}, u32[]{:S(2)}) collective-permute-start(f32[1,2,448,256]{3,2,1,0:T(8,128)} %get-tuple-element.26), channel_id=1, source_target_pairs={{0,4},{4,0},{8,12},{12,8},{1,5},{5,1},{9,13},{13,9},{2,6},{6,2},{1... | collective-permute-start | bytes 2752520 | tf_op jit(solution)/shard_map/ppermute | solution.py:274
  53.7 0.8 copy-start.7
  54.4 10.3 %copy-start = (f32[1,2,448,256]{3,2,1,0:T(8,128)S(1)}, f32[1,2,448,256]{3,2,1,0:T(8,128)}, u32[]{:S(2)}) copy-start(f32[1,2,448,256]{3,2,1,0:T(8,128)} %get-tuple-element.25) | copy-start | bytes 2752516
  64.7 13.2 %copy-start.1 = (f32[1,2,448,256]{3,2,1,0:T(8,128)S(1)}, f32[1,2,448,256]{3,2,1,0:T(8,128)}, u32[]{:S(2)}) copy-start(f32[1,2,448,256]{3,2,1,0:T(8,128)} %get-tuple-element.23) | copy-start | bytes 2752516
  64.7 2.7 %collective-permute-start.3 = (f32[1,2,448,256]{3,2,1,0:T(8,128)}, f32[1,2,448,256]{3,2,1,0:T(8,128)S(1)}, u32[]{:S(2)}, u32[]{:S(2)}) collective-permute-start(f32[1,2,448,256]{3,2,1,0:T(8,128)} %get-tuple-element.24), channel_id=1, source_target_pairs={{0,4},{4,0},{8,12},{12,8},{1,5},{5,1},{9,13},{13,9},{2,6},{6,2},{1... | collective-permute-start | bytes 2752520 | tf_op jit(solution)/shard_map/ppermute | solution.py:275
  64.9 13.0 %collective-permute-start.5 = (bf16[1,2,448,256]{3,2,1,0:T(8,128)(2,1)S(1)}, bf16[1,2,448,256]{3,2,1,0:T(8,128)(2,1)S(1)}, u32[]{:S(2)}, u32[]{:S(2)}) collective-permute-start(bf16[1,2,448,256]{3,2,1,0:T(8,128)(2,1)S(1)} %add_convert_fusion.1), channel_id=1, source_target_pairs={{0,8},{4,12},{8,0},{12,4},{1,9},{5,13},{9,1},{13,5},{2,10},{6,14},... | collective-permute-start | bytes 1376264 | tf_op jit(solution)/shard_map/ppermute | solution.py:275

commit v3 on v2

--- a/solution.py
+++ b/solution.py
@@ -12,11 +12,19 @@
 dpo_beta = 0.5
 
 
+def mask_bias(length, *, group, seq, prefix_rows):
+    shape = (group * seq, prefix_rows + seq)
+    key_index = lax.broadcasted_iota(jnp.int32, shape, 1)
+    tok_index = lax.broadcasted_iota(jnp.int32, shape, 0) % seq
+    in_prefix = key_index < prefix_rows
+    allowed = (in_prefix & (key_index < length)) | (
+        jnp.logical_not(in_prefix) & (key_index - prefix_rows <= tok_index))
+    return jnp.where(allowed, 0.0, -1e30).astype(jnp.float32)
+
+
 def attend_math(q_blk, og_blk, keys_pre, values_pre, keys_own, values_own, length, coef,
-                *, group, seq, prefix_rows):
+                *, group, seq, prefix_rows, bias=None):
     scale = HD ** (-0.5)
-    keys_all = prefix_rows + seq
-    rows = group * seq
     cot_blk = (coef * og_blk.astype(jnp.float32)).astype(jnp.bfloat16)
     q_rows = jnp.concatenate([q_blk[:, g * HD:(g + 1) * HD] for g in range(group)], 0)
     c_rows = jnp.concatenate([cot_blk[:, g * HD:(g + 1) * HD] for g in range(group)], 0)
@@ -26,15 +34,12 @@
     nt = (((1,), (1,)), ((), ()))
     tn = (((0,), (0,)), ((), ()))
     scores = lax.dot_general(q_rows, keys, nt, preferred_element_type=jnp.float32) * scale
-    key_index = lax.broadcasted_iota(jnp.int32, (rows, keys_all), 1)
-    tok_index = lax.broadcasted_iota(jnp.int32, (rows, keys_all), 0) % seq
-    in_prefix = key_index < prefix_rows
-    allowed = (in_prefix & (key_index < length)) | (
-        jnp.logical_not(in_prefix) & (key_index - prefix_rows <= tok_index))
-    scores = jnp.where(allowed, scores, -1e30)
+    if bias is None:
+        bias = mask_bias(length, group=group, seq=seq, prefix_rows=prefix_rows)
+    scores = scores + bias
     row_max = jnp.max(scores, -1, keepdims=True)
     raised = jnp.exp(scores - row_max)
-    prob = raised / jnp.sum(raised, -1, keepdims=True)
+    prob = raised * (1.0 / jnp.sum(raised, -1, keepdims=True))
     prob_low = prob.astype(jnp.bfloat16)
     output = jnp.dot(prob_low, values, preferred_element_type=jnp.float32)
     row_dot = jnp.sum(c_rows.astype(jnp.float32) * output, -1, keepdims=True)
@@ -76,33 +81,58 @@
     store_grads(*grads, member, dq_ref, dkv_ref, dpre_ref, **dims)
 
 
-def slot_kernel(sidx_ref, len_ref, coef_ref, q_ref, og_ref, skv_ref, pkv_ref, *rest,
-                group, seq, prefix_rows, chained):
+def pair_of(goal, goal_ref, pair_count):
+    pair = 0
+    for p in range(pair_count):
+        pair = jnp.where(goal_ref[p] == goal, p, pair)
+    return pair
+
+
+def slot_kernel(me_ref, goal_ref, slots_ref, len_ref, lr_ref, q_ref, og_ref, skv_ref, pkv_ref, *rest,
+                group, seq, prefix_rows, flip, pair_count, chained):
     if chained:
         rest = rest[2:]
-    dq_ref, dkv_ref, dpre_ref = rest
+    dq_ref, dkv_ref, dpre_ref, bias_ref = rest
+    k = pl.program_id(0)
     member = pl.program_id(1)
+    goal = me_ref[0] ^ flip
+    pair = pair_of(goal, goal_ref, pair_count)
+    length = len_ref[goal]
     dims = dict(group=group, seq=seq, prefix_rows=prefix_rows)
+
+    @pl.when((k == 0) & (member == 0))
+    def _():
+        bias_ref[...] = mask_bias(length, **dims)
+
+    gap = lr_ref[slots_ref[2 * pair]] - lr_ref[slots_ref[2 * pair + 1]]
+    x = jnp.full((1, 128), -dpo_beta * gap, jnp.float32)
+    weight = dpo_beta * (1.0 / (1.0 + jnp.exp(-x)))
+    coef = jnp.where(member == 0, -weight, weight)[:, :1]
     grads = attend_math(q_ref[0], og_ref[0], pkv_ref[0, 0], pkv_ref[0, 1], skv_ref[0, 0], skv_ref[0, 1],
-                        len_ref[0], coef_ref[member], **dims)
+                        length, coef, bias=bias_ref[...], **dims)
     store_grads(*grads, member, dq_ref, dkv_ref, dpre_ref, **dims)
 
 
-def attend_slot(sidx, length, coef, queries, out_grad, suffix_kv, prefix_one, chain):
+def attend_slot(flip, me, goals, slots, lengths, logratio, queries, out_grad, suffix_kv, prefix_one, chain):
     suffix_count, seq, qwidth = queries.shape
     kv_width = suffix_kv.shape[-1]
     kv_local = kv_width // HD
     group = qwidth // kv_width
     prefix_rows = prefix_one.shape[2]
+    pair_count = goals.shape[0]
     qb = group * HD
 
-    def q_map(k, m, sidx_ref):
-        return (sidx_ref[m], 0, k)
-
-    def skv_map(k, m, sidx_ref):
-        return (sidx_ref[m], 0, 0, k)
-
-    def pkv_map(k, m, sidx_ref):
+    def suffix_of(m, me_ref, goal_ref, slots_ref):
+        pair = pair_of(me_ref[0] ^ flip, goal_ref, pair_count)
+        return slots_ref[2 * pair + m]
+
+    def q_map(k, m, me_ref, goal_ref, slots_ref, len_ref):
+        return (suffix_of(m, me_ref, goal_ref, slots_ref), 0, k)
+
+    def skv_map(k, m, me_ref, goal_ref, slots_ref, len_ref):
+        return (suffix_of(m, me_ref, goal_ref, slots_ref), 0, 0, k)
+
+    def pkv_map(k, m, me_ref, goal_ref, slots_ref, len_ref):
         return (0, 0, 0, k)
 
     out_shape = (
@@ -111,23 +141,22 @@
         jax.ShapeDtypeStruct((1, 2, prefix_rows, kv_width), jnp.float32),
     )
     in_specs = [
-        pl.BlockSpec(memory_space=pltpu.SMEM),
         pl.BlockSpec(memory_space=pltpu.SMEM),
         pl.BlockSpec((1, seq, qb), q_map),
         pl.BlockSpec((1, seq, qb), q_map),
         pl.BlockSpec((1, 2, seq, HD), skv_map),
         pl.BlockSpec((1, 2, prefix_rows, HD), pkv_map),
     ]
-    operands = [length, coef, queries, out_grad, suffix_kv, prefix_one]
+    operands = [logratio, queries, out_grad, suffix_kv, prefix_one]
     aliases = {}
     if chain is not None:
         in_specs += [pl.BlockSpec(memory_space=pl.ANY)] * 2
         operands += list(chain)
-        aliases = {7: 0, 8: 1}
-    kernel = functools.partial(slot_kernel, group=group, seq=seq, prefix_rows=prefix_rows,
-                               chained=chain is not None)
+        aliases = {9: 0, 10: 1}
+    kernel = functools.partial(slot_kernel, group=group, seq=seq, prefix_rows=prefix_rows, flip=flip,
+                               pair_count=pair_count, chained=chain is not None)
     grid_spec = pltpu.PrefetchScalarGridSpec(
-        num_scalar_prefetch=1,
+        num_scalar_prefetch=4,
         grid=(kv_local, 2),
         in_specs=in_specs,
         out_specs=[
@@ -135,6 +164,7 @@
             pl.BlockSpec((1, 2, seq, HD), skv_map),
             pl.BlockSpec((1, 2, prefix_rows, HD), pkv_map),
         ],
+        scratch_shapes=[pltpu.VMEM((group * seq, prefix_rows + seq), jnp.float32)],
     )
     steps = 2 * kv_local
     cost = pl.CostEstimate(
@@ -149,7 +179,7 @@
         input_output_aliases=aliases,
         cost_estimate=cost,
         compiler_params=pltpu.CompilerParams(dimension_semantics=("arbitrary", "arbitrary")),
-    )(sidx, *operands)
+    )(me, goals, slots, lengths, *operands)
 
 
 def attend_all(slots, goals, lengths, coef, queries, out_grad, suffix_kv, prefix_all):
@@ -216,6 +246,11 @@
 
 
 def shards(queries, suffix_kv, out_grad, prefix_kv, logratio, pair_slots, pair_goal, prefix_len):
+    dp_size = lax.axis_size("dp")
+    pair_count = pair_slots.shape[0]
+    if dp_size == 4 and pair_count == dp_size:
+        return pipelined(queries, suffix_kv, out_grad, prefix_kv, logratio,
+                         pair_slots, pair_goal, prefix_len)
     suffix_count = queries.shape[0]
     chosen = pair_slots[:, 0]
     rejected = pair_slots[:, 1]
@@ -230,11 +265,6 @@
         - jnp.where(pick_chosen, weight[:, None], 0.0),
         0,
     )
-    dp_size = lax.axis_size("dp")
-    pair_count = pair_slots.shape[0]
-    if dp_size == 4 and pair_count == dp_size:
-        return pipelined(queries, suffix_kv, out_grad, prefix_kv, coefficient,
-                         pair_slots, pair_goal, prefix_len)
     slots = pair_slots.reshape(-1).astype(jnp.int32)
     goals = pair_goal[:, 0].astype(jnp.int32)
     prefix_all = lax.all_gather(prefix_kv, "dp", axis=0, tiled=True)
@@ -245,33 +275,26 @@
     return grad_q, grad_kv, prefix_grad.astype(jnp.bfloat16)
 
 
-def pipelined(queries, suffix_kv, out_grad, prefix_kv, coefficient, pair_slots, pair_goal, prefix_len):
-    me = lax.axis_index("dp")
+def pipelined(queries, suffix_kv, out_grad, prefix_kv, logratio, pair_slots, pair_goal, prefix_len):
     partner = [(i, i ^ 1) for i in range(4)]
     across = [(i, i ^ 2) for i in range(4)]
+    pre_across = lax.ppermute(prefix_kv, "dp", across)
     pre_partner = lax.ppermute(prefix_kv, "dp", partner)
-    pre_across = lax.ppermute(prefix_kv, "dp", across)
     pre_relay = lax.ppermute(pre_across, "dp", partner)
-    pair_ids = jnp.arange(pair_slots.shape[0], dtype=jnp.int32)
-    goals = pair_goal[:, 0].astype(jnp.int32)
-
-    def slot_args(goal):
-        pair = jnp.sum(jnp.where(goals == goal, pair_ids, 0))
-        sidx = lax.dynamic_index_in_dim(pair_slots, pair, 0, keepdims=False).astype(jnp.int32)
-        length = lax.dynamic_slice_in_dim(prefix_len, goal, 1).astype(jnp.int32)
-        return sidx, length, coefficient[sidx]
-
-    chain = None
-    partials = []
-    for goal, prefix_one in ((me, prefix_kv), (me ^ 2, pre_across), (me ^ 3, pre_relay),
-                             (me ^ 1, pre_partner)):
-        sidx, length, coef = slot_args(goal)
-        grad_q, grad_kv, partial = attend_slot(sidx, length, coef, queries, out_grad, suffix_kv,
-                                               prefix_one, chain)
-        chain = (grad_q, grad_kv)
-        partials.append(partial)
-    own, cross, relay, near = partials
+    me = lax.axis_index("dp").astype(jnp.int32).reshape(1)
+    tables = (me, pair_goal.reshape(-1).astype(jnp.int32), pair_slots.reshape(-1).astype(jnp.int32),
+              prefix_len.astype(jnp.int32), logratio)
+
+    def run(flip, prefix_one, chain):
+        grad_q, grad_kv, partial = attend_slot(flip, *tables, queries, out_grad, suffix_kv, prefix_one, chain)
+        return (grad_q, grad_kv), partial
+
+    chain, own = run(0, prefix_kv, None)
+    chain, cross = run(2, pre_across, chain)
+    chain, relay = run(3, pre_relay, chain)
     forward = (cross + lax.ppermute(relay, "dp", partner)).astype(jnp.bfloat16)
+    forward, pre_partner = lax.optimization_barrier((forward, pre_partner))
+    chain, near = run(1, pre_partner, chain)
     total = own + lax.ppermute(near, "dp", partner) + lax.ppermute(forward, "dp", across).astype(jnp.float32)
     return chain[0], chain[1], total.astype(jnp.bfloat16)
 

time: 79.2 us -> 63.6 us (0.80)
  between operations: 8.71 us -> 0.69 us
  local copies, waits for them, and re-layouts: 8.87 us -> 3.59 us
  other arithmetic: 3.51 us -> 1.09 us
  Pallas kernels: 40.5 us -> 38.7 us
  waiting for transfers between devices: 12.8 us -> 14 us
  starting transfers between devices: 4.32 us -> 5.25 us
    gather x4 -> x0, local copies, waits for them, and re-layouts: 4.66 us -> none  [slot_args(): return (sidx, length, coefficient[sidx])]
    reduce_sum x3 -> x0, other arithmetic: 2.37 us -> none  [the longest x1 1.41 us: slot_args(): pair = jnp.sum(jnp.where(goals == goal, pair_ids, 0))]
    ppermute x1, waiting for transfers between devices: 2.35 us -> 0.01 us  [pipelined(): lax.ppermute(near, 'dp', partner)]
    ppermute x1, waiting for transfers between devices: 0.01 us -> 2.17 us  [pipelined(): forward = (cross + lax.ppermute(relay, 'dp', partner)).astype(jnp.bfloat16)]
    pallas_call x4, Pallas kernels: 40.5 us -> 38.7 us  [attend_slot(): pl.pallas_call(kernel, grid_spec=grid_spec, out_shape=out_shape, input_ou...]
    dynamic_slice x2 -> x0, local copies, waits for them, and re-layouts: 1.71 us -> none  [the longest x1 1.05 us: slot_args(): lax.dynamic_index_in_dim(pair_slots, pair, 0, keepdims=False)]
    ppermute x1, starting transfers between devices: 0.14 us -> 1.48 us  [pipelined(): lax.ppermute(forward, 'dp', across).astype(jnp.float32)]
    unnamed x20 -> x13, local copies, waits for them, and re-layouts: 1.75 us -> 2.99 us
  transfers between devices with their start and end apart: 6 -> 6, of which waited for: 2 -> 3; matrix products, arithmetic and copies ran while one was open for 12% -> 2% of each run, Pallas kernels for 51% -> 30%
where the time goes in v3:
time: 63.6 us; the launch traced here: 63.3 us
  Pallas kernels  38.7 us (61%)
  waiting for transfers between devices  14 us (22%)
  starting transfers between devices  5.25 us (8%)
  local copies, waits for them, and re-layouts  3.59 us (6%)
  other arithmetic  1.09 us (2%)
  between operations  0.69 us (1%)
    pallas_call x4, Pallas kernels, attend_slot(): pl.pallas_call(kernel, grid_spec=grid_spec, out_shape=out_shape, input_ou...  38.7 us
    ppermute x1, waiting for transfers between devices, pipelined(): lax.ppermute(forward, 'dp', across).astype(jnp.float32)  11.3 us
    ppermute x1, starting transfers between devices, pipelined(): pre_across = lax.ppermute(prefix_kv, 'dp', across)  3.06 us
    unnamed x13, local copies, waits for them, and re-layouts  2.99 us
    ppermute x1, waiting for transfers between devices, pipelined(): forward = (cross + lax.ppermute(relay, 'dp', partner)).astype(jnp.bfloat16)  2.17 us
    ppermute x1, starting transfers between devices, pipelined(): lax.ppermute(forward, 'dp', across).astype(jnp.float32)  1.48 us
  transfers between devices with their start and end apart: 6, of which 3 were waited for; matrix products, arithmetic and copies ran while one was open for 2% of the time, Pallas kernels for 30%

profile of v3, /device:TPU:0, one launch (start us, length us, event | category | flops | bytes accessed | tf_op | source)
XLA Modules:
  0.0 63.3 jit_solution(15599558665240677418)
XLA Ops:
  0.6 3.1 %collective-permute-start = (bf16[1,2,448,256]{3,2,1,0:T(8,128)(2,1)}, bf16[1,2,448,256]{3,2,1,0:T(8,128)(2,1)S(1)}, u32[]{:S(2)}, u32[]{:S(2)}) collective-permute-start(bf16[1,2,448,256]{3,2,1,0:T(8,128)(2,1)} %pkv_ref.1), channel_id=1, source_target_pairs={{0,8},{4,12},{8,0},{12,4},{1,9},{5,13},{9,1},{13,5},{2,10},{6,14},... | collective-permute-start | bytes 1376264 | tf_op jit(solution)/shard_map/ppermute | solution.py:281
  3.7 0.8 %copy.18 = s32[4,2]{1,0:T(4,128)S(1)} copy(s32[4,2]{0,1:T(2,128)} %param.13) | data formatting | bytes 64 | tf_op args[5]
  4.5 0.6 reshape.17.slots_ref
  5.1 9.6 %shard_map.103 = (bf16[8,64,2048]{2,1,0:T(8,128)(2,1)}, bf16[8,2,64,256]{3,2,1,0:T(8,128)(2,1)}, f32[1,2,448,256]{3,2,1,0:T(8,128)}) custom-call(s32[1]{0:T(128)} %bitcast.me_ref, s32[4]{0:T(128)} %bitcast.2, s32[8]{0:T(128)} %reshape.17.slots_ref, s32[4]{0:T(128)} %len_ref.7, f32[8]{0:T(128)} %lr_ref.7, bf16[8,64,2048]{2,1,0:T(8,128)(2,1)} %q_ref.7, ...), custom_call_target="tpu_custom_call" | custom-call | flops 8800000000 | bytes 5111808 | tf_op jit(solution)/shard_map/pallas_call | solution.py:175
  14.7 0.0 collective-permute-done.pkv_ref
  14.7 0.0 copy-start.3
  14.7 0.1 collective-permute-start.1
  14.8 0.7 %copy-done.3 = bf16[1,2,448,256]{3,2,1,0:T(8,128)(2,1)} copy-done((bf16[1,2,448,256]{3,2,1,0:T(8,128)(2,1)}, bf16[1,2,448,256]{3,2,1,0:T(8,128)(2,1)S(1)}, u32[]{:S(2)}) %copy-start.3) | copy-done | bytes 458776
  15.4 9.6 %shard_map.104 = (bf16[8,64,2048]{2,1,0:T(8,128)(2,1)}, bf16[8,2,64,256]{3,2,1,0:T(8,128)(2,1)}, f32[1,2,448,256]{3,2,1,0:T(8,128)}) custom-call(s32[1]{0:T(128)} %bitcast.me_ref, s32[4]{0:T(128)} %bitcast.3, s32[8]{0:T(128)} %reshape.17.slots_ref, s32[4]{0:T(128)} %len_ref.7, f32[8]{0:T(128)} %lr_ref.7, ...), custom_call_target="tpu_custom_call", output_to_operand_aliasing={{0}: (9, {}), {1}: (10, {})} | custom-call | flops 8800000000 | bytes 5111808 | tf_op jit(solution)/shard_map/pallas_call | solution.py:175
  25.0 0.0 collective-permute-done.1.pkv_ref
  25.0 0.0 copy-start.5
  25.1 0.8 %copy-done.5 = bf16[1,2,448,256]{3,2,1,0:T(8,128)(2,1)} copy-done((bf16[1,2,448,256]{3,2,1,0:T(8,128)(2,1)}, bf16[1,2,448,256]{3,2,1,0:T(8,128)(2,1)S(1)}, u32[]{:S(2)}) %copy-start.5) | copy-done | bytes 458776
  25.8 0.0 copy-start.2
  25.8 0.0 copy-start
  25.8 9.7 %shard_map.105 = (bf16[8,64,2048]{2,1,0:T(8,128)(2,1)}, bf16[8,2,64,256]{3,2,1,0:T(8,128)(2,1)}, f32[1,2,448,256]{3,2,1,0:T(8,128)}) custom-call(s32[1]{0:T(128)} %bitcast.me_ref, s32[4]{0:T(128)} %bitcast.4, s32[8]{0:T(128)} %reshape.17.slots_ref, s32[4]{0:T(128)} %len_ref.7, f32[8]{0:T(128)} %lr_ref.7, ...), custom_call_target="tpu_custom_call", output_to_operand_aliasing={{0}: (9, {}), {1}: (10, {})} | custom-call | flops 8800000000 | bytes 5111808 | tf_op jit(solution)/shard_map/pallas_call | solution.py:175
  35.6 0.0 collective-permute-start.2
  35.6 0.0 copy-done.2
  35.6 0.5 collective-permute-start.3
  36.1 2.2 %collective-permute-done.2 = f32[1,2,448,256]{3,2,1,0:T(8,128)S(1)} collective-permute-done((f32[1,2,448,256]{3,2,1,0:T(8,128)}, f32[1,2,448,256]{3,2,1,0:T(8,128)S(1)}, u32[]{:S(2)}, u32[]{:S(2)}) %collective-permute-start.2) | collective-permute-done | bytes 917536 | tf_op jit(solution)/shard_map/ppermute | solution.py:295
  38.2 0.0 copy-done
  38.2 0.1 add_convert_fusion.1
  38.4 0.5 collective-permute-done.3.pkv_ref
  38.9 0.0 copy-start.4
  38.9 0.8 %copy-done.4 = bf16[1,2,448,256]{3,2,1,0:T(8,128)(2,1)} copy-done((bf16[1,2,448,256]{3,2,1,0:T(8,128)(2,1)}, bf16[1,2,448,256]{3,2,1,0:T(8,128)(2,1)S(1)}, u32[]{:S(2)}) %copy-start.4) | copy-done | bytes 458776
  39.7 0.0 copy-start.1
  39.7 9.7 %shard_map.106 = (bf16[8,64,2048]{2,1,0:T(8,128)(2,1)}, bf16[8,2,64,256]{3,2,1,0:T(8,128)(2,1)}, f32[1,2,448,256]{3,2,1,0:T(8,128)}) custom-call(s32[1]{0:T(128)} %bitcast.me_ref, s32[4]{0:T(128)} %bitcast.5, s32[8]{0:T(128)} %reshape.17.slots_ref, s32[4]{0:T(128)} %len_ref.7, f32[8]{0:T(128)} %lr_ref.7, ...), custom_call_target="tpu_custom_call", output_to_operand_aliasing={{0}: (9, {}), {1}: (10, {})} | custom-call | flops 8800000000 | bytes 5111808 | tf_op jit(solution)/shard_map/pallas_call | solution.py:175
  49.4 0.1 collective-permute-start.4
  49.5 1.5 %collective-permute-start.5 = (bf16[1,2,448,256]{3,2,1,0:T(8,128)(2,1)S(1)}, bf16[1,2,448,256]{3,2,1,0:T(8,128)(2,1)S(1)}, u32[]{:S(2)}, u32[]{:S(2)}) collective-permute-start(bf16[1,2,448,256]{3,2,1,0:T(8,128)(2,1)S(1)} %add_convert_fusion.1), channel_id=1, source_target_pairs={{0,8},{4,12},{8,0},{12,4},{1,9},{5,13},{9,1},{13,5},{2,10},{6,14},... | collective-permute-start | bytes 1376264 | tf_op jit(solution)/shard_map/ppermute | solution.py:298
  51.0 11.3 %collective-permute-done.5 = bf16[1,2,448,256]{3,2,1,0:T(8,128)(2,1)S(1)} collective-permute-done((bf16[1,2,448,256]{3,2,1,0:T(8,128)(2,1)S(1)}, bf16[1,2,448,256]{3,2,1,0:T(8,128)(2,1)S(1)}, u32[]{:S(2)}, u32[]{:S(2)}) %collective-permute-start.5) | collective-permute-done | bytes 458784 | tf_op jit(solution)/shard_map/ppermute | solution.py:298
  62.3 0.0 collective-permute-done.4
  62.3 0.0 copy-done.1
  62.3 1.0 %add_convert_fusion = bf16[1,2,448,256]{3,2,1,0:T(8,128)(2,1)} fusion(bf16[1,2,448,256]{3,2,1,0:T(8,128)(2,1)S(1)} %collective-permute-done.5, f32[1,2,448,256]{3,2,1,0:T(8,128)S(1)} %copy-done.1, f32[1,2,448,256]{3,2,1,0:T(8,128)S(1)} %collective-permute-done.4), kind=kLoop, calls=%fused_computation | loop fusion | flops 917504 | bytes 2752512 | tf_op jit(solution)/shard_map/convert_element_type | solution.py:299
Async XLA Ops:
  0.6 14.0 %collective-permute-start = (bf16[1,2,448,256]{3,2,1,0:T(8,128)(2,1)}, bf16[1,2,448,256]{3,2,1,0:T(8,128)(2,1)S(1)}, u32[]{:S(2)}, u32[]{:S(2)}) collective-permute-start(bf16[1,2,448,256]{3,2,1,0:T(8,128)(2,1)} %pkv_ref.1), channel_id=1, source_target_pairs={{0,8},{4,12},{8,0},{12,4},{1,9},{5,13},{9,1},{13,5},{2,10},{6,14},... | collective-permute-start | bytes 1376264 | tf_op jit(solution)/shard_map/ppermute | solution.py:281
  14.7 0.8 %copy-start.3 = (bf16[1,2,448,256]{3,2,1,0:T(8,128)(2,1)}, bf16[1,2,448,256]{3,2,1,0:T(8,128)(2,1)S(1)}, u32[]{:S(2)}) copy-start(bf16[1,2,448,256]{3,2,1,0:T(8,128)(2,1)S(1)} %collective-permute-done.pkv_ref) | copy-start | bytes 1376260
  14.7 10.4 %collective-permute-start.1 = (bf16[1,2,448,256]{3,2,1,0:T(8,128)(2,1)S(1)}, bf16[1,2,448,256]{3,2,1,0:T(8,128)(2,1)S(1)}, u32[]{:S(2)}, u32[]{:S(2)}) collective-permute-start(bf16[1,2,448,256]{3,2,1,0:T(8,128)(2,1)S(1)} %collective-permute-done.pkv_ref), channel_id=1, source_target_pairs={{0,4},{4,0},{8,12},{12,8},{1,5},{5,1},{9,13},{13,9},{2,6},{6,2},{1... | collective-permute-start | bytes 1376264 | tf_op jit(solution)/shard_map/ppermute | solution.py:283
  25.0 0.8 %copy-start.5 = (bf16[1,2,448,256]{3,2,1,0:T(8,128)(2,1)}, bf16[1,2,448,256]{3,2,1,0:T(8,128)(2,1)S(1)}, u32[]{:S(2)}) copy-start(bf16[1,2,448,256]{3,2,1,0:T(8,128)(2,1)S(1)} %collective-permute-done.1.pkv_ref) | copy-start | bytes 1376260
  25.8 9.7 %copy-start.2 = (bf16[1,2,448,256]{3,2,1,0:T(8,128)(2,1)S(1)}, bf16[1,2,448,256]{3,2,1,0:T(8,128)(2,1)}, u32[]{:S(2)}) copy-start(bf16[1,2,448,256]{3,2,1,0:T(8,128)(2,1)} %pkv_ref.1) | copy-start | bytes 1376260
  25.8 12.4 %copy-start = (f32[1,2,448,256]{3,2,1,0:T(8,128)S(1)}, f32[1,2,448,256]{3,2,1,0:T(8,128)}, u32[]{:S(2)}) copy-start(f32[1,2,448,256]{3,2,1,0:T(8,128)} %get-tuple-element.19) | copy-start | bytes 2752516
  35.6 2.7 %collective-permute-start.2 = (f32[1,2,448,256]{3,2,1,0:T(8,128)}, f32[1,2,448,256]{3,2,1,0:T(8,128)S(1)}, u32[]{:S(2)}, u32[]{:S(2)}) collective-permute-start(f32[1,2,448,256]{3,2,1,0:T(8,128)} %get-tuple-element.22), channel_id=1, source_target_pairs={{0,4},{4,0},{8,12},{12,8},{1,5},{5,1},{9,13},{13,9},{2,6},{6,2},{1... | collective-permute-start | bytes 2752520 | tf_op jit(solution)/shard_map/ppermute | solution.py:295
  35.6 3.3 %collective-permute-start.3 = (bf16[1,2,448,256]{3,2,1,0:T(8,128)(2,1)S(1)}, bf16[1,2,448,256]{3,2,1,0:T(8,128)(2,1)S(1)}, u32[]{:S(2)}, u32[]{:S(2)}) collective-permute-start(bf16[1,2,448,256]{3,2,1,0:T(8,128)(2,1)S(1)} %copy-done.2), channel_id=1, source_target_pairs={{0,4},{4,0},{8,12},{12,8},{1,5},{5,1},{9,13},{13,9},{2,6},{6,2},{1... | collective-permute-start | bytes 1376264 | tf_op jit(solution)/shard_map/ppermute | solution.py:282
  38.9 0.8 %copy-start.4 = (bf16[1,2,448,256]{3,2,1,0:T(8,128)(2,1)}, bf16[1,2,448,256]{3,2,1,0:T(8,128)(2,1)S(1)}, u32[]{:S(2)}) copy-start(bf16[1,2,448,256]{3,2,1,0:T(8,128)(2,1)S(1)} %collective-permute-done.3.pkv_ref) | copy-start | bytes 1376260
  39.7 22.7 %copy-start.1 = (f32[1,2,448,256]{3,2,1,0:T(8,128)S(1)}, f32[1,2,448,256]{3,2,1,0:T(8,128)}, u32[]{:S(2)}) copy-start(f32[1,2,448,256]{3,2,1,0:T(8,128)} %get-tuple-element.28) | copy-start | bytes 2752516
  49.4 12.9 %collective-permute-start.4 = (f32[1,2,448,256]{3,2,1,0:T(8,128)}, f32[1,2,448,256]{3,2,1,0:T(8,128)S(1)}, u32[]{:S(2)}, u32[]{:S(2)}) collective-permute-start(f32[1,2,448,256]{3,2,1,0:T(8,128)} %get-tuple-element.29), channel_id=1, source_target_pairs={{0,4},{4,0},{8,12},{12,8},{1,5},{5,1},{9,13},{13,9},{2,6},{6,2},{1... | collective-permute-start | bytes 2752520 | tf_op jit(solution)/shard_map/ppermute | solution.py:298
  49.5 12.8 %collective-permute-start.5 = (bf16[1,2,448,256]{3,2,1,0:T(8,128)(2,1)S(1)}, bf16[1,2,448,256]{3,2,1,0:T(8,128)(2,1)S(1)}, u32[]{:S(2)}, u32[]{:S(2)}) collective-permute-start(bf16[1,2,448,256]{3,2,1,0:T(8,128)(2,1)S(1)} %add_convert_fusion.1), channel_id=1, source_target_pairs={{0,8},{4,12},{8,0},{12,4},{1,9},{5,13},{9,1},{13,5},{2,10},{6,14},... | collective-permute-start | bytes 1376264 | tf_op jit(solution)/shard_map/ppermute | solution.py:298

commit v4 on v3

--- a/solution.py
+++ b/solution.py
@@ -280,7 +280,6 @@
     across = [(i, i ^ 2) for i in range(4)]
     pre_across = lax.ppermute(prefix_kv, "dp", across)
     pre_partner = lax.ppermute(prefix_kv, "dp", partner)
-    pre_relay = lax.ppermute(pre_across, "dp", partner)
     me = lax.axis_index("dp").astype(jnp.int32).reshape(1)
     tables = (me, pair_goal.reshape(-1).astype(jnp.int32), pair_slots.reshape(-1).astype(jnp.int32),
               prefix_len.astype(jnp.int32), logratio)
@@ -289,13 +288,16 @@
         grad_q, grad_kv, partial = attend_slot(flip, *tables, queries, out_grad, suffix_kv, prefix_one, chain)
         return (grad_q, grad_kv), partial
 
-    chain, own = run(0, prefix_kv, None)
+    chain, near = run(1, pre_partner, None)
+    pre_across, near = lax.optimization_barrier((pre_across, near))
+    pre_relay = lax.ppermute(pre_across, "dp", partner)
+    near_sent = lax.ppermute(near, "dp", partner)
     chain, cross = run(2, pre_across, chain)
     chain, relay = run(3, pre_relay, chain)
     forward = (cross + lax.ppermute(relay, "dp", partner)).astype(jnp.bfloat16)
-    forward, pre_partner = lax.optimization_barrier((forward, pre_partner))
-    chain, near = run(1, pre_partner, chain)
-    total = own + lax.ppermute(near, "dp", partner) + lax.ppermute(forward, "dp", across).astype(jnp.float32)
+    forward, own_prefix = lax.optimization_barrier((forward, prefix_kv))
+    chain, own = run(0, own_prefix, chain)
+    total = own + near_sent + lax.ppermute(forward, "dp", across).astype(jnp.float32)
     return chain[0], chain[1], total.astype(jnp.bfloat16)
 
 

time: 63.6 us -> 54.3 us (0.85)
  waiting for transfers between devices: 14 us -> 3.88 us
  other arithmetic: 1.09 us -> 2.25 us
    ppermute x1, waiting for transfers between devices: 11.3 us -> 1.7 us  [pipelined(): lax.ppermute(forward, 'dp', across).astype(jnp.float32)]
    convert_element_type x1, other arithmetic: 0.95 us -> 2.11 us  [pipelined(): return (chain[0], chain[1], total.astype(jnp.bfloat16))]
    unnamed x13 -> x11, local copies, waits for them, and re-layouts: 2.99 us -> 2.85 us
  transfers between devices with their start and end apart: 6 -> 6, of which waited for: 3 -> 2; matrix products, arithmetic and copies ran while one was open for 2% -> 3% of each run, Pallas kernels for 30% -> 53%
where the time goes in v4:
time: 54.3 us; the launch traced here: 54 us
  Pallas kernels  38.5 us (71%)
  starting transfers between devices  5.2 us (10%)
  waiting for transfers between devices  3.88 us (7%)
  local copies, waits for them, and re-layouts  3.5 us (6%)
  other arithmetic  2.25 us (4%)
  between operations  0.67 us (1%)
    pallas_call x4, Pallas kernels, attend_slot(): pl.pallas_call(kernel, grid_spec=grid_spec, out_shape=out_shape, input_ou...  38.5 us
    unnamed x11, local copies, waits for them, and re-layouts  2.85 us
    ppermute x1, starting transfers between devices, pipelined(): pre_across = lax.ppermute(prefix_kv, 'dp', across)  2.58 us
    ppermute x1, waiting for transfers between devices, pipelined(): forward = (cross + lax.ppermute(relay, 'dp', partner)).astype(jnp.bfloat16)  2.17 us
    convert_element_type x1, other arithmetic, pipelined(): return (chain[0], chain[1], total.astype(jnp.bfloat16))  2.11 us
    ppermute x1, waiting for transfers between devices, pipelined(): lax.ppermute(forward, 'dp', across).astype(jnp.float32)  1.7 us
    ppermute x1, starting transfers between devices, pipelined(): lax.ppermute(forward, 'dp', across).astype(jnp.float32)  1.33 us
  transfers between devices with their start and end apart: 6, of which 2 were waited for; matrix products, arithmetic and copies ran while one was open for 3% of the time, Pallas kernels for 53%

profile of v4, /device:TPU:0, one launch (start us, length us, event | category | flops | bytes accessed | tf_op | source)
XLA Modules:
  0.0 54.0 jit_solution(12681592185549605653)
XLA Ops:
  0.6 0.6 %collective-permute-start.1 = (bf16[1,2,448,256]{3,2,1,0:T(8,128)(2,1)}, bf16[1,2,448,256]{3,2,1,0:T(8,128)(2,1)S(1)}, u32[]{:S(2)}, u32[]{:S(2)}) collective-permute-start(bf16[1,2,448,256]{3,2,1,0:T(8,128)(2,1)} %pkv_ref), channel_id=1, source_target_pairs={{0,4},{4,0},{8,12},{12,8},{1,5},{5,1},{9,13},{13,9},{2,6},{6,2},{1... | collective-permute-start | bytes 1376264 | tf_op jit(solution)/shard_map/ppermute | solution.py:282
  1.2 2.6 %collective-permute-start = (bf16[1,2,448,256]{3,2,1,0:T(8,128)(2,1)}, bf16[1,2,448,256]{3,2,1,0:T(8,128)(2,1)S(1)}, u32[]{:S(2)}, u32[]{:S(2)}) collective-permute-start(bf16[1,2,448,256]{3,2,1,0:T(8,128)(2,1)} %pkv_ref), channel_id=1, source_target_pairs={{0,8},{4,12},{8,0},{12,4},{1,9},{5,13},{9,1},{13,5},{2,10},{6,14},... | collective-permute-start | bytes 1376264 | tf_op jit(solution)/shard_map/ppermute | solution.py:281
  3.8 0.8 %copy.18 = s32[4,2]{1,0:T(4,128)S(1)} copy(s32[4,2]{0,1:T(2,128)} %param.13) | data formatting | bytes 64 | tf_op args[5]
  4.5 0.7 %reshape.17.slots_ref = s32[8]{0:T(128)} reshape(s32[4,2]{1,0:T(4,128)S(1)} %copy.18) | data formatting | bytes 64 | tf_op jit(solution)/shard_map/reshape | solution.py:284
  5.2 0.0 collective-permute-done.1.pkv_ref
  5.2 0.0 copy-start.3
  5.2 0.8 %copy-done.3 = bf16[1,2,448,256]{3,2,1,0:T(8,128)(2,1)} copy-done((bf16[1,2,448,256]{3,2,1,0:T(8,128)(2,1)}, bf16[1,2,448,256]{3,2,1,0:T(8,128)(2,1)S(1)}, u32[]{:S(2)}) %copy-start.3) | copy-done | bytes 458776
  6.0 9.6 %shard_map.103 = (bf16[8,64,2048]{2,1,0:T(8,128)(2,1)}, bf16[8,2,64,256]{3,2,1,0:T(8,128)(2,1)}, f32[1,2,448,256]{3,2,1,0:T(8,128)}) custom-call(s32[1]{0:T(128)} %bitcast.me_ref, s32[4]{0:T(128)} %bitcast.2, s32[8]{0:T(128)} %reshape.17.slots_ref, s32[4]{0:T(128)} %len_ref.7, f32[8]{0:T(128)} %lr_ref.7, bf16[8,64,2048]{2,1,0:T(8,128)(2,1)} %q_ref.7, ...), custom_call_target="tpu_custom_call" | custom-call | flops 8800000000 | bytes 5111808 | tf_op jit(solution)/shard_map/pallas_call | solution.py:175
  15.6 0.0 collective-permute-done.pkv_ref
  15.6 0.0 copy-start.2
  15.6 0.2 collective-permute-start.2
  15.8 0.5 %copy-done.2 = bf16[1,2,448,256]{3,2,1,0:T(8,128)(2,1)} copy-done((bf16[1,2,448,256]{3,2,1,0:T(8,128)(2,1)}, bf16[1,2,448,256]{3,2,1,0:T(8,128)(2,1)S(1)}, u32[]{:S(2)}) %copy-start.2) | copy-done | bytes 458776
  16.3 9.6 %shard_map.104 = (bf16[8,64,2048]{2,1,0:T(8,128)(2,1)}, bf16[8,2,64,256]{3,2,1,0:T(8,128)(2,1)}, f32[1,2,448,256]{3,2,1,0:T(8,128)}) custom-call(s32[1]{0:T(128)} %bitcast.me_ref, s32[4]{0:T(128)} %bitcast.3, s32[8]{0:T(128)} %reshape.17.slots_ref, s32[4]{0:T(128)} %len_ref.7, f32[8]{0:T(128)} %lr_ref.7, ...), custom_call_target="tpu_custom_call", output_to_operand_aliasing={{0}: (9, {}), {1}: (10, {})} | custom-call | flops 8800000000 | bytes 5111808 | tf_op jit(solution)/shard_map/pallas_call | solution.py:175
  25.9 0.0 collective-permute-done.2.pkv_ref
  25.9 0.0 copy-start.4
  26.0 0.8 %copy-done.4 = bf16[1,2,448,256]{3,2,1,0:T(8,128)(2,1)} copy-done((bf16[1,2,448,256]{3,2,1,0:T(8,128)(2,1)}, bf16[1,2,448,256]{3,2,1,0:T(8,128)(2,1)S(1)}, u32[]{:S(2)}) %copy-start.4) | copy-done | bytes 458776
  26.7 0.0 copy-start.1
  26.7 0.0 copy-start
  26.7 9.7 %shard_map.105 = (bf16[8,64,2048]{2,1,0:T(8,128)(2,1)}, bf16[8,2,64,256]{3,2,1,0:T(8,128)(2,1)}, f32[1,2,448,256]{3,2,1,0:T(8,128)}) custom-call(s32[1]{0:T(128)} %bitcast.me_ref, s32[4]{0:T(128)} %bitcast.4, s32[8]{0:T(128)} %reshape.17.slots_ref, s32[4]{0:T(128)} %len_ref.7, f32[8]{0:T(128)} %lr_ref.7, ...), custom_call_target="tpu_custom_call", output_to_operand_aliasing={{0}: (9, {}), {1}: (10, {})} | custom-call | flops 8800000000 | bytes 5111808 | tf_op jit(solution)/shard_map/pallas_call | solution.py:175
  36.5 0.1 collective-permute-start.3
  36.6 0.0 copy-done.1
  36.6 0.4 collective-permute-start.4
  37.0 2.2 %collective-permute-done.3 = f32[1,2,448,256]{3,2,1,0:T(8,128)S(1)} collective-permute-done((f32[1,2,448,256]{3,2,1,0:T(8,128)}, f32[1,2,448,256]{3,2,1,0:T(8,128)S(1)}, u32[]{:S(2)}, u32[]{:S(2)}) %collective-permute-start.3) | collective-permute-done | bytes 917536 | tf_op jit(solution)/shard_map/ppermute | solution.py:297
  39.1 0.0 copy-done
  39.1 0.1 add_convert_fusion.1
  39.3 1.3 %collective-permute-start.5 = (bf16[1,2,448,256]{3,2,1,0:T(8,128)(2,1)S(1)}, bf16[1,2,448,256]{3,2,1,0:T(8,128)(2,1)S(1)}, u32[]{:S(2)}, u32[]{:S(2)}) collective-permute-start(bf16[1,2,448,256]{3,2,1,0:T(8,128)(2,1)S(1)} %add_convert_fusion.1), channel_id=1, source_target_pairs={{0,8},{4,12},{8,0},{12,4},{1,9},{5,13},{9,1},{13,5},{2,10},{6,14},... | collective-permute-start | bytes 1376264 | tf_op jit(solution)/shard_map/ppermute | solution.py:300
  40.6 9.6 %shard_map.106 = (bf16[8,64,2048]{2,1,0:T(8,128)(2,1)}, bf16[8,2,64,256]{3,2,1,0:T(8,128)(2,1)}, f32[1,2,448,256]{3,2,1,0:T(8,128)}) custom-call(s32[1]{0:T(128)} %bitcast.me_ref, s32[4]{0:T(128)} %bitcast.5, s32[8]{0:T(128)} %reshape.17.slots_ref, s32[4]{0:T(128)} %len_ref.7, f32[8]{0:T(128)} %lr_ref.7, ...), custom_call_target="tpu_custom_call", output_to_operand_aliasing={{0}: (9, {}), {1}: (10, {})} | custom-call | flops 8800000000 | bytes 5111808 | tf_op jit(solution)/shard_map/pallas_call | solution.py:175
  50.2 0.0 collective-permute-done.4
  50.2 1.7 %collective-permute-done.5 = bf16[1,2,448,256]{3,2,1,0:T(8,128)(2,1)S(1)} collective-permute-done((bf16[1,2,448,256]{3,2,1,0:T(8,128)(2,1)S(1)}, bf16[1,2,448,256]{3,2,1,0:T(8,128)(2,1)S(1)}, u32[]{:S(2)}, u32[]{:S(2)}) %collective-permute-start.5) | collective-permute-done | bytes 458784 | tf_op jit(solution)/shard_map/ppermute | solution.py:300
  51.9 2.1 %add_convert_fusion = bf16[1,2,448,256]{3,2,1,0:T(8,128)(2,1)} fusion(bf16[1,2,448,256]{3,2,1,0:T(8,128)(2,1)S(1)} %collective-permute-done.5, f32[1,2,448,256]{3,2,1,0:T(8,128)} %get-tuple-element.32, f32[1,2,448,256]{3,2,1,0:T(8,128)S(1)} %collective-permute-done.4), kind=kLoop, calls=%fused_computation | loop fusion | flops 917504 | bytes 2752512 | tf_op jit(solution)/shard_map/convert_element_type | solution.py:301
Async XLA Ops:
  0.6 4.6 %collective-permute-start.1 = (bf16[1,2,448,256]{3,2,1,0:T(8,128)(2,1)}, bf16[1,2,448,256]{3,2,1,0:T(8,128)(2,1)S(1)}, u32[]{:S(2)}, u32[]{:S(2)}) collective-permute-start(bf16[1,2,448,256]{3,2,1,0:T(8,128)(2,1)} %pkv_ref), channel_id=1, source_target_pairs={{0,4},{4,0},{8,12},{12,8},{1,5},{5,1},{9,13},{13,9},{2,6},{6,2},{1... | collective-permute-start | bytes 1376264 | tf_op jit(solution)/shard_map/ppermute | solution.py:282
  1.2 14.4 %collective-permute-start = (bf16[1,2,448,256]{3,2,1,0:T(8,128)(2,1)}, bf16[1,2,448,256]{3,2,1,0:T(8,128)(2,1)S(1)}, u32[]{:S(2)}, u32[]{:S(2)}) collective-permute-start(bf16[1,2,448,256]{3,2,1,0:T(8,128)(2,1)} %pkv_ref), channel_id=1, source_target_pairs={{0,8},{4,12},{8,0},{12,4},{1,9},{5,13},{9,1},{13,5},{2,10},{6,14},... | collective-permute-start | bytes 1376264 | tf_op jit(solution)/shard_map/ppermute | solution.py:281
  5.2 0.8 %copy-start.3 = (bf16[1,2,448,256]{3,2,1,0:T(8,128)(2,1)}, bf16[1,2,448,256]{3,2,1,0:T(8,128)(2,1)S(1)}, u32[]{:S(2)}) copy-start(bf16[1,2,448,256]{3,2,1,0:T(8,128)(2,1)S(1)} %collective-permute-done.1.pkv_ref) | copy-start | bytes 1376260
  15.6 0.8 %copy-start.2 = (bf16[1,2,448,256]{3,2,1,0:T(8,128)(2,1)}, bf16[1,2,448,256]{3,2,1,0:T(8,128)(2,1)S(1)}, u32[]{:S(2)}) copy-start(bf16[1,2,448,256]{3,2,1,0:T(8,128)(2,1)S(1)} %collective-permute-done.pkv_ref) | copy-start | bytes 1376260
  15.6 10.4 %collective-permute-start.2 = (bf16[1,2,448,256]{3,2,1,0:T(8,128)(2,1)S(1)}, bf16[1,2,448,256]{3,2,1,0:T(8,128)(2,1)S(1)}, u32[]{:S(2)}, u32[]{:S(2)}) collective-permute-start(bf16[1,2,448,256]{3,2,1,0:T(8,128)(2,1)S(1)} %collective-permute-done.pkv_ref), channel_id=1, source_target_pairs={{0,4},{4,0},{8,12},{12,8},{1,5},{5,1},{9,13},{13,9},{2,6},{6,2},{1... | collective-permute-start | bytes 1376264 | tf_op jit(solution)/shard_map/ppermute | solution.py:293
  25.9 0.8 %copy-start.4 = (bf16[1,2,448,256]{3,2,1,0:T(8,128)(2,1)}, bf16[1,2,448,256]{3,2,1,0:T(8,128)(2,1)S(1)}, u32[]{:S(2)}) copy-start(bf16[1,2,448,256]{3,2,1,0:T(8,128)(2,1)S(1)} %collective-permute-done.2.pkv_ref) | copy-start | bytes 1376260
  26.7 9.9 %copy-start.1 = (f32[1,2,448,256]{3,2,1,0:T(8,128)S(1)}, f32[1,2,448,256]{3,2,1,0:T(8,128)}, u32[]{:S(2)}) copy-start(f32[1,2,448,256]{3,2,1,0:T(8,128)} %get-tuple-element.33) | copy-start | bytes 2752516
  26.7 12.4 %copy-start = (f32[1,2,448,256]{3,2,1,0:T(8,128)S(1)}, f32[1,2,448,256]{3,2,1,0:T(8,128)}, u32[]{:S(2)}) copy-start(f32[1,2,448,256]{3,2,1,0:T(8,128)} %get-tuple-element.23) | copy-start | bytes 2752516
  36.5 2.7 %collective-permute-start.3 = (f32[1,2,448,256]{3,2,1,0:T(8,128)}, f32[1,2,448,256]{3,2,1,0:T(8,128)S(1)}, u32[]{:S(2)}, u32[]{:S(2)}) collective-permute-start(f32[1,2,448,256]{3,2,1,0:T(8,128)} %get-tuple-element.26), channel_id=1, source_target_pairs={{0,4},{4,0},{8,12},{12,8},{1,5},{5,1},{9,13},{13,9},{2,6},{6,2},{1... | collective-permute-start | bytes 2752520 | tf_op jit(solution)/shard_map/ppermute | solution.py:297
  36.6 13.6 %collective-permute-start.4 = (f32[1,2,448,256]{3,2,1,0:T(8,128)S(1)}, f32[1,2,448,256]{3,2,1,0:T(8,128)S(1)}, u32[]{:S(2)}, u32[]{:S(2)}) collective-permute-start(f32[1,2,448,256]{3,2,1,0:T(8,128)S(1)} %copy-done.1), channel_id=1, source_target_pairs={{0,4},{4,0},{8,12},{12,8},{1,5},{5,1},{9,13},{13,9},{2,6},{6,2},{1... | collective-permute-start | bytes 2752520 | tf_op jit(solution)/shard_map/ppermute | solution.py:294
  39.3 12.6 %collective-permute-start.5 = (bf16[1,2,448,256]{3,2,1,0:T(8,128)(2,1)S(1)}, bf16[1,2,448,256]{3,2,1,0:T(8,128)(2,1)S(1)}, u32[]{:S(2)}, u32[]{:S(2)}) collective-permute-start(bf16[1,2,448,256]{3,2,1,0:T(8,128)(2,1)S(1)} %add_convert_fusion.1), channel_id=1, source_target_pairs={{0,8},{4,12},{8,0},{12,4},{1,9},{5,13},{9,1},{13,5},{2,10},{6,14},... | collective-permute-start | bytes 1376264 | tf_op jit(solution)/shard_map/ppermute | solution.py:300

commit v5 on v4

--- a/solution.py
+++ b/solution.py
@@ -13,29 +13,26 @@
 
 
 def mask_bias(length, *, group, seq, prefix_rows):
-    shape = (group * seq, prefix_rows + seq)
+    shape = (group * seq, seq + prefix_rows)
     key_index = lax.broadcasted_iota(jnp.int32, shape, 1)
     tok_index = lax.broadcasted_iota(jnp.int32, shape, 0) % seq
-    in_prefix = key_index < prefix_rows
-    allowed = (in_prefix & (key_index < length)) | (
-        jnp.logical_not(in_prefix) & (key_index - prefix_rows <= tok_index))
+    in_suffix = key_index < seq
+    allowed = (in_suffix & (key_index <= tok_index)) | (
+        jnp.logical_not(in_suffix) & (key_index - seq < length))
     return jnp.where(allowed, 0.0, -1e30).astype(jnp.float32)
 
 
-def attend_math(q_blk, og_blk, keys_pre, values_pre, keys_own, values_own, length, coef,
-                *, group, seq, prefix_rows, bias=None):
+def attend_math(q_blk, og_blk, keys_pre, values_pre, keys_own, values_own, bias, coef, *, group, seq):
     scale = HD ** (-0.5)
     cot_blk = (coef * og_blk.astype(jnp.float32)).astype(jnp.bfloat16)
     q_rows = jnp.concatenate([q_blk[:, g * HD:(g + 1) * HD] for g in range(group)], 0)
     c_rows = jnp.concatenate([cot_blk[:, g * HD:(g + 1) * HD] for g in range(group)], 0)
-    keys = jnp.concatenate([keys_pre, keys_own], 0)
-    values = jnp.concatenate([values_pre, values_own], 0)
+    keys = jnp.concatenate([keys_own, keys_pre], 0)
+    values = jnp.concatenate([values_own, values_pre], 0)
 
     nt = (((1,), (1,)), ((), ()))
     tn = (((0,), (0,)), ((), ()))
     scores = lax.dot_general(q_rows, keys, nt, preferred_element_type=jnp.float32) * scale
-    if bias is None:
-        bias = mask_bias(length, group=group, seq=seq, prefix_rows=prefix_rows)
     scores = scores + bias
     row_max = jnp.max(scores, -1, keepdims=True)
     raised = jnp.exp(scores - row_max)
@@ -52,20 +49,25 @@
 
 
 def store_grads(grad_q, grad_k, grad_v, member, dq_ref, dkv_ref, dpre_ref, *, group, seq, prefix_rows):
+    active = grad_k.shape[0] - seq
     for g in range(group):
         dq_ref[0, :, g * HD:(g + 1) * HD] = grad_q[g * seq:(g + 1) * seq]
-    dkv_ref[0, 0] = grad_k[prefix_rows:].astype(jnp.bfloat16)
-    dkv_ref[0, 1] = grad_v[prefix_rows:].astype(jnp.bfloat16)
+    dkv_ref[0, 0] = grad_k[:seq].astype(jnp.bfloat16)
+    dkv_ref[0, 1] = grad_v[:seq].astype(jnp.bfloat16)
 
     @pl.when(member == 0)
     def _():
-        dpre_ref[0, 0] = grad_k[:prefix_rows]
-        dpre_ref[0, 1] = grad_v[:prefix_rows]
+        dpre_ref[0, 0, :active] = grad_k[seq:]
+        dpre_ref[0, 1, :active] = grad_v[seq:]
+        if active < prefix_rows:
+            zeros = jnp.zeros((prefix_rows - active, HD), jnp.float32)
+            dpre_ref[0, 0, active:] = zeros
+            dpre_ref[0, 1, active:] = zeros
 
     @pl.when(member != 0)
     def _():
-        dpre_ref[0, 0] += grad_k[:prefix_rows]
-        dpre_ref[0, 1] += grad_v[:prefix_rows]
+        dpre_ref[0, 0, :active] += grad_k[seq:]
+        dpre_ref[0, 1, :active] += grad_v[seq:]
 
 
 def attend_kernel(slots_ref, goal_ref, len_ref, coef_ref,
@@ -75,10 +77,10 @@
     member = pl.program_id(2)
     s = slots_ref[2 * p + member]
     length = len_ref[goal_ref[p]]
-    dims = dict(group=group, seq=seq, prefix_rows=prefix_rows)
+    bias = mask_bias(length, group=group, seq=seq, prefix_rows=prefix_rows)
     grads = attend_math(q_ref[0], og_ref[0], pkv_ref[0, 0], pkv_ref[0, 1], skv_ref[0, 0], skv_ref[0, 1],
-                        length, coef_ref[s], **dims)
-    store_grads(*grads, member, dq_ref, dkv_ref, dpre_ref, **dims)
+                        bias, coef_ref[s], group=group, seq=seq)
+    store_grads(*grads, member, dq_ref, dkv_ref, dpre_ref, group=group, seq=seq, prefix_rows=prefix_rows)
 
 
 def pair_of(goal, goal_ref, pair_count):
@@ -108,9 +110,16 @@
     x = jnp.full((1, 128), -dpo_beta * gap, jnp.float32)
     weight = dpo_beta * (1.0 / (1.0 + jnp.exp(-x)))
     coef = jnp.where(member == 0, -weight, weight)[:, :1]
-    grads = attend_math(q_ref[0], og_ref[0], pkv_ref[0, 0], pkv_ref[0, 1], skv_ref[0, 0], skv_ref[0, 1],
-                        length, coef, bias=bias_ref[...], **dims)
-    store_grads(*grads, member, dq_ref, dkv_ref, dpre_ref, **dims)
+    blocks = (seq + length + 127) // 128
+    for used in range(1, (seq + prefix_rows + 127) // 128 + 1):
+        @pl.when(blocks == used)
+        def _():
+            width = min(used * 128, seq + prefix_rows)
+            active = width - seq
+            grads = attend_math(q_ref[0], og_ref[0], pkv_ref[0, 0, :active], pkv_ref[0, 1, :active],
+                                skv_ref[0, 0], skv_ref[0, 1], bias_ref[:, :width], coef,
+                                group=group, seq=seq)
+            store_grads(*grads, member, dq_ref, dkv_ref, dpre_ref, **dims)
 
 
 def attend_slot(flip, me, goals, slots, lengths, logratio, queries, out_grad, suffix_kv, prefix_one, chain):

time: 54.3 us -> 52.7 us (0.971)
  Pallas kernels: 38.5 us -> 34.5 us
  waiting for transfers between devices: 3.88 us -> 7.56 us
  starting transfers between devices: 5.2 us -> 4.04 us
    pallas_call x4, Pallas kernels: 38.5 us -> 34.5 us  [attend_slot(): pl.pallas_call(kernel, grid_spec=grid_spec, out_shape=out_shape, input_ou...]
    ppermute x1, waiting for transfers between devices: 1.7 us -> 5.38 us  [pipelined(): lax.ppermute(forward, 'dp', across).astype(jnp.float32)]
    ppermute x1, starting transfers between devices: 1.33 us -> 0.33 us  [pipelined(): lax.ppermute(forward, 'dp', across).astype(jnp.float32)]
  transfers between devices with their start and end apart: 6 -> 6, of which waited for: 2 -> 2; matrix products, arithmetic and copies ran while one was open for 3% -> 3% of each run, Pallas kernels for 53% -> 50%
where the time goes in v5:
time: 52.7 us
  Pallas kernels  34.5 us (65%)
  waiting for transfers between devices  7.56 us (14%)
  starting transfers between devices  4.04 us (8%)
  local copies, waits for them, and re-layouts  3.64 us (7%)
  other arithmetic  2.25 us (4%)
  between operations  0.7 us (1%)
    pallas_call x4, Pallas kernels, attend_slot(): pl.pallas_call(kernel, grid_spec=grid_spec, out_shape=out_shape, input_ou...  34.5 us
    ppermute x1, waiting for transfers between devices, pipelined(): lax.ppermute(forward, 'dp', across).astype(jnp.float32)  5.38 us
    unnamed x11, local copies, waits for them, and re-layouts  2.98 us
    ppermute x1, starting transfers between devices, pipelined(): pre_across = lax.ppermute(prefix_kv, 'dp', across)  2.58 us
    ppermute x1, waiting for transfers between devices, pipelined(): forward = (cross + lax.ppermute(relay, 'dp', partner)).astype(jnp.bfloat16)  2.17 us
    convert_element_type x1, other arithmetic, pipelined(): return (chain[0], chain[1], total.astype(jnp.bfloat16))  2.11 us
  transfers between devices with their start and end apart: 6, of which 2 were waited for; matrix products, arithmetic and copies ran while one was open for 3% of the time, Pallas kernels for 50%

profile of v5, /device:TPU:0, one launch (start us, length us, event | category | flops | bytes accessed | tf_op | source)
XLA Modules:
  0.0 52.7 jit_solution(2265306559488693747)
XLA Ops:
  0.6 0.6 %collective-permute-start.1 = (bf16[1,2,448,256]{3,2,1,0:T(8,128)(2,1)}, bf16[1,2,448,256]{3,2,1,0:T(8,128)(2,1)S(1)}, u32[]{:S(2)}, u32[]{:S(2)}) collective-permute-start(bf16[1,2,448,256]{3,2,1,0:T(8,128)(2,1)} %pkv_ref), channel_id=1, source_target_pairs={{0,4},{4,0},{8,12},{12,8},{1,5},{5,1},{9,13},{13,9},{2,6},{6,2},{1... | collective-permute-start | bytes 1376264 | tf_op jit(solution)/shard_map/ppermute | solution.py:291
  1.2 2.6 %collective-permute-start = (bf16[1,2,448,256]{3,2,1,0:T(8,128)(2,1)}, bf16[1,2,448,256]{3,2,1,0:T(8,128)(2,1)S(1)}, u32[]{:S(2)}, u32[]{:S(2)}) collective-permute-start(bf16[1,2,448,256]{3,2,1,0:T(8,128)(2,1)} %pkv_ref), channel_id=1, source_target_pairs={{0,8},{4,12},{8,0},{12,4},{1,9},{5,13},{9,1},{13,5},{2,10},{6,14},... | collective-permute-start | bytes 1376264 | tf_op jit(solution)/shard_map/ppermute | solution.py:290
  3.8 0.8 %copy.18 = s32[4,2]{1,0:T(4,128)S(1)} copy(s32[4,2]{0,1:T(2,128)} %param.13) | data formatting | bytes 64 | tf_op args[5]
  4.5 0.7 %reshape.17.slots_ref = s32[8]{0:T(128)} reshape(s32[4,2]{1,0:T(4,128)S(1)} %copy.18) | data formatting | bytes 64 | tf_op jit(solution)/shard_map/reshape | solution.py:293
  5.2 0.0 collective-permute-done.1.pkv_ref
  5.2 0.0 copy-start.3
  5.2 0.8 %copy-done.3 = bf16[1,2,448,256]{3,2,1,0:T(8,128)(2,1)} copy-done((bf16[1,2,448,256]{3,2,1,0:T(8,128)(2,1)}, bf16[1,2,448,256]{3,2,1,0:T(8,128)(2,1)S(1)}, u32[]{:S(2)}) %copy-start.3) | copy-done | bytes 458776
  6.0 9.8 %shard_map.103 = (bf16[8,64,2048]{2,1,0:T(8,128)(2,1)}, bf16[8,2,64,256]{3,2,1,0:T(8,128)(2,1)}, f32[1,2,448,256]{3,2,1,0:T(8,128)}) custom-call(s32[1]{0:T(128)} %bitcast.me_ref, s32[4]{0:T(128)} %bitcast.2, s32[8]{0:T(128)} %reshape.17.slots_ref, s32[4]{0:T(128)} %len_ref.7, f32[8]{0:T(128)} %lr_ref.7, bf16[8,64,2048]{2,1,0:T(8,128)(2,1)} %q_ref.7, ...), custom_call_target="tpu_custom_call" | custom-call | flops 8800000000 | bytes 5111808 | tf_op jit(solution)/shard_map/pallas_call | solution.py:184
  15.7 0.0 collective-permute-done.pkv_ref
  15.7 0.0 copy-start.2
  15.7 0.1 collective-permute-start.2
  15.8 0.7 %copy-done.2 = bf16[1,2,448,256]{3,2,1,0:T(8,128)(2,1)} copy-done((bf16[1,2,448,256]{3,2,1,0:T(8,128)(2,1)}, bf16[1,2,448,256]{3,2,1,0:T(8,128)(2,1)S(1)}, u32[]{:S(2)}) %copy-start.2) | copy-done | bytes 458776
  16.5 9.8 %shard_map.104 = (bf16[8,64,2048]{2,1,0:T(8,128)(2,1)}, bf16[8,2,64,256]{3,2,1,0:T(8,128)(2,1)}, f32[1,2,448,256]{3,2,1,0:T(8,128)}) custom-call(s32[1]{0:T(128)} %bitcast.me_ref, s32[4]{0:T(128)} %bitcast.3, s32[8]{0:T(128)} %reshape.17.slots_ref, s32[4]{0:T(128)} %len_ref.7, f32[8]{0:T(128)} %lr_ref.7, ...), custom_call_target="tpu_custom_call", output_to_operand_aliasing={{0}: (9, {}), {1}: (10, {})} | custom-call | flops 8800000000 | bytes 5111808 | tf_op jit(solution)/shard_map/pallas_call | solution.py:184
  26.3 0.0 collective-permute-done.2.pkv_ref
  26.3 0.0 copy-start.4
  26.3 0.8 %copy-done.4 = bf16[1,2,448,256]{3,2,1,0:T(8,128)(2,1)} copy-done((bf16[1,2,448,256]{3,2,1,0:T(8,128)(2,1)}, bf16[1,2,448,256]{3,2,1,0:T(8,128)(2,1)S(1)}, u32[]{:S(2)}) %copy-start.4) | copy-done | bytes 458776
  27.1 0.0 copy-start.1
  27.1 0.0 copy-start
  27.1 8.0 %shard_map.105 = (bf16[8,64,2048]{2,1,0:T(8,128)(2,1)}, bf16[8,2,64,256]{3,2,1,0:T(8,128)(2,1)}, f32[1,2,448,256]{3,2,1,0:T(8,128)}) custom-call(s32[1]{0:T(128)} %bitcast.me_ref, s32[4]{0:T(128)} %bitcast.4, s32[8]{0:T(128)} %reshape.17.slots_ref, s32[4]{0:T(128)} %len_ref.7, f32[8]{0:T(128)} %lr_ref.7, ...), custom_call_target="tpu_custom_call", output_to_operand_aliasing={{0}: (9, {}), {1}: (10, {})} | custom-call | flops 8800000000 | bytes 5111808 | tf_op jit(solution)/shard_map/pallas_call | solution.py:184
  35.1 0.0 collective-permute-start.3
  35.1 0.0 copy-done.1
  35.1 0.5 collective-permute-start.4
  35.6 2.2 %collective-permute-done.3 = f32[1,2,448,256]{3,2,1,0:T(8,128)S(1)} collective-permute-done((f32[1,2,448,256]{3,2,1,0:T(8,128)}, f32[1,2,448,256]{3,2,1,0:T(8,128)S(1)}, u32[]{:S(2)}, u32[]{:S(2)}) %collective-permute-start.3) | collective-permute-done | bytes 917536 | tf_op jit(solution)/shard_map/ppermute | solution.py:306
  37.8 0.0 copy-done
  37.8 0.1 add_convert_fusion.1
  37.9 0.3 collective-permute-start.5
  38.3 6.9 %shard_map.106 = (bf16[8,64,2048]{2,1,0:T(8,128)(2,1)}, bf16[8,2,64,256]{3,2,1,0:T(8,128)(2,1)}, f32[1,2,448,256]{3,2,1,0:T(8,128)}) custom-call(s32[1]{0:T(128)} %bitcast.me_ref, s32[4]{0:T(128)} %bitcast.5, s32[8]{0:T(128)} %reshape.17.slots_ref, s32[4]{0:T(128)} %len_ref.7, f32[8]{0:T(128)} %lr_ref.7, ...), custom_call_target="tpu_custom_call", output_to_operand_aliasing={{0}: (9, {}), {1}: (10, {})} | custom-call | flops 8800000000 | bytes 5111808 | tf_op jit(solution)/shard_map/pallas_call | solution.py:184
  45.2 0.0 collective-permute-done.4
  45.2 5.4 %collective-permute-done.5 = bf16[1,2,448,256]{3,2,1,0:T(8,128)(2,1)S(1)} collective-permute-done((bf16[1,2,448,256]{3,2,1,0:T(8,128)(2,1)S(1)}, bf16[1,2,448,256]{3,2,1,0:T(8,128)(2,1)S(1)}, u32[]{:S(2)}, u32[]{:S(2)}) %collective-permute-start.5) | collective-permute-done | bytes 458784 | tf_op jit(solution)/shard_map/ppermute | solution.py:309
  50.6 2.1 %add_convert_fusion = bf16[1,2,448,256]{3,2,1,0:T(8,128)(2,1)} fusion(bf16[1,2,448,256]{3,2,1,0:T(8,128)(2,1)S(1)} %collective-permute-done.5, f32[1,2,448,256]{3,2,1,0:T(8,128)} %get-tuple-element.32, f32[1,2,448,256]{3,2,1,0:T(8,128)S(1)} %collective-permute-done.4), kind=kLoop, calls=%fused_computation | loop fusion | flops 917504 | bytes 2752512 | tf_op jit(solution)/shard_map/convert_element_type | solution.py:310
Async XLA Ops:
  0.6 4.6 %collective-permute-start.1 = (bf16[1,2,448,256]{3,2,1,0:T(8,128)(2,1)}, bf16[1,2,448,256]{3,2,1,0:T(8,128)(2,1)S(1)}, u32[]{:S(2)}, u32[]{:S(2)}) collective-permute-start(bf16[1,2,448,256]{3,2,1,0:T(8,128)(2,1)} %pkv_ref), channel_id=1, source_target_pairs={{0,4},{4,0},{8,12},{12,8},{1,5},{5,1},{9,13},{13,9},{2,6},{6,2},{1... | collective-permute-start | bytes 1376264 | tf_op jit(solution)/shard_map/ppermute | solution.py:291
  1.2 14.5 %collective-permute-start = (bf16[1,2,448,256]{3,2,1,0:T(8,128)(2,1)}, bf16[1,2,448,256]{3,2,1,0:T(8,128)(2,1)S(1)}, u32[]{:S(2)}, u32[]{:S(2)}) collective-permute-start(bf16[1,2,448,256]{3,2,1,0:T(8,128)(2,1)} %pkv_ref), channel_id=1, source_target_pairs={{0,8},{4,12},{8,0},{12,4},{1,9},{5,13},{9,1},{13,5},{2,10},{6,14},... | collective-permute-start | bytes 1376264 | tf_op jit(solution)/shard_map/ppermute | solution.py:290
  5.2 0.8 %copy-start.3 = (bf16[1,2,448,256]{3,2,1,0:T(8,128)(2,1)}, bf16[1,2,448,256]{3,2,1,0:T(8,128)(2,1)S(1)}, u32[]{:S(2)}) copy-start(bf16[1,2,448,256]{3,2,1,0:T(8,128)(2,1)S(1)} %collective-permute-done.1.pkv_ref) | copy-start | bytes 1376260
  15.7 0.8 %copy-start.2 = (bf16[1,2,448,256]{3,2,1,0:T(8,128)(2,1)}, bf16[1,2,448,256]{3,2,1,0:T(8,128)(2,1)S(1)}, u32[]{:S(2)}) copy-start(bf16[1,2,448,256]{3,2,1,0:T(8,128)(2,1)S(1)} %collective-permute-done.pkv_ref) | copy-start | bytes 1376260
  15.7 10.5 %collective-permute-start.2 = (bf16[1,2,448,256]{3,2,1,0:T(8,128)(2,1)S(1)}, bf16[1,2,448,256]{3,2,1,0:T(8,128)(2,1)S(1)}, u32[]{:S(2)}, u32[]{:S(2)}) collective-permute-start(bf16[1,2,448,256]{3,2,1,0:T(8,128)(2,1)S(1)} %collective-permute-done.pkv_ref), channel_id=1, source_target_pairs={{0,4},{4,0},{8,12},{12,8},{1,5},{5,1},{9,13},{13,9},{2,6},{6,2},{1... | collective-permute-start | bytes 1376264 | tf_op jit(solution)/shard_map/ppermute | solution.py:302
  26.3 0.8 %copy-start.4 = (bf16[1,2,448,256]{3,2,1,0:T(8,128)(2,1)}, bf16[1,2,448,256]{3,2,1,0:T(8,128)(2,1)S(1)}, u32[]{:S(2)}) copy-start(bf16[1,2,448,256]{3,2,1,0:T(8,128)(2,1)S(1)} %collective-permute-done.2.pkv_ref) | copy-start | bytes 1376260
  27.1 8.1 %copy-start.1 = (f32[1,2,448,256]{3,2,1,0:T(8,128)S(1)}, f32[1,2,448,256]{3,2,1,0:T(8,128)}, u32[]{:S(2)}) copy-start(f32[1,2,448,256]{3,2,1,0:T(8,128)} %get-tuple-element.33) | copy-start | bytes 2752516
  27.1 10.7 %copy-start = (f32[1,2,448,256]{3,2,1,0:T(8,128)S(1)}, f32[1,2,448,256]{3,2,1,0:T(8,128)}, u32[]{:S(2)}) copy-start(f32[1,2,448,256]{3,2,1,0:T(8,128)} %get-tuple-element.23) | copy-start | bytes 2752516
  35.1 2.7 %collective-permute-start.3 = (f32[1,2,448,256]{3,2,1,0:T(8,128)}, f32[1,2,448,256]{3,2,1,0:T(8,128)S(1)}, u32[]{:S(2)}, u32[]{:S(2)}) collective-permute-start(f32[1,2,448,256]{3,2,1,0:T(8,128)} %get-tuple-element.26), channel_id=1, source_target_pairs={{0,4},{4,0},{8,12},{12,8},{1,5},{5,1},{9,13},{13,9},{2,6},{6,2},{1... | collective-permute-start | bytes 2752520 | tf_op jit(solution)/shard_map/ppermute | solution.py:306
  35.1 10.1 %collective-permute-start.4 = (f32[1,2,448,256]{3,2,1,0:T(8,128)S(1)}, f32[1,2,448,256]{3,2,1,0:T(8,128)S(1)}, u32[]{:S(2)}, u32[]{:S(2)}) collective-permute-start(f32[1,2,448,256]{3,2,1,0:T(8,128)S(1)} %copy-done.1), channel_id=1, source_target_pairs={{0,4},{4,0},{8,12},{12,8},{1,5},{5,1},{9,13},{13,9},{2,6},{6,2},{1... | collective-permute-start | bytes 2752520 | tf_op jit(solution)/shard_map/ppermute | solution.py:303
  37.9 12.6 %collective-permute-start.5 = (bf16[1,2,448,256]{3,2,1,0:T(8,128)(2,1)S(1)}, bf16[1,2,448,256]{3,2,1,0:T(8,128)(2,1)S(1)}, u32[]{:S(2)}, u32[]{:S(2)}) collective-permute-start(bf16[1,2,448,256]{3,2,1,0:T(8,128)(2,1)S(1)} %add_convert_fusion.1), channel_id=1, source_target_pairs={{0,8},{4,12},{8,0},{12,4},{1,9},{5,13},{9,1},{13,5},{2,10},{6,14},... | collective-permute-start | bytes 1376264 | tf_op jit(solution)/shard_map/ppermute | solution.py:309

commit v6 on v5

--- a/solution.py
+++ b/solution.py
@@ -13,9 +13,9 @@
 
 
 def mask_bias(length, *, group, seq, prefix_rows):
-    shape = (group * seq, seq + prefix_rows)
-    key_index = lax.broadcasted_iota(jnp.int32, shape, 1)
-    tok_index = lax.broadcasted_iota(jnp.int32, shape, 0) % seq
+    shape = (seq + prefix_rows, group * seq)
+    key_index = lax.broadcasted_iota(jnp.int32, shape, 0)
+    tok_index = lax.broadcasted_iota(jnp.int32, shape, 1) % seq
     in_suffix = key_index < seq
     allowed = (in_suffix & (key_index <= tok_index)) | (
         jnp.logical_not(in_suffix) & (key_index - seq < length))
@@ -31,20 +31,20 @@
     values = jnp.concatenate([values_own, values_pre], 0)
 
     nt = (((1,), (1,)), ((), ()))
-    tn = (((0,), (0,)), ((), ()))
-    scores = lax.dot_general(q_rows, keys, nt, preferred_element_type=jnp.float32) * scale
-    scores = scores + bias
-    row_max = jnp.max(scores, -1, keepdims=True)
-    raised = jnp.exp(scores - row_max)
-    prob = raised * (1.0 / jnp.sum(raised, -1, keepdims=True))
-    prob_low = prob.astype(jnp.bfloat16)
-    output = jnp.dot(prob_low, values, preferred_element_type=jnp.float32)
-    row_dot = jnp.sum(c_rows.astype(jnp.float32) * output, -1, keepdims=True)
-    grad_prob = lax.dot_general(c_rows, values, nt, preferred_element_type=jnp.float32)
-    grad_score = (prob * (grad_prob - row_dot)).astype(jnp.bfloat16)
-    grad_q = (scale * jnp.dot(grad_score, keys, preferred_element_type=jnp.float32)).astype(jnp.bfloat16)
-    grad_k = scale * lax.dot_general(grad_score, q_rows, tn, preferred_element_type=jnp.float32)
-    grad_v = lax.dot_general(prob_low, c_rows, tn, preferred_element_type=jnp.float32)
+    scores_t = lax.dot_general(keys, q_rows, nt, preferred_element_type=jnp.float32) * scale
+    scores_t = scores_t + bias
+    col_max = jnp.max(scores_t, 0, keepdims=True)
+    raised = jnp.exp(scores_t - col_max)
+    prob_t = raised * (1.0 / jnp.sum(raised, 0, keepdims=True))
+    prob_low_t = prob_t.astype(jnp.bfloat16)
+    output_t = jnp.dot(values.T, prob_low_t, preferred_element_type=jnp.float32)
+    row_dot = jnp.sum(c_rows.T.astype(jnp.float32) * output_t, 0, keepdims=True)
+    grad_prob_t = lax.dot_general(values, c_rows, nt, preferred_element_type=jnp.float32)
+    grad_score_t = (prob_t * (grad_prob_t - row_dot)).astype(jnp.bfloat16)
+    grad_q_t = jnp.dot(keys.T, grad_score_t, preferred_element_type=jnp.float32)
+    grad_q = (scale * grad_q_t.T).astype(jnp.bfloat16)
+    grad_k = scale * jnp.dot(grad_score_t, q_rows, preferred_element_type=jnp.float32)
+    grad_v = jnp.dot(prob_low_t, c_rows, preferred_element_type=jnp.float32)
     return grad_q, grad_k, grad_v
 
 
@@ -117,7 +117,7 @@
             width = min(used * 128, seq + prefix_rows)
             active = width - seq
             grads = attend_math(q_ref[0], og_ref[0], pkv_ref[0, 0, :active], pkv_ref[0, 1, :active],
-                                skv_ref[0, 0], skv_ref[0, 1], bias_ref[:, :width], coef,
+                                skv_ref[0, 0], skv_ref[0, 1], bias_ref[:width], coef,
                                 group=group, seq=seq)
             store_grads(*grads, member, dq_ref, dkv_ref, dpre_ref, **dims)
 
@@ -173,7 +173,7 @@
             pl.BlockSpec((1, 2, seq, HD), skv_map),
             pl.BlockSpec((1, 2, prefix_rows, HD), pkv_map),
         ],
-        scratch_shapes=[pltpu.VMEM((group * seq, prefix_rows + seq), jnp.float32)],
+        scratch_shapes=[pltpu.VMEM((prefix_rows + seq, group * seq), jnp.float32)],
     )
     steps = 2 * kv_local
     cost = pl.CostEstimate(

time: 52.7 us -> 50.2 us (0.953); the launches traced: 52.7 us -> 49.6 us
  Pallas kernels: 34.5 us -> 30.5 us
  starting transfers between devices: 4.04 us -> 5.82 us
  waiting for transfers between devices: 7.56 us -> 6.67 us
    pallas_call x4, Pallas kernels: 34.5 us -> 30.5 us  [attend_slot(): pl.pallas_call(kernel, grid_spec=grid_spec, out_shape=out_shape, input_ou...]
    ppermute x1, starting transfers between devices: 0.33 us -> 2.18 us  [pipelined(): lax.ppermute(forward, 'dp', across).astype(jnp.float32)]
    ppermute x1, waiting for transfers between devices: 5.38 us -> 4.04 us  [pipelined(): lax.ppermute(forward, 'dp', across).astype(jnp.float32)]
  transfers between devices with their start and end apart: 6 -> 6, of which waited for: 2 -> 3; matrix products, arithmetic and copies ran while one was open for 3% -> 3% of each run, Pallas kernels for 50% -> 45%
where the time goes in v6:
time: 50.2 us; the launch traced here: 49.6 us
  Pallas kernels  30.5 us (61%)
  waiting for transfers between devices  6.67 us (13%)
  starting transfers between devices  5.82 us (12%)
  local copies, waits for them, and re-layouts  3.72 us (7%)
  other arithmetic  2.25 us (4%)
  between operations  0.68 us (1%)
    pallas_call x4, Pallas kernels, attend_slot(): pl.pallas_call(kernel, grid_spec=grid_spec, out_shape=out_shape, input_ou...  30.5 us
    ppermute x1, waiting for transfers between devices, pipelined(): lax.ppermute(forward, 'dp', across).astype(jnp.float32)  4.04 us
    unnamed x11, local copies, waits for them, and re-layouts  3.06 us
    ppermute x1, starting transfers between devices, pipelined(): pre_across = lax.ppermute(prefix_kv, 'dp', across)  2.58 us
    ppermute x1, starting transfers between devices, pipelined(): lax.ppermute(forward, 'dp', across).astype(jnp.float32)  2.18 us
    ppermute x1, waiting for transfers between devices, pipelined(): forward = (cross + lax.ppermute(relay, 'dp', partner)).astype(jnp.bfloat16)  2.17 us
    convert_element_type x1, other arithmetic, pipelined(): return (chain[0], chain[1], total.astype(jnp.bfloat16))  2.11 us
  transfers between devices with their start and end apart: 6, of which 3 were waited for; matrix products, arithmetic and copies ran while one was open for 3% of the time, Pallas kernels for 45%

profile of v6, /device:TPU:0, one launch (start us, length us, event | category | flops | bytes accessed | tf_op | source)
XLA Modules:
  0.0 49.6 jit_solution(11835284295324590691)
XLA Ops:
  0.6 0.6 %collective-permute-start.1 = (bf16[1,2,448,256]{3,2,1,0:T(8,128)(2,1)}, bf16[1,2,448,256]{3,2,1,0:T(8,128)(2,1)S(1)}, u32[]{:S(2)}, u32[]{:S(2)}) collective-permute-start(bf16[1,2,448,256]{3,2,1,0:T(8,128)(2,1)} %pkv_ref), channel_id=1, source_target_pairs={{0,4},{4,0},{8,12},{12,8},{1,5},{5,1},{9,13},{13,9},{2,6},{6,2},{1... | collective-permute-start | bytes 1376264 | tf_op jit(solution)/shard_map/ppermute | solution.py:291
  1.2 2.6 %collective-permute-start = (bf16[1,2,448,256]{3,2,1,0:T(8,128)(2,1)}, bf16[1,2,448,256]{3,2,1,0:T(8,128)(2,1)S(1)}, u32[]{:S(2)}, u32[]{:S(2)}) collective-permute-start(bf16[1,2,448,256]{3,2,1,0:T(8,128)(2,1)} %pkv_ref), channel_id=1, source_target_pairs={{0,8},{4,12},{8,0},{12,4},{1,9},{5,13},{9,1},{13,5},{2,10},{6,14},... | collective-permute-start | bytes 1376264 | tf_op jit(solution)/shard_map/ppermute | solution.py:290
  3.8 0.8 %copy.18 = s32[4,2]{1,0:T(4,128)S(1)} copy(s32[4,2]{0,1:T(2,128)} %param.13) | data formatting | bytes 64 | tf_op args[5]
  4.5 0.7 %reshape.17.slots_ref = s32[8]{0:T(128)} reshape(s32[4,2]{1,0:T(4,128)S(1)} %copy.18) | data formatting | bytes 64 | tf_op jit(solution)/shard_map/reshape | solution.py:293
  5.2 0.0 collective-permute-done.1.pkv_ref
  5.2 0.0 copy-start.3
  5.2 0.8 %copy-done.3 = bf16[1,2,448,256]{3,2,1,0:T(8,128)(2,1)} copy-done((bf16[1,2,448,256]{3,2,1,0:T(8,128)(2,1)}, bf16[1,2,448,256]{3,2,1,0:T(8,128)(2,1)S(1)}, u32[]{:S(2)}) %copy-start.3) | copy-done | bytes 458776
  6.0 8.7 %shard_map.103 = (bf16[8,64,2048]{2,1,0:T(8,128)(2,1)}, bf16[8,2,64,256]{3,2,1,0:T(8,128)(2,1)}, f32[1,2,448,256]{3,2,1,0:T(8,128)}) custom-call(s32[1]{0:T(128)} %bitcast.me_ref, s32[4]{0:T(128)} %bitcast.2, s32[8]{0:T(128)} %reshape.17.slots_ref, s32[4]{0:T(128)} %len_ref.7, f32[8]{0:T(128)} %lr_ref.7, bf16[8,64,2048]{2,1,0:T(8,128)(2,1)} %q_ref.7, ...), custom_call_target="tpu_custom_call" | custom-call | flops 8800000000 | bytes 5111808 | tf_op jit(solution)/shard_map/pallas_call | solution.py:184
  14.6 0.5 collective-permute-done.pkv_ref
  15.1 0.0 copy-start.2
  15.1 0.0 collective-permute-start.2
  15.1 0.8 %copy-done.2 = bf16[1,2,448,256]{3,2,1,0:T(8,128)(2,1)} copy-done((bf16[1,2,448,256]{3,2,1,0:T(8,128)(2,1)}, bf16[1,2,448,256]{3,2,1,0:T(8,128)(2,1)S(1)}, u32[]{:S(2)}) %copy-start.2) | copy-done | bytes 458776
  15.9 7.0 %shard_map.104 = (bf16[8,64,2048]{2,1,0:T(8,128)(2,1)}, bf16[8,2,64,256]{3,2,1,0:T(8,128)(2,1)}, f32[1,2,448,256]{3,2,1,0:T(8,128)}) custom-call(s32[1]{0:T(128)} %bitcast.me_ref, s32[4]{0:T(128)} %bitcast.3, s32[8]{0:T(128)} %reshape.17.slots_ref, s32[4]{0:T(128)} %len_ref.7, f32[8]{0:T(128)} %lr_ref.7, ...), custom_call_target="tpu_custom_call", output_to_operand_aliasing={{0}: (9, {}), {1}: (10, {})} | custom-call | flops 8800000000 | bytes 5111808 | tf_op jit(solution)/shard_map/pallas_call | solution.py:184
  22.9 0.0 collective-permute-done.2.pkv_ref
  22.9 0.0 copy-start.4
  22.9 0.8 %copy-done.4 = bf16[1,2,448,256]{3,2,1,0:T(8,128)(2,1)} copy-done((bf16[1,2,448,256]{3,2,1,0:T(8,128)(2,1)}, bf16[1,2,448,256]{3,2,1,0:T(8,128)(2,1)S(1)}, u32[]{:S(2)}) %copy-start.4) | copy-done | bytes 458776
  23.7 0.0 copy-start.1
  23.7 0.0 copy-start
  23.7 8.0 %shard_map.105 = (bf16[8,64,2048]{2,1,0:T(8,128)(2,1)}, bf16[8,2,64,256]{3,2,1,0:T(8,128)(2,1)}, f32[1,2,448,256]{3,2,1,0:T(8,128)}) custom-call(s32[1]{0:T(128)} %bitcast.me_ref, s32[4]{0:T(128)} %bitcast.4, s32[8]{0:T(128)} %reshape.17.slots_ref, s32[4]{0:T(128)} %len_ref.7, f32[8]{0:T(128)} %lr_ref.7, ...), custom_call_target="tpu_custom_call", output_to_operand_aliasing={{0}: (9, {}), {1}: (10, {})} | custom-call | flops 8800000000 | bytes 5111808 | tf_op jit(solution)/shard_map/pallas_call | solution.py:184
  31.7 0.0 collective-permute-start.3
  31.7 0.0 copy-done.1
  31.7 0.5 collective-permute-start.4
  32.2 2.2 %collective-permute-done.3 = f32[1,2,448,256]{3,2,1,0:T(8,128)S(1)} collective-permute-done((f32[1,2,448,256]{3,2,1,0:T(8,128)}, f32[1,2,448,256]{3,2,1,0:T(8,128)S(1)}, u32[]{:S(2)}, u32[]{:S(2)}) %collective-permute-start.3) | collective-permute-done | bytes 917536 | tf_op jit(solution)/shard_map/ppermute | solution.py:306
  34.4 0.0 copy-done
  34.4 0.1 add_convert_fusion.1
  34.5 2.2 %collective-permute-start.5 = (bf16[1,2,448,256]{3,2,1,0:T(8,128)(2,1)S(1)}, bf16[1,2,448,256]{3,2,1,0:T(8,128)(2,1)S(1)}, u32[]{:S(2)}, u32[]{:S(2)}) collective-permute-start(bf16[1,2,448,256]{3,2,1,0:T(8,128)(2,1)S(1)} %add_convert_fusion.1), channel_id=1, source_target_pairs={{0,8},{4,12},{8,0},{12,4},{1,9},{5,13},{9,1},{13,5},{2,10},{6,14},... | collective-permute-start | bytes 1376264 | tf_op jit(solution)/shard_map/ppermute | solution.py:309
  36.7 6.8 %shard_map.106 = (bf16[8,64,2048]{2,1,0:T(8,128)(2,1)}, bf16[8,2,64,256]{3,2,1,0:T(8,128)(2,1)}, f32[1,2,448,256]{3,2,1,0:T(8,128)}) custom-call(s32[1]{0:T(128)} %bitcast.me_ref, s32[4]{0:T(128)} %bitcast.5, s32[8]{0:T(128)} %reshape.17.slots_ref, s32[4]{0:T(128)} %len_ref.7, f32[8]{0:T(128)} %lr_ref.7, ...), custom_call_target="tpu_custom_call", output_to_operand_aliasing={{0}: (9, {}), {1}: (10, {})} | custom-call | flops 8800000000 | bytes 5111808 | tf_op jit(solution)/shard_map/pallas_call | solution.py:184
  43.5 0.0 collective-permute-done.4
  43.5 4.0 %collective-permute-done.5 = bf16[1,2,448,256]{3,2,1,0:T(8,128)(2,1)S(1)} collective-permute-done((bf16[1,2,448,256]{3,2,1,0:T(8,128)(2,1)S(1)}, bf16[1,2,448,256]{3,2,1,0:T(8,128)(2,1)S(1)}, u32[]{:S(2)}, u32[]{:S(2)}) %collective-permute-start.5) | collective-permute-done | bytes 458784 | tf_op jit(solution)/shard_map/ppermute | solution.py:309
  47.5 2.1 %add_convert_fusion = bf16[1,2,448,256]{3,2,1,0:T(8,128)(2,1)} fusion(bf16[1,2,448,256]{3,2,1,0:T(8,128)(2,1)S(1)} %collective-permute-done.5, f32[1,2,448,256]{3,2,1,0:T(8,128)} %get-tuple-element.32, f32[1,2,448,256]{3,2,1,0:T(8,128)S(1)} %collective-permute-done.4), kind=kLoop, calls=%fused_computation | loop fusion | flops 917504 | bytes 2752512 | tf_op jit(solution)/shard_map/convert_element_type | solution.py:310
Async XLA Ops:
  0.6 4.6 %collective-permute-start.1 = (bf16[1,2,448,256]{3,2,1,0:T(8,128)(2,1)}, bf16[1,2,448,256]{3,2,1,0:T(8,128)(2,1)S(1)}, u32[]{:S(2)}, u32[]{:S(2)}) collective-permute-start(bf16[1,2,448,256]{3,2,1,0:T(8,128)(2,1)} %pkv_ref), channel_id=1, source_target_pairs={{0,4},{4,0},{8,12},{12,8},{1,5},{5,1},{9,13},{13,9},{2,6},{6,2},{1... | collective-permute-start | bytes 1376264 | tf_op jit(solution)/shard_map/ppermute | solution.py:291
  1.2 13.9 %collective-permute-start = (bf16[1,2,448,256]{3,2,1,0:T(8,128)(2,1)}, bf16[1,2,448,256]{3,2,1,0:T(8,128)(2,1)S(1)}, u32[]{:S(2)}, u32[]{:S(2)}) collective-permute-start(bf16[1,2,448,256]{3,2,1,0:T(8,128)(2,1)} %pkv_ref), channel_id=1, source_target_pairs={{0,8},{4,12},{8,0},{12,4},{1,9},{5,13},{9,1},{13,5},{2,10},{6,14},... | collective-permute-start | bytes 1376264 | tf_op jit(solution)/shard_map/ppermute | solution.py:290
  5.2 0.8 %copy-start.3 = (bf16[1,2,448,256]{3,2,1,0:T(8,128)(2,1)}, bf16[1,2,448,256]{3,2,1,0:T(8,128)(2,1)S(1)}, u32[]{:S(2)}) copy-start(bf16[1,2,448,256]{3,2,1,0:T(8,128)(2,1)S(1)} %collective-permute-done.1.pkv_ref) | copy-start | bytes 1376260
  15.1 0.8 %copy-start.2 = (bf16[1,2,448,256]{3,2,1,0:T(8,128)(2,1)}, bf16[1,2,448,256]{3,2,1,0:T(8,128)(2,1)S(1)}, u32[]{:S(2)}) copy-start(bf16[1,2,448,256]{3,2,1,0:T(8,128)(2,1)S(1)} %collective-permute-done.pkv_ref) | copy-start | bytes 1376260
  15.1 7.8 %collective-permute-start.2 = (bf16[1,2,448,256]{3,2,1,0:T(8,128)(2,1)S(1)}, bf16[1,2,448,256]{3,2,1,0:T(8,128)(2,1)S(1)}, u32[]{:S(2)}, u32[]{:S(2)}) collective-permute-start(bf16[1,2,448,256]{3,2,1,0:T(8,128)(2,1)S(1)} %collective-permute-done.pkv_ref), channel_id=1, source_target_pairs={{0,4},{4,0},{8,12},{12,8},{1,5},{5,1},{9,13},{13,9},{2,6},{6,2},{1... | collective-permute-start | bytes 1376264 | tf_op jit(solution)/shard_map/ppermute | solution.py:302
  22.9 0.8 %copy-start.4 = (bf16[1,2,448,256]{3,2,1,0:T(8,128)(2,1)}, bf16[1,2,448,256]{3,2,1,0:T(8,128)(2,1)S(1)}, u32[]{:S(2)}) copy-start(bf16[1,2,448,256]{3,2,1,0:T(8,128)(2,1)S(1)} %collective-permute-done.2.pkv_ref) | copy-start | bytes 1376260
  23.7 8.0 %copy-start.1 = (f32[1,2,448,256]{3,2,1,0:T(8,128)S(1)}, f32[1,2,448,256]{3,2,1,0:T(8,128)}, u32[]{:S(2)}) copy-start(f32[1,2,448,256]{3,2,1,0:T(8,128)} %get-tuple-element.33) | copy-start | bytes 2752516
  23.7 10.7 %copy-start = (f32[1,2,448,256]{3,2,1,0:T(8,128)S(1)}, f32[1,2,448,256]{3,2,1,0:T(8,128)}, u32[]{:S(2)}) copy-start(f32[1,2,448,256]{3,2,1,0:T(8,128)} %get-tuple-element.23) | copy-start | bytes 2752516
  31.7 2.7 %collective-permute-start.3 = (f32[1,2,448,256]{3,2,1,0:T(8,128)}, f32[1,2,448,256]{3,2,1,0:T(8,128)S(1)}, u32[]{:S(2)}, u32[]{:S(2)}) collective-permute-start(f32[1,2,448,256]{3,2,1,0:T(8,128)} %get-tuple-element.26), channel_id=1, source_target_pairs={{0,4},{4,0},{8,12},{12,8},{1,5},{5,1},{9,13},{13,9},{2,6},{6,2},{1... | collective-permute-start | bytes 2752520 | tf_op jit(solution)/shard_map/ppermute | solution.py:306
  31.7 11.8 %collective-permute-start.4 = (f32[1,2,448,256]{3,2,1,0:T(8,128)S(1)}, f32[1,2,448,256]{3,2,1,0:T(8,128)S(1)}, u32[]{:S(2)}, u32[]{:S(2)}) collective-permute-start(f32[1,2,448,256]{3,2,1,0:T(8,128)S(1)} %copy-done.1), channel_id=1, source_target_pairs={{0,4},{4,0},{8,12},{12,8},{1,5},{5,1},{9,13},{13,9},{2,6},{6,2},{1... | collective-permute-start | bytes 2752520 | tf_op jit(solution)/shard_map/ppermute | solution.py:303
  34.5 13.0 %collective-permute-start.5 = (bf16[1,2,448,256]{3,2,1,0:T(8,128)(2,1)S(1)}, bf16[1,2,448,256]{3,2,1,0:T(8,128)(2,1)S(1)}, u32[]{:S(2)}, u32[]{:S(2)}) collective-permute-start(bf16[1,2,448,256]{3,2,1,0:T(8,128)(2,1)S(1)} %add_convert_fusion.1), channel_id=1, source_target_pairs={{0,8},{4,12},{8,0},{12,4},{1,9},{5,13},{9,1},{13,5},{2,10},{6,14},... | collective-permute-start | bytes 1376264 | tf_op jit(solution)/shard_map/ppermute | solution.py:309

commit v7 on v6

--- a/solution.py
+++ b/solution.py
@@ -86,15 +86,19 @@
 def pair_of(goal, goal_ref, pair_count):
     pair = 0
     for p in range(pair_count):
-        pair = jnp.where(goal_ref[p] == goal, p, pair)
+        pair = jnp.where(goal_ref[p, 0] == goal, p, pair)
     return pair
 
 
 def slot_kernel(me_ref, goal_ref, slots_ref, len_ref, lr_ref, q_ref, og_ref, skv_ref, pkv_ref, *rest,
-                group, seq, prefix_rows, flip, pair_count, chained):
+                group, seq, prefix_rows, flip, pair_count, chained, seeded, low):
     if chained:
         rest = rest[2:]
-    dq_ref, dkv_ref, dpre_ref, bias_ref = rest
+    seed_ref = None
+    if seeded:
+        seed_ref, rest = rest[0], rest[1:]
+    dq_ref, dkv_ref, dpre_ref, bias_ref = rest[:4]
+    acc_ref = rest[4] if low else dpre_ref
     k = pl.program_id(0)
     member = pl.program_id(1)
     goal = me_ref[0] ^ flip
@@ -106,7 +110,7 @@
     def _():
         bias_ref[...] = mask_bias(length, **dims)
 
-    gap = lr_ref[slots_ref[2 * pair]] - lr_ref[slots_ref[2 * pair + 1]]
+    gap = lr_ref[slots_ref[pair, 0]] - lr_ref[slots_ref[pair, 1]]
     x = jnp.full((1, 128), -dpo_beta * gap, jnp.float32)
     weight = dpo_beta * (1.0 / (1.0 + jnp.exp(-x)))
     coef = jnp.where(member == 0, -weight, weight)[:, :1]
@@ -115,14 +119,23 @@
         @pl.when(blocks == used)
         def _():
             width = min(used * 128, seq + prefix_rows)
-            active = width - seq
-            grads = attend_math(q_ref[0], og_ref[0], pkv_ref[0, 0, :active], pkv_ref[0, 1, :active],
+            grads = attend_math(q_ref[0], og_ref[0], pkv_ref[0, 0, :width - seq], pkv_ref[0, 1, :width - seq],
                                 skv_ref[0, 0], skv_ref[0, 1], bias_ref[:width], coef,
                                 group=group, seq=seq)
-            store_grads(*grads, member, dq_ref, dkv_ref, dpre_ref, **dims)
-
-
-def attend_slot(flip, me, goals, slots, lengths, logratio, queries, out_grad, suffix_kv, prefix_one, chain):
+            store_grads(*grads, member, dq_ref, dkv_ref, acc_ref, **dims)
+
+    if seeded:
+        @pl.when(member == 1)
+        def _():
+            dpre_ref[...] += seed_ref[...]
+    if low:
+        @pl.when(member == 1)
+        def _():
+            dpre_ref[...] = acc_ref[...].astype(dpre_ref.dtype)
+
+
+def attend_slot(flip, me, goals, slots, lengths, logratio, queries, out_grad, suffix_kv, prefix_one, chain,
+                seed=None, low=False):
     suffix_count, seq, qwidth = queries.shape
     kv_width = suffix_kv.shape[-1]
     kv_local = kv_width // HD
@@ -133,7 +146,7 @@
 
     def suffix_of(m, me_ref, goal_ref, slots_ref):
         pair = pair_of(me_ref[0] ^ flip, goal_ref, pair_count)
-        return slots_ref[2 * pair + m]
+        return slots_ref[pair, m]
 
     def q_map(k, m, me_ref, goal_ref, slots_ref, len_ref):
         return (suffix_of(m, me_ref, goal_ref, slots_ref), 0, k)
@@ -147,7 +160,7 @@
     out_shape = (
         jax.ShapeDtypeStruct((suffix_count, seq, qwidth), jnp.bfloat16),
         jax.ShapeDtypeStruct((suffix_count, 2, seq, kv_width), jnp.bfloat16),
-        jax.ShapeDtypeStruct((1, 2, prefix_rows, kv_width), jnp.float32),
+        jax.ShapeDtypeStruct((1, 2, prefix_rows, kv_width), jnp.bfloat16 if low else jnp.float32),
     )
     in_specs = [
         pl.BlockSpec(memory_space=pltpu.SMEM),
@@ -162,8 +175,15 @@
         in_specs += [pl.BlockSpec(memory_space=pl.ANY)] * 2
         operands += list(chain)
         aliases = {9: 0, 10: 1}
+    if seed is not None:
+        in_specs.append(pl.BlockSpec((1, 2, prefix_rows, HD), pkv_map))
+        operands.append(seed)
+    scratch = [pltpu.VMEM((prefix_rows + seq, group * seq), jnp.float32)]
+    if low:
+        scratch.append(pltpu.VMEM((1, 2, prefix_rows, HD), jnp.float32))
     kernel = functools.partial(slot_kernel, group=group, seq=seq, prefix_rows=prefix_rows, flip=flip,
-                               pair_count=pair_count, chained=chain is not None)
+                               pair_count=pair_count, chained=chain is not None, seeded=seed is not None,
+                               low=low)
     grid_spec = pltpu.PrefetchScalarGridSpec(
         num_scalar_prefetch=4,
         grid=(kv_local, 2),
@@ -173,7 +193,7 @@
             pl.BlockSpec((1, 2, seq, HD), skv_map),
             pl.BlockSpec((1, 2, prefix_rows, HD), pkv_map),
         ],
-        scratch_shapes=[pltpu.VMEM((prefix_rows + seq, group * seq), jnp.float32)],
+        scratch_shapes=scratch,
     )
     steps = 2 * kv_local
     cost = pl.CostEstimate(
@@ -290,11 +310,12 @@
     pre_across = lax.ppermute(prefix_kv, "dp", across)
     pre_partner = lax.ppermute(prefix_kv, "dp", partner)
     me = lax.axis_index("dp").astype(jnp.int32).reshape(1)
-    tables = (me, pair_goal.reshape(-1).astype(jnp.int32), pair_slots.reshape(-1).astype(jnp.int32),
+    tables = (me, pair_goal.astype(jnp.int32), pair_slots.astype(jnp.int32),
               prefix_len.astype(jnp.int32), logratio)
 
-    def run(flip, prefix_one, chain):
-        grad_q, grad_kv, partial = attend_slot(flip, *tables, queries, out_grad, suffix_kv, prefix_one, chain)
+    def run(flip, prefix_one, chain, **extra):
+        grad_q, grad_kv, partial = attend_slot(flip, *tables, queries, out_grad, suffix_kv, prefix_one, chain,
+                                               **extra)
         return (grad_q, grad_kv), partial
 
     chain, near = run(1, pre_partner, None)
@@ -302,11 +323,11 @@
     pre_relay = lax.ppermute(pre_across, "dp", partner)
     near_sent = lax.ppermute(near, "dp", partner)
     chain, cross = run(2, pre_across, chain)
-    chain, relay = run(3, pre_relay, chain)
-    forward = (cross + lax.ppermute(relay, "dp", partner)).astype(jnp.bfloat16)
+    chain, relay = run(3, pre_relay, chain, low=True)
+    forward = (cross + lax.ppermute(relay, "dp", partner).astype(jnp.float32)).astype(jnp.bfloat16)
     forward, own_prefix = lax.optimization_barrier((forward, prefix_kv))
-    chain, own = run(0, own_prefix, chain)
-    total = own + near_sent + lax.ppermute(forward, "dp", across).astype(jnp.float32)
+    chain, own = run(0, own_prefix, chain, seed=near_sent)
+    total = own + lax.ppermute(forward, "dp", across).astype(jnp.float32)
     return chain[0], chain[1], total.astype(jnp.bfloat16)
 
 

time: 50.2 us -> 49.8 us (level)
  waiting for transfers between devices: 6.67 us -> 5.06 us
  local copies, waits for them, and re-layouts: 3.72 us -> 5.28 us
  starting transfers between devices: 5.82 us -> 4.7 us
  Pallas kernels: 30.5 us -> 31.5 us
    unnamed x11 -> x12, local copies, waits for them, and re-layouts: 3.06 us -> 5.28 us
    ppermute x2, starting transfers between devices: 2.19 us -> 1 us  [the longest x1 1 us: pipelined(): total = own + lax.ppermute(forward, 'dp', across).astype(jnp.float32)]
    ppermute x2, waiting for transfers between devices: 6.21 us -> 5.03 us  [the longest x1 3.01 us: pipelined(): total = own + lax.ppermute(forward, 'dp', across).astype(jnp.float32)]
    pallas_call x4, Pallas kernels: 30.5 us -> 31.5 us  [attend_slot(): pl.pallas_call(kernel, grid_spec=grid_spec, out_shape=out_shape, input_ou...]
    reshape x1 -> x0, local copies, waits for them, and re-layouts: 0.65 us -> none  [pipelined(): pair_slots.reshape(-1).astype(jnp.int32)]
  transfers between devices with their start and end apart: 6 -> 6, of which waited for: 3 -> 2; matrix products, arithmetic and copies ran while one was open for 3% -> 5% of each run, Pallas kernels for 45% -> 64%
where the time goes in v7:
time: 49.8 us; the launch traced here: 49.4 us
  Pallas kernels  31.5 us (63%)
  local copies, waits for them, and re-layouts  5.28 us (11%)
  waiting for transfers between devices  5.06 us (10%)
  starting transfers between devices  4.7 us (9%)
  other arithmetic  2.14 us (4%)
  between operations  0.67 us (1%)
    pallas_call x4, Pallas kernels, attend_slot(): pl.pallas_call(kernel, grid_spec=grid_spec, out_shape=out_shape, input_ou...  31.5 us
    unnamed x12, local copies, waits for them, and re-layouts  5.28 us
    ppermute x1, waiting for transfers between devices, pipelined(): total = own + lax.ppermute(forward, 'dp', across).astype(jnp.float32)  3.01 us
    ppermute x1, starting transfers between devices, pipelined(): pre_across = lax.ppermute(prefix_kv, 'dp', across)  2.58 us
    convert_element_type x1, other arithmetic, pipelined(): return (chain[0], chain[1], total.astype(jnp.bfloat16))  2.04 us
    ppermute x1, waiting for transfers between devices, pipelined(): lax.ppermute(relay, 'dp', partner).astype(jnp.float32)  2.02 us
    ppermute x1, starting transfers between devices, pipelined(): total = own + lax.ppermute(forward, 'dp', across).astype(jnp.float32)  1 us
  transfers between devices with their start and end apart: 6, of which 2 were waited for; matrix products, arithmetic and copies ran while one was open for 5% of the time, Pallas kernels for 64%

profile of v7, /device:TPU:0, one launch (start us, length us, event | category | flops | bytes accessed | tf_op | source)
XLA Modules:
  0.0 49.4 jit_solution(1622510348017450941)
XLA Ops:
  0.6 0.6 %collective-permute-start.1 = (bf16[1,2,448,256]{3,2,1,0:T(8,128)(2,1)}, bf16[1,2,448,256]{3,2,1,0:T(8,128)(2,1)S(1)}, u32[]{:S(2)}, u32[]{:S(2)}) collective-permute-start(bf16[1,2,448,256]{3,2,1,0:T(8,128)(2,1)} %pkv_ref), channel_id=1, source_target_pairs={{0,4},{4,0},{8,12},{12,8},{1,5},{5,1},{9,13},{13,9},{2,6},{6,2},{1... | collective-permute-start | bytes 1376264 | tf_op jit(solution)/shard_map/ppermute | solution.py:311
  1.2 2.6 %collective-permute-start = (bf16[1,2,448,256]{3,2,1,0:T(8,128)(2,1)}, bf16[1,2,448,256]{3,2,1,0:T(8,128)(2,1)S(1)}, u32[]{:S(2)}, u32[]{:S(2)}) collective-permute-start(bf16[1,2,448,256]{3,2,1,0:T(8,128)(2,1)} %pkv_ref), channel_id=1, source_target_pairs={{0,8},{4,12},{8,0},{12,4},{1,9},{5,13},{9,1},{13,5},{2,10},{6,14},... | collective-permute-start | bytes 1376264 | tf_op jit(solution)/shard_map/ppermute | solution.py:310
  3.8 1.3 %copy.24.slots_ref = s32[4,2]{1,0:T(4,128)} copy(s32[4,2]{0,1:T(2,128)} %param.13) | data formatting | bytes 64 | tf_op args[5]
  5.1 1.3 %copy.23.goal_ref = s32[4,1]{1,0:T(4,128)} copy(s32[4,1]{0,1:T(1,128)} %param.14) | data formatting | bytes 32 | tf_op args[6]
  6.4 0.0 collective-permute-done.1.pkv_ref
  6.4 0.0 copy-start.3
  6.4 0.8 %copy-done.3 = bf16[1,2,448,256]{3,2,1,0:T(8,128)(2,1)} copy-done((bf16[1,2,448,256]{3,2,1,0:T(8,128)(2,1)}, bf16[1,2,448,256]{3,2,1,0:T(8,128)(2,1)S(1)}, u32[]{:S(2)}) %copy-start.3) | copy-done | bytes 458776
  7.2 7.9 %shard_map.103 = (bf16[8,64,2048]{2,1,0:T(8,128)(2,1)}, bf16[8,2,64,256]{3,2,1,0:T(8,128)(2,1)}, f32[1,2,448,256]{3,2,1,0:T(8,128)}) custom-call(s32[1]{0:T(128)} %bitcast.me_ref, s32[4,1]{1,0:T(4,128)} %copy.23.goal_ref, s32[4,2]{1,0:T(4,128)} %copy.24.slots_ref, s32[4]{0:T(128)} %len_ref.7, f32[8]{0:T(128)} %lr_ref.7, bf16[8,64,2048]{2,1,0:T(8,128)(2,1)} %q_ref.7, ...), custom_call_target="tpu_custom_call" | custom-call | flops 8800000000 | bytes 5111808 | tf_op jit(solution)/shard_map/pallas_call | solution.py:204
  15.1 0.0 collective-permute-done.pkv_ref
  15.1 0.0 copy-start.2
  15.1 0.1 collective-permute-start.2
  15.2 0.5 %collective-permute-start.4 = (f32[1,2,448,256]{3,2,1,0:T(8,128)}, f32[1,2,448,256]{3,2,1,0:T(8,128)S(1)}, u32[]{:S(2)}, u32[]{:S(2)}) collective-permute-start(f32[1,2,448,256]{3,2,1,0:T(8,128)} %get-tuple-element.30), channel_id=1, source_target_pairs={{0,4},{4,0},{8,12},{12,8},{1,5},{5,1},{9,13},{13,9},{2,6},{6,2},{1... | collective-permute-start | bytes 2752520 | tf_op jit(solution)/shard_map/ppermute | solution.py:324
  15.7 0.2 copy-done.2
  15.9 8.7 %shard_map.104 = (bf16[8,64,2048]{2,1,0:T(8,128)(2,1)}, bf16[8,2,64,256]{3,2,1,0:T(8,128)(2,1)}, f32[1,2,448,256]{3,2,1,0:T(8,128)}) custom-call(s32[1]{0:T(128)} %bitcast.me_ref, s32[4,1]{1,0:T(4,128)} %copy.23.goal_ref, s32[4,2]{1,0:T(4,128)} %copy.24.slots_ref, s32[4]{0:T(128)} %len_ref.7, ...), custom_call_target="tpu_custom_call", output_to_operand_aliasing={{0}: (9, {}), {1}: (10, {})} | custom-call | flops 8800000000 | bytes 5111808 | tf_op jit(solution)/shard_map/pallas_call | solution.py:204
  24.6 0.0 collective-permute-done.2.pkv_ref
  24.6 0.0 copy-start.4
  24.6 0.8 %copy-done.4 = bf16[1,2,448,256]{3,2,1,0:T(8,128)(2,1)} copy-done((bf16[1,2,448,256]{3,2,1,0:T(8,128)(2,1)}, bf16[1,2,448,256]{3,2,1,0:T(8,128)(2,1)S(1)}, u32[]{:S(2)}) %copy-start.4) | copy-done | bytes 458776
  25.4 0.0 copy-start
  25.4 7.2 %shard_map.105 = (bf16[8,64,2048]{2,1,0:T(8,128)(2,1)}, bf16[8,2,64,256]{3,2,1,0:T(8,128)(2,1)}, bf16[1,2,448,256]{3,2,1,0:T(8,128)(2,1)}) custom-call(s32[1]{0:T(128)} %bitcast.me_ref, s32[4,1]{1,0:T(4,128)} %copy.23.goal_ref, s32[4,2]{1,0:T(4,128)} %copy.24.slots_ref, s32[4]{0:T(128)} %len_ref.7, ...), custom_call_target="tpu_custom_call", output_to_operand_aliasing={{0}: (9, {}), {1}: (10, {})} | custom-call | flops 8800000000 | bytes 5111808 | tf_op jit(solution)/shard_map/pallas_call | solution.py:204
  32.6 0.0 collective-permute-start.3
  32.6 2.0 %collective-permute-done.3 = bf16[1,2,448,256]{3,2,1,0:T(8,128)(2,1)S(1)} collective-permute-done((bf16[1,2,448,256]{3,2,1,0:T(8,128)(2,1)}, bf16[1,2,448,256]{3,2,1,0:T(8,128)(2,1)S(1)}, u32[]{:S(2)}, u32[]{:S(2)}) %collective-permute-start.3) | collective-permute-done | bytes 458784 | tf_op jit(solution)/shard_map/ppermute | solution.py:327
  34.6 0.0 copy-done
  34.6 0.1 add_convert_fusion.1
  34.7 1.0 %collective-permute-start.5 = (bf16[1,2,448,256]{3,2,1,0:T(8,128)(2,1)S(1)}, bf16[1,2,448,256]{3,2,1,0:T(8,128)(2,1)S(1)}, u32[]{:S(2)}, u32[]{:S(2)}) collective-permute-start(bf16[1,2,448,256]{3,2,1,0:T(8,128)(2,1)S(1)} %add_convert_fusion.1), channel_id=1, source_target_pairs={{0,8},{4,12},{8,0},{12,4},{1,9},{5,13},{9,1},{13,5},{2,10},{6,14},... | collective-permute-start | bytes 1376264 | tf_op jit(solution)/shard_map/ppermute | solution.py:330
  35.7 0.0 collective-permute-done.4.rest_2_
  35.7 0.0 copy-start.1
  35.7 0.9 %copy-done.1 = f32[1,2,448,256]{3,2,1,0:T(8,128)} copy-done((f32[1,2,448,256]{3,2,1,0:T(8,128)}, f32[1,2,448,256]{3,2,1,0:T(8,128)S(1)}, u32[]{:S(2)}) %copy-start.1) | copy-done | bytes 917528
  36.7 7.7 %shard_map.106 = (bf16[8,64,2048]{2,1,0:T(8,128)(2,1)}, bf16[8,2,64,256]{3,2,1,0:T(8,128)(2,1)}, f32[1,2,448,256]{3,2,1,0:T(8,128)}) custom-call(s32[1]{0:T(128)} %bitcast.me_ref, s32[4,1]{1,0:T(4,128)} %copy.23.goal_ref, s32[4,2]{1,0:T(4,128)} %copy.24.slots_ref, s32[4]{0:T(128)} %len_ref.7, ...), custom_call_target="tpu_custom_call", output_to_operand_aliasing={{0}: (9, {}), {1}: (10, {})} | custom-call | flops 8800000000 | bytes 5111808 | tf_op jit(solution)/shard_map/pallas_call | solution.py:204
  44.4 3.0 %collective-permute-done.5 = bf16[1,2,448,256]{3,2,1,0:T(8,128)(2,1)S(1)} collective-permute-done((bf16[1,2,448,256]{3,2,1,0:T(8,128)(2,1)S(1)}, bf16[1,2,448,256]{3,2,1,0:T(8,128)(2,1)S(1)}, u32[]{:S(2)}, u32[]{:S(2)}) %collective-permute-start.5) | collective-permute-done | bytes 458784 | tf_op jit(solution)/shard_map/ppermute | solution.py:330
  47.4 2.0 %add_convert_fusion = bf16[1,2,448,256]{3,2,1,0:T(8,128)(2,1)} fusion(f32[1,2,448,256]{3,2,1,0:T(8,128)} %get-tuple-element.33, bf16[1,2,448,256]{3,2,1,0:T(8,128)(2,1)S(1)} %collective-permute-done.5), kind=kLoop, calls=%fused_computation | loop fusion | flops 688128 | bytes 1835008 | tf_op jit(solution)/shard_map/convert_element_type | solution.py:331
Async XLA Ops:
  0.6 5.8 %collective-permute-start.1 = (bf16[1,2,448,256]{3,2,1,0:T(8,128)(2,1)}, bf16[1,2,448,256]{3,2,1,0:T(8,128)(2,1)S(1)}, u32[]{:S(2)}, u32[]{:S(2)}) collective-permute-start(bf16[1,2,448,256]{3,2,1,0:T(8,128)(2,1)} %pkv_ref), channel_id=1, source_target_pairs={{0,4},{4,0},{8,12},{12,8},{1,5},{5,1},{9,13},{13,9},{2,6},{6,2},{1... | collective-permute-start | bytes 1376264 | tf_op jit(solution)/shard_map/ppermute | solution.py:311
  1.2 13.9 %collective-permute-start = (bf16[1,2,448,256]{3,2,1,0:T(8,128)(2,1)}, bf16[1,2,448,256]{3,2,1,0:T(8,128)(2,1)S(1)}, u32[]{:S(2)}, u32[]{:S(2)}) collective-permute-start(bf16[1,2,448,256]{3,2,1,0:T(8,128)(2,1)} %pkv_ref), channel_id=1, source_target_pairs={{0,8},{4,12},{8,0},{12,4},{1,9},{5,13},{9,1},{13,5},{2,10},{6,14},... | collective-permute-start | bytes 1376264 | tf_op jit(solution)/shard_map/ppermute | solution.py:310
  6.4 0.8 %copy-start.3 = (bf16[1,2,448,256]{3,2,1,0:T(8,128)(2,1)}, bf16[1,2,448,256]{3,2,1,0:T(8,128)(2,1)S(1)}, u32[]{:S(2)}) copy-start(bf16[1,2,448,256]{3,2,1,0:T(8,128)(2,1)S(1)} %collective-permute-done.1.pkv_ref) | copy-start | bytes 1376260
  15.1 0.8 %copy-start.2 = (bf16[1,2,448,256]{3,2,1,0:T(8,128)(2,1)}, bf16[1,2,448,256]{3,2,1,0:T(8,128)(2,1)S(1)}, u32[]{:S(2)}) copy-start(bf16[1,2,448,256]{3,2,1,0:T(8,128)(2,1)S(1)} %collective-permute-done.pkv_ref) | copy-start | bytes 1376260
  15.1 9.5 %collective-permute-start.2 = (bf16[1,2,448,256]{3,2,1,0:T(8,128)(2,1)S(1)}, bf16[1,2,448,256]{3,2,1,0:T(8,128)(2,1)S(1)}, u32[]{:S(2)}, u32[]{:S(2)}) collective-permute-start(bf16[1,2,448,256]{3,2,1,0:T(8,128)(2,1)S(1)} %collective-permute-done.pkv_ref), channel_id=1, source_target_pairs={{0,4},{4,0},{8,12},{12,8},{1,5},{5,1},{9,13},{13,9},{2,6},{6,2},{1... | collective-permute-start | bytes 1376264 | tf_op jit(solution)/shard_map/ppermute | solution.py:323
  15.2 20.6 %collective-permute-start.4 = (f32[1,2,448,256]{3,2,1,0:T(8,128)}, f32[1,2,448,256]{3,2,1,0:T(8,128)S(1)}, u32[]{:S(2)}, u32[]{:S(2)}) collective-permute-start(f32[1,2,448,256]{3,2,1,0:T(8,128)} %get-tuple-element.30), channel_id=1, source_target_pairs={{0,4},{4,0},{8,12},{12,8},{1,5},{5,1},{9,13},{13,9},{2,6},{6,2},{1... | collective-permute-start | bytes 2752520 | tf_op jit(solution)/shard_map/ppermute | solution.py:324
  24.6 0.8 %copy-start.4 = (bf16[1,2,448,256]{3,2,1,0:T(8,128)(2,1)}, bf16[1,2,448,256]{3,2,1,0:T(8,128)(2,1)S(1)}, u32[]{:S(2)}) copy-start(bf16[1,2,448,256]{3,2,1,0:T(8,128)(2,1)S(1)} %collective-permute-done.2.pkv_ref) | copy-start | bytes 1376260
  25.4 9.3 %copy-start = (f32[1,2,448,256]{3,2,1,0:T(8,128)S(1)}, f32[1,2,448,256]{3,2,1,0:T(8,128)}, u32[]{:S(2)}) copy-start(f32[1,2,448,256]{3,2,1,0:T(8,128)} %get-tuple-element.23) | copy-start | bytes 2752516
  32.6 2.0 %collective-permute-start.3 = (bf16[1,2,448,256]{3,2,1,0:T(8,128)(2,1)}, bf16[1,2,448,256]{3,2,1,0:T(8,128)(2,1)S(1)}, u32[]{:S(2)}, u32[]{:S(2)}) collective-permute-start(bf16[1,2,448,256]{3,2,1,0:T(8,128)(2,1)} %get-tuple-element.26), channel_id=1, source_target_pairs={{0,4},{4,0},{8,12},{12,8},{1,5},{5,1},{9,13},{13,9},{2,6},{6,2},{1... | collective-permute-start | bytes 1376264 | tf_op jit(solution)/shard_map/ppermute | solution.py:327
  34.7 12.6 %collective-permute-start.5 = (bf16[1,2,448,256]{3,2,1,0:T(8,128)(2,1)S(1)}, bf16[1,2,448,256]{3,2,1,0:T(8,128)(2,1)S(1)}, u32[]{:S(2)}, u32[]{:S(2)}) collective-permute-start(bf16[1,2,448,256]{3,2,1,0:T(8,128)(2,1)S(1)} %add_convert_fusion.1), channel_id=1, source_target_pairs={{0,8},{4,12},{8,0},{12,4},{1,9},{5,13},{9,1},{13,5},{2,10},{6,14},... | collective-permute-start | bytes 1376264 | tf_op jit(solution)/shard_map/ppermute | solution.py:330
  35.7 0.9 %copy-start.1 = (f32[1,2,448,256]{3,2,1,0:T(8,128)}, f32[1,2,448,256]{3,2,1,0:T(8,128)S(1)}, u32[]{:S(2)}) copy-start(f32[1,2,448,256]{3,2,1,0:T(8,128)S(1)} %collective-permute-done.4.rest_2_) | copy-start | bytes 2752516

commit v8 on v7

--- a/solution.py
+++ b/solution.py
@@ -86,7 +86,7 @@
 def pair_of(goal, goal_ref, pair_count):
     pair = 0
     for p in range(pair_count):
-        pair = jnp.where(goal_ref[p, 0] == goal, p, pair)
+        pair = jnp.where(goal_ref[p] == goal, p, pair)
     return pair
 
 
@@ -304,13 +304,26 @@
     return grad_q, grad_kv, prefix_grad.astype(jnp.bfloat16)
 
 
+def add_round_kernel(a_ref, b_ref, o_ref):
+    o_ref[...] = (a_ref[...] + b_ref[...].astype(jnp.float32)).astype(o_ref.dtype)
+
+
+def add_round(a, b):
+    return pl.pallas_call(
+        add_round_kernel,
+        out_shape=jax.ShapeDtypeStruct(a.shape, jnp.bfloat16),
+        in_specs=[pl.BlockSpec(memory_space=pltpu.VMEM)] * 2,
+        out_specs=pl.BlockSpec(memory_space=pltpu.VMEM),
+    )(a, b)
+
+
 def pipelined(queries, suffix_kv, out_grad, prefix_kv, logratio, pair_slots, pair_goal, prefix_len):
     partner = [(i, i ^ 1) for i in range(4)]
     across = [(i, i ^ 2) for i in range(4)]
     pre_across = lax.ppermute(prefix_kv, "dp", across)
     pre_partner = lax.ppermute(prefix_kv, "dp", partner)
     me = lax.axis_index("dp").astype(jnp.int32).reshape(1)
-    tables = (me, pair_goal.astype(jnp.int32), pair_slots.astype(jnp.int32),
+    tables = (me, pair_goal.reshape(-1).astype(jnp.int32), pair_slots.astype(jnp.int32),
               prefix_len.astype(jnp.int32), logratio)
 
     def run(flip, prefix_one, chain, **extra):
@@ -327,8 +340,7 @@
     forward = (cross + lax.ppermute(relay, "dp", partner).astype(jnp.float32)).astype(jnp.bfloat16)
     forward, own_prefix = lax.optimization_barrier((forward, prefix_kv))
     chain, own = run(0, own_prefix, chain, seed=near_sent)
-    total = own + lax.ppermute(forward, "dp", across).astype(jnp.float32)
-    return chain[0], chain[1], total.astype(jnp.bfloat16)
+    return chain[0], chain[1], add_round(own, lax.ppermute(forward, "dp", across))
 
 
 def solution(mesh):

time: 49.8 us -> 51 us (1.024)
  waiting for transfers between devices: 5.06 us -> 7.33 us
  other arithmetic: 2.14 us -> 0.1 us
  Pallas kernels: 31.5 us -> 33.1 us
  starting transfers between devices: 4.7 us -> 4.09 us
    ppermute x1, waiting for transfers between devices: 0.02 us -> 2.57 us  [pipelined(): pre_across = lax.ppermute(prefix_kv, 'dp', across)]
    pallas_call x0 -> x1, Pallas kernels: none -> 2.14 us  [add_round(): pl.pallas_call(add_round_kernel, out_shape=jax.ShapeDtypeStruct(a.shape,...]
    convert_element_type x1 -> x0, other arithmetic: 2.04 us -> none  [pipelined(): return (chain[0], chain[1], total.astype(jnp.bfloat16))]
    ppermute x1, starting transfers between devices: 1 us -> 0.44 us  [pipelined(): lax.ppermute(forward, 'dp', across)]
    pallas_call x4, Pallas kernels: 31.5 us -> 31 us  [attend_slot(): pl.pallas_call(kernel, grid_spec=grid_spec, out_shape=out_shape, input_ou...]
    unnamed x12 -> x13, local copies, waits for them, and re-layouts: 5.28 us -> 4.91 us
  transfers between devices with their start and end apart: 6 -> 6, of which waited for: 2 -> 3; matrix products, arithmetic and copies ran while one was open for 5% -> 3% of each run, Pallas kernels for 64% -> 62%
where the time goes in v8:
time: 51 us; the launch traced here: 50.2 us
  Pallas kernels  33.1 us (65%)
  waiting for transfers between devices  7.33 us (14%)
  local copies, waits for them, and re-layouts  4.91 us (10%)
  starting transfers between devices  4.09 us (8%)
  between operations  0.67 us (1%)
    pallas_call x4, Pallas kernels, attend_slot(): pl.pallas_call(kernel, grid_spec=grid_spec, out_shape=out_shape, input_ou...  31 us
    unnamed x13, local copies, waits for them, and re-layouts  4.91 us
    ppermute x1, waiting for transfers between devices, pipelined(): lax.ppermute(forward, 'dp', across)  2.74 us
    ppermute x1, starting transfers between devices, pipelined(): pre_across = lax.ppermute(prefix_kv, 'dp', across)  2.58 us
    ppermute x1, waiting for transfers between devices, pipelined(): pre_across = lax.ppermute(prefix_kv, 'dp', across)  2.57 us
    pallas_call x1, Pallas kernels, add_round(): pl.pallas_call(add_round_kernel, out_shape=jax.ShapeDtypeStruct(a.shape,...  2.14 us
    ppermute x1, waiting for transfers between devices, pipelined(): lax.ppermute(relay, 'dp', partner).astype(jnp.float32)  2.02 us
  transfers between devices with their start and end apart: 6, of which 3 were waited for; matrix products, arithmetic and copies ran while one was open for 3% of the time, Pallas kernels for 62%

profile of v8, /device:TPU:0, one launch (start us, length us, event | category | flops | bytes accessed | tf_op | source)
XLA Modules:
  0.0 50.2 jit_solution(1931098695500553684)
XLA Ops:
  0.6 0.6 %collective-permute-start.1 = (bf16[1,2,448,256]{3,2,1,0:T(8,128)(2,1)}, bf16[1,2,448,256]{3,2,1,0:T(8,128)(2,1)S(1)}, u32[]{:S(2)}, u32[]{:S(2)}) collective-permute-start(bf16[1,2,448,256]{3,2,1,0:T(8,128)(2,1)} %pkv_ref), channel_id=1, source_target_pairs={{0,4},{4,0},{8,12},{12,8},{1,5},{5,1},{9,13},{13,9},{2,6},{6,2},{1... | collective-permute-start | bytes 1376264 | tf_op jit(solution)/shard_map/ppermute | solution.py:324
  1.2 2.6 %collective-permute-start = (bf16[1,2,448,256]{3,2,1,0:T(8,128)(2,1)}, bf16[1,2,448,256]{3,2,1,0:T(8,128)(2,1)S(1)}, u32[]{:S(2)}, u32[]{:S(2)}) collective-permute-start(bf16[1,2,448,256]{3,2,1,0:T(8,128)(2,1)} %pkv_ref), channel_id=1, source_target_pairs={{0,8},{4,12},{8,0},{12,4},{1,9},{5,13},{9,1},{13,5},{2,10},{6,14},... | collective-permute-start | bytes 1376264 | tf_op jit(solution)/shard_map/ppermute | solution.py:323
  3.8 1.3 %copy.20.slots_ref = s32[4,2]{1,0:T(4,128)} copy(s32[4,2]{0,1:T(2,128)} %param.13) | data formatting | bytes 64 | tf_op args[5]
  5.1 0.0 collective-permute-done.1.pkv_ref
  5.1 0.0 copy-start.4
  5.1 0.8 %copy-done.4 = bf16[1,2,448,256]{3,2,1,0:T(8,128)(2,1)} copy-done((bf16[1,2,448,256]{3,2,1,0:T(8,128)(2,1)}, bf16[1,2,448,256]{3,2,1,0:T(8,128)(2,1)S(1)}, u32[]{:S(2)}) %copy-start.4) | copy-done | bytes 458776
  5.9 6.6 %shard_map.103 = (bf16[8,64,2048]{2,1,0:T(8,128)(2,1)}, bf16[8,2,64,256]{3,2,1,0:T(8,128)(2,1)}, f32[1,2,448,256]{3,2,1,0:T(8,128)}) custom-call(s32[1]{0:T(128)} %bitcast.me_ref, s32[4]{0:T(128)} %bitcast.2, s32[4,2]{1,0:T(4,128)} %copy.20.slots_ref, s32[4]{0:T(128)} %len_ref.7, f32[8]{0:T(128)} %lr_ref.7, bf16[8,64,2048]{2,1,0:T(8,128)(2,1)} %q_ref.7, ...), custom_call_target="tpu_custom_call" | custom-call | flops 8800000000 | bytes 5111808 | tf_op jit(solution)/shard_map/pallas_call | solution.py:204
  12.5 2.6 %collective-permute-done.pkv_ref = bf16[1,2,448,256]{3,2,1,0:T(8,128)(2,1)S(1)} collective-permute-done((bf16[1,2,448,256]{3,2,1,0:T(8,128)(2,1)}, bf16[1,2,448,256]{3,2,1,0:T(8,128)(2,1)S(1)}, u32[]{:S(2)}, u32[]{:S(2)}) %collective-permute-start) | collective-permute-done | bytes 458784 | tf_op jit(solution)/shard_map/ppermute | solution.py:323
  15.1 0.0 copy-start.3
  15.1 0.0 collective-permute-start.2
  15.1 0.5 %collective-permute-start.4 = (f32[1,2,448,256]{3,2,1,0:T(8,128)}, f32[1,2,448,256]{3,2,1,0:T(8,128)S(1)}, u32[]{:S(2)}, u32[]{:S(2)}) collective-permute-start(f32[1,2,448,256]{3,2,1,0:T(8,128)} %get-tuple-element.30), channel_id=1, source_target_pairs={{0,4},{4,0},{8,12},{12,8},{1,5},{5,1},{9,13},{13,9},{2,6},{6,2},{1... | collective-permute-start | bytes 2752520 | tf_op jit(solution)/shard_map/ppermute | solution.py:337
  15.6 0.3 copy-done.3
  15.9 8.7 %shard_map.104 = (bf16[8,64,2048]{2,1,0:T(8,128)(2,1)}, bf16[8,2,64,256]{3,2,1,0:T(8,128)(2,1)}, f32[1,2,448,256]{3,2,1,0:T(8,128)}) custom-call(s32[1]{0:T(128)} %bitcast.me_ref, s32[4]{0:T(128)} %bitcast.3, s32[4,2]{1,0:T(4,128)} %copy.20.slots_ref, s32[4]{0:T(128)} %len_ref.7, f32[8]{0:T(128)} %lr_ref.7, ...), custom_call_target="tpu_custom_call", output_to_operand_aliasing={{0}: (9, {}), {1}: (10, {})} | custom-call | flops 8800000000 | bytes 5111808 | tf_op jit(solution)/shard_map/pallas_call | solution.py:204
  24.6 0.0 collective-permute-done.2.pkv_ref
  24.6 0.0 copy-start.5
  24.6 0.8 %copy-done.5 = bf16[1,2,448,256]{3,2,1,0:T(8,128)(2,1)} copy-done((bf16[1,2,448,256]{3,2,1,0:T(8,128)(2,1)}, bf16[1,2,448,256]{3,2,1,0:T(8,128)(2,1)S(1)}, u32[]{:S(2)}) %copy-start.5) | copy-done | bytes 458776
  25.4 0.0 copy-start
  25.4 7.2 %shard_map.105 = (bf16[8,64,2048]{2,1,0:T(8,128)(2,1)}, bf16[8,2,64,256]{3,2,1,0:T(8,128)(2,1)}, bf16[1,2,448,256]{3,2,1,0:T(8,128)(2,1)}) custom-call(s32[1]{0:T(128)} %bitcast.me_ref, s32[4]{0:T(128)} %bitcast.4, s32[4,2]{1,0:T(4,128)} %copy.20.slots_ref, s32[4]{0:T(128)} %len_ref.7, f32[8]{0:T(128)} %lr_ref.7, ...), custom_call_target="tpu_custom_call", output_to_operand_aliasing={{0}: (9, {}), {1}: (10, {})} | custom-call | flops 8800000000 | bytes 5111808 | tf_op jit(solution)/shard_map/pallas_call | solution.py:204
  32.6 0.0 collective-permute-start.3
  32.6 2.0 %collective-permute-done.3 = bf16[1,2,448,256]{3,2,1,0:T(8,128)(2,1)S(1)} collective-permute-done((bf16[1,2,448,256]{3,2,1,0:T(8,128)(2,1)}, bf16[1,2,448,256]{3,2,1,0:T(8,128)(2,1)S(1)}, u32[]{:S(2)}, u32[]{:S(2)}) %collective-permute-start.3) | collective-permute-done | bytes 458784 | tf_op jit(solution)/shard_map/ppermute | solution.py:340
  34.6 0.0 copy-done
  34.6 0.1 add_convert_fusion
  34.7 0.4 collective-permute-start.5
  35.1 0.0 collective-permute-done.4.rest_2_
  35.1 0.0 copy-start.2
  35.1 1.0 %copy-done.2 = f32[1,2,448,256]{3,2,1,0:T(8,128)} copy-done((f32[1,2,448,256]{3,2,1,0:T(8,128)}, f32[1,2,448,256]{3,2,1,0:T(8,128)S(1)}, u32[]{:S(2)}) %copy-start.2) | copy-done | bytes 917528
  36.1 8.4 %shard_map.106 = (bf16[8,64,2048]{2,1,0:T(8,128)(2,1)}, bf16[8,2,64,256]{3,2,1,0:T(8,128)(2,1)}, f32[1,2,448,256]{3,2,1,0:T(8,128)}) custom-call(s32[1]{0:T(128)} %bitcast.me_ref, s32[4]{0:T(128)} %bitcast.5, s32[4,2]{1,0:T(4,128)} %copy.20.slots_ref, s32[4]{0:T(128)} %len_ref.7, f32[8]{0:T(128)} %lr_ref.7, ...), custom_call_target="tpu_custom_call", output_to_operand_aliasing={{0}: (9, {}), {1}: (10, {})} | custom-call | flops 8800000000 | bytes 5111808 | tf_op jit(solution)/shard_map/pallas_call | solution.py:204
  44.6 2.7 %collective-permute-done.5.b_ref = bf16[1,2,448,256]{3,2,1,0:T(8,128)(2,1)S(1)} collective-permute-done((bf16[1,2,448,256]{3,2,1,0:T(8,128)(2,1)S(1)}, bf16[1,2,448,256]{3,2,1,0:T(8,128)(2,1)S(1)}, u32[]{:S(2)}, u32[]{:S(2)}) %collective-permute-start.5) | collective-permute-done | bytes 458784 | tf_op jit(solution)/shard_map/ppermute | solution.py:343
  47.3 0.0 copy-start.1
  47.3 0.8 %copy-done.1 = bf16[1,2,448,256]{3,2,1,0:T(8,128)(2,1)} copy-done((bf16[1,2,448,256]{3,2,1,0:T(8,128)(2,1)}, bf16[1,2,448,256]{3,2,1,0:T(8,128)(2,1)S(1)}, u32[]{:S(2)}) %copy-start.1) | copy-done | bytes 458776
  48.1 2.1 %shard_map.107 = bf16[1,2,448,256]{3,2,1,0:T(8,128)(2,1)} custom-call(f32[1,2,448,256]{3,2,1,0:T(8,128)} %get-tuple-element.33.a_ref, bf16[1,2,448,256]{3,2,1,0:T(8,128)(2,1)} %copy-done.1), custom_call_target="tpu_custom_call" | custom-call | tf_op jit(solution)/shard_map/pallas_call | solution.py:312
Async XLA Ops:
  0.6 4.5 %collective-permute-start.1 = (bf16[1,2,448,256]{3,2,1,0:T(8,128)(2,1)}, bf16[1,2,448,256]{3,2,1,0:T(8,128)(2,1)S(1)}, u32[]{:S(2)}, u32[]{:S(2)}) collective-permute-start(bf16[1,2,448,256]{3,2,1,0:T(8,128)(2,1)} %pkv_ref), channel_id=1, source_target_pairs={{0,4},{4,0},{8,12},{12,8},{1,5},{5,1},{9,13},{13,9},{2,6},{6,2},{1... | collective-permute-start | bytes 1376264 | tf_op jit(solution)/shard_map/ppermute | solution.py:324
  1.2 13.9 %collective-permute-start = (bf16[1,2,448,256]{3,2,1,0:T(8,128)(2,1)}, bf16[1,2,448,256]{3,2,1,0:T(8,128)(2,1)S(1)}, u32[]{:S(2)}, u32[]{:S(2)}) collective-permute-start(bf16[1,2,448,256]{3,2,1,0:T(8,128)(2,1)} %pkv_ref), channel_id=1, source_target_pairs={{0,8},{4,12},{8,0},{12,4},{1,9},{5,13},{9,1},{13,5},{2,10},{6,14},... | collective-permute-start | bytes 1376264 | tf_op jit(solution)/shard_map/ppermute | solution.py:323
  5.1 0.8 %copy-start.4 = (bf16[1,2,448,256]{3,2,1,0:T(8,128)(2,1)}, bf16[1,2,448,256]{3,2,1,0:T(8,128)(2,1)S(1)}, u32[]{:S(2)}) copy-start(bf16[1,2,448,256]{3,2,1,0:T(8,128)(2,1)S(1)} %collective-permute-done.1.pkv_ref) | copy-start | bytes 1376260
  15.1 0.8 %copy-start.3 = (bf16[1,2,448,256]{3,2,1,0:T(8,128)(2,1)}, bf16[1,2,448,256]{3,2,1,0:T(8,128)(2,1)S(1)}, u32[]{:S(2)}) copy-start(bf16[1,2,448,256]{3,2,1,0:T(8,128)(2,1)S(1)} %collective-permute-done.pkv_ref) | copy-start | bytes 1376260
  15.1 9.5 %collective-permute-start.2 = (bf16[1,2,448,256]{3,2,1,0:T(8,128)(2,1)S(1)}, bf16[1,2,448,256]{3,2,1,0:T(8,128)(2,1)S(1)}, u32[]{:S(2)}, u32[]{:S(2)}) collective-permute-start(bf16[1,2,448,256]{3,2,1,0:T(8,128)(2,1)S(1)} %collective-permute-done.pkv_ref), channel_id=1, source_target_pairs={{0,4},{4,0},{8,12},{12,8},{1,5},{5,1},{9,13},{13,9},{2,6},{6,2},{1... | collective-permute-start | bytes 1376264 | tf_op jit(solution)/shard_map/ppermute | solution.py:336
  15.1 20.0 %collective-permute-start.4 = (f32[1,2,448,256]{3,2,1,0:T(8,128)}, f32[1,2,448,256]{3,2,1,0:T(8,128)S(1)}, u32[]{:S(2)}, u32[]{:S(2)}) collective-permute-start(f32[1,2,448,256]{3,2,1,0:T(8,128)} %get-tuple-element.30), channel_id=1, source_target_pairs={{0,4},{4,0},{8,12},{12,8},{1,5},{5,1},{9,13},{13,9},{2,6},{6,2},{1... | collective-permute-start | bytes 2752520 | tf_op jit(solution)/shard_map/ppermute | solution.py:337
  24.6 0.8 %copy-start.5 = (bf16[1,2,448,256]{3,2,1,0:T(8,128)(2,1)}, bf16[1,2,448,256]{3,2,1,0:T(8,128)(2,1)S(1)}, u32[]{:S(2)}) copy-start(bf16[1,2,448,256]{3,2,1,0:T(8,128)(2,1)S(1)} %collective-permute-done.2.pkv_ref) | copy-start | bytes 1376260
  25.4 9.2 %copy-start = (f32[1,2,448,256]{3,2,1,0:T(8,128)S(1)}, f32[1,2,448,256]{3,2,1,0:T(8,128)}, u32[]{:S(2)}) copy-start(f32[1,2,448,256]{3,2,1,0:T(8,128)} %get-tuple-element.23) | copy-start | bytes 2752516
  32.6 2.0 %collective-permute-start.3 = (bf16[1,2,448,256]{3,2,1,0:T(8,128)(2,1)}, bf16[1,2,448,256]{3,2,1,0:T(8,128)(2,1)S(1)}, u32[]{:S(2)}, u32[]{:S(2)}) collective-permute-start(bf16[1,2,448,256]{3,2,1,0:T(8,128)(2,1)} %get-tuple-element.26), channel_id=1, source_target_pairs={{0,4},{4,0},{8,12},{12,8},{1,5},{5,1},{9,13},{13,9},{2,6},{6,2},{1... | collective-permute-start | bytes 1376264 | tf_op jit(solution)/shard_map/ppermute | solution.py:340
  34.7 12.6 %collective-permute-start.5 = (bf16[1,2,448,256]{3,2,1,0:T(8,128)(2,1)S(1)}, bf16[1,2,448,256]{3,2,1,0:T(8,128)(2,1)S(1)}, u32[]{:S(2)}, u32[]{:S(2)}) collective-permute-start(bf16[1,2,448,256]{3,2,1,0:T(8,128)(2,1)S(1)} %add_convert_fusion), channel_id=1, source_target_pairs={{0,8},{4,12},{8,0},{12,4},{1,9},{5,13},{9,1},{13,5},{2,10},{6,14},... | collective-permute-start | bytes 1376264 | tf_op jit(solution)/shard_map/ppermute | solution.py:343
  35.1 1.0 %copy-start.2 = (f32[1,2,448,256]{3,2,1,0:T(8,128)}, f32[1,2,448,256]{3,2,1,0:T(8,128)S(1)}, u32[]{:S(2)}) copy-start(f32[1,2,448,256]{3,2,1,0:T(8,128)S(1)} %collective-permute-done.4.rest_2_) | copy-start | bytes 2752516
  47.3 0.8 %copy-start.1 = (bf16[1,2,448,256]{3,2,1,0:T(8,128)(2,1)}, bf16[1,2,448,256]{3,2,1,0:T(8,128)(2,1)S(1)}, u32[]{:S(2)}) copy-start(bf16[1,2,448,256]{3,2,1,0:T(8,128)(2,1)S(1)} %collective-permute-done.5.b_ref) | copy-start | bytes 1376260

commit v9 on v7

--- a/solution.py
+++ b/solution.py
@@ -86,7 +86,7 @@
 def pair_of(goal, goal_ref, pair_count):
     pair = 0
     for p in range(pair_count):
-        pair = jnp.where(goal_ref[p, 0] == goal, p, pair)
+        pair = jnp.where(goal_ref[p] == goal, p, pair)
     return pair
 
 
@@ -110,7 +110,7 @@
     def _():
         bias_ref[...] = mask_bias(length, **dims)
 
-    gap = lr_ref[slots_ref[pair, 0]] - lr_ref[slots_ref[pair, 1]]
+    gap = lr_ref[slots_ref[0, pair]] - lr_ref[slots_ref[1, pair]]
     x = jnp.full((1, 128), -dpo_beta * gap, jnp.float32)
     weight = dpo_beta * (1.0 / (1.0 + jnp.exp(-x)))
     coef = jnp.where(member == 0, -weight, weight)[:, :1]
@@ -146,7 +146,7 @@
 
     def suffix_of(m, me_ref, goal_ref, slots_ref):
         pair = pair_of(me_ref[0] ^ flip, goal_ref, pair_count)
-        return slots_ref[pair, m]
+        return slots_ref[m, pair]
 
     def q_map(k, m, me_ref, goal_ref, slots_ref, len_ref):
         return (suffix_of(m, me_ref, goal_ref, slots_ref), 0, k)
@@ -310,7 +310,7 @@
     pre_across = lax.ppermute(prefix_kv, "dp", across)
     pre_partner = lax.ppermute(prefix_kv, "dp", partner)
     me = lax.axis_index("dp").astype(jnp.int32).reshape(1)
-    tables = (me, pair_goal.astype(jnp.int32), pair_slots.astype(jnp.int32),
+    tables = (me, pair_goal.reshape(-1).astype(jnp.int32), pair_slots.T.astype(jnp.int32),
               prefix_len.astype(jnp.int32), logratio)
 
     def run(flip, prefix_one, chain, **extra):

time: 49.8 us -> 49.7 us (level)
  local copies, waits for them, and re-layouts: 5.28 us -> 2.72 us
  starting transfers between devices: 4.7 us -> 6.26 us
  waiting for transfers between devices: 5.06 us -> 6.11 us
    unnamed x12 -> x10, local copies, waits for them, and re-layouts: 5.28 us -> 2.72 us
    ppermute x1, waiting for transfers between devices: 0.02 us -> 1.85 us  [pipelined(): pre_across = lax.ppermute(prefix_kv, 'dp', across)]
    ppermute x1, starting transfers between devices: 1 us -> 2.61 us  [pipelined(): total = own + lax.ppermute(forward, 'dp', across).astype(jnp.float32)]
    ppermute x1, waiting for transfers between devices: 3.01 us -> 2.23 us  [pipelined(): total = own + lax.ppermute(forward, 'dp', across).astype(jnp.float32)]
  transfers between devices with their start and end apart: 6 -> 6, of which waited for: 2 -> 3; matrix products, arithmetic and copies ran while one was open for 5% -> 0% of each run, Pallas kernels for 64% -> 64%
where the time goes in v9:
time: 49.7 us; the launch traced here: 49.3 us
  Pallas kernels  31.4 us (63%)
  starting transfers between devices  6.26 us (13%)
  waiting for transfers between devices  6.11 us (12%)
  local copies, waits for them, and re-layouts  2.72 us (5%)
  other arithmetic  2.14 us (4%)
  between operations  0.67 us (1%)
    pallas_call x4, Pallas kernels, attend_slot(): pl.pallas_call(kernel, grid_spec=grid_spec, out_shape=out_shape, input_ou...  31.4 us
    unnamed x10, local copies, waits for them, and re-layouts  2.72 us
    ppermute x1, starting transfers between devices, pipelined(): total = own + lax.ppermute(forward, 'dp', across).astype(jnp.float32)  2.61 us
    ppermute x1, starting transfers between devices, pipelined(): pre_across = lax.ppermute(prefix_kv, 'dp', across)  2.58 us
    ppermute x1, waiting for transfers between devices, pipelined(): total = own + lax.ppermute(forward, 'dp', across).astype(jnp.float32)  2.23 us
    convert_element_type x1, other arithmetic, pipelined(): return (chain[0], chain[1], total.astype(jnp.bfloat16))  2.04 us
    ppermute x1, waiting for transfers between devices, pipelined(): lax.ppermute(relay, 'dp', partner).astype(jnp.float32)  2.02 us
    ppermute x1, waiting for transfers between devices, pipelined(): pre_across = lax.ppermute(prefix_kv, 'dp', across)  1.85 us
  transfers between devices with their start and end apart: 6, of which 3 were waited for; matrix products, arithmetic and copies ran while one was open for 0% of the time, Pallas kernels for 64%

profile of v9, /device:TPU:0, one launch (start us, length us, event | category | flops | bytes accessed | tf_op | source)
XLA Modules:
  0.0 49.3 jit_solution(3470063002345511272)
XLA Ops:
  0.6 0.6 %collective-permute-start.1 = (bf16[1,2,448,256]{3,2,1,0:T(8,128)(2,1)}, bf16[1,2,448,256]{3,2,1,0:T(8,128)(2,1)S(1)}, u32[]{:S(2)}, u32[]{:S(2)}) collective-permute-start(bf16[1,2,448,256]{3,2,1,0:T(8,128)(2,1)} %pkv_ref), channel_id=1, source_target_pairs={{0,4},{4,0},{8,12},{12,8},{1,5},{5,1},{9,13},{13,9},{2,6},{6,2},{1... | collective-permute-start | bytes 1376264 | tf_op jit(solution)/shard_map/ppermute | solution.py:311
  1.2 2.6 %collective-permute-start = (bf16[1,2,448,256]{3,2,1,0:T(8,128)(2,1)}, bf16[1,2,448,256]{3,2,1,0:T(8,128)(2,1)S(1)}, u32[]{:S(2)}, u32[]{:S(2)}) collective-permute-start(bf16[1,2,448,256]{3,2,1,0:T(8,128)(2,1)} %pkv_ref), channel_id=1, source_target_pairs={{0,8},{4,12},{8,0},{12,4},{1,9},{5,13},{9,1},{13,5},{2,10},{6,14},... | collective-permute-start | bytes 1376264 | tf_op jit(solution)/shard_map/ppermute | solution.py:310
  3.8 0.0 collective-permute-done.1.pkv_ref
  3.8 0.0 copy-start.3
  3.8 0.8 %copy-done.3 = bf16[1,2,448,256]{3,2,1,0:T(8,128)(2,1)} copy-done((bf16[1,2,448,256]{3,2,1,0:T(8,128)(2,1)}, bf16[1,2,448,256]{3,2,1,0:T(8,128)(2,1)S(1)}, u32[]{:S(2)}) %copy-start.3) | copy-done | bytes 458776
  4.5 8.7 %shard_map.103 = (bf16[8,64,2048]{2,1,0:T(8,128)(2,1)}, bf16[8,2,64,256]{3,2,1,0:T(8,128)(2,1)}, f32[1,2,448,256]{3,2,1,0:T(8,128)}) custom-call(s32[1]{0:T(128)} %bitcast.me_ref, s32[4]{0:T(128)} %bitcast.7, s32[2,4]{1,0:T(2,128)} %bitcast.3, s32[4]{0:T(128)} %len_ref.7, f32[8]{0:T(128)} %lr_ref.7, bf16[8,64,2048]{2,1,0:T(8,128)(2,1)} %q_ref.7, ...), custom_call_target="tpu_custom_call" | custom-call | flops 8800000000 | bytes 5111808 | tf_op jit(solution)/shard_map/pallas_call | solution.py:204
  13.2 1.9 %collective-permute-done.pkv_ref = bf16[1,2,448,256]{3,2,1,0:T(8,128)(2,1)S(1)} collective-permute-done((bf16[1,2,448,256]{3,2,1,0:T(8,128)(2,1)}, bf16[1,2,448,256]{3,2,1,0:T(8,128)(2,1)S(1)}, u32[]{:S(2)}, u32[]{:S(2)}) %collective-permute-start) | collective-permute-done | bytes 458784 | tf_op jit(solution)/shard_map/ppermute | solution.py:310
  15.1 0.0 copy-start.2
  15.1 0.0 collective-permute-start.2
  15.1 0.5 %collective-permute-start.4 = (f32[1,2,448,256]{3,2,1,0:T(8,128)}, f32[1,2,448,256]{3,2,1,0:T(8,128)S(1)}, u32[]{:S(2)}, u32[]{:S(2)}) collective-permute-start(f32[1,2,448,256]{3,2,1,0:T(8,128)} %get-tuple-element.30), channel_id=1, source_target_pairs={{0,4},{4,0},{8,12},{12,8},{1,5},{5,1},{9,13},{13,9},{2,6},{6,2},{1... | collective-permute-start | bytes 2752520 | tf_op jit(solution)/shard_map/ppermute | solution.py:324
  15.6 0.3 copy-done.2
  15.9 7.1 %shard_map.104 = (bf16[8,64,2048]{2,1,0:T(8,128)(2,1)}, bf16[8,2,64,256]{3,2,1,0:T(8,128)(2,1)}, f32[1,2,448,256]{3,2,1,0:T(8,128)}) custom-call(s32[1]{0:T(128)} %bitcast.me_ref, s32[4]{0:T(128)} %bitcast.8, s32[2,4]{1,0:T(2,128)} %bitcast.4, s32[4]{0:T(128)} %len_ref.7, f32[8]{0:T(128)} %lr_ref.7, ...), custom_call_target="tpu_custom_call", output_to_operand_aliasing={{0}: (9, {}), {1}: (10, {})} | custom-call | flops 8800000000 | bytes 5111808 | tf_op jit(solution)/shard_map/pallas_call | solution.py:204
  22.9 0.0 collective-permute-done.2.pkv_ref
  22.9 0.0 copy-start.4
  22.9 0.8 %copy-done.4 = bf16[1,2,448,256]{3,2,1,0:T(8,128)(2,1)} copy-done((bf16[1,2,448,256]{3,2,1,0:T(8,128)(2,1)}, bf16[1,2,448,256]{3,2,1,0:T(8,128)(2,1)S(1)}, u32[]{:S(2)}) %copy-start.4) | copy-done | bytes 458776
  23.7 0.0 copy-start
  23.7 8.0 %shard_map.105 = (bf16[8,64,2048]{2,1,0:T(8,128)(2,1)}, bf16[8,2,64,256]{3,2,1,0:T(8,128)(2,1)}, bf16[1,2,448,256]{3,2,1,0:T(8,128)(2,1)}) custom-call(s32[1]{0:T(128)} %bitcast.me_ref, s32[4]{0:T(128)} %bitcast.9, s32[2,4]{1,0:T(2,128)} %bitcast.5, s32[4]{0:T(128)} %len_ref.7, f32[8]{0:T(128)} %lr_ref.7, ...), custom_call_target="tpu_custom_call", output_to_operand_aliasing={{0}: (9, {}), {1}: (10, {})} | custom-call | flops 8800000000 | bytes 5111808 | tf_op jit(solution)/shard_map/pallas_call | solution.py:204
  31.7 0.0 collective-permute-start.3
  31.7 2.0 %collective-permute-done.3 = bf16[1,2,448,256]{3,2,1,0:T(8,128)(2,1)S(1)} collective-permute-done((bf16[1,2,448,256]{3,2,1,0:T(8,128)(2,1)}, bf16[1,2,448,256]{3,2,1,0:T(8,128)(2,1)S(1)}, u32[]{:S(2)}, u32[]{:S(2)}) %collective-permute-start.3) | collective-permute-done | bytes 458784 | tf_op jit(solution)/shard_map/ppermute | solution.py:327
  33.8 0.0 copy-done
  33.8 0.1 add_convert_fusion.1
  33.9 2.6 %collective-permute-start.5 = (bf16[1,2,448,256]{3,2,1,0:T(8,128)(2,1)S(1)}, bf16[1,2,448,256]{3,2,1,0:T(8,128)(2,1)S(1)}, u32[]{:S(2)}, u32[]{:S(2)}) collective-permute-start(bf16[1,2,448,256]{3,2,1,0:T(8,128)(2,1)S(1)} %add_convert_fusion.1), channel_id=1, source_target_pairs={{0,8},{4,12},{8,0},{12,4},{1,9},{5,13},{9,1},{13,5},{2,10},{6,14},... | collective-permute-start | bytes 1376264 | tf_op jit(solution)/shard_map/ppermute | solution.py:330
  36.5 0.0 collective-permute-done.4.rest_2_
  36.5 0.0 copy-start.1
  36.5 0.9 %copy-done.1 = f32[1,2,448,256]{3,2,1,0:T(8,128)} copy-done((f32[1,2,448,256]{3,2,1,0:T(8,128)}, f32[1,2,448,256]{3,2,1,0:T(8,128)S(1)}, u32[]{:S(2)}) %copy-start.1) | copy-done | bytes 917528
  37.4 7.7 %shard_map.106 = (bf16[8,64,2048]{2,1,0:T(8,128)(2,1)}, bf16[8,2,64,256]{3,2,1,0:T(8,128)(2,1)}, f32[1,2,448,256]{3,2,1,0:T(8,128)}) custom-call(s32[1]{0:T(128)} %bitcast.me_ref, s32[4]{0:T(128)} %bitcast.10, s32[2,4]{1,0:T(2,128)} %bitcast.6, s32[4]{0:T(128)} %len_ref.7, f32[8]{0:T(128)} %lr_ref.7, ...), custom_call_target="tpu_custom_call", output_to_operand_aliasing={{0}: (9, {}), {1}: (10, {})} | custom-call | flops 8800000000 | bytes 5111808 | tf_op jit(solution)/shard_map/pallas_call | solution.py:204
  45.1 2.2 %collective-permute-done.5 = bf16[1,2,448,256]{3,2,1,0:T(8,128)(2,1)S(1)} collective-permute-done((bf16[1,2,448,256]{3,2,1,0:T(8,128)(2,1)S(1)}, bf16[1,2,448,256]{3,2,1,0:T(8,128)(2,1)S(1)}, u32[]{:S(2)}, u32[]{:S(2)}) %collective-permute-start.5) | collective-permute-done | bytes 458784 | tf_op jit(solution)/shard_map/ppermute | solution.py:330
  47.3 2.0 %add_convert_fusion = bf16[1,2,448,256]{3,2,1,0:T(8,128)(2,1)} fusion(f32[1,2,448,256]{3,2,1,0:T(8,128)} %get-tuple-element.33, bf16[1,2,448,256]{3,2,1,0:T(8,128)(2,1)S(1)} %collective-permute-done.5), kind=kLoop, calls=%fused_computation | loop fusion | flops 688128 | bytes 1835008 | tf_op jit(solution)/shard_map/convert_element_type | solution.py:331
Async XLA Ops:
  0.6 3.1 %collective-permute-start.1 = (bf16[1,2,448,256]{3,2,1,0:T(8,128)(2,1)}, bf16[1,2,448,256]{3,2,1,0:T(8,128)(2,1)S(1)}, u32[]{:S(2)}, u32[]{:S(2)}) collective-permute-start(bf16[1,2,448,256]{3,2,1,0:T(8,128)(2,1)} %pkv_ref), channel_id=1, source_target_pairs={{0,4},{4,0},{8,12},{12,8},{1,5},{5,1},{9,13},{13,9},{2,6},{6,2},{1... | collective-permute-start | bytes 1376264 | tf_op jit(solution)/shard_map/ppermute | solution.py:311
  1.2 13.9 %collective-permute-start = (bf16[1,2,448,256]{3,2,1,0:T(8,128)(2,1)}, bf16[1,2,448,256]{3,2,1,0:T(8,128)(2,1)S(1)}, u32[]{:S(2)}, u32[]{:S(2)}) collective-permute-start(bf16[1,2,448,256]{3,2,1,0:T(8,128)(2,1)} %pkv_ref), channel_id=1, source_target_pairs={{0,8},{4,12},{8,0},{12,4},{1,9},{5,13},{9,1},{13,5},{2,10},{6,14},... | collective-permute-start | bytes 1376264 | tf_op jit(solution)/shard_map/ppermute | solution.py:310
  3.8 0.8 %copy-start.3 = (bf16[1,2,448,256]{3,2,1,0:T(8,128)(2,1)}, bf16[1,2,448,256]{3,2,1,0:T(8,128)(2,1)S(1)}, u32[]{:S(2)}) copy-start(bf16[1,2,448,256]{3,2,1,0:T(8,128)(2,1)S(1)} %collective-permute-done.1.pkv_ref) | copy-start | bytes 1376260
  15.1 0.8 %copy-start.2 = (bf16[1,2,448,256]{3,2,1,0:T(8,128)(2,1)}, bf16[1,2,448,256]{3,2,1,0:T(8,128)(2,1)S(1)}, u32[]{:S(2)}) copy-start(bf16[1,2,448,256]{3,2,1,0:T(8,128)(2,1)S(1)} %collective-permute-done.pkv_ref) | copy-start | bytes 1376260
  15.1 7.8 %collective-permute-start.2 = (bf16[1,2,448,256]{3,2,1,0:T(8,128)(2,1)S(1)}, bf16[1,2,448,256]{3,2,1,0:T(8,128)(2,1)S(1)}, u32[]{:S(2)}, u32[]{:S(2)}) collective-permute-start(bf16[1,2,448,256]{3,2,1,0:T(8,128)(2,1)S(1)} %collective-permute-done.pkv_ref), channel_id=1, source_target_pairs={{0,4},{4,0},{8,12},{12,8},{1,5},{5,1},{9,13},{13,9},{2,6},{6,2},{1... | collective-permute-start | bytes 1376264 | tf_op jit(solution)/shard_map/ppermute | solution.py:323
  15.1 21.4 %collective-permute-start.4 = (f32[1,2,448,256]{3,2,1,0:T(8,128)}, f32[1,2,448,256]{3,2,1,0:T(8,128)S(1)}, u32[]{:S(2)}, u32[]{:S(2)}) collective-permute-start(f32[1,2,448,256]{3,2,1,0:T(8,128)} %get-tuple-element.30), channel_id=1, source_target_pairs={{0,4},{4,0},{8,12},{12,8},{1,5},{5,1},{9,13},{13,9},{2,6},{6,2},{1... | collective-permute-start | bytes 2752520 | tf_op jit(solution)/shard_map/ppermute | solution.py:324
  22.9 0.8 %copy-start.4 = (bf16[1,2,448,256]{3,2,1,0:T(8,128)(2,1)}, bf16[1,2,448,256]{3,2,1,0:T(8,128)(2,1)S(1)}, u32[]{:S(2)}) copy-start(bf16[1,2,448,256]{3,2,1,0:T(8,128)(2,1)S(1)} %collective-permute-done.2.pkv_ref) | copy-start | bytes 1376260
  23.7 10.1 %copy-start = (f32[1,2,448,256]{3,2,1,0:T(8,128)S(1)}, f32[1,2,448,256]{3,2,1,0:T(8,128)}, u32[]{:S(2)}) copy-start(f32[1,2,448,256]{3,2,1,0:T(8,128)} %get-tuple-element.23) | copy-start | bytes 2752516
  31.7 2.0 %collective-permute-start.3 = (bf16[1,2,448,256]{3,2,1,0:T(8,128)(2,1)}, bf16[1,2,448,256]{3,2,1,0:T(8,128)(2,1)S(1)}, u32[]{:S(2)}, u32[]{:S(2)}) collective-permute-start(bf16[1,2,448,256]{3,2,1,0:T(8,128)(2,1)} %get-tuple-element.26), channel_id=1, source_target_pairs={{0,4},{4,0},{8,12},{12,8},{1,5},{5,1},{9,13},{13,9},{2,6},{6,2},{1... | collective-permute-start | bytes 1376264 | tf_op jit(solution)/shard_map/ppermute | solution.py:327
  33.9 13.4 %collective-permute-start.5 = (bf16[1,2,448,256]{3,2,1,0:T(8,128)(2,1)S(1)}, bf16[1,2,448,256]{3,2,1,0:T(8,128)(2,1)S(1)}, u32[]{:S(2)}, u32[]{:S(2)}) collective-permute-start(bf16[1,2,448,256]{3,2,1,0:T(8,128)(2,1)S(1)} %add_convert_fusion.1), channel_id=1, source_target_pairs={{0,8},{4,12},{8,0},{12,4},{1,9},{5,13},{9,1},{13,5},{2,10},{6,14},... | collective-permute-start | bytes 1376264 | tf_op jit(solution)/shard_map/ppermute | solution.py:330
  36.5 0.9 %copy-start.1 = (f32[1,2,448,256]{3,2,1,0:T(8,128)}, f32[1,2,448,256]{3,2,1,0:T(8,128)S(1)}, u32[]{:S(2)}) copy-start(f32[1,2,448,256]{3,2,1,0:T(8,128)S(1)} %collective-permute-done.4.rest_2_) | copy-start | bytes 2752516

commit v10 on v9

--- a/solution.py
+++ b/solution.py
@@ -8,6 +8,7 @@
 from jax.sharding import PartitionSpec as P
 
 HD = 128
+LOG2E = 1.4426950408889634
 
 dpo_beta = 0.5
 
@@ -31,16 +32,16 @@
     values = jnp.concatenate([values_own, values_pre], 0)
 
     nt = (((1,), (1,)), ((), ()))
-    scores_t = lax.dot_general(keys, q_rows, nt, preferred_element_type=jnp.float32) * scale
+    scores_t = lax.dot_general(keys, q_rows, nt, preferred_element_type=jnp.float32) * (scale * LOG2E)
     scores_t = scores_t + bias
     col_max = jnp.max(scores_t, 0, keepdims=True)
-    raised = jnp.exp(scores_t - col_max)
-    prob_t = raised * (1.0 / jnp.sum(raised, 0, keepdims=True))
-    prob_low_t = prob_t.astype(jnp.bfloat16)
+    raised = jnp.exp2(scores_t - col_max)
+    inv_sum = 1.0 / jnp.sum(raised, 0, keepdims=True)
+    prob_low_t = (raised * inv_sum).astype(jnp.bfloat16)
     output_t = jnp.dot(values.T, prob_low_t, preferred_element_type=jnp.float32)
     row_dot = jnp.sum(c_rows.T.astype(jnp.float32) * output_t, 0, keepdims=True)
     grad_prob_t = lax.dot_general(values, c_rows, nt, preferred_element_type=jnp.float32)
-    grad_score_t = (prob_t * (grad_prob_t - row_dot)).astype(jnp.bfloat16)
+    grad_score_t = (raised * ((grad_prob_t - row_dot) * inv_sum)).astype(jnp.bfloat16)
     grad_q_t = jnp.dot(keys.T, grad_score_t, preferred_element_type=jnp.float32)
     grad_q = (scale * grad_q_t.T).astype(jnp.bfloat16)
     grad_k = scale * jnp.dot(grad_score_t, q_rows, preferred_element_type=jnp.float32)

time: 49.7 us -> 50.3 us (1.012)
  waiting for transfers between devices: 6.11 us -> 9.95 us
  starting transfers between devices: 6.26 us -> 3.72 us
  Pallas kernels: 31.4 us -> 30.7 us
    ppermute x1, starting transfers between devices: 2.61 us -> 0.07 us  [pipelined(): total = own + lax.ppermute(forward, 'dp', across).astype(jnp.float32)]
    ppermute x1, waiting for transfers between devices: 2.23 us -> 4.4 us  [pipelined(): total = own + lax.ppermute(forward, 'dp', across).astype(jnp.float32)]
    ppermute x1, waiting for transfers between devices: 1.85 us -> 3.52 us  [pipelined(): pre_across = lax.ppermute(prefix_kv, 'dp', across)]
    pallas_call x4, Pallas kernels: 31.4 us -> 30.7 us  [attend_slot(): pl.pallas_call(kernel, grid_spec=grid_spec, out_shape=out_shape, input_ou...]
  transfers between devices with their start and end apart: 6 -> 6, of which waited for: 3 -> 3; matrix products, arithmetic and copies ran while one was open for 0% -> 0% of each run, Pallas kernels for 64% -> 61%
where the time goes in v10:
time: 50.3 us; the launch traced here: 50 us
  Pallas kernels  30.7 us (61%)
  waiting for transfers between devices  9.95 us (20%)
  starting transfers between devices  3.72 us (7%)
  local copies, waits for them, and re-layouts  2.71 us (5%)
  other arithmetic  2.14 us (4%)
  between operations  0.69 us (1%)
    pallas_call x4, Pallas kernels, attend_slot(): pl.pallas_call(kernel, grid_spec=grid_spec, out_shape=out_shape, input_ou...  30.7 us
    ppermute x1, waiting for transfers between devices, pipelined(): total = own + lax.ppermute(forward, 'dp', across).astype(jnp.float32)  4.4 us
    ppermute x1, waiting for transfers between devices, pipelined(): pre_across = lax.ppermute(prefix_kv, 'dp', across)  3.52 us
    unnamed x10, local copies, waits for them, and re-layouts  2.71 us
    ppermute x1, starting transfers between devices, pipelined(): pre_across = lax.ppermute(prefix_kv, 'dp', across)  2.58 us
    convert_element_type x1, other arithmetic, pipelined(): return (chain[0], chain[1], total.astype(jnp.bfloat16))  2.04 us
    ppermute x1, waiting for transfers between devices, pipelined(): lax.ppermute(relay, 'dp', partner).astype(jnp.float32)  2.02 us
  transfers between devices with their start and end apart: 6, of which 3 were waited for; matrix products, arithmetic and copies ran while one was open for 0% of the time, Pallas kernels for 61%

profile of v10, /device:TPU:0, one launch (start us, length us, event | category | flops | bytes accessed | tf_op | source)
XLA Modules:
  0.0 50.0 jit_solution(3573315869995406710)
XLA Ops:
  0.6 0.6 %collective-permute-start.1 = (bf16[1,2,448,256]{3,2,1,0:T(8,128)(2,1)}, bf16[1,2,448,256]{3,2,1,0:T(8,128)(2,1)S(1)}, u32[]{:S(2)}, u32[]{:S(2)}) collective-permute-start(bf16[1,2,448,256]{3,2,1,0:T(8,128)(2,1)} %pkv_ref), channel_id=1, source_target_pairs={{0,4},{4,0},{8,12},{12,8},{1,5},{5,1},{9,13},{13,9},{2,6},{6,2},{1... | collective-permute-start | bytes 1376264 | tf_op jit(solution)/shard_map/ppermute | solution.py:312
  1.2 2.6 %collective-permute-start = (bf16[1,2,448,256]{3,2,1,0:T(8,128)(2,1)}, bf16[1,2,448,256]{3,2,1,0:T(8,128)(2,1)S(1)}, u32[]{:S(2)}, u32[]{:S(2)}) collective-permute-start(bf16[1,2,448,256]{3,2,1,0:T(8,128)(2,1)} %pkv_ref), channel_id=1, source_target_pairs={{0,8},{4,12},{8,0},{12,4},{1,9},{5,13},{9,1},{13,5},{2,10},{6,14},... | collective-permute-start | bytes 1376264 | tf_op jit(solution)/shard_map/ppermute | solution.py:311
  3.8 0.0 collective-permute-done.1.pkv_ref
  3.8 0.0 copy-start.3
  3.8 0.8 %copy-done.3 = bf16[1,2,448,256]{3,2,1,0:T(8,128)(2,1)} copy-done((bf16[1,2,448,256]{3,2,1,0:T(8,128)(2,1)}, bf16[1,2,448,256]{3,2,1,0:T(8,128)(2,1)S(1)}, u32[]{:S(2)}) %copy-start.3) | copy-done | bytes 458776
  4.5 7.0 %shard_map.103 = (bf16[8,64,2048]{2,1,0:T(8,128)(2,1)}, bf16[8,2,64,256]{3,2,1,0:T(8,128)(2,1)}, f32[1,2,448,256]{3,2,1,0:T(8,128)}) custom-call(s32[1]{0:T(128)} %bitcast.me_ref, s32[4]{0:T(128)} %bitcast.7, s32[2,4]{1,0:T(2,128)} %bitcast.3, s32[4]{0:T(128)} %len_ref.7, f32[8]{0:T(128)} %lr_ref.7, bf16[8,64,2048]{2,1,0:T(8,128)(2,1)} %q_ref.7, ...), custom_call_target="tpu_custom_call" | custom-call | flops 8800000000 | bytes 5111808 | tf_op jit(solution)/shard_map/pallas_call | solution.py:205
  11.6 3.5 %collective-permute-done.pkv_ref = bf16[1,2,448,256]{3,2,1,0:T(8,128)(2,1)S(1)} collective-permute-done((bf16[1,2,448,256]{3,2,1,0:T(8,128)(2,1)}, bf16[1,2,448,256]{3,2,1,0:T(8,128)(2,1)S(1)}, u32[]{:S(2)}, u32[]{:S(2)}) %collective-permute-start) | collective-permute-done | bytes 458784 | tf_op jit(solution)/shard_map/ppermute | solution.py:311
  15.1 0.0 copy-start.2
  15.1 0.0 collective-permute-start.2
  15.1 0.5 %collective-permute-start.4 = (f32[1,2,448,256]{3,2,1,0:T(8,128)}, f32[1,2,448,256]{3,2,1,0:T(8,128)S(1)}, u32[]{:S(2)}, u32[]{:S(2)}) collective-permute-start(f32[1,2,448,256]{3,2,1,0:T(8,128)} %get-tuple-element.30), channel_id=1, source_target_pairs={{0,4},{4,0},{8,12},{12,8},{1,5},{5,1},{9,13},{13,9},{2,6},{6,2},{1... | collective-permute-start | bytes 2752520 | tf_op jit(solution)/shard_map/ppermute | solution.py:325
  15.6 0.3 copy-done.2
  15.9 8.5 %shard_map.104 = (bf16[8,64,2048]{2,1,0:T(8,128)(2,1)}, bf16[8,2,64,256]{3,2,1,0:T(8,128)(2,1)}, f32[1,2,448,256]{3,2,1,0:T(8,128)}) custom-call(s32[1]{0:T(128)} %bitcast.me_ref, s32[4]{0:T(128)} %bitcast.8, s32[2,4]{1,0:T(2,128)} %bitcast.4, s32[4]{0:T(128)} %len_ref.7, f32[8]{0:T(128)} %lr_ref.7, ...), custom_call_target="tpu_custom_call", output_to_operand_aliasing={{0}: (9, {}), {1}: (10, {})} | custom-call | flops 8800000000 | bytes 5111808 | tf_op jit(solution)/shard_map/pallas_call | solution.py:205
  24.4 0.0 collective-permute-done.2.pkv_ref
  24.4 0.0 copy-start.4
  24.4 0.8 %copy-done.4 = bf16[1,2,448,256]{3,2,1,0:T(8,128)(2,1)} copy-done((bf16[1,2,448,256]{3,2,1,0:T(8,128)(2,1)}, bf16[1,2,448,256]{3,2,1,0:T(8,128)(2,1)S(1)}, u32[]{:S(2)}) %copy-start.4) | copy-done | bytes 458776
  25.2 0.0 copy-start
  25.2 8.0 %shard_map.105 = (bf16[8,64,2048]{2,1,0:T(8,128)(2,1)}, bf16[8,2,64,256]{3,2,1,0:T(8,128)(2,1)}, bf16[1,2,448,256]{3,2,1,0:T(8,128)(2,1)}) custom-call(s32[1]{0:T(128)} %bitcast.me_ref, s32[4]{0:T(128)} %bitcast.9, s32[2,4]{1,0:T(2,128)} %bitcast.5, s32[4]{0:T(128)} %len_ref.7, f32[8]{0:T(128)} %lr_ref.7, ...), custom_call_target="tpu_custom_call", output_to_operand_aliasing={{0}: (9, {}), {1}: (10, {})} | custom-call | flops 8800000000 | bytes 5111808 | tf_op jit(solution)/shard_map/pallas_call | solution.py:205
  33.2 0.0 collective-permute-start.3
  33.2 2.0 %collective-permute-done.3 = bf16[1,2,448,256]{3,2,1,0:T(8,128)(2,1)S(1)} collective-permute-done((bf16[1,2,448,256]{3,2,1,0:T(8,128)(2,1)}, bf16[1,2,448,256]{3,2,1,0:T(8,128)(2,1)S(1)}, u32[]{:S(2)}, u32[]{:S(2)}) %collective-permute-start.3) | collective-permute-done | bytes 458784 | tf_op jit(solution)/shard_map/ppermute | solution.py:328
  35.2 0.0 copy-done
  35.2 0.1 add_convert_fusion.1
  35.3 0.1 collective-permute-start.5
  35.4 0.0 collective-permute-done.4.rest_2_
  35.4 0.0 copy-start.1
  35.4 0.9 %copy-done.1 = f32[1,2,448,256]{3,2,1,0:T(8,128)} copy-done((f32[1,2,448,256]{3,2,1,0:T(8,128)}, f32[1,2,448,256]{3,2,1,0:T(8,128)S(1)}, u32[]{:S(2)}) %copy-start.1) | copy-done | bytes 917528
  36.3 7.2 %shard_map.106 = (bf16[8,64,2048]{2,1,0:T(8,128)(2,1)}, bf16[8,2,64,256]{3,2,1,0:T(8,128)(2,1)}, f32[1,2,448,256]{3,2,1,0:T(8,128)}) custom-call(s32[1]{0:T(128)} %bitcast.me_ref, s32[4]{0:T(128)} %bitcast.10, s32[2,4]{1,0:T(2,128)} %bitcast.6, s32[4]{0:T(128)} %len_ref.7, f32[8]{0:T(128)} %lr_ref.7, ...), custom_call_target="tpu_custom_call", output_to_operand_aliasing={{0}: (9, {}), {1}: (10, {})} | custom-call | flops 8800000000 | bytes 5111808 | tf_op jit(solution)/shard_map/pallas_call | solution.py:205
  43.5 4.4 %collective-permute-done.5 = bf16[1,2,448,256]{3,2,1,0:T(8,128)(2,1)S(1)} collective-permute-done((bf16[1,2,448,256]{3,2,1,0:T(8,128)(2,1)S(1)}, bf16[1,2,448,256]{3,2,1,0:T(8,128)(2,1)S(1)}, u32[]{:S(2)}, u32[]{:S(2)}) %collective-permute-start.5) | collective-permute-done | bytes 458784 | tf_op jit(solution)/shard_map/ppermute | solution.py:331
  47.9 2.0 %add_convert_fusion = bf16[1,2,448,256]{3,2,1,0:T(8,128)(2,1)} fusion(f32[1,2,448,256]{3,2,1,0:T(8,128)} %get-tuple-element.33, bf16[1,2,448,256]{3,2,1,0:T(8,128)(2,1)S(1)} %collective-permute-done.5), kind=kLoop, calls=%fused_computation | loop fusion | flops 688128 | bytes 1835008 | tf_op jit(solution)/shard_map/convert_element_type | solution.py:332
Async XLA Ops:
  0.6 3.1 %collective-permute-start.1 = (bf16[1,2,448,256]{3,2,1,0:T(8,128)(2,1)}, bf16[1,2,448,256]{3,2,1,0:T(8,128)(2,1)S(1)}, u32[]{:S(2)}, u32[]{:S(2)}) collective-permute-start(bf16[1,2,448,256]{3,2,1,0:T(8,128)(2,1)} %pkv_ref), channel_id=1, source_target_pairs={{0,4},{4,0},{8,12},{12,8},{1,5},{5,1},{9,13},{13,9},{2,6},{6,2},{1... | collective-permute-start | bytes 1376264 | tf_op jit(solution)/shard_map/ppermute | solution.py:312
  1.2 13.9 %collective-permute-start = (bf16[1,2,448,256]{3,2,1,0:T(8,128)(2,1)}, bf16[1,2,448,256]{3,2,1,0:T(8,128)(2,1)S(1)}, u32[]{:S(2)}, u32[]{:S(2)}) collective-permute-start(bf16[1,2,448,256]{3,2,1,0:T(8,128)(2,1)} %pkv_ref), channel_id=1, source_target_pairs={{0,8},{4,12},{8,0},{12,4},{1,9},{5,13},{9,1},{13,5},{2,10},{6,14},... | collective-permute-start | bytes 1376264 | tf_op jit(solution)/shard_map/ppermute | solution.py:311
  3.8 0.8 %copy-start.3 = (bf16[1,2,448,256]{3,2,1,0:T(8,128)(2,1)}, bf16[1,2,448,256]{3,2,1,0:T(8,128)(2,1)S(1)}, u32[]{:S(2)}) copy-start(bf16[1,2,448,256]{3,2,1,0:T(8,128)(2,1)S(1)} %collective-permute-done.1.pkv_ref) | copy-start | bytes 1376260
  15.1 0.8 %copy-start.2 = (bf16[1,2,448,256]{3,2,1,0:T(8,128)(2,1)}, bf16[1,2,448,256]{3,2,1,0:T(8,128)(2,1)S(1)}, u32[]{:S(2)}) copy-start(bf16[1,2,448,256]{3,2,1,0:T(8,128)(2,1)S(1)} %collective-permute-done.pkv_ref) | copy-start | bytes 1376260
  15.1 9.3 %collective-permute-start.2 = (bf16[1,2,448,256]{3,2,1,0:T(8,128)(2,1)S(1)}, bf16[1,2,448,256]{3,2,1,0:T(8,128)(2,1)S(1)}, u32[]{:S(2)}, u32[]{:S(2)}) collective-permute-start(bf16[1,2,448,256]{3,2,1,0:T(8,128)(2,1)S(1)} %collective-permute-done.pkv_ref), channel_id=1, source_target_pairs={{0,4},{4,0},{8,12},{12,8},{1,5},{5,1},{9,13},{13,9},{2,6},{6,2},{1... | collective-permute-start | bytes 1376264 | tf_op jit(solution)/shard_map/ppermute | solution.py:324
  15.1 20.3 %collective-permute-start.4 = (f32[1,2,448,256]{3,2,1,0:T(8,128)}, f32[1,2,448,256]{3,2,1,0:T(8,128)S(1)}, u32[]{:S(2)}, u32[]{:S(2)}) collective-permute-start(f32[1,2,448,256]{3,2,1,0:T(8,128)} %get-tuple-element.30), channel_id=1, source_target_pairs={{0,4},{4,0},{8,12},{12,8},{1,5},{5,1},{9,13},{13,9},{2,6},{6,2},{1... | collective-permute-start | bytes 2752520 | tf_op jit(solution)/shard_map/ppermute | solution.py:325
  24.4 0.8 %copy-start.4 = (bf16[1,2,448,256]{3,2,1,0:T(8,128)(2,1)}, bf16[1,2,448,256]{3,2,1,0:T(8,128)(2,1)S(1)}, u32[]{:S(2)}) copy-start(bf16[1,2,448,256]{3,2,1,0:T(8,128)(2,1)S(1)} %collective-permute-done.2.pkv_ref) | copy-start | bytes 1376260
  25.2 10.0 %copy-start = (f32[1,2,448,256]{3,2,1,0:T(8,128)S(1)}, f32[1,2,448,256]{3,2,1,0:T(8,128)}, u32[]{:S(2)}) copy-start(f32[1,2,448,256]{3,2,1,0:T(8,128)} %get-tuple-element.23) | copy-start | bytes 2752516
  33.2 2.0 %collective-permute-start.3 = (bf16[1,2,448,256]{3,2,1,0:T(8,128)(2,1)}, bf16[1,2,448,256]{3,2,1,0:T(8,128)(2,1)S(1)}, u32[]{:S(2)}, u32[]{:S(2)}) collective-permute-start(bf16[1,2,448,256]{3,2,1,0:T(8,128)(2,1)} %get-tuple-element.26), channel_id=1, source_target_pairs={{0,4},{4,0},{8,12},{12,8},{1,5},{5,1},{9,13},{13,9},{2,6},{6,2},{1... | collective-permute-start | bytes 1376264 | tf_op jit(solution)/shard_map/ppermute | solution.py:328
  35.3 12.6 %collective-permute-start.5 = (bf16[1,2,448,256]{3,2,1,0:T(8,128)(2,1)S(1)}, bf16[1,2,448,256]{3,2,1,0:T(8,128)(2,1)S(1)}, u32[]{:S(2)}, u32[]{:S(2)}) collective-permute-start(bf16[1,2,448,256]{3,2,1,0:T(8,128)(2,1)S(1)} %add_convert_fusion.1), channel_id=1, source_target_pairs={{0,8},{4,12},{8,0},{12,4},{1,9},{5,13},{9,1},{13,5},{2,10},{6,14},... | collective-permute-start | bytes 1376264 | tf_op jit(solution)/shard_map/ppermute | solution.py:331
  35.4 0.9 %copy-start.1 = (f32[1,2,448,256]{3,2,1,0:T(8,128)}, f32[1,2,448,256]{3,2,1,0:T(8,128)S(1)}, u32[]{:S(2)}) copy-start(f32[1,2,448,256]{3,2,1,0:T(8,128)S(1)} %collective-permute-done.4.rest_2_) | copy-start | bytes 2752516

commit v11 on v10

--- a/solution.py
+++ b/solution.py
@@ -49,26 +49,28 @@
     return grad_q, grad_k, grad_v
 
 
-def store_grads(grad_q, grad_k, grad_v, member, dq_ref, dkv_ref, dpre_ref, *, group, seq, prefix_rows):
+def store_grads(grad_q, grad_k, grad_v, member, dq_ref, dkv_ref, dpre_ref, *, group, seq, prefix_rows, head=0):
     active = grad_k.shape[0] - seq
+    kv_cols = pl.ds(pl.multiple_of(head * HD, HD), HD)
     for g in range(group):
-        dq_ref[0, :, g * HD:(g + 1) * HD] = grad_q[g * seq:(g + 1) * seq]
-    dkv_ref[0, 0] = grad_k[:seq].astype(jnp.bfloat16)
-    dkv_ref[0, 1] = grad_v[:seq].astype(jnp.bfloat16)
+        q_cols = pl.ds(pl.multiple_of((head * group + g) * HD, HD), HD)
+        dq_ref[0, :, q_cols] = grad_q[g * seq:(g + 1) * seq]
+    dkv_ref[0, 0, :, kv_cols] = grad_k[:seq].astype(jnp.bfloat16)
+    dkv_ref[0, 1, :, kv_cols] = grad_v[:seq].astype(jnp.bfloat16)
 
     @pl.when(member == 0)
     def _():
-        dpre_ref[0, 0, :active] = grad_k[seq:]
-        dpre_ref[0, 1, :active] = grad_v[seq:]
+        dpre_ref[0, 0, :active, kv_cols] = grad_k[seq:]
+        dpre_ref[0, 1, :active, kv_cols] = grad_v[seq:]
         if active < prefix_rows:
             zeros = jnp.zeros((prefix_rows - active, HD), jnp.float32)
-            dpre_ref[0, 0, active:] = zeros
-            dpre_ref[0, 1, active:] = zeros
+            dpre_ref[0, 0, active:, kv_cols] = zeros
+            dpre_ref[0, 1, active:, kv_cols] = zeros
 
     @pl.when(member != 0)
     def _():
-        dpre_ref[0, 0, :active] += grad_k[seq:]
-        dpre_ref[0, 1, :active] += grad_v[seq:]
+        dpre_ref[0, 0, :active, kv_cols] += grad_k[seq:]
+        dpre_ref[0, 1, :active, kv_cols] += grad_v[seq:]
 
 
 def attend_kernel(slots_ref, goal_ref, len_ref, coef_ref,
@@ -100,14 +102,15 @@
         seed_ref, rest = rest[0], rest[1:]
     dq_ref, dkv_ref, dpre_ref, bias_ref = rest[:4]
     acc_ref = rest[4] if low else dpre_ref
-    k = pl.program_id(0)
-    member = pl.program_id(1)
+    member = pl.program_id(0)
     goal = me_ref[0] ^ flip
     pair = pair_of(goal, goal_ref, pair_count)
     length = len_ref[goal]
     dims = dict(group=group, seq=seq, prefix_rows=prefix_rows)
-
-    @pl.when((k == 0) & (member == 0))
+    heads = skv_ref.shape[-1] // HD
+    qb = group * HD
+
+    @pl.when(member == 0)
     def _():
         bias_ref[...] = mask_bias(length, **dims)
 
@@ -116,14 +119,22 @@
     weight = dpo_beta * (1.0 / (1.0 + jnp.exp(-x)))
     coef = jnp.where(member == 0, -weight, weight)[:, :1]
     blocks = (seq + length + 127) // 128
-    for used in range(1, (seq + prefix_rows + 127) // 128 + 1):
-        @pl.when(blocks == used)
-        def _():
-            width = min(used * 128, seq + prefix_rows)
-            grads = attend_math(q_ref[0], og_ref[0], pkv_ref[0, 0, :width - seq], pkv_ref[0, 1, :width - seq],
-                                skv_ref[0, 0], skv_ref[0, 1], bias_ref[:width], coef,
-                                group=group, seq=seq)
-            store_grads(*grads, member, dq_ref, dkv_ref, acc_ref, **dims)
+
+    def one_head(h, carry):
+        q_cols = pl.ds(pl.multiple_of(h * qb, qb), qb)
+        kv_cols = pl.ds(pl.multiple_of(h * HD, HD), HD)
+        for used in range(1, (seq + prefix_rows + 127) // 128 + 1):
+            @pl.when(blocks == used)
+            def _():
+                width = min(used * 128, seq + prefix_rows)
+                grads = attend_math(q_ref[0, :, q_cols], og_ref[0, :, q_cols],
+                                    pkv_ref[0, 0, :width - seq, kv_cols], pkv_ref[0, 1, :width - seq, kv_cols],
+                                    skv_ref[0, 0, :, kv_cols], skv_ref[0, 1, :, kv_cols], bias_ref[:width], coef,
+                                    group=group, seq=seq)
+                store_grads(*grads, member, dq_ref, dkv_ref, acc_ref, head=h, **dims)
+        return carry
+
+    lax.fori_loop(0, heads, one_head, 0)
 
     if seeded:
         @pl.when(member == 1)
@@ -149,14 +160,14 @@
         pair = pair_of(me_ref[0] ^ flip, goal_ref, pair_count)
         return slots_ref[m, pair]
 
-    def q_map(k, m, me_ref, goal_ref, slots_ref, len_ref):
-        return (suffix_of(m, me_ref, goal_ref, slots_ref), 0, k)
-
-    def skv_map(k, m, me_ref, goal_ref, slots_ref, len_ref):
-        return (suffix_of(m, me_ref, goal_ref, slots_ref), 0, 0, k)
-
-    def pkv_map(k, m, me_ref, goal_ref, slots_ref, len_ref):
-        return (0, 0, 0, k)
+    def q_map(m, me_ref, goal_ref, slots_ref, len_ref):
+        return (suffix_of(m, me_ref, goal_ref, slots_ref), 0, 0)
+
+    def skv_map(m, me_ref, goal_ref, slots_ref, len_ref):
+        return (suffix_of(m, me_ref, goal_ref, slots_ref), 0, 0, 0)
+
+    def pkv_map(m, me_ref, goal_ref, slots_ref, len_ref):
+        return (0, 0, 0, 0)
 
     out_shape = (
         jax.ShapeDtypeStruct((suffix_count, seq, qwidth), jnp.bfloat16),
@@ -165,10 +176,10 @@
     )
     in_specs = [
         pl.BlockSpec(memory_space=pltpu.SMEM),
-        pl.BlockSpec((1, seq, qb), q_map),
-        pl.BlockSpec((1, seq, qb), q_map),
-        pl.BlockSpec((1, 2, seq, HD), skv_map),
-        pl.BlockSpec((1, 2, prefix_rows, HD), pkv_map),
+        pl.BlockSpec((1, seq, qwidth), q_map),
+        pl.BlockSpec((1, seq, qwidth), q_map),
+        pl.BlockSpec((1, 2, seq, kv_width), skv_map),
+        pl.BlockSpec((1, 2, prefix_rows, kv_width), pkv_map),
     ]
     operands = [logratio, queries, out_grad, suffix_kv, prefix_one]
     aliases = {}
@@ -177,22 +188,22 @@
         operands += list(chain)
         aliases = {9: 0, 10: 1}
     if seed is not None:
-        in_specs.append(pl.BlockSpec((1, 2, prefix_rows, HD), pkv_map))
+        in_specs.append(pl.BlockSpec((1, 2, prefix_rows, kv_width), pkv_map))
         operands.append(seed)
     scratch = [pltpu.VMEM((prefix_rows + seq, group * seq), jnp.float32)]
     if low:
-        scratch.append(pltpu.VMEM((1, 2, prefix_rows, HD), jnp.float32))
+        scratch.append(pltpu.VMEM((1, 2, prefix_rows, kv_width), jnp.float32))
     kernel = functools.partial(slot_kernel, group=group, seq=seq, prefix_rows=prefix_rows, flip=flip,
                                pair_count=pair_count, chained=chain is not None, seeded=seed is not None,
                                low=low)
     grid_spec = pltpu.PrefetchScalarGridSpec(
         num_scalar_prefetch=4,
-        grid=(kv_local, 2),
+        grid=(2,),
         in_specs=in_specs,
         out_specs=[
-            pl.BlockSpec((1, seq, qb), q_map),
-            pl.BlockSpec((1, 2, seq, HD), skv_map),
-            pl.BlockSpec((1, 2, prefix_rows, HD), pkv_map),
+            pl.BlockSpec((1, seq, qwidth), q_map),
+            pl.BlockSpec((1, 2, seq, kv_width), skv_map),
+            pl.BlockSpec((1, 2, prefix_rows, kv_width), pkv_map),
         ],
         scratch_shapes=scratch,
     )
@@ -208,7 +219,7 @@
         out_shape=out_shape,
         input_output_aliases=aliases,
         cost_estimate=cost,
-        compiler_params=pltpu.CompilerParams(dimension_semantics=("arbitrary", "arbitrary")),
+        compiler_params=pltpu.CompilerParams(dimension_semantics=("arbitrary",)),
     )(me, goals, slots, lengths, *operands)
 
 

time: 50.3 us -> 49.9 us (level)
  waiting for transfers between devices: 9.95 us -> 5.36 us
  starting transfers between devices: 3.72 us -> 7.87 us
    ppermute x1, starting transfers between devices: 0.07 us -> 4.21 us  [pipelined(): total = own + lax.ppermute(forward, 'dp', across).astype(jnp.float32)]
    ppermute x1, waiting for transfers between devices: 4.4 us -> 1.4 us  [pipelined(): total = own + lax.ppermute(forward, 'dp', across).astype(jnp.float32)]
    ppermute x1, waiting for transfers between devices: 3.52 us -> 1.94 us  [pipelined(): pre_across = lax.ppermute(prefix_kv, 'dp', across)]
  transfers between devices with their start and end apart: 6 -> 6, of which waited for: 3 -> 3; matrix products, arithmetic and copies ran while one was open for 0% -> 0% of each run, Pallas kernels for 61% -> 62%
where the time goes in v11:
time: 49.9 us; the launch traced here: 50 us
  Pallas kernels  31.2 us (63%)
  starting transfers between devices  7.87 us (16%)
  waiting for transfers between devices  5.36 us (11%)
  local copies, waits for them, and re-layouts  2.72 us (5%)
  other arithmetic  2.14 us (4%)
  between operations  0.67 us (1%)
    pallas_call x4, Pallas kernels, attend_slot(): pl.pallas_call(kernel, grid_spec=grid_spec, out_shape=out_shape, input_ou...  31.2 us
    ppermute x1, starting transfers between devices, pipelined(): total = own + lax.ppermute(forward, 'dp', across).astype(jnp.float32)  4.21 us
    unnamed x10, local copies, waits for them, and re-layouts  2.72 us
    ppermute x1, starting transfers between devices, pipelined(): pre_across = lax.ppermute(prefix_kv, 'dp', across)  2.58 us
    convert_element_type x1, other arithmetic, pipelined(): return (chain[0], chain[1], total.astype(jnp.bfloat16))  2.04 us
    ppermute x1, waiting for transfers between devices, pipelined(): lax.ppermute(relay, 'dp', partner).astype(jnp.float32)  2.01 us
    ppermute x1, waiting for transfers between devices, pipelined(): pre_across = lax.ppermute(prefix_kv, 'dp', across)  1.94 us
    ppermute x1, waiting for transfers between devices, pipelined(): total = own + lax.ppermute(forward, 'dp', across).astype(jnp.float32)  1.4 us
  transfers between devices with their start and end apart: 6, of which 3 were waited for; matrix products, arithmetic and copies ran while one was open for 0% of the time, Pallas kernels for 62%

profile of v11, /device:TPU:0, one launch (start us, length us, event | category | flops | bytes accessed | tf_op | source)
XLA Modules:
  0.0 50.0 jit_solution(15065392613564427012)
XLA Ops:
  0.6 0.6 %collective-permute-start.1 = (bf16[1,2,448,256]{3,2,1,0:T(8,128)(2,1)}, bf16[1,2,448,256]{3,2,1,0:T(8,128)(2,1)S(1)}, u32[]{:S(2)}, u32[]{:S(2)}) collective-permute-start(bf16[1,2,448,256]{3,2,1,0:T(8,128)(2,1)} %pkv_ref), channel_id=1, source_target_pairs={{0,4},{4,0},{8,12},{12,8},{1,5},{5,1},{9,13},{13,9},{2,6},{6,2},{1... | collective-permute-start | bytes 1376264 | tf_op jit(solution)/shard_map/ppermute | solution.py:323
  1.2 2.6 %collective-permute-start = (bf16[1,2,448,256]{3,2,1,0:T(8,128)(2,1)}, bf16[1,2,448,256]{3,2,1,0:T(8,128)(2,1)S(1)}, u32[]{:S(2)}, u32[]{:S(2)}) collective-permute-start(bf16[1,2,448,256]{3,2,1,0:T(8,128)(2,1)} %pkv_ref), channel_id=1, source_target_pairs={{0,8},{4,12},{8,0},{12,4},{1,9},{5,13},{9,1},{13,5},{2,10},{6,14},... | collective-permute-start | bytes 1376264 | tf_op jit(solution)/shard_map/ppermute | solution.py:322
  3.8 0.0 collective-permute-done.1.pkv_ref
  3.8 0.0 copy-start.3
  3.8 0.8 %copy-done.3 = bf16[1,2,448,256]{3,2,1,0:T(8,128)(2,1)} copy-done((bf16[1,2,448,256]{3,2,1,0:T(8,128)(2,1)}, bf16[1,2,448,256]{3,2,1,0:T(8,128)(2,1)S(1)}, u32[]{:S(2)}) %copy-start.3) | copy-done | bytes 458776
  4.5 8.6 %shard_map.103 = (bf16[8,64,2048]{2,1,0:T(8,128)(2,1)}, bf16[8,2,64,256]{3,2,1,0:T(8,128)(2,1)}, f32[1,2,448,256]{3,2,1,0:T(8,128)}) custom-call(s32[1]{0:T(128)} %bitcast.me_ref, s32[4]{0:T(128)} %bitcast.7, s32[2,4]{1,0:T(2,128)} %bitcast.3, s32[4]{0:T(128)} %len_ref.7, f32[8]{0:T(128)} %lr_ref.7, bf16[8,64,2048]{2,1,0:T(8,128)(2,1)} %q_ref.7, ...), custom_call_target="tpu_custom_call" | custom-call | flops 8800000000 | bytes 5111808 | tf_op jit(solution)/shard_map/pallas_call | solution.py:216
  13.1 1.9 %collective-permute-done.pkv_ref = bf16[1,2,448,256]{3,2,1,0:T(8,128)(2,1)S(1)} collective-permute-done((bf16[1,2,448,256]{3,2,1,0:T(8,128)(2,1)}, bf16[1,2,448,256]{3,2,1,0:T(8,128)(2,1)S(1)}, u32[]{:S(2)}, u32[]{:S(2)}) %collective-permute-start) | collective-permute-done | bytes 458784 | tf_op jit(solution)/shard_map/ppermute | solution.py:322
  15.1 0.0 copy-start.2
  15.1 0.0 collective-permute-start.2
  15.1 0.5 %collective-permute-start.4 = (f32[1,2,448,256]{3,2,1,0:T(8,128)}, f32[1,2,448,256]{3,2,1,0:T(8,128)S(1)}, u32[]{:S(2)}, u32[]{:S(2)}) collective-permute-start(f32[1,2,448,256]{3,2,1,0:T(8,128)} %get-tuple-element.30), channel_id=1, source_target_pairs={{0,4},{4,0},{8,12},{12,8},{1,5},{5,1},{9,13},{13,9},{2,6},{6,2},{1... | collective-permute-start | bytes 2752520 | tf_op jit(solution)/shard_map/ppermute | solution.py:336
  15.6 0.3 copy-done.2
  15.9 7.0 %shard_map.104 = (bf16[8,64,2048]{2,1,0:T(8,128)(2,1)}, bf16[8,2,64,256]{3,2,1,0:T(8,128)(2,1)}, f32[1,2,448,256]{3,2,1,0:T(8,128)}) custom-call(s32[1]{0:T(128)} %bitcast.me_ref, s32[4]{0:T(128)} %bitcast.8, s32[2,4]{1,0:T(2,128)} %bitcast.4, s32[4]{0:T(128)} %len_ref.7, f32[8]{0:T(128)} %lr_ref.7, ...), custom_call_target="tpu_custom_call", output_to_operand_aliasing={{0}: (9, {}), {1}: (10, {})} | custom-call | flops 8800000000 | bytes 5111808 | tf_op jit(solution)/shard_map/pallas_call | solution.py:216
  22.9 0.0 collective-permute-done.2.pkv_ref
  22.9 0.0 copy-start.4
  22.9 0.8 %copy-done.4 = bf16[1,2,448,256]{3,2,1,0:T(8,128)(2,1)} copy-done((bf16[1,2,448,256]{3,2,1,0:T(8,128)(2,1)}, bf16[1,2,448,256]{3,2,1,0:T(8,128)(2,1)S(1)}, u32[]{:S(2)}) %copy-start.4) | copy-done | bytes 458776
  23.7 0.0 copy-start
  23.7 7.1 %shard_map.105 = (bf16[8,64,2048]{2,1,0:T(8,128)(2,1)}, bf16[8,2,64,256]{3,2,1,0:T(8,128)(2,1)}, bf16[1,2,448,256]{3,2,1,0:T(8,128)(2,1)}) custom-call(s32[1]{0:T(128)} %bitcast.me_ref, s32[4]{0:T(128)} %bitcast.9, s32[2,4]{1,0:T(2,128)} %bitcast.5, s32[4]{0:T(128)} %len_ref.7, f32[8]{0:T(128)} %lr_ref.7, ...), custom_call_target="tpu_custom_call", output_to_operand_aliasing={{0}: (9, {}), {1}: (10, {})} | custom-call | flops 8800000000 | bytes 5111808 | tf_op jit(solution)/shard_map/pallas_call | solution.py:216
  30.8 0.0 collective-permute-start.3
  30.8 2.0 %collective-permute-done.3 = bf16[1,2,448,256]{3,2,1,0:T(8,128)(2,1)S(1)} collective-permute-done((bf16[1,2,448,256]{3,2,1,0:T(8,128)(2,1)}, bf16[1,2,448,256]{3,2,1,0:T(8,128)(2,1)S(1)}, u32[]{:S(2)}, u32[]{:S(2)}) %collective-permute-start.3) | collective-permute-done | bytes 458784 | tf_op jit(solution)/shard_map/ppermute | solution.py:339
  32.8 0.0 copy-done
  32.8 0.1 add_convert_fusion.1
  32.9 4.2 %collective-permute-start.5 = (bf16[1,2,448,256]{3,2,1,0:T(8,128)(2,1)S(1)}, bf16[1,2,448,256]{3,2,1,0:T(8,128)(2,1)S(1)}, u32[]{:S(2)}, u32[]{:S(2)}) collective-permute-start(bf16[1,2,448,256]{3,2,1,0:T(8,128)(2,1)S(1)} %add_convert_fusion.1), channel_id=1, source_target_pairs={{0,8},{4,12},{8,0},{12,4},{1,9},{5,13},{9,1},{13,5},{2,10},{6,14},... | collective-permute-start | bytes 1376264 | tf_op jit(solution)/shard_map/ppermute | solution.py:342
  37.1 0.0 collective-permute-done.4.rest_2_
  37.1 0.0 copy-start.1
  37.1 0.9 %copy-done.1 = f32[1,2,448,256]{3,2,1,0:T(8,128)} copy-done((f32[1,2,448,256]{3,2,1,0:T(8,128)}, f32[1,2,448,256]{3,2,1,0:T(8,128)S(1)}, u32[]{:S(2)}) %copy-start.1) | copy-done | bytes 917528
  38.1 8.5 %shard_map.106 = (bf16[8,64,2048]{2,1,0:T(8,128)(2,1)}, bf16[8,2,64,256]{3,2,1,0:T(8,128)(2,1)}, f32[1,2,448,256]{3,2,1,0:T(8,128)}) custom-call(s32[1]{0:T(128)} %bitcast.me_ref, s32[4]{0:T(128)} %bitcast.10, s32[2,4]{1,0:T(2,128)} %bitcast.6, s32[4]{0:T(128)} %len_ref.7, f32[8]{0:T(128)} %lr_ref.7, ...), custom_call_target="tpu_custom_call", output_to_operand_aliasing={{0}: (9, {}), {1}: (10, {})} | custom-call | flops 8800000000 | bytes 5111808 | tf_op jit(solution)/shard_map/pallas_call | solution.py:216
  46.5 1.4 %collective-permute-done.5 = bf16[1,2,448,256]{3,2,1,0:T(8,128)(2,1)S(1)} collective-permute-done((bf16[1,2,448,256]{3,2,1,0:T(8,128)(2,1)S(1)}, bf16[1,2,448,256]{3,2,1,0:T(8,128)(2,1)S(1)}, u32[]{:S(2)}, u32[]{:S(2)}) %collective-permute-start.5) | collective-permute-done | bytes 458784 | tf_op jit(solution)/shard_map/ppermute | solution.py:342
  47.9 2.0 %add_convert_fusion = bf16[1,2,448,256]{3,2,1,0:T(8,128)(2,1)} fusion(f32[1,2,448,256]{3,2,1,0:T(8,128)} %get-tuple-element.33, bf16[1,2,448,256]{3,2,1,0:T(8,128)(2,1)S(1)} %collective-permute-done.5), kind=kLoop, calls=%fused_computation | loop fusion | flops 688128 | bytes 1835008 | tf_op jit(solution)/shard_map/convert_element_type | solution.py:343
Async XLA Ops:
  0.6 3.1 %collective-permute-start.1 = (bf16[1,2,448,256]{3,2,1,0:T(8,128)(2,1)}, bf16[1,2,448,256]{3,2,1,0:T(8,128)(2,1)S(1)}, u32[]{:S(2)}, u32[]{:S(2)}) collective-permute-start(bf16[1,2,448,256]{3,2,1,0:T(8,128)(2,1)} %pkv_ref), channel_id=1, source_target_pairs={{0,4},{4,0},{8,12},{12,8},{1,5},{5,1},{9,13},{13,9},{2,6},{6,2},{1... | collective-permute-start | bytes 1376264 | tf_op jit(solution)/shard_map/ppermute | solution.py:323
  1.2 13.9 %collective-permute-start = (bf16[1,2,448,256]{3,2,1,0:T(8,128)(2,1)}, bf16[1,2,448,256]{3,2,1,0:T(8,128)(2,1)S(1)}, u32[]{:S(2)}, u32[]{:S(2)}) collective-permute-start(bf16[1,2,448,256]{3,2,1,0:T(8,128)(2,1)} %pkv_ref), channel_id=1, source_target_pairs={{0,8},{4,12},{8,0},{12,4},{1,9},{5,13},{9,1},{13,5},{2,10},{6,14},... | collective-permute-start | bytes 1376264 | tf_op jit(solution)/shard_map/ppermute | solution.py:322
  3.8 0.8 %copy-start.3 = (bf16[1,2,448,256]{3,2,1,0:T(8,128)(2,1)}, bf16[1,2,448,256]{3,2,1,0:T(8,128)(2,1)S(1)}, u32[]{:S(2)}) copy-start(bf16[1,2,448,256]{3,2,1,0:T(8,128)(2,1)S(1)} %collective-permute-done.1.pkv_ref) | copy-start | bytes 1376260
  15.1 0.8 %copy-start.2 = (bf16[1,2,448,256]{3,2,1,0:T(8,128)(2,1)}, bf16[1,2,448,256]{3,2,1,0:T(8,128)(2,1)S(1)}, u32[]{:S(2)}) copy-start(bf16[1,2,448,256]{3,2,1,0:T(8,128)(2,1)S(1)} %collective-permute-done.pkv_ref) | copy-start | bytes 1376260
  15.1 7.8 %collective-permute-start.2 = (bf16[1,2,448,256]{3,2,1,0:T(8,128)(2,1)S(1)}, bf16[1,2,448,256]{3,2,1,0:T(8,128)(2,1)S(1)}, u32[]{:S(2)}, u32[]{:S(2)}) collective-permute-start(bf16[1,2,448,256]{3,2,1,0:T(8,128)(2,1)S(1)} %collective-permute-done.pkv_ref), channel_id=1, source_target_pairs={{0,4},{4,0},{8,12},{12,8},{1,5},{5,1},{9,13},{13,9},{2,6},{6,2},{1... | collective-permute-start | bytes 1376264 | tf_op jit(solution)/shard_map/ppermute | solution.py:335
  15.1 22.0 %collective-permute-start.4 = (f32[1,2,448,256]{3,2,1,0:T(8,128)}, f32[1,2,448,256]{3,2,1,0:T(8,128)S(1)}, u32[]{:S(2)}, u32[]{:S(2)}) collective-permute-start(f32[1,2,448,256]{3,2,1,0:T(8,128)} %get-tuple-element.30), channel_id=1, source_target_pairs={{0,4},{4,0},{8,12},{12,8},{1,5},{5,1},{9,13},{13,9},{2,6},{6,2},{1... | collective-permute-start | bytes 2752520 | tf_op jit(solution)/shard_map/ppermute | solution.py:336
  22.9 0.8 %copy-start.4 = (bf16[1,2,448,256]{3,2,1,0:T(8,128)(2,1)}, bf16[1,2,448,256]{3,2,1,0:T(8,128)(2,1)S(1)}, u32[]{:S(2)}) copy-start(bf16[1,2,448,256]{3,2,1,0:T(8,128)(2,1)S(1)} %collective-permute-done.2.pkv_ref) | copy-start | bytes 1376260
  23.7 9.1 %copy-start = (f32[1,2,448,256]{3,2,1,0:T(8,128)S(1)}, f32[1,2,448,256]{3,2,1,0:T(8,128)}, u32[]{:S(2)}) copy-start(f32[1,2,448,256]{3,2,1,0:T(8,128)} %get-tuple-element.23) | copy-start | bytes 2752516
  30.8 2.0 %collective-permute-start.3 = (bf16[1,2,448,256]{3,2,1,0:T(8,128)(2,1)}, bf16[1,2,448,256]{3,2,1,0:T(8,128)(2,1)S(1)}, u32[]{:S(2)}, u32[]{:S(2)}) collective-permute-start(bf16[1,2,448,256]{3,2,1,0:T(8,128)(2,1)} %get-tuple-element.26), channel_id=1, source_target_pairs={{0,4},{4,0},{8,12},{12,8},{1,5},{5,1},{9,13},{13,9},{2,6},{6,2},{1... | collective-permute-start | bytes 1376264 | tf_op jit(solution)/shard_map/ppermute | solution.py:339
  32.9 15.0 %collective-permute-start.5 = (bf16[1,2,448,256]{3,2,1,0:T(8,128)(2,1)S(1)}, bf16[1,2,448,256]{3,2,1,0:T(8,128)(2,1)S(1)}, u32[]{:S(2)}, u32[]{:S(2)}) collective-permute-start(bf16[1,2,448,256]{3,2,1,0:T(8,128)(2,1)S(1)} %add_convert_fusion.1), channel_id=1, source_target_pairs={{0,8},{4,12},{8,0},{12,4},{1,9},{5,13},{9,1},{13,5},{2,10},{6,14},... | collective-permute-start | bytes 1376264 | tf_op jit(solution)/shard_map/ppermute | solution.py:342
  37.1 0.9 %copy-start.1 = (f32[1,2,448,256]{3,2,1,0:T(8,128)}, f32[1,2,448,256]{3,2,1,0:T(8,128)S(1)}, u32[]{:S(2)}) copy-start(f32[1,2,448,256]{3,2,1,0:T(8,128)S(1)} %collective-permute-done.4.rest_2_) | copy-start | bytes 2752516

commit v12 on v11

--- a/solution.py
+++ b/solution.py
@@ -139,7 +139,7 @@
     if seeded:
         @pl.when(member == 1)
         def _():
-            dpre_ref[...] += seed_ref[...]
+            acc_ref[...] += seed_ref[...]
     if low:
         @pl.when(member == 1)
         def _():
@@ -338,8 +338,8 @@
     chain, relay = run(3, pre_relay, chain, low=True)
     forward = (cross + lax.ppermute(relay, "dp", partner).astype(jnp.float32)).astype(jnp.bfloat16)
     forward, own_prefix = lax.optimization_barrier((forward, prefix_kv))
-    chain, own = run(0, own_prefix, chain, seed=near_sent)
-    total = own + lax.ppermute(forward, "dp", across).astype(jnp.float32)
+    chain, own = run(0, own_prefix, chain, seed=near_sent, low=True)
+    total = own.astype(jnp.float32) + lax.ppermute(forward, "dp", across).astype(jnp.float32)
     return chain[0], chain[1], total.astype(jnp.bfloat16)
 
 

time: 49.9 us -> 49.3 us (0.988)
  waiting for transfers between devices: 5.36 us -> 9.43 us
  starting transfers between devices: 7.87 us -> 3.92 us
  Pallas kernels: 31.2 us -> 30.3 us
    ppermute x1, starting transfers between devices: 4.21 us -> 0.26 us  [pipelined(): lax.ppermute(forward, 'dp', across).astype(jnp.float32)]
    ppermute x1, waiting for transfers between devices: 1.4 us -> 3.9 us  [pipelined(): lax.ppermute(forward, 'dp', across).astype(jnp.float32)]
    ppermute x1, waiting for transfers between devices: 1.94 us -> 3.5 us  [pipelined(): pre_across = lax.ppermute(prefix_kv, 'dp', across)]
    pallas_call x4, Pallas kernels: 31.2 us -> 30.3 us  [attend_slot(): pl.pallas_call(kernel, grid_spec=grid_spec, out_shape=out_shape, input_ou...]
where the time goes in v12:
time: 49.3 us; the launch traced here: 49 us
  Pallas kernels  30.3 us (61%)
  waiting for transfers between devices  9.43 us (19%)
  starting transfers between devices  3.92 us (8%)
  local copies, waits for them, and re-layouts  2.72 us (6%)
  other arithmetic  2 us (4%)
  between operations  0.67 us (1%)
    pallas_call x4, Pallas kernels, attend_slot(): pl.pallas_call(kernel, grid_spec=grid_spec, out_shape=out_shape, input_ou...  30.3 us
    ppermute x1, waiting for transfers between devices, pipelined(): lax.ppermute(forward, 'dp', across).astype(jnp.float32)  3.9 us
    ppermute x1, waiting for transfers between devices, pipelined(): pre_across = lax.ppermute(prefix_kv, 'dp', across)  3.5 us
    unnamed x10, local copies, waits for them, and re-layouts  2.72 us
    ppermute x1, starting transfers between devices, pipelined(): pre_across = lax.ppermute(prefix_kv, 'dp', across)  2.58 us
    ppermute x1, waiting for transfers between devices, pipelined(): lax.ppermute(relay, 'dp', partner).astype(jnp.float32)  2.01 us
    convert_element_type x1, other arithmetic, pipelined(): return (chain[0], chain[1], total.astype(jnp.bfloat16))  1.9 us
  transfers between devices with their start and end apart: 6, of which 3 were waited for; matrix products, arithmetic and copies ran while one was open for 0% of the time, Pallas kernels for 62%

profile of v12, /device:TPU:0, one launch (start us, length us, event | category | flops | bytes accessed | tf_op | source)
XLA Modules:
  0.0 49.0 jit_solution(1003848615595509930)
XLA Ops:
  0.6 0.6 %collective-permute-start.1 = (bf16[1,2,448,256]{3,2,1,0:T(8,128)(2,1)}, bf16[1,2,448,256]{3,2,1,0:T(8,128)(2,1)S(1)}, u32[]{:S(2)}, u32[]{:S(2)}) collective-permute-start(bf16[1,2,448,256]{3,2,1,0:T(8,128)(2,1)} %pkv_ref), channel_id=1, source_target_pairs={{0,4},{4,0},{8,12},{12,8},{1,5},{5,1},{9,13},{13,9},{2,6},{6,2},{1... | collective-permute-start | bytes 1376264 | tf_op jit(solution)/shard_map/ppermute | solution.py:323
  1.2 2.6 %collective-permute-start = (bf16[1,2,448,256]{3,2,1,0:T(8,128)(2,1)}, bf16[1,2,448,256]{3,2,1,0:T(8,128)(2,1)S(1)}, u32[]{:S(2)}, u32[]{:S(2)}) collective-permute-start(bf16[1,2,448,256]{3,2,1,0:T(8,128)(2,1)} %pkv_ref), channel_id=1, source_target_pairs={{0,8},{4,12},{8,0},{12,4},{1,9},{5,13},{9,1},{13,5},{2,10},{6,14},... | collective-permute-start | bytes 1376264 | tf_op jit(solution)/shard_map/ppermute | solution.py:322
  3.8 0.0 collective-permute-done.1.pkv_ref
  3.8 0.0 copy-start.3
  3.8 0.8 %copy-done.3 = bf16[1,2,448,256]{3,2,1,0:T(8,128)(2,1)} copy-done((bf16[1,2,448,256]{3,2,1,0:T(8,128)(2,1)}, bf16[1,2,448,256]{3,2,1,0:T(8,128)(2,1)S(1)}, u32[]{:S(2)}) %copy-start.3) | copy-done | bytes 458776
  4.5 7.0 %shard_map.103 = (bf16[8,64,2048]{2,1,0:T(8,128)(2,1)}, bf16[8,2,64,256]{3,2,1,0:T(8,128)(2,1)}, f32[1,2,448,256]{3,2,1,0:T(8,128)}) custom-call(s32[1]{0:T(128)} %bitcast.me_ref, s32[4]{0:T(128)} %bitcast.7, s32[2,4]{1,0:T(2,128)} %bitcast.3, s32[4]{0:T(128)} %len_ref.7, f32[8]{0:T(128)} %lr_ref.7, bf16[8,64,2048]{2,1,0:T(8,128)(2,1)} %q_ref.7, ...), custom_call_target="tpu_custom_call" | custom-call | flops 8800000000 | bytes 5111808 | tf_op jit(solution)/shard_map/pallas_call | solution.py:216
  11.6 3.5 %collective-permute-done.pkv_ref = bf16[1,2,448,256]{3,2,1,0:T(8,128)(2,1)S(1)} collective-permute-done((bf16[1,2,448,256]{3,2,1,0:T(8,128)(2,1)}, bf16[1,2,448,256]{3,2,1,0:T(8,128)(2,1)S(1)}, u32[]{:S(2)}, u32[]{:S(2)}) %collective-permute-start) | collective-permute-done | bytes 458784 | tf_op jit(solution)/shard_map/ppermute | solution.py:322
  15.1 0.0 copy-start.2
  15.1 0.0 collective-permute-start.2
  15.1 0.5 %collective-permute-start.4 = (f32[1,2,448,256]{3,2,1,0:T(8,128)}, f32[1,2,448,256]{3,2,1,0:T(8,128)S(1)}, u32[]{:S(2)}, u32[]{:S(2)}) collective-permute-start(f32[1,2,448,256]{3,2,1,0:T(8,128)} %get-tuple-element.30), channel_id=1, source_target_pairs={{0,4},{4,0},{8,12},{12,8},{1,5},{5,1},{9,13},{13,9},{2,6},{6,2},{1... | collective-permute-start | bytes 2752520 | tf_op jit(solution)/shard_map/ppermute | solution.py:336
  15.6 0.3 copy-done.2
  15.9 7.0 %shard_map.104 = (bf16[8,64,2048]{2,1,0:T(8,128)(2,1)}, bf16[8,2,64,256]{3,2,1,0:T(8,128)(2,1)}, f32[1,2,448,256]{3,2,1,0:T(8,128)}) custom-call(s32[1]{0:T(128)} %bitcast.me_ref, s32[4]{0:T(128)} %bitcast.8, s32[2,4]{1,0:T(2,128)} %bitcast.4, s32[4]{0:T(128)} %len_ref.7, f32[8]{0:T(128)} %lr_ref.7, ...), custom_call_target="tpu_custom_call", output_to_operand_aliasing={{0}: (9, {}), {1}: (10, {})} | custom-call | flops 8800000000 | bytes 5111808 | tf_op jit(solution)/shard_map/pallas_call | solution.py:216
  22.9 0.0 collective-permute-done.2.pkv_ref
  22.9 0.0 copy-start.4
  22.9 0.8 %copy-done.4 = bf16[1,2,448,256]{3,2,1,0:T(8,128)(2,1)} copy-done((bf16[1,2,448,256]{3,2,1,0:T(8,128)(2,1)}, bf16[1,2,448,256]{3,2,1,0:T(8,128)(2,1)S(1)}, u32[]{:S(2)}) %copy-start.4) | copy-done | bytes 458776
  23.7 0.0 copy-start
  23.7 8.6 %shard_map.105 = (bf16[8,64,2048]{2,1,0:T(8,128)(2,1)}, bf16[8,2,64,256]{3,2,1,0:T(8,128)(2,1)}, bf16[1,2,448,256]{3,2,1,0:T(8,128)(2,1)}) custom-call(s32[1]{0:T(128)} %bitcast.me_ref, s32[4]{0:T(128)} %bitcast.9, s32[2,4]{1,0:T(2,128)} %bitcast.5, s32[4]{0:T(128)} %len_ref.7, f32[8]{0:T(128)} %lr_ref.7, ...), custom_call_target="tpu_custom_call", output_to_operand_aliasing={{0}: (9, {}), {1}: (10, {})} | custom-call | flops 8800000000 | bytes 5111808 | tf_op jit(solution)/shard_map/pallas_call | solution.py:216
  32.3 0.0 collective-permute-start.3
  32.3 2.0 %collective-permute-done.3 = bf16[1,2,448,256]{3,2,1,0:T(8,128)(2,1)S(1)} collective-permute-done((bf16[1,2,448,256]{3,2,1,0:T(8,128)(2,1)}, bf16[1,2,448,256]{3,2,1,0:T(8,128)(2,1)S(1)}, u32[]{:S(2)}, u32[]{:S(2)}) %collective-permute-start.3) | collective-permute-done | bytes 458784 | tf_op jit(solution)/shard_map/ppermute | solution.py:339
  34.4 0.0 copy-done
  34.4 0.1 add_convert_fusion.1
  34.5 0.3 collective-permute-start.5
  34.7 0.0 collective-permute-done.4.rest_2_
  34.7 0.0 copy-start.1
  34.7 0.9 %copy-done.1 = f32[1,2,448,256]{3,2,1,0:T(8,128)} copy-done((f32[1,2,448,256]{3,2,1,0:T(8,128)}, f32[1,2,448,256]{3,2,1,0:T(8,128)S(1)}, u32[]{:S(2)}) %copy-start.1) | copy-done | bytes 917528
  35.7 7.5 %shard_map.106 = (bf16[8,64,2048]{2,1,0:T(8,128)(2,1)}, bf16[8,2,64,256]{3,2,1,0:T(8,128)(2,1)}, bf16[1,2,448,256]{3,2,1,0:T(8,128)(2,1)}) custom-call(s32[1]{0:T(128)} %bitcast.me_ref, s32[4]{0:T(128)} %bitcast.10, s32[2,4]{1,0:T(2,128)} %bitcast.6, s32[4]{0:T(128)} %len_ref.7, f32[8]{0:T(128)} %lr_ref.7, ...), custom_call_target="tpu_custom_call", output_to_operand_aliasing={{0}: (9, {}), {1}: (10, {})} | custom-call | flops 8800000000 | bytes 5111808 | tf_op jit(solution)/shard_map/pallas_call | solution.py:216
  43.2 3.9 %collective-permute-done.5 = bf16[1,2,448,256]{3,2,1,0:T(8,128)(2,1)S(1)} collective-permute-done((bf16[1,2,448,256]{3,2,1,0:T(8,128)(2,1)S(1)}, bf16[1,2,448,256]{3,2,1,0:T(8,128)(2,1)S(1)}, u32[]{:S(2)}, u32[]{:S(2)}) %collective-permute-start.5) | collective-permute-done | bytes 458784 | tf_op jit(solution)/shard_map/ppermute | solution.py:342
  47.1 1.9 %add_convert_fusion = bf16[1,2,448,256]{3,2,1,0:T(8,128)(2,1)} fusion(bf16[1,2,448,256]{3,2,1,0:T(8,128)(2,1)S(1)} %collective-permute-done.5, bf16[1,2,448,256]{3,2,1,0:T(8,128)(2,1)} %get-tuple-element.33), kind=kLoop, calls=%fused_computation | loop fusion | flops 917504 | bytes 1376256 | tf_op jit(solution)/shard_map/convert_element_type | solution.py:343
Async XLA Ops:
  0.6 3.1 %collective-permute-start.1 = (bf16[1,2,448,256]{3,2,1,0:T(8,128)(2,1)}, bf16[1,2,448,256]{3,2,1,0:T(8,128)(2,1)S(1)}, u32[]{:S(2)}, u32[]{:S(2)}) collective-permute-start(bf16[1,2,448,256]{3,2,1,0:T(8,128)(2,1)} %pkv_ref), channel_id=1, source_target_pairs={{0,4},{4,0},{8,12},{12,8},{1,5},{5,1},{9,13},{13,9},{2,6},{6,2},{1... | collective-permute-start | bytes 1376264 | tf_op jit(solution)/shard_map/ppermute | solution.py:323
  1.2 13.9 %collective-permute-start = (bf16[1,2,448,256]{3,2,1,0:T(8,128)(2,1)}, bf16[1,2,448,256]{3,2,1,0:T(8,128)(2,1)S(1)}, u32[]{:S(2)}, u32[]{:S(2)}) collective-permute-start(bf16[1,2,448,256]{3,2,1,0:T(8,128)(2,1)} %pkv_ref), channel_id=1, source_target_pairs={{0,8},{4,12},{8,0},{12,4},{1,9},{5,13},{9,1},{13,5},{2,10},{6,14},... | collective-permute-start | bytes 1376264 | tf_op jit(solution)/shard_map/ppermute | solution.py:322
  3.8 0.8 %copy-start.3 = (bf16[1,2,448,256]{3,2,1,0:T(8,128)(2,1)}, bf16[1,2,448,256]{3,2,1,0:T(8,128)(2,1)S(1)}, u32[]{:S(2)}) copy-start(bf16[1,2,448,256]{3,2,1,0:T(8,128)(2,1)S(1)} %collective-permute-done.1.pkv_ref) | copy-start | bytes 1376260
  15.1 0.8 %copy-start.2 = (bf16[1,2,448,256]{3,2,1,0:T(8,128)(2,1)}, bf16[1,2,448,256]{3,2,1,0:T(8,128)(2,1)S(1)}, u32[]{:S(2)}) copy-start(bf16[1,2,448,256]{3,2,1,0:T(8,128)(2,1)S(1)} %collective-permute-done.pkv_ref) | copy-start | bytes 1376260
  15.1 7.8 %collective-permute-start.2 = (bf16[1,2,448,256]{3,2,1,0:T(8,128)(2,1)S(1)}, bf16[1,2,448,256]{3,2,1,0:T(8,128)(2,1)S(1)}, u32[]{:S(2)}, u32[]{:S(2)}) collective-permute-start(bf16[1,2,448,256]{3,2,1,0:T(8,128)(2,1)S(1)} %collective-permute-done.pkv_ref), channel_id=1, source_target_pairs={{0,4},{4,0},{8,12},{12,8},{1,5},{5,1},{9,13},{13,9},{2,6},{6,2},{1... | collective-permute-start | bytes 1376264 | tf_op jit(solution)/shard_map/ppermute | solution.py:335
  15.1 19.6 %collective-permute-start.4 = (f32[1,2,448,256]{3,2,1,0:T(8,128)}, f32[1,2,448,256]{3,2,1,0:T(8,128)S(1)}, u32[]{:S(2)}, u32[]{:S(2)}) collective-permute-start(f32[1,2,448,256]{3,2,1,0:T(8,128)} %get-tuple-element.30), channel_id=1, source_target_pairs={{0,4},{4,0},{8,12},{12,8},{1,5},{5,1},{9,13},{13,9},{2,6},{6,2},{1... | collective-permute-start | bytes 2752520 | tf_op jit(solution)/shard_map/ppermute | solution.py:336
  22.9 0.8 %copy-start.4 = (bf16[1,2,448,256]{3,2,1,0:T(8,128)(2,1)}, bf16[1,2,448,256]{3,2,1,0:T(8,128)(2,1)S(1)}, u32[]{:S(2)}) copy-start(bf16[1,2,448,256]{3,2,1,0:T(8,128)(2,1)S(1)} %collective-permute-done.2.pkv_ref) | copy-start | bytes 1376260
  23.7 10.7 %copy-start = (f32[1,2,448,256]{3,2,1,0:T(8,128)S(1)}, f32[1,2,448,256]{3,2,1,0:T(8,128)}, u32[]{:S(2)}) copy-start(f32[1,2,448,256]{3,2,1,0:T(8,128)} %get-tuple-element.23) | copy-start | bytes 2752516
  32.3 2.0 %collective-permute-start.3 = (bf16[1,2,448,256]{3,2,1,0:T(8,128)(2,1)}, bf16[1,2,448,256]{3,2,1,0:T(8,128)(2,1)S(1)}, u32[]{:S(2)}, u32[]{:S(2)}) collective-permute-start(bf16[1,2,448,256]{3,2,1,0:T(8,128)(2,1)} %get-tuple-element.26), channel_id=1, source_target_pairs={{0,4},{4,0},{8,12},{12,8},{1,5},{5,1},{9,13},{13,9},{2,6},{6,2},{1... | collective-permute-start | bytes 1376264 | tf_op jit(solution)/shard_map/ppermute | solution.py:339
  34.5 12.6 %collective-permute-start.5 = (bf16[1,2,448,256]{3,2,1,0:T(8,128)(2,1)S(1)}, bf16[1,2,448,256]{3,2,1,0:T(8,128)(2,1)S(1)}, u32[]{:S(2)}, u32[]{:S(2)}) collective-permute-start(bf16[1,2,448,256]{3,2,1,0:T(8,128)(2,1)S(1)} %add_convert_fusion.1), channel_id=1, source_target_pairs={{0,8},{4,12},{8,0},{12,4},{1,9},{5,13},{9,1},{13,5},{2,10},{6,14},... | collective-permute-start | bytes 1376264 | tf_op jit(solution)/shard_map/ppermute | solution.py:342
  34.7 0.9 %copy-start.1 = (f32[1,2,448,256]{3,2,1,0:T(8,128)}, f32[1,2,448,256]{3,2,1,0:T(8,128)S(1)}, u32[]{:S(2)}) copy-start(f32[1,2,448,256]{3,2,1,0:T(8,128)S(1)} %collective-permute-done.4.rest_2_) | copy-start | bytes 2752516

commit v13 on v11

--- a/solution.py
+++ b/solution.py
@@ -118,15 +118,15 @@
     x = jnp.full((1, 128), -dpo_beta * gap, jnp.float32)
     weight = dpo_beta * (1.0 / (1.0 + jnp.exp(-x)))
     coef = jnp.where(member == 0, -weight, weight)[:, :1]
-    blocks = (seq + length + 127) // 128
+    blocks = (length + 63) // 64
 
     def one_head(h, carry):
         q_cols = pl.ds(pl.multiple_of(h * qb, qb), qb)
         kv_cols = pl.ds(pl.multiple_of(h * HD, HD), HD)
-        for used in range(1, (seq + prefix_rows + 127) // 128 + 1):
+        for used in range(1, (prefix_rows + 63) // 64 + 1):
             @pl.when(blocks == used)
             def _():
-                width = min(used * 128, seq + prefix_rows)
+                width = min(seq + used * 64, seq + prefix_rows)
                 grads = attend_math(q_ref[0, :, q_cols], og_ref[0, :, q_cols],
                                     pkv_ref[0, 0, :width - seq, kv_cols], pkv_ref[0, 1, :width - seq, kv_cols],
                                     skv_ref[0, 0, :, kv_cols], skv_ref[0, 1, :, kv_cols], bias_ref[:width], coef,

time: 49.9 us -> 50.2 us (level); the launches traced: 50 us -> 49.3 us
  starting transfers between devices: 7.87 us -> 4.44 us
  waiting for transfers between devices: 5.36 us -> 8.41 us
    ppermute x1, starting transfers between devices: 4.21 us -> 0.78 us  [pipelined(): total = own + lax.ppermute(forward, 'dp', across).astype(jnp.float32)]
    ppermute x1, waiting for transfers between devices: 1.94 us -> 3.79 us  [pipelined(): pre_across = lax.ppermute(prefix_kv, 'dp', across)]
    ppermute x1, waiting for transfers between devices: 1.4 us -> 2.59 us  [pipelined(): total = own + lax.ppermute(forward, 'dp', across).astype(jnp.float32)]
  transfers between devices with their start and end apart: 6 -> 6, of which waited for: 3 -> 3; matrix products, arithmetic and copies ran while one was open for 0% -> 0% of each run, Pallas kernels for 62% -> 63%
where the time goes in v13:
time: 50.2 us; the launch traced here: 49.3 us
  Pallas kernels  30.9 us (62%)
  waiting for transfers between devices  8.41 us (17%)
  starting transfers between devices  4.44 us (9%)
  local copies, waits for them, and re-layouts  2.72 us (5%)
  other arithmetic  2.14 us (4%)
  between operations  0.67 us (1%)
    pallas_call x4, Pallas kernels, attend_slot(): pl.pallas_call(kernel, grid_spec=grid_spec, out_shape=out_shape, input_ou...  30.9 us
    ppermute x1, waiting for transfers between devices, pipelined(): pre_across = lax.ppermute(prefix_kv, 'dp', across)  3.79 us
    unnamed x10, local copies, waits for them, and re-layouts  2.72 us
    ppermute x1, waiting for transfers between devices, pipelined(): total = own + lax.ppermute(forward, 'dp', across).astype(jnp.float32)  2.59 us
    ppermute x1, starting transfers between devices, pipelined(): pre_across = lax.ppermute(prefix_kv, 'dp', across)  2.58 us
    convert_element_type x1, other arithmetic, pipelined(): return (chain[0], chain[1], total.astype(jnp.bfloat16))  2.04 us
    ppermute x1, waiting for transfers between devices, pipelined(): lax.ppermute(relay, 'dp', partner).astype(jnp.float32)  2.01 us
  transfers between devices with their start and end apart: 6, of which 3 were waited for; matrix products, arithmetic and copies ran while one was open for 0% of the time, Pallas kernels for 63%

profile of v13, /device:TPU:0, one launch (start us, length us, event | category | flops | bytes accessed | tf_op | source)
XLA Modules:
  0.0 49.3 jit_solution(13614443457592292534)
XLA Ops:
  0.6 0.6 %collective-permute-start.1 = (bf16[1,2,448,256]{3,2,1,0:T(8,128)(2,1)}, bf16[1,2,448,256]{3,2,1,0:T(8,128)(2,1)S(1)}, u32[]{:S(2)}, u32[]{:S(2)}) collective-permute-start(bf16[1,2,448,256]{3,2,1,0:T(8,128)(2,1)} %pkv_ref), channel_id=1, source_target_pairs={{0,4},{4,0},{8,12},{12,8},{1,5},{5,1},{9,13},{13,9},{2,6},{6,2},{1... | collective-permute-start | bytes 1376264 | tf_op jit(solution)/shard_map/ppermute | solution.py:323
  1.2 2.6 %collective-permute-start = (bf16[1,2,448,256]{3,2,1,0:T(8,128)(2,1)}, bf16[1,2,448,256]{3,2,1,0:T(8,128)(2,1)S(1)}, u32[]{:S(2)}, u32[]{:S(2)}) collective-permute-start(bf16[1,2,448,256]{3,2,1,0:T(8,128)(2,1)} %pkv_ref), channel_id=1, source_target_pairs={{0,8},{4,12},{8,0},{12,4},{1,9},{5,13},{9,1},{13,5},{2,10},{6,14},... | collective-permute-start | bytes 1376264 | tf_op jit(solution)/shard_map/ppermute | solution.py:322
  3.8 0.0 collective-permute-done.1.pkv_ref
  3.8 0.0 copy-start.3
  3.8 0.8 %copy-done.3 = bf16[1,2,448,256]{3,2,1,0:T(8,128)(2,1)} copy-done((bf16[1,2,448,256]{3,2,1,0:T(8,128)(2,1)}, bf16[1,2,448,256]{3,2,1,0:T(8,128)(2,1)S(1)}, u32[]{:S(2)}) %copy-start.3) | copy-done | bytes 458776
  4.5 6.8 %shard_map.103 = (bf16[8,64,2048]{2,1,0:T(8,128)(2,1)}, bf16[8,2,64,256]{3,2,1,0:T(8,128)(2,1)}, f32[1,2,448,256]{3,2,1,0:T(8,128)}) custom-call(s32[1]{0:T(128)} %bitcast.me_ref, s32[4]{0:T(128)} %bitcast.7, s32[2,4]{1,0:T(2,128)} %bitcast.3, s32[4]{0:T(128)} %len_ref.7, f32[8]{0:T(128)} %lr_ref.7, bf16[8,64,2048]{2,1,0:T(8,128)(2,1)} %q_ref.7, ...), custom_call_target="tpu_custom_call" | custom-call | flops 8800000000 | bytes 5111808 | tf_op jit(solution)/shard_map/pallas_call | solution.py:216
  11.3 3.8 %collective-permute-done.pkv_ref = bf16[1,2,448,256]{3,2,1,0:T(8,128)(2,1)S(1)} collective-permute-done((bf16[1,2,448,256]{3,2,1,0:T(8,128)(2,1)}, bf16[1,2,448,256]{3,2,1,0:T(8,128)(2,1)S(1)}, u32[]{:S(2)}, u32[]{:S(2)}) %collective-permute-start) | collective-permute-done | bytes 458784 | tf_op jit(solution)/shard_map/ppermute | solution.py:322
  15.1 0.0 copy-start.2
  15.1 0.0 collective-permute-start.2
  15.1 0.5 %collective-permute-start.4 = (f32[1,2,448,256]{3,2,1,0:T(8,128)}, f32[1,2,448,256]{3,2,1,0:T(8,128)S(1)}, u32[]{:S(2)}, u32[]{:S(2)}) collective-permute-start(f32[1,2,448,256]{3,2,1,0:T(8,128)} %get-tuple-element.30), channel_id=1, source_target_pairs={{0,4},{4,0},{8,12},{12,8},{1,5},{5,1},{9,13},{13,9},{2,6},{6,2},{1... | collective-permute-start | bytes 2752520 | tf_op jit(solution)/shard_map/ppermute | solution.py:336
  15.6 0.3 copy-done.2
  15.9 6.9 %shard_map.104 = (bf16[8,64,2048]{2,1,0:T(8,128)(2,1)}, bf16[8,2,64,256]{3,2,1,0:T(8,128)(2,1)}, f32[1,2,448,256]{3,2,1,0:T(8,128)}) custom-call(s32[1]{0:T(128)} %bitcast.me_ref, s32[4]{0:T(128)} %bitcast.8, s32[2,4]{1,0:T(2,128)} %bitcast.4, s32[4]{0:T(128)} %len_ref.7, f32[8]{0:T(128)} %lr_ref.7, ...), custom_call_target="tpu_custom_call", output_to_operand_aliasing={{0}: (9, {}), {1}: (10, {})} | custom-call | flops 8800000000 | bytes 5111808 | tf_op jit(solution)/shard_map/pallas_call | solution.py:216
  22.8 0.0 collective-permute-done.2.pkv_ref
  22.8 0.0 copy-start.4
  22.8 0.8 %copy-done.4 = bf16[1,2,448,256]{3,2,1,0:T(8,128)(2,1)} copy-done((bf16[1,2,448,256]{3,2,1,0:T(8,128)(2,1)}, bf16[1,2,448,256]{3,2,1,0:T(8,128)(2,1)S(1)}, u32[]{:S(2)}) %copy-start.4) | copy-done | bytes 458776
  23.6 0.0 copy-start
  23.6 8.9 %shard_map.105 = (bf16[8,64,2048]{2,1,0:T(8,128)(2,1)}, bf16[8,2,64,256]{3,2,1,0:T(8,128)(2,1)}, bf16[1,2,448,256]{3,2,1,0:T(8,128)(2,1)}) custom-call(s32[1]{0:T(128)} %bitcast.me_ref, s32[4]{0:T(128)} %bitcast.9, s32[2,4]{1,0:T(2,128)} %bitcast.5, s32[4]{0:T(128)} %len_ref.7, f32[8]{0:T(128)} %lr_ref.7, ...), custom_call_target="tpu_custom_call", output_to_operand_aliasing={{0}: (9, {}), {1}: (10, {})} | custom-call | flops 8800000000 | bytes 5111808 | tf_op jit(solution)/shard_map/pallas_call | solution.py:216
  32.5 0.0 collective-permute-start.3
  32.5 2.0 %collective-permute-done.3 = bf16[1,2,448,256]{3,2,1,0:T(8,128)(2,1)S(1)} collective-permute-done((bf16[1,2,448,256]{3,2,1,0:T(8,128)(2,1)}, bf16[1,2,448,256]{3,2,1,0:T(8,128)(2,1)S(1)}, u32[]{:S(2)}, u32[]{:S(2)}) %collective-permute-start.3) | collective-permute-done | bytes 458784 | tf_op jit(solution)/shard_map/ppermute | solution.py:339
  34.5 0.0 copy-done
  34.5 0.1 add_convert_fusion.1
  34.6 0.8 %collective-permute-start.5 = (bf16[1,2,448,256]{3,2,1,0:T(8,128)(2,1)S(1)}, bf16[1,2,448,256]{3,2,1,0:T(8,128)(2,1)S(1)}, u32[]{:S(2)}, u32[]{:S(2)}) collective-permute-start(bf16[1,2,448,256]{3,2,1,0:T(8,128)(2,1)S(1)} %add_convert_fusion.1), channel_id=1, source_target_pairs={{0,8},{4,12},{8,0},{12,4},{1,9},{5,13},{9,1},{13,5},{2,10},{6,14},... | collective-permute-start | bytes 1376264 | tf_op jit(solution)/shard_map/ppermute | solution.py:342
  35.4 0.0 collective-permute-done.4.rest_2_
  35.4 0.0 copy-start.1
  35.4 0.9 %copy-done.1 = f32[1,2,448,256]{3,2,1,0:T(8,128)} copy-done((f32[1,2,448,256]{3,2,1,0:T(8,128)}, f32[1,2,448,256]{3,2,1,0:T(8,128)S(1)}, u32[]{:S(2)}) %copy-start.1) | copy-done | bytes 917528
  36.4 8.3 %shard_map.106 = (bf16[8,64,2048]{2,1,0:T(8,128)(2,1)}, bf16[8,2,64,256]{3,2,1,0:T(8,128)(2,1)}, f32[1,2,448,256]{3,2,1,0:T(8,128)}) custom-call(s32[1]{0:T(128)} %bitcast.me_ref, s32[4]{0:T(128)} %bitcast.10, s32[2,4]{1,0:T(2,128)} %bitcast.6, s32[4]{0:T(128)} %len_ref.7, f32[8]{0:T(128)} %lr_ref.7, ...), custom_call_target="tpu_custom_call", output_to_operand_aliasing={{0}: (9, {}), {1}: (10, {})} | custom-call | flops 8800000000 | bytes 5111808 | tf_op jit(solution)/shard_map/pallas_call | solution.py:216
  44.7 2.6 %collective-permute-done.5 = bf16[1,2,448,256]{3,2,1,0:T(8,128)(2,1)S(1)} collective-permute-done((bf16[1,2,448,256]{3,2,1,0:T(8,128)(2,1)S(1)}, bf16[1,2,448,256]{3,2,1,0:T(8,128)(2,1)S(1)}, u32[]{:S(2)}, u32[]{:S(2)}) %collective-permute-start.5) | collective-permute-done | bytes 458784 | tf_op jit(solution)/shard_map/ppermute | solution.py:342
  47.3 2.0 %add_convert_fusion = bf16[1,2,448,256]{3,2,1,0:T(8,128)(2,1)} fusion(f32[1,2,448,256]{3,2,1,0:T(8,128)} %get-tuple-element.33, bf16[1,2,448,256]{3,2,1,0:T(8,128)(2,1)S(1)} %collective-permute-done.5), kind=kLoop, calls=%fused_computation | loop fusion | flops 688128 | bytes 1835008 | tf_op jit(solution)/shard_map/convert_element_type | solution.py:343
Async XLA Ops:
  0.6 3.1 %collective-permute-start.1 = (bf16[1,2,448,256]{3,2,1,0:T(8,128)(2,1)}, bf16[1,2,448,256]{3,2,1,0:T(8,128)(2,1)S(1)}, u32[]{:S(2)}, u32[]{:S(2)}) collective-permute-start(bf16[1,2,448,256]{3,2,1,0:T(8,128)(2,1)} %pkv_ref), channel_id=1, source_target_pairs={{0,4},{4,0},{8,12},{12,8},{1,5},{5,1},{9,13},{13,9},{2,6},{6,2},{1... | collective-permute-start | bytes 1376264 | tf_op jit(solution)/shard_map/ppermute | solution.py:323
  1.2 13.9 %collective-permute-start = (bf16[1,2,448,256]{3,2,1,0:T(8,128)(2,1)}, bf16[1,2,448,256]{3,2,1,0:T(8,128)(2,1)S(1)}, u32[]{:S(2)}, u32[]{:S(2)}) collective-permute-start(bf16[1,2,448,256]{3,2,1,0:T(8,128)(2,1)} %pkv_ref), channel_id=1, source_target_pairs={{0,8},{4,12},{8,0},{12,4},{1,9},{5,13},{9,1},{13,5},{2,10},{6,14},... | collective-permute-start | bytes 1376264 | tf_op jit(solution)/shard_map/ppermute | solution.py:322
  3.8 0.8 %copy-start.3 = (bf16[1,2,448,256]{3,2,1,0:T(8,128)(2,1)}, bf16[1,2,448,256]{3,2,1,0:T(8,128)(2,1)S(1)}, u32[]{:S(2)}) copy-start(bf16[1,2,448,256]{3,2,1,0:T(8,128)(2,1)S(1)} %collective-permute-done.1.pkv_ref) | copy-start | bytes 1376260
  15.1 0.8 %copy-start.2 = (bf16[1,2,448,256]{3,2,1,0:T(8,128)(2,1)}, bf16[1,2,448,256]{3,2,1,0:T(8,128)(2,1)S(1)}, u32[]{:S(2)}) copy-start(bf16[1,2,448,256]{3,2,1,0:T(8,128)(2,1)S(1)} %collective-permute-done.pkv_ref) | copy-start | bytes 1376260
  15.1 7.7 %collective-permute-start.2 = (bf16[1,2,448,256]{3,2,1,0:T(8,128)(2,1)S(1)}, bf16[1,2,448,256]{3,2,1,0:T(8,128)(2,1)S(1)}, u32[]{:S(2)}, u32[]{:S(2)}) collective-permute-start(bf16[1,2,448,256]{3,2,1,0:T(8,128)(2,1)S(1)} %collective-permute-done.pkv_ref), channel_id=1, source_target_pairs={{0,4},{4,0},{8,12},{12,8},{1,5},{5,1},{9,13},{13,9},{2,6},{6,2},{1... | collective-permute-start | bytes 1376264 | tf_op jit(solution)/shard_map/ppermute | solution.py:335
  15.1 20.3 %collective-permute-start.4 = (f32[1,2,448,256]{3,2,1,0:T(8,128)}, f32[1,2,448,256]{3,2,1,0:T(8,128)S(1)}, u32[]{:S(2)}, u32[]{:S(2)}) collective-permute-start(f32[1,2,448,256]{3,2,1,0:T(8,128)} %get-tuple-element.30), channel_id=1, source_target_pairs={{0,4},{4,0},{8,12},{12,8},{1,5},{5,1},{9,13},{13,9},{2,6},{6,2},{1... | collective-permute-start | bytes 2752520 | tf_op jit(solution)/shard_map/ppermute | solution.py:336
  22.8 0.8 %copy-start.4 = (bf16[1,2,448,256]{3,2,1,0:T(8,128)(2,1)}, bf16[1,2,448,256]{3,2,1,0:T(8,128)(2,1)S(1)}, u32[]{:S(2)}) copy-start(bf16[1,2,448,256]{3,2,1,0:T(8,128)(2,1)S(1)} %collective-permute-done.2.pkv_ref) | copy-start | bytes 1376260
  23.6 11.0 %copy-start = (f32[1,2,448,256]{3,2,1,0:T(8,128)S(1)}, f32[1,2,448,256]{3,2,1,0:T(8,128)}, u32[]{:S(2)}) copy-start(f32[1,2,448,256]{3,2,1,0:T(8,128)} %get-tuple-element.23) | copy-start | bytes 2752516
  32.5 2.0 %collective-permute-start.3 = (bf16[1,2,448,256]{3,2,1,0:T(8,128)(2,1)}, bf16[1,2,448,256]{3,2,1,0:T(8,128)(2,1)S(1)}, u32[]{:S(2)}, u32[]{:S(2)}) collective-permute-start(bf16[1,2,448,256]{3,2,1,0:T(8,128)(2,1)} %get-tuple-element.26), channel_id=1, source_target_pairs={{0,4},{4,0},{8,12},{12,8},{1,5},{5,1},{9,13},{13,9},{2,6},{6,2},{1... | collective-permute-start | bytes 1376264 | tf_op jit(solution)/shard_map/ppermute | solution.py:339
  34.6 12.6 %collective-permute-start.5 = (bf16[1,2,448,256]{3,2,1,0:T(8,128)(2,1)S(1)}, bf16[1,2,448,256]{3,2,1,0:T(8,128)(2,1)S(1)}, u32[]{:S(2)}, u32[]{:S(2)}) collective-permute-start(bf16[1,2,448,256]{3,2,1,0:T(8,128)(2,1)S(1)} %add_convert_fusion.1), channel_id=1, source_target_pairs={{0,8},{4,12},{8,0},{12,4},{1,9},{5,13},{9,1},{13,5},{2,10},{6,14},... | collective-permute-start | bytes 1376264 | tf_op jit(solution)/shard_map/ppermute | solution.py:342
  35.4 0.9 %copy-start.1 = (f32[1,2,448,256]{3,2,1,0:T(8,128)}, f32[1,2,448,256]{3,2,1,0:T(8,128)S(1)}, u32[]{:S(2)}) copy-start(f32[1,2,448,256]{3,2,1,0:T(8,128)S(1)} %collective-permute-done.4.rest_2_) | copy-start | bytes 2752516

commit v14 on v11

--- a/solution.py
+++ b/solution.py
@@ -93,8 +93,17 @@
     return pair
 
 
+def flip_of(me, flip):
+    if isinstance(flip, tuple):
+        return jnp.where(me % 2 == 0, flip[0], flip[1])
+    return flip
+
+
 def slot_kernel(me_ref, goal_ref, slots_ref, len_ref, lr_ref, q_ref, og_ref, skv_ref, pkv_ref, *rest,
                 group, seq, prefix_rows, flip, pair_count, chained, seeded, low):
+    pkv_other = None
+    if isinstance(flip, tuple):
+        pkv_other, rest = rest[0], rest[1:]
     if chained:
         rest = rest[2:]
     seed_ref = None
@@ -103,7 +112,18 @@
     dq_ref, dkv_ref, dpre_ref, bias_ref = rest[:4]
     acc_ref = rest[4] if low else dpre_ref
     member = pl.program_id(0)
-    goal = me_ref[0] ^ flip
+    goal = me_ref[0] ^ flip_of(me_ref[0], flip)
+    if pkv_other is not None:
+        pre_ref = rest[-1]
+
+        @pl.when((member == 0) & (me_ref[0] % 2 == 0))
+        def _():
+            pre_ref[...] = pkv_ref[...]
+
+        @pl.when((member == 0) & (me_ref[0] % 2 != 0))
+        def _():
+            pre_ref[...] = pkv_other[...]
+        pkv_ref = pre_ref
     pair = pair_of(goal, goal_ref, pair_count)
     length = len_ref[goal]
     dims = dict(group=group, seq=seq, prefix_rows=prefix_rows)
@@ -147,17 +167,20 @@
 
 
 def attend_slot(flip, me, goals, slots, lengths, logratio, queries, out_grad, suffix_kv, prefix_one, chain,
-                seed=None, low=False):
+                seed=None, low=False, weight=1.0):
     suffix_count, seq, qwidth = queries.shape
     kv_width = suffix_kv.shape[-1]
     kv_local = kv_width // HD
     group = qwidth // kv_width
+    pair_other = None
+    if isinstance(prefix_one, tuple):
+        prefix_one, pair_other = prefix_one
     prefix_rows = prefix_one.shape[2]
     pair_count = goals.shape[0]
     qb = group * HD
 
     def suffix_of(m, me_ref, goal_ref, slots_ref):
-        pair = pair_of(me_ref[0] ^ flip, goal_ref, pair_count)
+        pair = pair_of(me_ref[0] ^ flip_of(me_ref[0], flip), goal_ref, pair_count)
         return slots_ref[m, pair]
 
     def q_map(m, me_ref, goal_ref, slots_ref, len_ref):
@@ -182,17 +205,22 @@
         pl.BlockSpec((1, 2, prefix_rows, kv_width), pkv_map),
     ]
     operands = [logratio, queries, out_grad, suffix_kv, prefix_one]
+    if pair_other is not None:
+        in_specs.append(pl.BlockSpec((1, 2, prefix_rows, kv_width), pkv_map))
+        operands.append(pair_other)
     aliases = {}
     if chain is not None:
         in_specs += [pl.BlockSpec(memory_space=pl.ANY)] * 2
         operands += list(chain)
-        aliases = {9: 0, 10: 1}
+        aliases = {4 + len(operands) - 2: 0, 4 + len(operands) - 1: 1}
     if seed is not None:
         in_specs.append(pl.BlockSpec((1, 2, prefix_rows, kv_width), pkv_map))
         operands.append(seed)
     scratch = [pltpu.VMEM((prefix_rows + seq, group * seq), jnp.float32)]
     if low:
         scratch.append(pltpu.VMEM((1, 2, prefix_rows, kv_width), jnp.float32))
+    if pair_other is not None:
+        scratch.append(pltpu.VMEM((1, 2, prefix_rows, kv_width), prefix_one.dtype))
     kernel = functools.partial(slot_kernel, group=group, seq=seq, prefix_rows=prefix_rows, flip=flip,
                                pair_count=pair_count, chained=chain is not None, seeded=seed is not None,
                                low=low)
@@ -209,9 +237,9 @@
     )
     steps = 2 * kv_local
     cost = pl.CostEstimate(
-        flops=steps * 2_200_000_000,
+        flops=int(steps * 2_200_000_000 * weight),
         transcendentals=steps * group * seq * (prefix_rows + seq),
-        bytes_accessed=steps * (4 * seq * qb + 4 * seq * HD + 6 * prefix_rows * HD) * 2,
+        bytes_accessed=int(weight * steps * (4 * seq * qb + 4 * seq * HD + 6 * prefix_rows * HD) * 2),
     )
     return pl.pallas_call(
         kernel,
@@ -319,7 +347,9 @@
 def pipelined(queries, suffix_kv, out_grad, prefix_kv, logratio, pair_slots, pair_goal, prefix_len):
     partner = [(i, i ^ 1) for i in range(4)]
     across = [(i, i ^ 2) for i in range(4)]
-    pre_across = lax.ppermute(prefix_kv, "dp", across)
+    odd_to_even = [(1, 0), (3, 2)]
+    even_to_odd = [(0, 1), (2, 3)]
+    pre_a = lax.ppermute(prefix_kv, "dp", [(0, 2), (2, 0)])
     pre_partner = lax.ppermute(prefix_kv, "dp", partner)
     me = lax.axis_index("dp").astype(jnp.int32).reshape(1)
     tables = (me, pair_goal.reshape(-1).astype(jnp.int32), pair_slots.T.astype(jnp.int32),
@@ -331,15 +361,24 @@
         return (grad_q, grad_kv), partial
 
     chain, near = run(1, pre_partner, None)
-    pre_across, near = lax.optimization_barrier((pre_across, near))
-    pre_relay = lax.ppermute(pre_across, "dp", partner)
+    pre_a, near, later = lax.optimization_barrier((pre_a, near, prefix_kv))
+    relay_a = lax.ppermute(pre_a, "dp", even_to_odd)
+    pre_b = lax.ppermute(later, "dp", [(1, 3), (3, 1)])
     near_sent = lax.ppermute(near, "dp", partner)
-    chain, cross = run(2, pre_across, chain)
-    chain, relay = run(3, pre_relay, chain, low=True)
-    forward = (cross + lax.ppermute(relay, "dp", partner).astype(jnp.float32)).astype(jnp.bfloat16)
-    forward, own_prefix = lax.optimization_barrier((forward, prefix_kv))
+    chain, early = run((2, 3), (pre_a, relay_a), chain, low=True)
+    relay_b = lax.ppermute(pre_b, "dp", odd_to_even)
+    first = (early.astype(jnp.float32)
+             + lax.ppermute(early, "dp", odd_to_even).astype(jnp.float32)).astype(jnp.bfloat16)
+    first, relay_b = lax.optimization_barrier((first, relay_b))
+    first_sent = lax.ppermute(first, "dp", [(0, 2), (2, 0)])
+    chain, late = run((3, 2), (relay_b, pre_b), chain, low=True)
+    second = (late.astype(jnp.float32)
+              + lax.ppermute(late, "dp", even_to_odd).astype(jnp.float32)).astype(jnp.bfloat16)
+    second, own_prefix = lax.optimization_barrier((second, prefix_kv))
+    second_sent = lax.ppermute(second, "dp", [(1, 3), (3, 1)])
     chain, own = run(0, own_prefix, chain, seed=near_sent)
-    total = own + lax.ppermute(forward, "dp", across).astype(jnp.float32)
+    even = lax.axis_index("dp") % 2 == 0
+    total = own + jnp.where(even, first_sent, second_sent).astype(jnp.float32)
     return chain[0], chain[1], total.astype(jnp.bfloat16)
 
 

time: 49.9 us -> 58.8 us (1.18)
  the two profiles are of different devices: /device:TPU:0 before, /device:TPU:1 now
where the time goes in v14:
time: 58.8 us; the launch traced here: 58.7 us
  Pallas kernels  30.7 us (52%)
  starting transfers between devices  14.6 us (25%)
  waiting for transfers between devices  5.81 us (10%)
  other arithmetic  4.35 us (7%)
  local copies, waits for them, and re-layouts  2.3 us (4%)
  between operations  0.84 us (1%)
    pallas_call x4, Pallas kernels, attend_slot(): pl.pallas_call(kernel, grid_spec=grid_spec, out_shape=out_shape, input_ou...  30.7 us
    ppermute x1, starting transfers between devices, pipelined(): pre_b = lax.ppermute(later, 'dp', [(1, 3), (3, 1)])  5.82 us
    ppermute x1, waiting for transfers between devices, pipelined(): second_sent = lax.ppermute(second, 'dp', [(1, 3), (3, 1)])  2.57 us
    unnamed x14, local copies, waits for them, and re-layouts  2.3 us
    convert_element_type x1, other arithmetic, pipelined(): return (chain[0], chain[1], total.astype(jnp.bfloat16))  2.08 us
    ppermute x1, starting transfers between devices, pipelined(): second_sent = lax.ppermute(second, 'dp', [(1, 3), (3, 1)])  1.92 us
    ppermute x1, waiting for transfers between devices, pipelined(): lax.ppermute(late, 'dp', even_to_odd).astype(jnp.float32)  1.91 us
    ppermute x1, starting transfers between devices, pipelined(): relay_b = lax.ppermute(pre_b, 'dp', odd_to_even)  1.5 us
  transfers between devices with their start and end apart: 10, of which 3 were waited for; matrix products, arithmetic and copies ran while one was open for 4% of the time, Pallas kernels for 52%

profile of v14, /device:TPU:1, one launch (start us, length us, event | category | flops | bytes accessed | tf_op | source)
XLA Modules:
  0.0 58.7 jit_solution(4821071794747418529)
XLA Ops:
  0.6 0.1 collective-permute-start.1
  0.7 0.7 %collective-permute-start = (bf16[1,2,448,256]{3,2,1,0:T(8,128)(2,1)}, bf16[1,2,448,256]{3,2,1,0:T(8,128)(2,1)S(1)}, u32[]{:S(2)}, u32[]{:S(2)}) collective-permute-start(bf16[1,2,448,256]{3,2,1,0:T(8,128)(2,1)} %pkv_ref), channel_id=1, source_target_pairs={{0,8},{8,0},{1,9},{9,1},{2,10},{10,2},{3,11},{11,3},{16,24},{24,16... | collective-permute-start | bytes 1376264 | tf_op jit(solution)/shard_map/ppermute | solution.py:352
  1.4 1.3 %collective-permute-done.1.pkv_ref = bf16[1,2,448,256]{3,2,1,0:T(8,128)(2,1)S(1)} collective-permute-done((bf16[1,2,448,256]{3,2,1,0:T(8,128)(2,1)}, bf16[1,2,448,256]{3,2,1,0:T(8,128)(2,1)S(1)}, u32[]{:S(2)}, u32[]{:S(2)}) %collective-permute-start.1) | collective-permute-done | bytes 458784 | tf_op jit(solution)/shard_map/ppermute | solution.py:353
  2.7 0.8 %copy-done.5 = bf16[1,2,448,256]{3,2,1,0:T(8,128)(2,1)} copy-done((bf16[1,2,448,256]{3,2,1,0:T(8,128)(2,1)}, bf16[1,2,448,256]{3,2,1,0:T(8,128)(2,1)S(1)}, u32[]{:S(2)}) %copy-start.5) | copy-done | bytes 458776
  3.5 7.2 %shard_map.103 = (bf16[8,64,2048]{2,1,0:T(8,128)(2,1)}, bf16[8,2,64,256]{3,2,1,0:T(8,128)(2,1)}, f32[1,2,448,256]{3,2,1,0:T(8,128)}) custom-call(s32[1]{0:T(128)} %bitcast.me_ref, s32[4]{0:T(128)} %bitcast.7, s32[2,4]{1,0:T(2,128)} %bitcast.3, s32[4]{0:T(128)} %len_ref.7, f32[8]{0:T(128)} %lr_ref.7, bf16[8,64,2048]{2,1,0:T(8,128)(2,1)} %q_ref.7, ...), custom_call_target="tpu_custom_call" | custom-call | flops 8800000000 | bytes 5111808 | tf_op jit(solution)/shard_map/pallas_call | solution.py:244
  10.7 0.0 collective-permute-done.pkv_ref
  10.7 0.0 copy-start.3
  10.7 1.3 %collective-permute-start.2 = (bf16[1,2,448,256]{3,2,1,0:T(8,128)(2,1)S(1)}, bf16[1,2,448,256]{3,2,1,0:T(8,128)(2,1)S(1)}, u32[]{:S(2)}, u32[]{:S(2)}) collective-permute-start(bf16[1,2,448,256]{3,2,1,0:T(8,128)(2,1)S(1)} %collective-permute-done.pkv_ref), channel_id=1, source_target_pairs={{0,4},{8,12},{1,5},{9,13},{2,6},{10,14},{3,7},{11,15},{16,20},{24,... | collective-permute-start | bytes 1376264 | tf_op jit(solution)/shard_map/ppermute | solution.py:365
  12.0 5.8 %collective-permute-start.4 = (bf16[1,2,448,256]{3,2,1,0:T(8,128)(2,1)S(1)}, bf16[1,2,448,256]{3,2,1,0:T(8,128)(2,1)S(1)}, u32[]{:S(2)}, u32[]{:S(2)}) collective-permute-start(bf16[1,2,448,256]{3,2,1,0:T(8,128)(2,1)S(1)} %copy-done.1), channel_id=1, source_target_pairs={{4,12},{12,4},{5,13},{13,5},{6,14},{14,6},{7,15},{15,7},{20,28},{2... | collective-permute-start | bytes 1376264 | tf_op jit(solution)/shard_map/ppermute | solution.py:366
  17.8 0.0 collective-permute-done.2.rest_0_
  17.9 0.8 %copy-done.6 = bf16[1,2,448,256]{3,2,1,0:T(8,128)(2,1)} copy-done((bf16[1,2,448,256]{3,2,1,0:T(8,128)(2,1)}, bf16[1,2,448,256]{3,2,1,0:T(8,128)(2,1)S(1)}, u32[]{:S(2)}) %copy-start.6) | copy-done | bytes 458776
  18.6 8.9 %shard_map.104 = (bf16[8,64,2048]{2,1,0:T(8,128)(2,1)}, bf16[8,2,64,256]{3,2,1,0:T(8,128)(2,1)}, bf16[1,2,448,256]{3,2,1,0:T(8,128)(2,1)}) custom-call(s32[1]{0:T(128)} %bitcast.me_ref, s32[4]{0:T(128)} %bitcast.8, s32[2,4]{1,0:T(2,128)} %bitcast.4, s32[4]{0:T(128)} %len_ref.7, f32[8]{0:T(128)} %lr_ref.7, ...), custom_call_target="tpu_custom_call", output_to_operand_aliasing={{0}: (10, {}), {1}: (11, {})} | custom-call | flops 8800000000 | bytes 5111808 | tf_op jit(solution)/shard_map/pallas_call | solution.py:244
  27.5 1.3 %collective-permute-start.3 = (bf16[1,2,448,256]{3,2,1,0:T(8,128)(2,1)}, bf16[1,2,448,256]{3,2,1,0:T(8,128)(2,1)S(1)}, u32[]{:S(2)}, u32[]{:S(2)}) collective-permute-start(bf16[1,2,448,256]{3,2,1,0:T(8,128)(2,1)} %get-tuple-element.26), channel_id=1, source_target_pairs={{4,0},{12,8},{5,1},{13,9},{6,2},{14,10},{7,3},{15,11},{20,16},{28,... | collective-permute-start | bytes 1376264 | tf_op jit(solution)/shard_map/ppermute | solution.py:371
  28.8 0.0 collective-permute-done.4.rest_0_
  28.8 1.5 %collective-permute-start.5 = (bf16[1,2,448,256]{3,2,1,0:T(8,128)(2,1)S(1)}, bf16[1,2,448,256]{3,2,1,0:T(8,128)(2,1)S(1)}, u32[]{:S(2)}, u32[]{:S(2)}) collective-permute-start(bf16[1,2,448,256]{3,2,1,0:T(8,128)(2,1)S(1)} %collective-permute-done.4.rest_0_), channel_id=1, source_target_pairs={{4,0},{12,8},{5,1},{13,9},{6,2},{14,10},{7,3},{15,11},{20,16},{28,... | collective-permute-start | bytes 1376264 | tf_op jit(solution)/shard_map/ppermute | solution.py:369
  30.4 0.1 collective-permute-start.7
  30.4 0.0 collective-permute-done.3
  30.4 1.1 %add_convert_fusion.2 = bf16[1,2,448,256]{3,2,1,0:T(8,128)(2,1)S(1)} fusion(bf16[1,2,448,256]{3,2,1,0:T(8,128)(2,1)S(1)} %collective-permute-done.3, bf16[1,2,448,256]{3,2,1,0:T(8,128)(2,1)} %get-tuple-element.26), kind=kLoop, calls=%fused_computation.2 | loop fusion | flops 917504 | bytes 1376256 | tf_op jit(solution)/shard_map/convert_element_type | solution.py:371
  31.6 0.0 collective-permute-done.5.pkv_ref
  31.6 0.0 copy-start.4
  31.6 0.7 %copy-done.4 = bf16[1,2,448,256]{3,2,1,0:T(8,128)(2,1)} copy-done((bf16[1,2,448,256]{3,2,1,0:T(8,128)(2,1)}, bf16[1,2,448,256]{3,2,1,0:T(8,128)(2,1)S(1)}, u32[]{:S(2)}) %copy-start.4) | copy-done | bytes 458776
  32.4 7.2 %shard_map.105 = (bf16[8,64,2048]{2,1,0:T(8,128)(2,1)}, bf16[8,2,64,256]{3,2,1,0:T(8,128)(2,1)}, bf16[1,2,448,256]{3,2,1,0:T(8,128)(2,1)}) custom-call(s32[1]{0:T(128)} %bitcast.me_ref, s32[4]{0:T(128)} %bitcast.9, s32[2,4]{1,0:T(2,128)} %bitcast.5, s32[4]{0:T(128)} %len_ref.7, f32[8]{0:T(128)} %lr_ref.7, ...), custom_call_target="tpu_custom_call", output_to_operand_aliasing={{0}: (10, {}), {1}: (11, {})} | custom-call | flops 8800000000 | bytes 5111808 | tf_op jit(solution)/shard_map/pallas_call | solution.py:244
  39.5 1.3 %collective-permute-start.6 = (bf16[1,2,448,256]{3,2,1,0:T(8,128)(2,1)}, bf16[1,2,448,256]{3,2,1,0:T(8,128)(2,1)S(1)}, u32[]{:S(2)}, u32[]{:S(2)}) collective-permute-start(bf16[1,2,448,256]{3,2,1,0:T(8,128)(2,1)} %get-tuple-element.31), channel_id=1, source_target_pairs={{0,4},{8,12},{1,5},{9,13},{2,6},{10,14},{3,7},{11,15},{16,20},{24,... | collective-permute-start | bytes 1376264 | tf_op jit(solution)/shard_map/ppermute | solution.py:376
  40.8 0.7 %collective-permute-start.8 = (bf16[1,2,448,256]{3,2,1,0:T(8,128)(2,1)S(1)}, bf16[1,2,448,256]{3,2,1,0:T(8,128)(2,1)S(1)}, u32[]{:S(2)}, u32[]{:S(2)}) collective-permute-start(bf16[1,2,448,256]{3,2,1,0:T(8,128)(2,1)S(1)} %add_convert_fusion.2), channel_id=1, source_target_pairs={{0,8},{8,0},{1,9},{9,1},{2,10},{10,2},{3,11},{11,3},{16,24},{24,16... | collective-permute-start | bytes 1376264 | tf_op jit(solution)/shard_map/ppermute | solution.py:373
  41.5 1.9 %collective-permute-done.6 = bf16[1,2,448,256]{3,2,1,0:T(8,128)(2,1)S(1)} collective-permute-done((bf16[1,2,448,256]{3,2,1,0:T(8,128)(2,1)}, bf16[1,2,448,256]{3,2,1,0:T(8,128)(2,1)S(1)}, u32[]{:S(2)}, u32[]{:S(2)}) %collective-permute-start.6) | collective-permute-done | bytes 458784 | tf_op jit(solution)/shard_map/ppermute | solution.py:376
  43.5 1.1 %add_convert_fusion.1 = bf16[1,2,448,256]{3,2,1,0:T(8,128)(2,1)S(1)} fusion(bf16[1,2,448,256]{3,2,1,0:T(8,128)(2,1)S(1)} %collective-permute-done.6, bf16[1,2,448,256]{3,2,1,0:T(8,128)(2,1)} %get-tuple-element.31), kind=kLoop, calls=%fused_computation.1 | loop fusion | flops 917504 | bytes 1376256 | tf_op jit(solution)/shard_map/convert_element_type | solution.py:376
  44.6 1.9 %collective-permute-start.9 = (bf16[1,2,448,256]{3,2,1,0:T(8,128)(2,1)S(1)}, bf16[1,2,448,256]{3,2,1,0:T(8,128)(2,1)S(1)}, u32[]{:S(2)}, u32[]{:S(2)}) collective-permute-start(bf16[1,2,448,256]{3,2,1,0:T(8,128)(2,1)S(1)} %add_convert_fusion.1), channel_id=1, source_target_pairs={{4,12},{12,4},{5,13},{13,5},{6,14},{14,6},{7,15},{15,7},{20,28},{2... | collective-permute-start | bytes 1376264 | tf_op jit(solution)/shard_map/ppermute | solution.py:378
  46.5 0.0 collective-permute-done.7.rest_2_
  46.5 7.5 %shard_map.106 = (bf16[8,64,2048]{2,1,0:T(8,128)(2,1)}, bf16[8,2,64,256]{3,2,1,0:T(8,128)(2,1)}, f32[1,2,448,256]{3,2,1,0:T(8,128)}) custom-call(s32[1]{0:T(128)} %bitcast.me_ref, s32[4]{0:T(128)} %bitcast.10, s32[2,4]{1,0:T(2,128)} %bitcast.6, s32[4]{0:T(128)} %len_ref.7, f32[8]{0:T(128)} %lr_ref.7, ...), custom_call_target="tpu_custom_call", output_to_operand_aliasing={{0}: (9, {}), {1}: (10, {})} | custom-call | flops 8800000000 | bytes 5111808 | tf_op jit(solution)/shard_map/pallas_call | solution.py:244
  54.0 0.0 collective-permute-done.8
  54.0 2.6 %collective-permute-done.9 = bf16[1,2,448,256]{3,2,1,0:T(8,128)(2,1)S(1)} collective-permute-done((bf16[1,2,448,256]{3,2,1,0:T(8,128)(2,1)S(1)}, bf16[1,2,448,256]{3,2,1,0:T(8,128)(2,1)S(1)}, u32[]{:S(2)}, u32[]{:S(2)}) %collective-permute-start.9) | collective-permute-done | bytes 458784 | tf_op jit(solution)/shard_map/ppermute | solution.py:378
  56.6 2.1 %add_convert_fusion = bf16[1,2,448,256]{3,2,1,0:T(8,128)(2,1)} fusion(f32[1,2,448,256]{3,2,1,0:T(8,128)} %get-tuple-element.38, bf16[1,2,448,256]{3,2,1,0:T(8,128)(2,1)S(1)} %collective-permute-done.8, bf16[1,2,448,256]{3,2,1,0:T(8,128)(2,1)S(1)} %collective-permute-done.9, pred[]{:T(512)S(6)} %eq.5), kind=kLoop, calls=%fused_computation | loop fusion | flops 917504 | bytes 2293761 | tf_op jit(solution)/shard_map/convert_element_type | solution.py:382
  (9 shorter events, 0.0 us)
Async XLA Ops:
  0.6 2.1 %collective-permute-start.1 = (bf16[1,2,448,256]{3,2,1,0:T(8,128)(2,1)}, bf16[1,2,448,256]{3,2,1,0:T(8,128)(2,1)S(1)}, u32[]{:S(2)}, u32[]{:S(2)}) collective-permute-start(bf16[1,2,448,256]{3,2,1,0:T(8,128)(2,1)} %pkv_ref), channel_id=1, source_target_pairs={{0,4},{4,0},{8,12},{12,8},{1,5},{5,1},{9,13},{13,9},{2,6},{6,2},{1... | collective-permute-start | bytes 1376264 | tf_op jit(solution)/shard_map/ppermute | solution.py:353
  0.7 10.0 %collective-permute-start = (bf16[1,2,448,256]{3,2,1,0:T(8,128)(2,1)}, bf16[1,2,448,256]{3,2,1,0:T(8,128)(2,1)S(1)}, u32[]{:S(2)}, u32[]{:S(2)}) collective-permute-start(bf16[1,2,448,256]{3,2,1,0:T(8,128)(2,1)} %pkv_ref), channel_id=1, source_target_pairs={{0,8},{8,0},{1,9},{9,1},{2,10},{10,2},{3,11},{11,3},{16,24},{24,16... | collective-permute-start | bytes 1376264 | tf_op jit(solution)/shard_map/ppermute | solution.py:352
  2.7 0.8 %copy-start.5 = (bf16[1,2,448,256]{3,2,1,0:T(8,128)(2,1)}, bf16[1,2,448,256]{3,2,1,0:T(8,128)(2,1)S(1)}, u32[]{:S(2)}) copy-start(bf16[1,2,448,256]{3,2,1,0:T(8,128)(2,1)S(1)} %collective-permute-done.1.pkv_ref) | copy-start | bytes 1376260
  3.5 8.5 %copy-start.1 = (bf16[1,2,448,256]{3,2,1,0:T(8,128)(2,1)S(1)}, bf16[1,2,448,256]{3,2,1,0:T(8,128)(2,1)}, u32[]{:S(2)}) copy-start(bf16[1,2,448,256]{3,2,1,0:T(8,128)(2,1)} %pkv_ref) | copy-start | bytes 1376260
  10.7 7.2 %copy-start.3 = (bf16[1,2,448,256]{3,2,1,0:T(8,128)(2,1)}, bf16[1,2,448,256]{3,2,1,0:T(8,128)(2,1)S(1)}, u32[]{:S(2)}) copy-start(bf16[1,2,448,256]{3,2,1,0:T(8,128)(2,1)S(1)} %collective-permute-done.pkv_ref) | copy-start | bytes 1376260
  10.7 7.1 %collective-permute-start.2 = (bf16[1,2,448,256]{3,2,1,0:T(8,128)(2,1)S(1)}, bf16[1,2,448,256]{3,2,1,0:T(8,128)(2,1)S(1)}, u32[]{:S(2)}, u32[]{:S(2)}) collective-permute-start(bf16[1,2,448,256]{3,2,1,0:T(8,128)(2,1)S(1)} %collective-permute-done.pkv_ref), channel_id=1, source_target_pairs={{0,4},{8,12},{1,5},{9,13},{2,6},{10,14},{3,7},{11,15},{16,20},{24,... | collective-permute-start | bytes 1376264 | tf_op jit(solution)/shard_map/ppermute | solution.py:365
  12.0 16.8 %collective-permute-start.4 = (bf16[1,2,448,256]{3,2,1,0:T(8,128)(2,1)S(1)}, bf16[1,2,448,256]{3,2,1,0:T(8,128)(2,1)S(1)}, u32[]{:S(2)}, u32[]{:S(2)}) collective-permute-start(bf16[1,2,448,256]{3,2,1,0:T(8,128)(2,1)S(1)} %copy-done.1), channel_id=1, source_target_pairs={{4,12},{12,4},{5,13},{13,5},{6,14},{14,6},{7,15},{15,7},{20,28},{2... | collective-permute-start | bytes 1376264 | tf_op jit(solution)/shard_map/ppermute | solution.py:366
  17.8 0.8 %copy-start.6 = (bf16[1,2,448,256]{3,2,1,0:T(8,128)(2,1)}, bf16[1,2,448,256]{3,2,1,0:T(8,128)(2,1)S(1)}, u32[]{:S(2)}) copy-start(bf16[1,2,448,256]{3,2,1,0:T(8,128)(2,1)S(1)} %collective-permute-done.2.rest_0_) | copy-start | bytes 1376260
  18.6 11.7 %copy-start = (f32[1,2,448,256]{3,2,1,0:T(8,128)S(1)}, f32[1,2,448,256]{3,2,1,0:T(8,128)}, u32[]{:S(2)}) copy-start(f32[1,2,448,256]{3,2,1,0:T(8,128)} %get-tuple-element.35) | copy-start | bytes 2752516
  27.5 2.9 %collective-permute-start.3 = (bf16[1,2,448,256]{3,2,1,0:T(8,128)(2,1)}, bf16[1,2,448,256]{3,2,1,0:T(8,128)(2,1)S(1)}, u32[]{:S(2)}, u32[]{:S(2)}) collective-permute-start(bf16[1,2,448,256]{3,2,1,0:T(8,128)(2,1)} %get-tuple-element.26), channel_id=1, source_target_pairs={{4,0},{12,8},{5,1},{13,9},{6,2},{14,10},{7,3},{15,11},{20,16},{28,... | collective-permute-start | bytes 1376264 | tf_op jit(solution)/shard_map/ppermute | solution.py:371
  28.8 2.8 %copy-start.2 = (bf16[1,2,448,256]{3,2,1,0:T(8,128)(2,1)}, bf16[1,2,448,256]{3,2,1,0:T(8,128)(2,1)S(1)}, u32[]{:S(2)}) copy-start(bf16[1,2,448,256]{3,2,1,0:T(8,128)(2,1)S(1)} %collective-permute-done.4.rest_0_) | copy-start | bytes 1376260
  28.8 2.7 %collective-permute-start.5 = (bf16[1,2,448,256]{3,2,1,0:T(8,128)(2,1)S(1)}, bf16[1,2,448,256]{3,2,1,0:T(8,128)(2,1)S(1)}, u32[]{:S(2)}, u32[]{:S(2)}) collective-permute-start(bf16[1,2,448,256]{3,2,1,0:T(8,128)(2,1)S(1)} %collective-permute-done.4.rest_0_), channel_id=1, source_target_pairs={{4,0},{12,8},{5,1},{13,9},{6,2},{14,10},{7,3},{15,11},{20,16},{28,... | collective-permute-start | bytes 1376264 | tf_op jit(solution)/shard_map/ppermute | solution.py:369
  30.4 16.2 %collective-permute-start.7 = (f32[1,2,448,256]{3,2,1,0:T(8,128)S(1)}, f32[1,2,448,256]{3,2,1,0:T(8,128)}, u32[]{:S(2)}, u32[]{:S(2)}) collective-permute-start(f32[1,2,448,256]{3,2,1,0:T(8,128)S(1)} %copy-done), channel_id=1, source_target_pairs={{0,4},{4,0},{8,12},{12,8},{1,5},{5,1},{9,13},{13,9},{2,6},{6,2},{1... | collective-permute-start | bytes 2752520 | tf_op jit(solution)/shard_map/ppermute | solution.py:367
  31.6 0.8 %copy-start.4 = (bf16[1,2,448,256]{3,2,1,0:T(8,128)(2,1)}, bf16[1,2,448,256]{3,2,1,0:T(8,128)(2,1)S(1)}, u32[]{:S(2)}) copy-start(bf16[1,2,448,256]{3,2,1,0:T(8,128)(2,1)S(1)} %collective-permute-done.5.pkv_ref) | copy-start | bytes 1376260
  39.5 3.9 %collective-permute-start.6 = (bf16[1,2,448,256]{3,2,1,0:T(8,128)(2,1)}, bf16[1,2,448,256]{3,2,1,0:T(8,128)(2,1)S(1)}, u32[]{:S(2)}, u32[]{:S(2)}) collective-permute-start(bf16[1,2,448,256]{3,2,1,0:T(8,128)(2,1)} %get-tuple-element.31), channel_id=1, source_target_pairs={{0,4},{8,12},{1,5},{9,13},{2,6},{10,14},{3,7},{11,15},{16,20},{24,... | collective-permute-start | bytes 1376264 | tf_op jit(solution)/shard_map/ppermute | solution.py:376
  40.8 13.2 %collective-permute-start.8 = (bf16[1,2,448,256]{3,2,1,0:T(8,128)(2,1)S(1)}, bf16[1,2,448,256]{3,2,1,0:T(8,128)(2,1)S(1)}, u32[]{:S(2)}, u32[]{:S(2)}) collective-permute-start(bf16[1,2,448,256]{3,2,1,0:T(8,128)(2,1)S(1)} %add_convert_fusion.2), channel_id=1, source_target_pairs={{0,8},{8,0},{1,9},{9,1},{2,10},{10,2},{3,11},{11,3},{16,24},{24,16... | collective-permute-start | bytes 1376264 | tf_op jit(solution)/shard_map/ppermute | solution.py:373
  44.6 12.0 %collective-permute-start.9 = (bf16[1,2,448,256]{3,2,1,0:T(8,128)(2,1)S(1)}, bf16[1,2,448,256]{3,2,1,0:T(8,128)(2,1)S(1)}, u32[]{:S(2)}, u32[]{:S(2)}) collective-permute-start(bf16[1,2,448,256]{3,2,1,0:T(8,128)(2,1)S(1)} %add_convert_fusion.1), channel_id=1, source_target_pairs={{4,12},{12,4},{5,13},{13,5},{6,14},{14,6},{7,15},{15,7},{20,28},{2... | collective-permute-start | bytes 1376264 | tf_op jit(solution)/shard_map/ppermute | solution.py:378

commit v15 on v11

--- a/solution.py
+++ b/solution.py
@@ -139,7 +139,7 @@
     if seeded:
         @pl.when(member == 1)
         def _():
-            dpre_ref[...] += seed_ref[...]
+            dpre_ref[...] += seed_ref[...].astype(jnp.float32)
     if low:
         @pl.when(member == 1)
         def _():
@@ -330,13 +330,14 @@
                                                **extra)
         return (grad_q, grad_kv), partial
 
-    chain, near = run(1, pre_partner, None)
+    chain, near = run(1, pre_partner, None, low=True)
     pre_across, near = lax.optimization_barrier((pre_across, near))
     pre_relay = lax.ppermute(pre_across, "dp", partner)
     near_sent = lax.ppermute(near, "dp", partner)
-    chain, cross = run(2, pre_across, chain)
+    chain, cross = run(2, pre_across, chain, low=True)
     chain, relay = run(3, pre_relay, chain, low=True)
-    forward = (cross + lax.ppermute(relay, "dp", partner).astype(jnp.float32)).astype(jnp.bfloat16)
+    forward = (cross.astype(jnp.float32)
+               + lax.ppermute(relay, "dp", partner).astype(jnp.float32)).astype(jnp.bfloat16)
     forward, own_prefix = lax.optimization_barrier((forward, prefix_kv))
     chain, own = run(0, own_prefix, chain, seed=near_sent)
     total = own + lax.ppermute(forward, "dp", across).astype(jnp.float32)

time: 49.9 us -> 49.4 us (0.990)
  starting transfers between devices: 7.87 us -> 3.9 us
  waiting for transfers between devices: 5.36 us -> 9.26 us
  Pallas kernels: 31.2 us -> 30 us
    ppermute x1, starting transfers between devices: 4.21 us -> 0.25 us  [pipelined(): total = own + lax.ppermute(forward, 'dp', across).astype(jnp.float32)]
    ppermute x1, waiting for transfers between devices: 1.4 us -> 3.85 us  [pipelined(): total = own + lax.ppermute(forward, 'dp', across).astype(jnp.float32)]
    ppermute x1, waiting for transfers between devices: 1.94 us -> 3.6 us  [pipelined(): pre_across = lax.ppermute(prefix_kv, 'dp', across)]
    pallas_call x4, Pallas kernels: 31.2 us -> 30 us  [attend_slot(): pl.pallas_call(kernel, grid_spec=grid_spec, out_shape=out_shape, input_ou...]
    ppermute x1, waiting for transfers between devices: 2.01 us -> 1.51 us  [pipelined(): lax.ppermute(relay, 'dp', partner).astype(jnp.float32)]
    unnamed x10 -> x12, local copies, waits for them, and re-layouts: 2.72 us -> 3.07 us
  transfers between devices with their start and end apart: 6 -> 6, of which waited for: 3 -> 4; matrix products, arithmetic and copies ran while one was open for 0% -> 0% of each run, Pallas kernels for 62% -> 44%
where the time goes in v15:
time: 49.4 us; the launch traced here: 49.1 us
  Pallas kernels  30 us (61%)
  waiting for transfers between devices  9.26 us (19%)
  starting transfers between devices  3.9 us (8%)
  local copies, waits for them, and re-layouts  3.07 us (6%)
  other arithmetic  2.15 us (4%)
  between operations  0.67 us (1%)
    pallas_call x4, Pallas kernels, attend_slot(): pl.pallas_call(kernel, grid_spec=grid_spec, out_shape=out_shape, input_ou...  30 us
    ppermute x1, waiting for transfers between devices, pipelined(): total = own + lax.ppermute(forward, 'dp', across).astype(jnp.float32)  3.85 us
    ppermute x1, waiting for transfers between devices, pipelined(): pre_across = lax.ppermute(prefix_kv, 'dp', across)  3.6 us
    unnamed x12, local copies, waits for them, and re-layouts  3.07 us
    ppermute x1, starting transfers between devices, pipelined(): pre_across = lax.ppermute(prefix_kv, 'dp', across)  2.58 us
    convert_element_type x1, other arithmetic, pipelined(): return (chain[0], chain[1], total.astype(jnp.bfloat16))  2.04 us
    ppermute x1, waiting for transfers between devices, pipelined(): lax.ppermute(relay, 'dp', partner).astype(jnp.float32)  1.51 us
  transfers between devices with their start and end apart: 6, of which 4 were waited for; matrix products, arithmetic and copies ran while one was open for 0% of the time, Pallas kernels for 44%

profile of v15, /device:TPU:0, one launch (start us, length us, event | category | flops | bytes accessed | tf_op | source)
XLA Modules:
  0.0 49.1 jit_solution(14369627875117754210)
XLA Ops:
  0.6 0.6 %collective-permute-start.1 = (bf16[1,2,448,256]{3,2,1,0:T(8,128)(2,1)}, bf16[1,2,448,256]{3,2,1,0:T(8,128)(2,1)S(1)}, u32[]{:S(2)}, u32[]{:S(2)}) collective-permute-start(bf16[1,2,448,256]{3,2,1,0:T(8,128)(2,1)} %pkv_ref), channel_id=1, source_target_pairs={{0,4},{4,0},{8,12},{12,8},{1,5},{5,1},{9,13},{13,9},{2,6},{6,2},{1... | collective-permute-start | bytes 1376264 | tf_op jit(solution)/shard_map/ppermute | solution.py:323
  1.2 2.6 %collective-permute-start = (bf16[1,2,448,256]{3,2,1,0:T(8,128)(2,1)}, bf16[1,2,448,256]{3,2,1,0:T(8,128)(2,1)S(1)}, u32[]{:S(2)}, u32[]{:S(2)}) collective-permute-start(bf16[1,2,448,256]{3,2,1,0:T(8,128)(2,1)} %pkv_ref), channel_id=1, source_target_pairs={{0,8},{4,12},{8,0},{12,4},{1,9},{5,13},{9,1},{13,5},{2,10},{6,14},... | collective-permute-start | bytes 1376264 | tf_op jit(solution)/shard_map/ppermute | solution.py:322
  3.8 0.0 collective-permute-done.1.pkv_ref
  3.8 0.0 copy-start.4
  3.8 0.8 %copy-done.4 = bf16[1,2,448,256]{3,2,1,0:T(8,128)(2,1)} copy-done((bf16[1,2,448,256]{3,2,1,0:T(8,128)(2,1)}, bf16[1,2,448,256]{3,2,1,0:T(8,128)(2,1)S(1)}, u32[]{:S(2)}) %copy-start.4) | copy-done | bytes 458776
  4.5 7.0 %shard_map.103 = (bf16[8,64,2048]{2,1,0:T(8,128)(2,1)}, bf16[8,2,64,256]{3,2,1,0:T(8,128)(2,1)}, bf16[1,2,448,256]{3,2,1,0:T(8,128)(2,1)}) custom-call(s32[1]{0:T(128)} %bitcast.me_ref, s32[4]{0:T(128)} %bitcast.7, s32[2,4]{1,0:T(2,128)} %bitcast.3, s32[4]{0:T(128)} %len_ref.7, f32[8]{0:T(128)} %lr_ref.7, bf16[8,64,2048]{2,1,0:T(8,128)(2,1)} %q_ref.7, ...), custom_call_target="tpu_custom_call" | custom-call | flops 8800000000 | bytes 5111808 | tf_op jit(solution)/shard_map/pallas_call | solution.py:216
  11.5 3.6 %collective-permute-done.pkv_ref = bf16[1,2,448,256]{3,2,1,0:T(8,128)(2,1)S(1)} collective-permute-done((bf16[1,2,448,256]{3,2,1,0:T(8,128)(2,1)}, bf16[1,2,448,256]{3,2,1,0:T(8,128)(2,1)S(1)}, u32[]{:S(2)}, u32[]{:S(2)}) %collective-permute-start) | collective-permute-done | bytes 458784 | tf_op jit(solution)/shard_map/ppermute | solution.py:322
  15.1 0.0 copy-start.2
  15.1 0.0 collective-permute-start.2
  15.1 0.8 %copy-done.2 = bf16[1,2,448,256]{3,2,1,0:T(8,128)(2,1)} copy-done((bf16[1,2,448,256]{3,2,1,0:T(8,128)(2,1)}, bf16[1,2,448,256]{3,2,1,0:T(8,128)(2,1)S(1)}, u32[]{:S(2)}) %copy-start.2) | copy-done | bytes 458776
  15.9 7.0 %shard_map.104 = (bf16[8,64,2048]{2,1,0:T(8,128)(2,1)}, bf16[8,2,64,256]{3,2,1,0:T(8,128)(2,1)}, bf16[1,2,448,256]{3,2,1,0:T(8,128)(2,1)}) custom-call(s32[1]{0:T(128)} %bitcast.me_ref, s32[4]{0:T(128)} %bitcast.8, s32[2,4]{1,0:T(2,128)} %bitcast.4, s32[4]{0:T(128)} %len_ref.7, f32[8]{0:T(128)} %lr_ref.7, ...), custom_call_target="tpu_custom_call", output_to_operand_aliasing={{0}: (9, {}), {1}: (10, {})} | custom-call | flops 8800000000 | bytes 5111808 | tf_op jit(solution)/shard_map/pallas_call | solution.py:216
  22.8 0.0 collective-permute-done.2.pkv_ref
  22.8 0.0 copy-start.5
  22.8 0.8 %copy-done.5 = bf16[1,2,448,256]{3,2,1,0:T(8,128)(2,1)} copy-done((bf16[1,2,448,256]{3,2,1,0:T(8,128)(2,1)}, bf16[1,2,448,256]{3,2,1,0:T(8,128)(2,1)S(1)}, u32[]{:S(2)}) %copy-start.5) | copy-done | bytes 458776
  23.6 0.0 copy-start.1
  23.6 0.0 copy-start
  23.6 8.6 %shard_map.105 = (bf16[8,64,2048]{2,1,0:T(8,128)(2,1)}, bf16[8,2,64,256]{3,2,1,0:T(8,128)(2,1)}, bf16[1,2,448,256]{3,2,1,0:T(8,128)(2,1)}) custom-call(s32[1]{0:T(128)} %bitcast.me_ref, s32[4]{0:T(128)} %bitcast.9, s32[2,4]{1,0:T(2,128)} %bitcast.5, s32[4]{0:T(128)} %len_ref.7, f32[8]{0:T(128)} %lr_ref.7, ...), custom_call_target="tpu_custom_call", output_to_operand_aliasing={{0}: (9, {}), {1}: (10, {})} | custom-call | flops 8800000000 | bytes 5111808 | tf_op jit(solution)/shard_map/pallas_call | solution.py:216
  32.2 0.0 collective-permute-start.3
  32.3 0.0 copy-done.1
  32.3 0.5 collective-permute-start.4
  32.8 1.5 %collective-permute-done.3 = bf16[1,2,448,256]{3,2,1,0:T(8,128)(2,1)S(1)} collective-permute-done((bf16[1,2,448,256]{3,2,1,0:T(8,128)(2,1)}, bf16[1,2,448,256]{3,2,1,0:T(8,128)(2,1)S(1)}, u32[]{:S(2)}, u32[]{:S(2)}) %collective-permute-start.3) | collective-permute-done | bytes 458784 | tf_op jit(solution)/shard_map/ppermute | solution.py:340
  34.3 0.0 copy-done
  34.3 0.1 add_convert_fusion.1
  34.4 0.2 collective-permute-start.5
  34.6 0.3 collective-permute-done.4.rest_2_
  34.9 0.0 copy-start.3
  34.9 0.8 %copy-done.3 = bf16[1,2,448,256]{3,2,1,0:T(8,128)(2,1)} copy-done((bf16[1,2,448,256]{3,2,1,0:T(8,128)(2,1)}, bf16[1,2,448,256]{3,2,1,0:T(8,128)(2,1)S(1)}, u32[]{:S(2)}) %copy-start.3) | copy-done | bytes 458776
  35.7 7.5 %shard_map.106 = (bf16[8,64,2048]{2,1,0:T(8,128)(2,1)}, bf16[8,2,64,256]{3,2,1,0:T(8,128)(2,1)}, f32[1,2,448,256]{3,2,1,0:T(8,128)}) custom-call(s32[1]{0:T(128)} %bitcast.me_ref, s32[4]{0:T(128)} %bitcast.10, s32[2,4]{1,0:T(2,128)} %bitcast.6, s32[4]{0:T(128)} %len_ref.7, f32[8]{0:T(128)} %lr_ref.7, ...), custom_call_target="tpu_custom_call", output_to_operand_aliasing={{0}: (9, {}), {1}: (10, {})} | custom-call | flops 8800000000 | bytes 5111808 | tf_op jit(solution)/shard_map/pallas_call | solution.py:216
  43.2 3.9 %collective-permute-done.5 = bf16[1,2,448,256]{3,2,1,0:T(8,128)(2,1)S(1)} collective-permute-done((bf16[1,2,448,256]{3,2,1,0:T(8,128)(2,1)S(1)}, bf16[1,2,448,256]{3,2,1,0:T(8,128)(2,1)S(1)}, u32[]{:S(2)}, u32[]{:S(2)}) %collective-permute-start.5) | collective-permute-done | bytes 458784 | tf_op jit(solution)/shard_map/ppermute | solution.py:343
  47.0 2.0 %add_convert_fusion = bf16[1,2,448,256]{3,2,1,0:T(8,128)(2,1)} fusion(f32[1,2,448,256]{3,2,1,0:T(8,128)} %get-tuple-element.33, bf16[1,2,448,256]{3,2,1,0:T(8,128)(2,1)S(1)} %collective-permute-done.5), kind=kLoop, calls=%fused_computation | loop fusion | flops 688128 | bytes 1835008 | tf_op jit(solution)/shard_map/convert_element_type | solution.py:344
Async XLA Ops:
  0.6 3.1 %collective-permute-start.1 = (bf16[1,2,448,256]{3,2,1,0:T(8,128)(2,1)}, bf16[1,2,448,256]{3,2,1,0:T(8,128)(2,1)S(1)}, u32[]{:S(2)}, u32[]{:S(2)}) collective-permute-start(bf16[1,2,448,256]{3,2,1,0:T(8,128)(2,1)} %pkv_ref), channel_id=1, source_target_pairs={{0,4},{4,0},{8,12},{12,8},{1,5},{5,1},{9,13},{13,9},{2,6},{6,2},{1... | collective-permute-start | bytes 1376264 | tf_op jit(solution)/shard_map/ppermute | solution.py:323
  1.2 13.9 %collective-permute-start = (bf16[1,2,448,256]{3,2,1,0:T(8,128)(2,1)}, bf16[1,2,448,256]{3,2,1,0:T(8,128)(2,1)S(1)}, u32[]{:S(2)}, u32[]{:S(2)}) collective-permute-start(bf16[1,2,448,256]{3,2,1,0:T(8,128)(2,1)} %pkv_ref), channel_id=1, source_target_pairs={{0,8},{4,12},{8,0},{12,4},{1,9},{5,13},{9,1},{13,5},{2,10},{6,14},... | collective-permute-start | bytes 1376264 | tf_op jit(solution)/shard_map/ppermute | solution.py:322
  3.8 0.8 %copy-start.4 = (bf16[1,2,448,256]{3,2,1,0:T(8,128)(2,1)}, bf16[1,2,448,256]{3,2,1,0:T(8,128)(2,1)S(1)}, u32[]{:S(2)}) copy-start(bf16[1,2,448,256]{3,2,1,0:T(8,128)(2,1)S(1)} %collective-permute-done.1.pkv_ref) | copy-start | bytes 1376260
  15.1 0.8 %copy-start.2 = (bf16[1,2,448,256]{3,2,1,0:T(8,128)(2,1)}, bf16[1,2,448,256]{3,2,1,0:T(8,128)(2,1)S(1)}, u32[]{:S(2)}) copy-start(bf16[1,2,448,256]{3,2,1,0:T(8,128)(2,1)S(1)} %collective-permute-done.pkv_ref) | copy-start | bytes 1376260
  15.1 7.7 %collective-permute-start.2 = (bf16[1,2,448,256]{3,2,1,0:T(8,128)(2,1)S(1)}, bf16[1,2,448,256]{3,2,1,0:T(8,128)(2,1)S(1)}, u32[]{:S(2)}, u32[]{:S(2)}) collective-permute-start(bf16[1,2,448,256]{3,2,1,0:T(8,128)(2,1)S(1)} %collective-permute-done.pkv_ref), channel_id=1, source_target_pairs={{0,4},{4,0},{8,12},{12,8},{1,5},{5,1},{9,13},{13,9},{2,6},{6,2},{1... | collective-permute-start | bytes 1376264 | tf_op jit(solution)/shard_map/ppermute | solution.py:335
  22.8 0.8 %copy-start.5 = (bf16[1,2,448,256]{3,2,1,0:T(8,128)(2,1)}, bf16[1,2,448,256]{3,2,1,0:T(8,128)(2,1)S(1)}, u32[]{:S(2)}) copy-start(bf16[1,2,448,256]{3,2,1,0:T(8,128)(2,1)S(1)} %collective-permute-done.2.pkv_ref) | copy-start | bytes 1376260
  23.6 8.7 %copy-start.1 = (bf16[1,2,448,256]{3,2,1,0:T(8,128)(2,1)S(1)}, bf16[1,2,448,256]{3,2,1,0:T(8,128)(2,1)}, u32[]{:S(2)}) copy-start(bf16[1,2,448,256]{3,2,1,0:T(8,128)(2,1)} %get-tuple-element.30) | copy-start | bytes 1376260
  23.6 10.7 %copy-start = (bf16[1,2,448,256]{3,2,1,0:T(8,128)(2,1)S(1)}, bf16[1,2,448,256]{3,2,1,0:T(8,128)(2,1)}, u32[]{:S(2)}) copy-start(bf16[1,2,448,256]{3,2,1,0:T(8,128)(2,1)} %get-tuple-element.23) | copy-start | bytes 1376260
  32.2 2.0 %collective-permute-start.3 = (bf16[1,2,448,256]{3,2,1,0:T(8,128)(2,1)}, bf16[1,2,448,256]{3,2,1,0:T(8,128)(2,1)S(1)}, u32[]{:S(2)}, u32[]{:S(2)}) collective-permute-start(bf16[1,2,448,256]{3,2,1,0:T(8,128)(2,1)} %get-tuple-element.26), channel_id=1, source_target_pairs={{0,4},{4,0},{8,12},{12,8},{1,5},{5,1},{9,13},{13,9},{2,6},{6,2},{1... | collective-permute-start | bytes 1376264 | tf_op jit(solution)/shard_map/ppermute | solution.py:340
  32.3 2.7 %collective-permute-start.4 = (bf16[1,2,448,256]{3,2,1,0:T(8,128)(2,1)S(1)}, bf16[1,2,448,256]{3,2,1,0:T(8,128)(2,1)S(1)}, u32[]{:S(2)}, u32[]{:S(2)}) collective-permute-start(bf16[1,2,448,256]{3,2,1,0:T(8,128)(2,1)S(1)} %copy-done.1), channel_id=1, source_target_pairs={{0,4},{4,0},{8,12},{12,8},{1,5},{5,1},{9,13},{13,9},{2,6},{6,2},{1... | collective-permute-start | bytes 1376264 | tf_op jit(solution)/shard_map/ppermute | solution.py:336
  34.4 12.6 %collective-permute-start.5 = (bf16[1,2,448,256]{3,2,1,0:T(8,128)(2,1)S(1)}, bf16[1,2,448,256]{3,2,1,0:T(8,128)(2,1)S(1)}, u32[]{:S(2)}, u32[]{:S(2)}) collective-permute-start(bf16[1,2,448,256]{3,2,1,0:T(8,128)(2,1)S(1)} %add_convert_fusion.1), channel_id=1, source_target_pairs={{0,8},{4,12},{8,0},{12,4},{1,9},{5,13},{9,1},{13,5},{2,10},{6,14},... | collective-permute-start | bytes 1376264 | tf_op jit(solution)/shard_map/ppermute | solution.py:343
  34.9 0.8 %copy-start.3 = (bf16[1,2,448,256]{3,2,1,0:T(8,128)(2,1)}, bf16[1,2,448,256]{3,2,1,0:T(8,128)(2,1)S(1)}, u32[]{:S(2)}) copy-start(bf16[1,2,448,256]{3,2,1,0:T(8,128)(2,1)S(1)} %collective-permute-done.4.rest_2_) | copy-start | bytes 1376260

commit v16 on v11

--- a/solution.py
+++ b/solution.py
@@ -13,8 +13,8 @@
 dpo_beta = 0.5
 
 
-def mask_bias(length, *, group, seq, prefix_rows):
-    shape = (seq + prefix_rows, group * seq)
+def mask_bias(length, *, group, seq, prefix_rows, rows=None):
+    shape = (seq + prefix_rows if rows is None else rows, group * seq)
     key_index = lax.broadcasted_iota(jnp.int32, shape, 0)
     tok_index = lax.broadcasted_iota(jnp.int32, shape, 1) % seq
     in_suffix = key_index < seq
@@ -110,10 +110,6 @@
     heads = skv_ref.shape[-1] // HD
     qb = group * HD
 
-    @pl.when(member == 0)
-    def _():
-        bias_ref[...] = mask_bias(length, **dims)
-
     gap = lr_ref[slots_ref[0, pair]] - lr_ref[slots_ref[1, pair]]
     x = jnp.full((1, 128), -dpo_beta * gap, jnp.float32)
     weight = dpo_beta * (1.0 / (1.0 + jnp.exp(-x)))
@@ -127,6 +123,11 @@
             @pl.when(blocks == used)
             def _():
                 width = min(used * 128, seq + prefix_rows)
+
+                @pl.when((member == 0) & (h == 0))
+                def _():
+                    bias_ref[:width] = mask_bias(length, rows=width, **dims)
+
                 grads = attend_math(q_ref[0, :, q_cols], og_ref[0, :, q_cols],
                                     pkv_ref[0, 0, :width - seq, kv_cols], pkv_ref[0, 1, :width - seq, kv_cols],
                                     skv_ref[0, 0, :, kv_cols], skv_ref[0, 1, :, kv_cols], bias_ref[:width], coef,

time: 49.9 us -> 49.5 us (level)
  starting transfers between devices: 7.87 us -> 6.22 us
  waiting for transfers between devices: 5.36 us -> 6.2 us
    ppermute x1, starting transfers between devices: 4.21 us -> 2.57 us  [pipelined(): total = own + lax.ppermute(forward, 'dp', across).astype(jnp.float32)]
    ppermute x1, waiting for transfers between devices: 1.4 us -> 2.26 us  [pipelined(): total = own + lax.ppermute(forward, 'dp', across).astype(jnp.float32)]
  transfers between devices with their start and end apart: 6 -> 6, of which waited for: 3 -> 3; matrix products, arithmetic and copies ran while one was open for 0% -> 0% of each run, Pallas kernels for 62% -> 64%
where the time goes in v16:
time: 49.5 us; the launch traced here: 49.1 us
  Pallas kernels  31.2 us (63%)
  starting transfers between devices  6.22 us (13%)
  waiting for transfers between devices  6.2 us (13%)
  local copies, waits for them, and re-layouts  2.72 us (5%)
  other arithmetic  2.14 us (4%)
  between operations  0.67 us (1%)
    pallas_call x4, Pallas kernels, attend_slot(): pl.pallas_call(kernel, grid_spec=grid_spec, out_shape=out_shape, input_ou...  31.2 us
    unnamed x10, local copies, waits for them, and re-layouts  2.72 us
    ppermute x1, starting transfers between devices, pipelined(): pre_across = lax.ppermute(prefix_kv, 'dp', across)  2.58 us
    ppermute x1, starting transfers between devices, pipelined(): total = own + lax.ppermute(forward, 'dp', across).astype(jnp.float32)  2.57 us
    ppermute x1, waiting for transfers between devices, pipelined(): total = own + lax.ppermute(forward, 'dp', across).astype(jnp.float32)  2.26 us
    convert_element_type x1, other arithmetic, pipelined(): return (chain[0], chain[1], total.astype(jnp.bfloat16))  2.04 us
    ppermute x1, waiting for transfers between devices, pipelined(): lax.ppermute(relay, 'dp', partner).astype(jnp.float32)  2.01 us
    ppermute x1, waiting for transfers between devices, pipelined(): pre_across = lax.ppermute(prefix_kv, 'dp', across)  1.92 us
  transfers between devices with their start and end apart: 6, of which 3 were waited for; matrix products, arithmetic and copies ran while one was open for 0% of the time, Pallas kernels for 64%

profile of v16, /device:TPU:0, one launch (start us, length us, event | category | flops | bytes accessed | tf_op | source)
XLA Modules:
  0.0 49.1 jit_solution(5751920348882352876)
XLA Ops:
  0.6 0.6 %collective-permute-start.1 = (bf16[1,2,448,256]{3,2,1,0:T(8,128)(2,1)}, bf16[1,2,448,256]{3,2,1,0:T(8,128)(2,1)S(1)}, u32[]{:S(2)}, u32[]{:S(2)}) collective-permute-start(bf16[1,2,448,256]{3,2,1,0:T(8,128)(2,1)} %pkv_ref), channel_id=1, source_target_pairs={{0,4},{4,0},{8,12},{12,8},{1,5},{5,1},{9,13},{13,9},{2,6},{6,2},{1... | collective-permute-start | bytes 1376264 | tf_op jit(solution)/shard_map/ppermute | solution.py:324
  1.2 2.6 %collective-permute-start = (bf16[1,2,448,256]{3,2,1,0:T(8,128)(2,1)}, bf16[1,2,448,256]{3,2,1,0:T(8,128)(2,1)S(1)}, u32[]{:S(2)}, u32[]{:S(2)}) collective-permute-start(bf16[1,2,448,256]{3,2,1,0:T(8,128)(2,1)} %pkv_ref), channel_id=1, source_target_pairs={{0,8},{4,12},{8,0},{12,4},{1,9},{5,13},{9,1},{13,5},{2,10},{6,14},... | collective-permute-start | bytes 1376264 | tf_op jit(solution)/shard_map/ppermute | solution.py:323
  3.8 0.0 collective-permute-done.1.pkv_ref
  3.8 0.0 copy-start.3
  3.8 0.8 %copy-done.3 = bf16[1,2,448,256]{3,2,1,0:T(8,128)(2,1)} copy-done((bf16[1,2,448,256]{3,2,1,0:T(8,128)(2,1)}, bf16[1,2,448,256]{3,2,1,0:T(8,128)(2,1)S(1)}, u32[]{:S(2)}) %copy-start.3) | copy-done | bytes 458776
  4.5 8.6 %shard_map.103 = (bf16[8,64,2048]{2,1,0:T(8,128)(2,1)}, bf16[8,2,64,256]{3,2,1,0:T(8,128)(2,1)}, f32[1,2,448,256]{3,2,1,0:T(8,128)}) custom-call(s32[1]{0:T(128)} %bitcast.me_ref, s32[4]{0:T(128)} %bitcast.7, s32[2,4]{1,0:T(2,128)} %bitcast.3, s32[4]{0:T(128)} %len_ref.7, f32[8]{0:T(128)} %lr_ref.7, bf16[8,64,2048]{2,1,0:T(8,128)(2,1)} %q_ref.7, ...), custom_call_target="tpu_custom_call" | custom-call | flops 8800000000 | bytes 5111808 | tf_op jit(solution)/shard_map/pallas_call | solution.py:217
  13.2 1.9 %collective-permute-done.pkv_ref = bf16[1,2,448,256]{3,2,1,0:T(8,128)(2,1)S(1)} collective-permute-done((bf16[1,2,448,256]{3,2,1,0:T(8,128)(2,1)}, bf16[1,2,448,256]{3,2,1,0:T(8,128)(2,1)S(1)}, u32[]{:S(2)}, u32[]{:S(2)}) %collective-permute-start) | collective-permute-done | bytes 458784 | tf_op jit(solution)/shard_map/ppermute | solution.py:323
  15.1 0.0 copy-start.2
  15.1 0.0 collective-permute-start.2
  15.1 0.5 %collective-permute-start.4 = (f32[1,2,448,256]{3,2,1,0:T(8,128)}, f32[1,2,448,256]{3,2,1,0:T(8,128)S(1)}, u32[]{:S(2)}, u32[]{:S(2)}) collective-permute-start(f32[1,2,448,256]{3,2,1,0:T(8,128)} %get-tuple-element.30), channel_id=1, source_target_pairs={{0,4},{4,0},{8,12},{12,8},{1,5},{5,1},{9,13},{13,9},{2,6},{6,2},{1... | collective-permute-start | bytes 2752520 | tf_op jit(solution)/shard_map/ppermute | solution.py:337
  15.6 0.3 copy-done.2
  15.9 7.0 %shard_map.104 = (bf16[8,64,2048]{2,1,0:T(8,128)(2,1)}, bf16[8,2,64,256]{3,2,1,0:T(8,128)(2,1)}, f32[1,2,448,256]{3,2,1,0:T(8,128)}) custom-call(s32[1]{0:T(128)} %bitcast.me_ref, s32[4]{0:T(128)} %bitcast.8, s32[2,4]{1,0:T(2,128)} %bitcast.4, s32[4]{0:T(128)} %len_ref.7, f32[8]{0:T(128)} %lr_ref.7, ...), custom_call_target="tpu_custom_call", output_to_operand_aliasing={{0}: (9, {}), {1}: (10, {})} | custom-call | flops 8800000000 | bytes 5111808 | tf_op jit(solution)/shard_map/pallas_call | solution.py:217
  22.9 0.0 collective-permute-done.2.pkv_ref
  22.9 0.0 copy-start.4
  22.9 0.8 %copy-done.4 = bf16[1,2,448,256]{3,2,1,0:T(8,128)(2,1)} copy-done((bf16[1,2,448,256]{3,2,1,0:T(8,128)(2,1)}, bf16[1,2,448,256]{3,2,1,0:T(8,128)(2,1)S(1)}, u32[]{:S(2)}) %copy-start.4) | copy-done | bytes 458776
  23.7 0.0 copy-start
  23.7 7.9 %shard_map.105 = (bf16[8,64,2048]{2,1,0:T(8,128)(2,1)}, bf16[8,2,64,256]{3,2,1,0:T(8,128)(2,1)}, bf16[1,2,448,256]{3,2,1,0:T(8,128)(2,1)}) custom-call(s32[1]{0:T(128)} %bitcast.me_ref, s32[4]{0:T(128)} %bitcast.9, s32[2,4]{1,0:T(2,128)} %bitcast.5, s32[4]{0:T(128)} %len_ref.7, f32[8]{0:T(128)} %lr_ref.7, ...), custom_call_target="tpu_custom_call", output_to_operand_aliasing={{0}: (9, {}), {1}: (10, {})} | custom-call | flops 8800000000 | bytes 5111808 | tf_op jit(solution)/shard_map/pallas_call | solution.py:217
  31.6 0.0 collective-permute-start.3
  31.6 2.0 %collective-permute-done.3 = bf16[1,2,448,256]{3,2,1,0:T(8,128)(2,1)S(1)} collective-permute-done((bf16[1,2,448,256]{3,2,1,0:T(8,128)(2,1)}, bf16[1,2,448,256]{3,2,1,0:T(8,128)(2,1)S(1)}, u32[]{:S(2)}, u32[]{:S(2)}) %collective-permute-start.3) | collective-permute-done | bytes 458784 | tf_op jit(solution)/shard_map/ppermute | solution.py:340
  33.6 0.0 copy-done
  33.6 0.1 add_convert_fusion.1
  33.7 2.6 %collective-permute-start.5 = (bf16[1,2,448,256]{3,2,1,0:T(8,128)(2,1)S(1)}, bf16[1,2,448,256]{3,2,1,0:T(8,128)(2,1)S(1)}, u32[]{:S(2)}, u32[]{:S(2)}) collective-permute-start(bf16[1,2,448,256]{3,2,1,0:T(8,128)(2,1)S(1)} %add_convert_fusion.1), channel_id=1, source_target_pairs={{0,8},{4,12},{8,0},{12,4},{1,9},{5,13},{9,1},{13,5},{2,10},{6,14},... | collective-permute-start | bytes 1376264 | tf_op jit(solution)/shard_map/ppermute | solution.py:343
  36.3 0.0 collective-permute-done.4.rest_2_
  36.3 0.0 copy-start.1
  36.3 0.9 %copy-done.1 = f32[1,2,448,256]{3,2,1,0:T(8,128)} copy-done((f32[1,2,448,256]{3,2,1,0:T(8,128)}, f32[1,2,448,256]{3,2,1,0:T(8,128)S(1)}, u32[]{:S(2)}) %copy-start.1) | copy-done | bytes 917528
  37.2 7.6 %shard_map.106 = (bf16[8,64,2048]{2,1,0:T(8,128)(2,1)}, bf16[8,2,64,256]{3,2,1,0:T(8,128)(2,1)}, f32[1,2,448,256]{3,2,1,0:T(8,128)}) custom-call(s32[1]{0:T(128)} %bitcast.me_ref, s32[4]{0:T(128)} %bitcast.10, s32[2,4]{1,0:T(2,128)} %bitcast.6, s32[4]{0:T(128)} %len_ref.7, f32[8]{0:T(128)} %lr_ref.7, ...), custom_call_target="tpu_custom_call", output_to_operand_aliasing={{0}: (9, {}), {1}: (10, {})} | custom-call | flops 8800000000 | bytes 5111808 | tf_op jit(solution)/shard_map/pallas_call | solution.py:217
  44.8 2.3 %collective-permute-done.5 = bf16[1,2,448,256]{3,2,1,0:T(8,128)(2,1)S(1)} collective-permute-done((bf16[1,2,448,256]{3,2,1,0:T(8,128)(2,1)S(1)}, bf16[1,2,448,256]{3,2,1,0:T(8,128)(2,1)S(1)}, u32[]{:S(2)}, u32[]{:S(2)}) %collective-permute-start.5) | collective-permute-done | bytes 458784 | tf_op jit(solution)/shard_map/ppermute | solution.py:343
  47.1 2.0 %add_convert_fusion = bf16[1,2,448,256]{3,2,1,0:T(8,128)(2,1)} fusion(f32[1,2,448,256]{3,2,1,0:T(8,128)} %get-tuple-element.33, bf16[1,2,448,256]{3,2,1,0:T(8,128)(2,1)S(1)} %collective-permute-done.5), kind=kLoop, calls=%fused_computation | loop fusion | flops 688128 | bytes 1835008 | tf_op jit(solution)/shard_map/convert_element_type | solution.py:344
Async XLA Ops:
  0.6 3.1 %collective-permute-start.1 = (bf16[1,2,448,256]{3,2,1,0:T(8,128)(2,1)}, bf16[1,2,448,256]{3,2,1,0:T(8,128)(2,1)S(1)}, u32[]{:S(2)}, u32[]{:S(2)}) collective-permute-start(bf16[1,2,448,256]{3,2,1,0:T(8,128)(2,1)} %pkv_ref), channel_id=1, source_target_pairs={{0,4},{4,0},{8,12},{12,8},{1,5},{5,1},{9,13},{13,9},{2,6},{6,2},{1... | collective-permute-start | bytes 1376264 | tf_op jit(solution)/shard_map/ppermute | solution.py:324
  1.2 13.9 %collective-permute-start = (bf16[1,2,448,256]{3,2,1,0:T(8,128)(2,1)}, bf16[1,2,448,256]{3,2,1,0:T(8,128)(2,1)S(1)}, u32[]{:S(2)}, u32[]{:S(2)}) collective-permute-start(bf16[1,2,448,256]{3,2,1,0:T(8,128)(2,1)} %pkv_ref), channel_id=1, source_target_pairs={{0,8},{4,12},{8,0},{12,4},{1,9},{5,13},{9,1},{13,5},{2,10},{6,14},... | collective-permute-start | bytes 1376264 | tf_op jit(solution)/shard_map/ppermute | solution.py:323
  3.8 0.8 %copy-start.3 = (bf16[1,2,448,256]{3,2,1,0:T(8,128)(2,1)}, bf16[1,2,448,256]{3,2,1,0:T(8,128)(2,1)S(1)}, u32[]{:S(2)}) copy-start(bf16[1,2,448,256]{3,2,1,0:T(8,128)(2,1)S(1)} %collective-permute-done.1.pkv_ref) | copy-start | bytes 1376260
  15.1 0.8 %copy-start.2 = (bf16[1,2,448,256]{3,2,1,0:T(8,128)(2,1)}, bf16[1,2,448,256]{3,2,1,0:T(8,128)(2,1)S(1)}, u32[]{:S(2)}) copy-start(bf16[1,2,448,256]{3,2,1,0:T(8,128)(2,1)S(1)} %collective-permute-done.pkv_ref) | copy-start | bytes 1376260
  15.1 7.8 %collective-permute-start.2 = (bf16[1,2,448,256]{3,2,1,0:T(8,128)(2,1)S(1)}, bf16[1,2,448,256]{3,2,1,0:T(8,128)(2,1)S(1)}, u32[]{:S(2)}, u32[]{:S(2)}) collective-permute-start(bf16[1,2,448,256]{3,2,1,0:T(8,128)(2,1)S(1)} %collective-permute-done.pkv_ref), channel_id=1, source_target_pairs={{0,4},{4,0},{8,12},{12,8},{1,5},{5,1},{9,13},{13,9},{2,6},{6,2},{1... | collective-permute-start | bytes 1376264 | tf_op jit(solution)/shard_map/ppermute | solution.py:336
  15.1 21.2 %collective-permute-start.4 = (f32[1,2,448,256]{3,2,1,0:T(8,128)}, f32[1,2,448,256]{3,2,1,0:T(8,128)S(1)}, u32[]{:S(2)}, u32[]{:S(2)}) collective-permute-start(f32[1,2,448,256]{3,2,1,0:T(8,128)} %get-tuple-element.30), channel_id=1, source_target_pairs={{0,4},{4,0},{8,12},{12,8},{1,5},{5,1},{9,13},{13,9},{2,6},{6,2},{1... | collective-permute-start | bytes 2752520 | tf_op jit(solution)/shard_map/ppermute | solution.py:337
  22.9 0.8 %copy-start.4 = (bf16[1,2,448,256]{3,2,1,0:T(8,128)(2,1)}, bf16[1,2,448,256]{3,2,1,0:T(8,128)(2,1)S(1)}, u32[]{:S(2)}) copy-start(bf16[1,2,448,256]{3,2,1,0:T(8,128)(2,1)S(1)} %collective-permute-done.2.pkv_ref) | copy-start | bytes 1376260
  23.7 9.9 %copy-start = (f32[1,2,448,256]{3,2,1,0:T(8,128)S(1)}, f32[1,2,448,256]{3,2,1,0:T(8,128)}, u32[]{:S(2)}) copy-start(f32[1,2,448,256]{3,2,1,0:T(8,128)} %get-tuple-element.23) | copy-start | bytes 2752516
  31.6 2.0 %collective-permute-start.3 = (bf16[1,2,448,256]{3,2,1,0:T(8,128)(2,1)}, bf16[1,2,448,256]{3,2,1,0:T(8,128)(2,1)S(1)}, u32[]{:S(2)}, u32[]{:S(2)}) collective-permute-start(bf16[1,2,448,256]{3,2,1,0:T(8,128)(2,1)} %get-tuple-element.26), channel_id=1, source_target_pairs={{0,4},{4,0},{8,12},{12,8},{1,5},{5,1},{9,13},{13,9},{2,6},{6,2},{1... | collective-permute-start | bytes 1376264 | tf_op jit(solution)/shard_map/ppermute | solution.py:340
  33.7 13.4 %collective-permute-start.5 = (bf16[1,2,448,256]{3,2,1,0:T(8,128)(2,1)S(1)}, bf16[1,2,448,256]{3,2,1,0:T(8,128)(2,1)S(1)}, u32[]{:S(2)}, u32[]{:S(2)}) collective-permute-start(bf16[1,2,448,256]{3,2,1,0:T(8,128)(2,1)S(1)} %add_convert_fusion.1), channel_id=1, source_target_pairs={{0,8},{4,12},{8,0},{12,4},{1,9},{5,13},{9,1},{13,5},{2,10},{6,14},... | collective-permute-start | bytes 1376264 | tf_op jit(solution)/shard_map/ppermute | solution.py:343
  36.3 0.9 %copy-start.1 = (f32[1,2,448,256]{3,2,1,0:T(8,128)}, f32[1,2,448,256]{3,2,1,0:T(8,128)S(1)}, u32[]{:S(2)}) copy-start(f32[1,2,448,256]{3,2,1,0:T(8,128)S(1)} %collective-permute-done.4.rest_2_) | copy-start | bytes 2752516
